TPU v7x, 32 devices: a whole 2x2x4 slice. The times are simulated.
32 devices in a mesh: groups: 2 (over y), head: 8 (over z, x), req: 2 (over core).
Axes of the slice: x: 2, y: 2, z: 4, core: 2. Of those that a mesh axis runs over, the one named last changes fastest.
Arguments:
- tokens: bfloat16 [2, 64, 2048], P('req', ('groups', 'head')), parts along dimension 1, may hold values from -4 to 4
- ssm_state: bfloat16 [2, 8, 128, 64, 128], P('req', 'groups', 'head'), parts along dimension 1, may hold values from -2 to 2
- conv_x_state: bfloat16 [2, 8, 3, 8192], P('req', 'groups', None, 'head'), parts along dimension 1, may hold values from -6 to 6
- conv_bc_state: bfloat16 [2, 8, 3, 2048], P('req', 'groups', None, 'head'), parts along dimension 1, may hold values from -6 to 6
- expert_ids: int32 [2, 64, 2], P('req', ('groups', 'head')), parts along dimension 1, may hold values from 0 to 7, all different within a row; in each aligned block of 4 rows (0 to 3, 4 to 7, ..., all dimensions but the last counted through in order) at most 2 rows name the same one
- mixer_gain: float32 [2048], replicated, may hold values from 0.5 to 1.5
- weight_xz: bfloat16 [2048, 16384], P(None, 'head'), may hold values from -0.125 to 0.125
- weight_bc: bfloat16 [2048, 2048], P(None, 'head'), may hold values from -0.125 to 0.125
- weight_delta: bfloat16 [2048, 128], P(None, 'head'), may hold values from -0.125 to 0.125
- delta_bias: float32 [128], P('head'), may hold values from -4 to -1
- decay_log: float32 [128], P('head'), may hold values from 0 to 2.8
- skip_gain: float32 [128], P('head'), may hold values from 0.5 to 1.5
- conv_x_kernel: float32 [4, 8192], P(None, 'head'), may hold values from -3 to 3
- conv_x_bias: float32 [8192], P('head'), may hold values from -3 to 3
- conv_bc_kernel: float32 [4, 2048], P(None, 'head'), may hold values from -3 to 3
- conv_bc_bias: float32 [2048], P('head'), may hold values from -3 to 3
- gated_gain: float32 [8192], P('head'), may hold values from 0.5 to 1.5
- weight_out: bfloat16 [8192, 2048], P('head'), may hold values from -0.0625 to 0.0625
- ffn_gain: float32 [2048], replicated, may hold values from 0.5 to 1.5
- router_weight: bfloat16 [2048, 8], replicated, may hold values from -0.125 to 0.125
- weight_up: bfloat16 [2048, 16384], P(None, 'head'), may hold values from -0.125 to 0.125
- weight_down: bfloat16 [16384, 2048], P('head'), may hold values from -0.125 to 0.125
Outputs:
- layer_out: bfloat16 [2, 64, 2048], P('req', ('groups', 'head')), parts along dimension 1
- new_state: bfloat16 [2, 8, 128, 64, 128], P('req', 'groups', 'head'), parts along dimension 1
- new_conv_x: bfloat16 [2, 8, 3, 8192], P('req', 'groups', None, 'head'), parts along dimension 1
- new_conv_bc: bfloat16 [2, 8, 3, 2048], P('req', 'groups', None, 'head'), parts along dimension 1
There are 2 independent parts, one for each index of `groups`. A program takes and returns all parts, laid end to end along the dimension named above; an argument that names none is the same for every part. Nothing has to cross between parts.
Inputs may be any that keep to these rules, and one draw needn't show every extreme that they name: `expert_ids`: each row names 2 different experts; in each aligned block of 4 rows no expert is named more than 2 times, and the bound is reached.
All inputs are finite; a program needn't handle non-finite values.
Results may differ from a plain program's by a relative error of at most 0.017.
Values may be sent and summed in bfloat16 or wider, within the bound.
No kernel may reach another device: no remote copies, remote signals or barrier semaphores. Data moves between devices by JAX's collectives and lax.ppermute only.
A program may use at most 128 MiB of HBM per device.

v0:
```python
import jax
import jax.numpy as jnp
from jax import lax
from jax.sharding import PartitionSpec as P

HEADS = 128
G = 8
EXPERTS = 8
TOP = 2
STEPS = 8
CAP = 2


eps = 1e-05
highest = lax.Precision.HIGHEST


def norm_rows(values, gain):
    mean_square = jnp.mean(values * values, axis=-1, keepdims=True)
    return values * lax.rsqrt(mean_square + eps) * gain


def causal_conv(past_rows, fresh_rows, kernel, offset):
    window = jnp.concatenate([past_rows, fresh_rows], axis=1)
    window_wide = window.astype(jnp.float32)
    fresh_count = fresh_rows.shape[1]
    running = offset + kernel[0] * window_wide[:, 0:fresh_count]
    for tap_index in range(1, kernel.shape[0]):
        running = running + kernel[tap_index] * window_wide[:, tap_index : tap_index + fresh_count]
    return (jax.nn.silu(running), window[:, fresh_count:])


def route_share(ffn_in, router_weight, chosen_ids):
    logits = jnp.dot(ffn_in, router_weight, preferred_element_type=jnp.float32)
    match_table = (chosen_ids[:, :, None] == jnp.arange(EXPERTS)[None, None, :]).astype(jnp.float32)
    picked = jnp.einsum("mke,me->mk", match_table, logits, precision=highest)
    first_weight = jax.nn.sigmoid(picked[:, 0] - picked[:, 1])
    return jnp.stack([first_weight, 1.0 - first_weight], axis=1)


def expert_hidden(rows_in, weight_up):
    return jnp.square(
        jnp.maximum(jnp.dot(rows_in, weight_up, preferred_element_type=jnp.float32), 0.0)
    ).astype(jnp.bfloat16)


def shards(
    tokens,
    ssm_state,
    conv_x_state,
    conv_bc_state,
    expert_ids,
    mixer_gain,
    weight_xz,
    weight_bc,
    weight_delta,
    delta_bias,
    decay_log,
    skip_gain,
    conv_x_kernel,
    conv_x_bias,
    conv_bc_kernel,
    conv_bc_bias,
    gated_gain,
    weight_out,
    ffn_gain,
    router_weight,
    weight_up,
    weight_down,
):
    head_count = lax.axis_size("head")
    my_index = lax.axis_index("head")
    tok_local = tokens.shape[1]
    width = tokens.shape[2]
    requests = ssm_state.shape[1]
    heads_local = ssm_state.shape[2]
    head_dim = ssm_state.shape[3]
    state_dim = ssm_state.shape[4]
    gathered = lax.all_gather(tokens, "head", axis=1, tiled=True)
    inputs = gathered.reshape(requests * STEPS, width)
    normed = norm_rows(inputs.astype(jnp.float32), mixer_gain).astype(jnp.bfloat16)
    proj_xz = jnp.dot(normed, weight_xz, preferred_element_type=jnp.float32).reshape(
        requests, STEPS, heads_local, 2, head_dim
    )
    x_fresh = (
        proj_xz[:, :, :, 0, :].reshape(requests, STEPS, heads_local * head_dim).astype(jnp.bfloat16)
    )
    z_gate = proj_xz[:, :, :, 1, :]
    bc_fresh = (
        jnp.dot(normed, weight_bc, preferred_element_type=jnp.float32)
        .reshape(requests, STEPS, -1)
        .astype(jnp.bfloat16)
    )
    delta = jax.nn.softplus(
        jnp.dot(normed, weight_delta, preferred_element_type=jnp.float32).reshape(
            requests, STEPS, heads_local
        )
        + delta_bias
    )
    x_conv, conv_x_new = causal_conv(conv_x_state[0], x_fresh, conv_x_kernel, conv_x_bias)
    bc_conv, conv_bc_new = causal_conv(conv_bc_state[0], bc_fresh, conv_bc_kernel, conv_bc_bias)
    bc_conv = bc_conv.astype(jnp.bfloat16)
    bc_list = [
        lax.all_gather(bc_conv[:, step_index], "head", axis=1, tiled=True)
        for step_index in range(STEPS)
    ]
    head_global = my_index * heads_local + jnp.arange(heads_local)
    group_pick = (head_global[:, None] // (HEADS // G) == jnp.arange(G)[None, :]).astype(
        jnp.float32
    )
    x_heads = x_conv.reshape(requests, STEPS, heads_local, head_dim)
    decay_rate = jnp.exp(delta * -jnp.exp(decay_log))
    ssm_now = ssm_state[0]
    readings = []
    for step_index in range(STEPS):
        bc_values = bc_list[step_index].astype(jnp.float32).reshape(requests, 2, G, state_dim)
        b_heads = jnp.einsum("rgn,hg->rhn", bc_values[:, 0], group_pick, precision=highest)
        c_heads = jnp.einsum("rgn,hg->rhn", bc_values[:, 1], group_pick, precision=highest)
        x_step = x_heads[:, step_index]
        fresh_state = (
            decay_rate[:, step_index, :, None, None] * ssm_now.astype(jnp.float32)
            + (delta[:, step_index, :, None] * x_step)[..., None] * b_heads[:, :, None, :]
        )
        readings.append(
            jnp.einsum("rhpn,rhn->rhp", fresh_state, c_heads, precision=highest)
            + skip_gain[:, None] * x_step
        )
        ssm_now = fresh_state.astype(jnp.bfloat16)
    gated_out = jnp.stack(readings, axis=1) * jax.nn.silu(z_gate)
    group_normed = (
        norm_rows(gated_out, gated_gain.reshape(heads_local, head_dim))
        .astype(jnp.bfloat16)
        .reshape(requests * STEPS, heads_local * head_dim)
    )
    per_expert = head_count // EXPERTS
    mixer_out = lax.psum_scatter(
        jnp.dot(group_normed, weight_out, preferred_element_type=jnp.float32),
        "head",
        scatter_dimension=0,
        tiled=True,
    )
    residual = (tokens[0].astype(jnp.float32) + mixer_out).astype(jnp.bfloat16)
    ffn_in = norm_rows(residual.astype(jnp.float32), ffn_gain).astype(jnp.bfloat16)
    share = route_share(ffn_in, router_weight, expert_ids[0])
    chosen = expert_ids[0].reshape(-1)
    onehot = (chosen[:, None] == jnp.arange(EXPERTS)[None, :]).astype(jnp.int32)
    earlier = jnp.cumsum(onehot, axis=0) - onehot
    position = jnp.sum(earlier * onehot, axis=1)
    slot_index = chosen * CAP + position
    place = (jnp.arange(EXPERTS * CAP)[:, None] == slot_index[None, :]).astype(jnp.bfloat16)
    routed_rows = jnp.repeat(ffn_in, TOP, axis=0)
    packed = jnp.dot(place, routed_rows, preferred_element_type=jnp.float32).astype(jnp.bfloat16)
    outgoing = jnp.repeat(packed.reshape(EXPERTS, CAP, width), per_expert, axis=0)
    received = lax.all_to_all(outgoing, "head", split_axis=0, concat_axis=0, tiled=True)
    flat_rows = received.reshape(-1, width)
    hidden = expert_hidden(flat_rows, weight_up)
    computed = jnp.dot(hidden, weight_down, preferred_element_type=jnp.float32).reshape(
        received.shape[0], received.shape[1], width
    )
    returned = lax.all_to_all(
        computed.astype(jnp.bfloat16), "head", split_axis=0, concat_axis=0, tiled=True
    ).astype(computed.dtype)
    summed = (
        returned.reshape(EXPERTS, per_expert, CAP, width).sum(axis=1).reshape(EXPERTS * CAP, width)
    )
    per_route = jnp.dot(place.astype(jnp.float32).T, summed, precision=highest).reshape(
        tok_local, TOP, width
    )
    combined = jnp.sum(share[:, :, None] * per_route, axis=1)
    layer_out = (residual.astype(jnp.float32) + combined).astype(jnp.bfloat16)
    return (layer_out[None], ssm_now[None], conv_x_new[None], conv_bc_new[None])


def solution(mesh):
    return jax.shard_map(
        shards,
        mesh=mesh,
        in_specs=(
            P("req", ("groups", "head"), None),
            P("req", "groups", "head", None, None),
            P("req", "groups", None, "head"),
            P("req", "groups", None, "head"),
            P("req", ("groups", "head"), None),
            P(),
            P(None, "head"),
            P(None, "head"),
            P(None, "head"),
            P("head"),
            P("head"),
            P("head"),
            P(None, "head"),
            P("head"),
            P(None, "head"),
            P("head"),
            P("head"),
            P("head", None),
            P(),
            P(),
            P(None, "head"),
            P("head", None),
        ),
        out_specs=(
            P("req", ("groups", "head"), None),
            P("req", "groups", "head", None, None),
            P("req", "groups", None, "head"),
            P("req", "groups", None, "head"),
        ),
        check_vma=False,
    )
```

profile of v0, /device:TPU:0, one launch (start us, length us, event | category | flops | bytes accessed | tf_op | source)
XLA Modules:
  0.0 379.3 jit_solution(9792849408418765199)
XLA Ops:
  7.2 0.8 copy.187
  8.1 32.5 %all_gather.27 = bf16[1,32,2048]{2,0,1:T(2,128)(2,1)S(1)} all-gather(bf16[1,4,2048]{2,0,1:T(2,128)(2,1)S(1)} %copy.187), channel_id=1, replica_groups=mesh['groups'=2,'head'=8,'req'=2] {'head'}, dimensions={1}, use_global_device_ids=true | all-gather | bytes 147456 | tf_op jit(solution)/shard_map/all_gather | solution.py:79
  40.6 0.2 fusion.62
  40.9 0.7 copy.290
  41.6 0.8 fusion.168
  42.4 1.0 convolution_convert_fusion.2
  43.5 0.7 multiply_convert_fusion.2
  44.2 20.7 %all-gather = bf16[4,1,2048]{2,1,0:T(2,128)(2,1)S(1)} all-gather(bf16[4,1,256]{2,1,0:T(2,128)(2,1)S(1)} %get-tuple-element.73), channel_id=2, replica_groups=mesh['groups'=2,'head'=8,'req'=2] {'head'}, dimensions={2}, use_global_device_ids=true | all-gather | bytes 18432 | tf_op jit(solution)/shard_map/all_gather | solution.py:104
  65.0 0.2 convolution_bitcast_fusion.7
  65.2 0.8 fusion.118
  66.0 16.4 %all-gather.1 = bf16[4,1,2048]{2,1,0:T(2,128)(2,1)S(1)} all-gather(bf16[4,1,256]{2,1,0:T(2,128)(2,1)S(1)} %get-tuple-element.72), channel_id=3, replica_groups=mesh['groups'=2,'head'=8,'req'=2] {'head'}, dimensions={2}, use_global_device_ids=true | all-gather | bytes 18432 | tf_op jit(solution)/shard_map/all_gather | solution.py:104
  82.5 0.2 convolution_bitcast_fusion.6
  82.7 0.8 fusion.117
  83.5 18.4 %all-gather.2 = bf16[4,1,2048]{2,1,0:T(2,128)(2,1)S(1)} all-gather(bf16[4,1,256]{2,1,0:T(2,128)(2,1)S(1)} %get-tuple-element.71), channel_id=4, replica_groups=mesh['groups'=2,'head'=8,'req'=2] {'head'}, dimensions={2}, use_global_device_ids=true | all-gather | bytes 18432 | tf_op jit(solution)/shard_map/all_gather | solution.py:104
  102.0 0.2 convolution_bitcast_fusion.5
  102.2 0.8 fusion.116
  103.0 16.4 %all-gather.3 = bf16[4,1,2048]{2,1,0:T(2,128)(2,1)S(1)} all-gather(bf16[4,1,256]{2,1,0:T(2,128)(2,1)S(1)} %get-tuple-element.70), channel_id=5, replica_groups=mesh['groups'=2,'head'=8,'req'=2] {'head'}, dimensions={2}, use_global_device_ids=true | all-gather | bytes 18432 | tf_op jit(solution)/shard_map/all_gather | solution.py:104
  119.5 0.2 convolution_bitcast_fusion.4
  119.7 0.8 fusion.115
  120.5 18.4 %all-gather.4 = bf16[4,1,2048]{2,1,0:T(2,128)(2,1)S(1)} all-gather(bf16[4,1,256]{2,1,0:T(2,128)(2,1)S(1)} %get-tuple-element.69), channel_id=6, replica_groups=mesh['groups'=2,'head'=8,'req'=2] {'head'}, dimensions={2}, use_global_device_ids=true | all-gather | bytes 18432 | tf_op jit(solution)/shard_map/all_gather | solution.py:104
  139.0 0.8 convolution_bitcast_fusion.3
  139.8 0.8 fusion.114
  140.6 16.4 %all-gather.5 = bf16[4,1,2048]{2,1,0:T(2,128)(2,1)S(1)} all-gather(bf16[4,1,256]{2,1,0:T(2,128)(2,1)S(1)} %get-tuple-element.68), channel_id=7, replica_groups=mesh['groups'=2,'head'=8,'req'=2] {'head'}, dimensions={2}, use_global_device_ids=true | all-gather | bytes 18432 | tf_op jit(solution)/shard_map/all_gather | solution.py:104
  157.2 0.8 convolution_bitcast_fusion.2
  157.9 0.8 fusion.113
  158.7 18.4 %all-gather.6 = bf16[4,1,2048]{2,1,0:T(2,128)(2,1)S(1)} all-gather(bf16[4,1,256]{2,1,0:T(2,128)(2,1)S(1)} %get-tuple-element.67), channel_id=8, replica_groups=mesh['groups'=2,'head'=8,'req'=2] {'head'}, dimensions={2}, use_global_device_ids=true | all-gather | bytes 18432 | tf_op jit(solution)/shard_map/all_gather | solution.py:104
  177.3 0.8 convolution_bitcast_fusion.1
  178.0 0.8 fusion.112
  178.8 16.6 %all-gather.7 = bf16[4,1,2048]{2,1,0:T(2,128)(2,1)S(1)} all-gather(bf16[4,1,256]{2,1,0:T(2,128)(2,1)S(1)} %get-tuple-element.66), channel_id=9, replica_groups=mesh['groups'=2,'head'=8,'req'=2] {'head'}, dimensions={2}, use_global_device_ids=true | all-gather | bytes 18432 | tf_op jit(solution)/shard_map/all_gather | solution.py:104
  195.5 0.8 convolution_bitcast_fusion
  196.3 0.8 fusion.111
  197.1 12.4 %copy.190 = bf16[2048,2048]{0,1:T(8,128)(2,1)} copy(bf16[2048,2048]{1,0:T(8,128)(2,1)} %param.28) | data formatting | bytes 16777216 | tf_op args[6]
  209.6 7.2 %fusion.74 = f32[4,8,16,2,64]{4,1,3,2,0:T(8,128)S(1)} fusion(bf16[16,2,64,2048,1]{3,2,1,0,4:T(8,128)(2,1)} %bitcast.433, bf16[1,32,2048]{2,1,0:T(8,128)(2,1)S(1)} %get-tuple-element.33, f32[2048]{0:T(1024)S(1)} %copy-done.31, f32[32]{0:T(128)S(1)} %add_rsqrt_fusion.2), kind=kOutput, calls=%fused_computation.102 | convolution fusion | flops 268697600 | bytes 8790144 | tf_op jit(solution)/shard_map/dot_general | solution.py:82
  217.3 0.2 reshape.348
  217.6 0.2 multiply_exponential_fusion
  218.2 4.3 %fusion.24 = f32[4,16,1,64]{3,2,1,0:T(1,128)S(1)} fusion(f32[4,16,128,1]{2,3,1,0:T(1,128)} %bitcast.467, bf16[1,4,16,64,128]{4,3,2,1,0:T(8,128)(2,1)S(1)} %copy-done.1, f32[4,16,128]{2,1,0:T(8,128)S(1)} %convolution_bitcast_fusion.7, f32[4,16,64]{2,1,0:T(8,128)S(1)} %get-tuple-element.49, f32[4,16]{1,0:T(4,128)S(1)} %bitcast.496), kind=kOutput, calls=%fused_computation.43 | convolution fusion | flops 8388608 | bytes 1147136 | tf_op jit(solution)/shard_map/rhpn,rhn->rhp/dot_general | solution.py:125
  222.5 5.0 %fusion.22 = f32[4,16,1,64]{3,2,1,0:T(1,128)S(1)} fusion(f32[4,16,128,1]{2,3,1,0:T(1,128)} %bitcast.468, f32[4,16,128]{2,1,0:T(8,128)S(1)} %convolution_bitcast_fusion.6, f32[4,16,64]{2,1,0:T(8,128)S(1)} %get-tuple-element.48, f32[4,16]{1,0:T(4,128)S(1)} %bitcast.491, bf16[1,4,16,64,128]{4,3,2,1,0:T(8,128)(2,1)S(1)} %copy-done.1, ...), kind=kOutput, calls=%fused_computation.41 | convolution fusion | flops 11010048 | bytes 1196544 | tf_op jit(solution)/shard_map/rhpn,rhn->rhp/dot_general | solution.py:125
  227.5 5.3 %fusion.20 = f32[4,16,1,64]{3,2,1,0:T(1,128)S(1)} fusion(f32[4,16,128,1]{2,3,1,0:T(1,128)S(1)} %bitcast.469, f32[4,16,128]{2,1,0:T(8,128)S(1)} %convolution_bitcast_fusion.5, f32[4,16,64]{2,1,0:T(8,128)S(1)} %get-tuple-element.47, f32[4,16]{1,0:T(4,128)S(1)} %bitcast.487, f32[4,16,128]{2,1,0:T(8,128)S(1)} %convolution_bitcast_fusion.6, ...), kind=kOutput, calls=%fused_computation.38 | convolution fusion | flops 13631488 | bytes 1245952 | tf_op jit(solution)/shard_map/rhpn,rhn->rhp/dot_general | solution.py:125
  232.9 3.2 fusion.17
  236.1 6.9 %fusion.18 = f32[4,16,1,64]{3,2,1,0:T(1,128)S(1)} fusion(f32[4,16,128,1]{2,3,1,0:T(1,128)S(1)} %bitcast.470, f32[4,16,128]{2,1,0:T(8,128)S(1)} %convolution_bitcast_fusion.4, f32[4,16,64]{2,1,0:T(8,128)S(1)} %get-tuple-element.46, f32[4,16]{1,0:T(4,128)S(1)} %bitcast.485, f32[4,16,128]{2,1,0:T(8,128)S(1)} %convolution_bitcast_fusion.5, ...), kind=kOutput, calls=%fused_computation.35 | convolution fusion | flops 16252928 | bytes 1295360 | tf_op jit(solution)/shard_map/rhpn,rhn->rhp/dot_general | solution.py:125
  243.1 3.6 fusion.16
  246.7 4.7 %fusion.14 = f32[4,16,1,64]{3,2,1,0:T(1,128)S(1)} fusion(f32[4,16,128,1]{2,3,1,0:T(1,128)S(1)} %bitcast.472, f32[4,16,128]{2,1,0:T(8,128)S(1)} %copy-done.8, f32[4,16,64]{2,1,0:T(8,128)S(1)} %get-tuple-element.44, f32[4,16]{1,0:T(4,128)S(1)} %bitcast.511, bf16[4,16,64,128]{3,2,1,0:T(8,128)(2,1)S(1)} %fusion.17, f32[4,16,128]{2,1,0:T(8,128)S(1)} %copy-done.6, ...), kind=kOutput, calls=%fused_computation.29 | convolution fusion | flops 11010048 | bytes 1196544 | tf_op jit(solution)/shard_map/rhpn,rhn->rhp/dot_general | solution.py:125
  251.4 5.3 %fusion.12 = f32[4,16,1,64]{3,2,1,0:T(1,128)S(1)} fusion(f32[4,16,128,1]{2,3,1,0:T(1,128)S(1)} %bitcast.473, f32[4,16,128]{2,1,0:T(8,128)S(1)} %copy-done.10, f32[4,16,64]{2,1,0:T(8,128)S(1)} %get-tuple-element.43, f32[4,16]{1,0:T(4,128)S(1)} %bitcast.508, f32[4,16,128]{2,1,0:T(8,128)S(1)} %copy-done.8, f32[4,16,64]{2,1,0:T(8,128)S(1)} %get-tuple-element.44, ...), kind=kOutput, calls=%fused_computation.26 | convolution fusion | flops 13631488 | bytes 1245952 | tf_op jit(solution)/shard_map/rhpn,rhn->rhp/dot_general | solution.py:125
  256.8 6.7 %fusion.6 = f32[4,16,1,64]{3,2,1,0:T(1,128)S(1)} fusion(f32[4,16,128,1]{2,3,1,0:T(1,128)S(1)} %bitcast.474, f32[4,16,128]{2,1,0:T(8,128)S(1)} %copy-done.12, f32[4,16,64]{2,1,0:T(8,128)S(1)} %get-tuple-element.42, f32[4,16]{1,0:T(4,128)S(1)} %bitcast.506, f32[4,16,128]{2,1,0:T(8,128)S(1)} %copy-done.10, f32[4,16,64]{2,1,0:T(8,128)S(1)} %get-tuple-element.43, ...), kind=kOutput, calls=%fused_computation.19 | convolution fusion | flops 16252928 | bytes 1295360 | tf_op jit(solution)/shard_map/rhpn,rhn->rhp/dot_general | solution.py:125
  263.6 0.4 stack.42
  264.0 0.8 fusion.70
  264.9 0.8 copy.219
  266.4 3.7 fusion.84
  270.4 7.0 %add_convert_fusion = bf16[1,4,16,64,128]{4,3,2,1,0:T(8,128)(2,1)} fusion(bf16[1,4,16,64,128]{4,3,2,1,0:T(8,128)(2,1)S(1)} %copy-done.1, f32[4,16,128]{2,1,0:T(8,128)S(1)} %copy-done.13, f32[4,16,64]{2,1,0:T(8,128)S(1)} %get-tuple-element.42, f32[4,16,128]{2,1,0:T(8,128)S(1)} %copy-done.11, f32[4,16,64]{2,1,0:T(8,128)S(1)} %get-tuple-element.43, ...), kind=kLoop, calls=%fused_computation.12 | loop fusion | flops 20971520 | bytes 2492416 | tf_op jit(solution)/shard_map/convert_element_type | solution.py:128
  277.7 0.2 select_reduce_fusion
  278.1 0.6 copy.223
  278.7 0.6 copy.224
  279.3 0.6 dynamic-slice
  280.5 59.2 %all-reduce.3.cloned.1.call-done = f32[32,2048]{1,0:T(8,128)} async-done(((f32[32,2048]{1,0:T(8,128)}), f32[32,2048]{1,0:T(8,128)}) %all-reduce.3.cloned.1.call-update) | async-done | bytes 262160
  339.8 1.0 fusion.89
  341.2 0.7 reshape_broadcast_in_dim_reshape.3
  341.9 3.9 %all-to-all-start = ((bf16[8,2,2048]{2,1,0:T(2,128)(2,1)}), bf16[8,2,2048]{2,1,0:T(2,128)(2,1)S(1)}, u32[]{:S(2)}, u32[]{:S(2)}) async-start(bf16[8,2,2048]{2,1,0:T(2,128)(2,1)} %reshape_broadcast_in_dim_reshape.3), calls=%async_computation | async-start | bytes 131072 | tf_op jit(solution)/shard_map/all_to_all | solution.py:154
  345.7 0.2 fusion.119
  346.0 6.6 %all-to-all-done = bf16[8,2,2048]{2,1,0:T(2,128)(2,1)S(1)} async-done(((bf16[8,2,2048]{2,1,0:T(2,128)(2,1)}), bf16[8,2,2048]{2,1,0:T(2,128)(2,1)S(1)}, u32[]{:S(2)}, u32[]{:S(2)}) %all-to-all-start) | async-done | bytes 65568 | tf_op jit(solution)/shard_map/all_to_all | solution.py:154
  352.7 8.0 %convolution_convert_fusion.1 = bf16[16,2048]{1,0:T(8,128)(2,1)S(1)} fusion(bf16[2048,2048]{1,0:T(8,128)(2,1)} %param.43, bf16[16,2048]{1,0:T(8,128)(2,1)S(1)} %reshape.358, bf16[2048,2048]{1,0:T(8,128)(2,1)} %param.42), kind=kOutput, calls=%fused_computation.6 | convolution fusion | flops 268566528 | bytes 16908288 | tf_op jit(solution)/shard_map/dot_general | solution.py:157
  360.7 0.7 convert_element_type.233
  361.4 3.3 all-to-all-start.1
  364.8 6.8 %all-to-all-done.1 = bf16[8,2,2048]{2,1,0:T(2,128)(2,1)S(1)} async-done(((bf16[8,2,2048]{2,1,0:T(2,128)(2,1)}), bf16[8,2,2048]{2,1,0:T(2,128)(2,1)S(1)}, u32[]{:S(2)}, u32[]{:S(2)}) %all-to-all-start.1) | async-done | bytes 65568 | tf_op jit(solution)/shard_map/all_to_all | solution.py:160
  371.8 0.6 fusion.106
  (163 shorter events, 3.9 us)
Async XLA Ops:
  7.2 35.3 %copy-start = (bf16[2048,256]{1,0:T(8,128)(2,1)S(1)}, bf16[2048,256]{1,0:T(8,128)(2,1)}, u32[]{:S(2)}) copy-start(bf16[2048,256]{1,0:T(8,128)(2,1)} %param.29) | copy-start | bytes 3145732
  7.2 190.0 %copy-start.46 = (f32[16]{0:T(128)S(1)}, f32[16]{0:T(128)}, u32[]{:S(2)}) copy-start(f32[16]{0:T(128)} %param.32) | copy-start | bytes 196
  7.2 332.6 %all-reduce.3.cloned.1.call-start = ((), (), s32[]{:S(2)}) async-start(), calls=%async_computation.2 | async-start | bytes 524288
  197.1 12.4 %copy-start.31 = (f32[2048]{0:T(1024)S(1)}, f32[2048]{0:T(1024)}, u32[]{:S(2)}) copy-start(f32[2048]{0:T(1024)} %param.27) | copy-start | bytes 24580
  209.5 7.5 %copy-start.21 = (bf16[1,4,3,1024]{3,1,2,0:T(4,128)(2,1)S(1)}, bf16[1,4,3,1024]{3,1,2,0:T(4,128)(2,1)}, u32[]{:S(2)}) copy-start(bf16[1,4,3,1024]{3,1,2,0:T(4,128)(2,1)} %param.24) | copy-start | bytes 73732
  209.5 7.5 %copy-start.30 = (f32[4,1024]{1,0:T(4,128)S(1)}, f32[4,1024]{1,0:T(4,128)}, u32[]{:S(2)}) copy-start(f32[4,1024]{1,0:T(4,128)} %param.34) | copy-start | bytes 49156
  209.5 7.6 %copy-start.41 = (f32[1024]{0:T(1024)S(1)}, f32[1024]{0:T(1024)}, u32[]{:S(2)}) copy-start(f32[1024]{0:T(1024)} %param.35) | copy-start | bytes 12292
  216.8 0.8 copy-start.44
  216.8 0.8 copy-start.47
  216.8 1.4 copy-start.1
  217.9 18.1 %copy-start.22 = (f32[4,1,16]{2,1,0:T(1,128)}, f32[4,1,16]{2,1,0:T(1,128)S(1)}, u32[]{:S(2)}) copy-start(f32[4,1,16]{2,1,0:T(1,128)S(1)} %get-tuple-element.54) | copy-start | bytes 772
  217.9 18.1 %copy-start.24 = (f32[4,1,16]{2,1,0:T(1,128)}, f32[4,1,16]{2,1,0:T(1,128)S(1)}, u32[]{:S(2)}) copy-start(f32[4,1,16]{2,1,0:T(1,128)S(1)} %get-tuple-element.55) | copy-start | bytes 772
  217.9 18.1 %copy-start.26 = (f32[4,1,16]{2,1,0:T(1,128)}, f32[4,1,16]{2,1,0:T(1,128)S(1)}, u32[]{:S(2)}) copy-start(f32[4,1,16]{2,1,0:T(1,128)S(1)} %get-tuple-element.56) | copy-start | bytes 772
  217.9 18.1 %copy-start.28 = (f32[4,1,16]{2,1,0:T(1,128)}, f32[4,1,16]{2,1,0:T(1,128)S(1)}, u32[]{:S(2)}) copy-start(f32[4,1,16]{2,1,0:T(1,128)S(1)} %get-tuple-element.57) | copy-start | bytes 772
  218.0 38.8 %copy-start.32 = (f32[4,1,16]{2,1,0:T(1,128)}, f32[4,1,16]{2,1,0:T(1,128)S(1)}, u32[]{:S(2)}) copy-start(f32[4,1,16]{2,1,0:T(1,128)S(1)} %get-tuple-element.50) | copy-start | bytes 772
  218.0 38.8 %copy-start.34 = (f32[4,1,16]{2,1,0:T(1,128)}, f32[4,1,16]{2,1,0:T(1,128)S(1)}, u32[]{:S(2)}) copy-start(f32[4,1,16]{2,1,0:T(1,128)S(1)} %get-tuple-element.51) | copy-start | bytes 772
  218.0 38.8 %copy-start.36 = (f32[4,1,16]{2,1,0:T(1,128)}, f32[4,1,16]{2,1,0:T(1,128)S(1)}, u32[]{:S(2)}) copy-start(f32[4,1,16]{2,1,0:T(1,128)S(1)} %get-tuple-element.52) | copy-start | bytes 772
  218.0 38.8 %copy-start.38 = (f32[4,1,16]{2,1,0:T(1,128)}, f32[4,1,16]{2,1,0:T(1,128)S(1)}, u32[]{:S(2)}) copy-start(f32[4,1,16]{2,1,0:T(1,128)S(1)} %get-tuple-element.53) | copy-start | bytes 772
  218.1 38.6 %copy-start.2 = (f32[4,16,64]{2,1,0:T(8,128)}, f32[4,16,64]{2,1,0:T(8,128)S(1)}, u32[]{:S(2)}) copy-start(f32[4,16,64]{2,1,0:T(8,128)S(1)} %get-tuple-element.44) | copy-start | bytes 49156
  218.2 38.6 %copy-start.4 = (f32[4,16,64]{2,1,0:T(8,128)}, f32[4,16,64]{2,1,0:T(8,128)S(1)}, u32[]{:S(2)}) copy-start(f32[4,16,64]{2,1,0:T(8,128)S(1)} %get-tuple-element.45) | copy-start | bytes 49156
  222.5 5.0 %copy-start.15 = (f32[16,4,128]{2,0,1:T(8,128)S(1)}, f32[16,4,128]{2,0,1:T(8,128)}, u32[]{:S(2)}) copy-start(f32[16,4,128]{2,0,1:T(8,128)} %fusion.116) | copy-start | bytes 98308
  232.9 3.2 copy-start.16
  236.1 7.0 %copy-start.6 = (f32[4,16,128]{2,1,0:T(8,128)S(1)}, f32[4,16,128]{2,1,0:T(8,128)}, u32[]{:S(2)}) copy-start(f32[4,16,128]{2,1,0:T(8,128)} %convolution_bitcast_fusion.3) | copy-start | bytes 98308
  236.1 7.0 %copy-start.17 = (f32[16,4,128]{2,0,1:T(8,128)S(1)}, f32[16,4,128]{2,0,1:T(8,128)}, u32[]{:S(2)}) copy-start(f32[16,4,128]{2,0,1:T(8,128)} %fusion.114) | copy-start | bytes 98308
  243.0 3.6 copy-start.8
  243.0 3.6 copy-start.18
  246.6 4.7 %copy-start.10 = (f32[4,16,128]{2,1,0:T(8,128)S(1)}, f32[4,16,128]{2,1,0:T(8,128)}, u32[]{:S(2)}) copy-start(f32[4,16,128]{2,1,0:T(8,128)} %convolution_bitcast_fusion.1) | copy-start | bytes 98308
  246.7 4.7 %copy-start.19 = (f32[16,4,128]{2,0,1:T(8,128)S(1)}, f32[16,4,128]{2,0,1:T(8,128)}, u32[]{:S(2)}) copy-start(f32[16,4,128]{2,0,1:T(8,128)} %fusion.112) | copy-start | bytes 98308
  251.4 5.4 %copy-start.12 = (f32[4,16,128]{2,1,0:T(8,128)S(1)}, f32[4,16,128]{2,1,0:T(8,128)}, u32[]{:S(2)}) copy-start(f32[4,16,128]{2,1,0:T(8,128)} %convolution_bitcast_fusion) | copy-start | bytes 98308
  251.4 5.4 %copy-start.20 = (f32[16,4,128]{2,0,1:T(8,128)S(1)}, f32[16,4,128]{2,0,1:T(8,128)}, u32[]{:S(2)}) copy-start(f32[16,4,128]{2,0,1:T(8,128)} %fusion.111) | copy-start | bytes 98308
  256.8 6.7 %copy-start.43 = (f32[16]{0:T(128)S(1)}, f32[16]{0:T(128)}, u32[]{:S(2)}) copy-start(f32[16]{0:T(128)} %param.33) | copy-start | bytes 196
  266.3 3.9 %copy-start.3 = (f32[4,16,64]{2,1,0:T(8,128)S(1)}, f32[4,16,64]{2,1,0:T(8,128)}, u32[]{:S(2)}) copy-start(f32[4,16,64]{2,1,0:T(8,128)} %copy-done.2) | copy-start | bytes 49156
  266.3 3.9 %copy-start.5 = (f32[4,16,64]{2,1,0:T(8,128)S(1)}, f32[4,16,64]{2,1,0:T(8,128)}, u32[]{:S(2)}) copy-start(f32[4,16,64]{2,1,0:T(8,128)} %copy-done.4) | copy-start | bytes 49156
  266.3 3.9 %copy-start.7 = (f32[4,16,128]{2,1,0:T(8,128)S(1)}, f32[4,16,128]{2,1,0:T(8,128)}, u32[]{:S(2)}) copy-start(f32[4,16,128]{2,1,0:T(8,128)} %convolution_bitcast_fusion.3) | copy-start | bytes 98308
  266.3 3.9 %copy-start.9 = (f32[4,16,128]{2,1,0:T(8,128)S(1)}, f32[4,16,128]{2,1,0:T(8,128)}, u32[]{:S(2)}) copy-start(f32[4,16,128]{2,1,0:T(8,128)} %convolution_bitcast_fusion.2) | copy-start | bytes 98308
  266.3 3.9 %copy-start.11 = (f32[4,16,128]{2,1,0:T(8,128)S(1)}, f32[4,16,128]{2,1,0:T(8,128)}, u32[]{:S(2)}) copy-start(f32[4,16,128]{2,1,0:T(8,128)} %convolution_bitcast_fusion.1) | copy-start | bytes 98308
  266.3 3.9 %copy-start.13 = (f32[4,16,128]{2,1,0:T(8,128)S(1)}, f32[4,16,128]{2,1,0:T(8,128)}, u32[]{:S(2)}) copy-start(f32[4,16,128]{2,1,0:T(8,128)} %convolution_bitcast_fusion) | copy-start | bytes 98308
  266.4 3.9 %copy-start.23 = (f32[4,1,16]{2,1,0:T(1,128)S(1)}, f32[4,1,16]{2,1,0:T(1,128)}, u32[]{:S(2)}) copy-start(f32[4,1,16]{2,1,0:T(1,128)} %copy-done.22) | copy-start | bytes 772
  266.4 3.9 %copy-start.25 = (f32[4,1,16]{2,1,0:T(1,128)S(1)}, f32[4,1,16]{2,1,0:T(1,128)}, u32[]{:S(2)}) copy-start(f32[4,1,16]{2,1,0:T(1,128)} %copy-done.24) | copy-start | bytes 772
  266.4 3.9 %copy-start.27 = (f32[4,1,16]{2,1,0:T(1,128)S(1)}, f32[4,1,16]{2,1,0:T(1,128)}, u32[]{:S(2)}) copy-start(f32[4,1,16]{2,1,0:T(1,128)} %copy-done.26) | copy-start | bytes 772
  266.4 3.9 %copy-start.29 = (f32[4,1,16]{2,1,0:T(1,128)S(1)}, f32[4,1,16]{2,1,0:T(1,128)}, u32[]{:S(2)}) copy-start(f32[4,1,16]{2,1,0:T(1,128)} %copy-done.28) | copy-start | bytes 772
  266.4 3.9 %copy-start.33 = (f32[4,1,16]{2,1,0:T(1,128)S(1)}, f32[4,1,16]{2,1,0:T(1,128)}, u32[]{:S(2)}) copy-start(f32[4,1,16]{2,1,0:T(1,128)} %copy-done.32) | copy-start | bytes 772
  266.4 3.9 %copy-start.35 = (f32[4,1,16]{2,1,0:T(1,128)S(1)}, f32[4,1,16]{2,1,0:T(1,128)}, u32[]{:S(2)}) copy-start(f32[4,1,16]{2,1,0:T(1,128)} %copy-done.34) | copy-start | bytes 772
  266.4 3.9 %copy-start.37 = (f32[4,1,16]{2,1,0:T(1,128)S(1)}, f32[4,1,16]{2,1,0:T(1,128)}, u32[]{:S(2)}) copy-start(f32[4,1,16]{2,1,0:T(1,128)} %copy-done.36) | copy-start | bytes 772
  266.4 3.9 %copy-start.39 = (f32[4,1,16]{2,1,0:T(1,128)S(1)}, f32[4,1,16]{2,1,0:T(1,128)}, u32[]{:S(2)}) copy-start(f32[4,1,16]{2,1,0:T(1,128)} %copy-done.38) | copy-start | bytes 772
  270.2 7.2 %copy-start.42 = (s32[1,4,2]{1,2,0:T(2,128)S(1)}, s32[1,4,2]{1,2,0:T(2,128)}, u32[]{:S(2)}) copy-start(s32[1,4,2]{1,2,0:T(2,128)} %param.26) | copy-start | bytes 100
  270.2 9.1 %copy-start.48 = (u32[32]{0:T(128)S(1)}, u32[32]{0:T(128)}, u32[]{:S(2)}) copy-start(u32[32]{0:T(128)} %constant.62) | copy-start | bytes 388
  270.2 69.6 %copy-start.14 = (bf16[1,4,2048]{2,1,0:T(4,128)(2,1)S(1)}, bf16[1,4,2048]{2,1,0:T(4,128)(2,1)}, u32[]{:S(2)}) copy-start(bf16[1,4,2048]{2,1,0:T(4,128)(2,1)} %param.22) | copy-start | bytes 49156
  270.2 70.6 %copy-start.40 = (f32[2048]{0:T(1024)S(1)}, f32[2048]{0:T(1024)}, u32[]{:S(2)}) copy-start(f32[2048]{0:T(1024)} %param.40) | copy-start | bytes 24580
  270.2 70.7 %copy-start.45 = (bf16[2048,8]{0,1:T(8,128)(2,1)S(1)}, bf16[2048,8]{0,1:T(8,128)(2,1)}, u32[]{:S(2)}) copy-start(bf16[2048,8]{0,1:T(8,128)(2,1)} %param.41) | copy-start | bytes 98308
  341.9 10.8 %all-to-all-start = ((bf16[8,2,2048]{2,1,0:T(2,128)(2,1)}), bf16[8,2,2048]{2,1,0:T(2,128)(2,1)S(1)}, u32[]{:S(2)}, u32[]{:S(2)}) async-start(bf16[8,2,2048]{2,1,0:T(2,128)(2,1)} %reshape_broadcast_in_dim_reshape.3), calls=%async_computation | async-start | bytes 131072 | tf_op jit(solution)/shard_map/all_to_all | solution.py:154
  361.4 10.2 %all-to-all-start.1 = ((bf16[8,2,2048]{2,1,0:T(2,128)(2,1)}), bf16[8,2,2048]{2,1,0:T(2,128)(2,1)S(1)}, u32[]{:S(2)}, u32[]{:S(2)}) async-start(bf16[8,2,2048]{2,1,0:T(2,128)(2,1)} %convert_element_type.233), calls=%async_computation.1 | async-start | bytes 131072 | tf_op jit(solution)/shard_map/all_to_all | solution.py:160
Sparse Core Ops, SparseCore 0:
  270.3 69.3 all-reduce.2
where the time goes:
time: 380 us; the launch traced here: 379 us
  blocking collectives  174 us (46%)
  matrix products  72.9 us (19%)
  waiting for transfers between devices  72.7 us (19%)
  local copies, waits for them, and re-layouts  21.3 us (6%)
  between operations  15.7 us (4%)
  other arithmetic  15.1 us (4%)
  starting transfers between devices  7.27 us (2%)
    all_gather x8, blocking collectives, shards(): lax.all_gather(bc_conv[:, step_index], 'head', axis=1, tiled=True)  142 us
    unnamed x2, waiting for transfers between devices  59.2 us
    dot_general x8, matrix products, shards(): jnp.einsum('rhpn,rhn->rhp', fresh_state, c_heads, precision=highest)  41.8 us
    all_gather x1, blocking collectives, shards(): gathered = lax.all_gather(tokens, 'head', axis=1, tiled=True)  32.5 us
    unnamed x114, local copies, waits for them, and re-layouts  16.2 us
    convert_element_type x2, other arithmetic, shards(): ssm_now = fresh_state.astype(jnp.bfloat16)  10.2 us
    dot_general x1, matrix products, shards(): jnp.dot(hidden, weight_down, preferred_element_type=jnp.float32)  8.05 us
  transfers between devices with their start and end apart: 3, of which 3 were waited for; matrix products, arithmetic and copies ran while one was open for 3% of the time, Pallas kernels for 0%

commit v1 on v0

--- a/solution.py
+++ b/solution.py
@@ -100,10 +100,8 @@
     x_conv, conv_x_new = causal_conv(conv_x_state[0], x_fresh, conv_x_kernel, conv_x_bias)
     bc_conv, conv_bc_new = causal_conv(conv_bc_state[0], bc_fresh, conv_bc_kernel, conv_bc_bias)
     bc_conv = bc_conv.astype(jnp.bfloat16)
-    bc_list = [
-        lax.all_gather(bc_conv[:, step_index], "head", axis=1, tiled=True)
-        for step_index in range(STEPS)
-    ]
+    bc_all = lax.all_gather(bc_conv, "head", axis=2, tiled=True)
+    bc_list = [bc_all[:, step_index] for step_index in range(STEPS)]
     head_global = my_index * heads_local + jnp.arange(heads_local)
     group_pick = (head_global[:, None] // (HEADS // G) == jnp.arange(G)[None, :]).astype(
         jnp.float32

time: 380 us -> 271 us (0.71)
  blocking collectives: 174 us -> 63 us
    all_gather x8 -> x1, blocking collectives: 142 us -> 30.5 us  [shards(): bc_all = lax.all_gather(bc_conv, 'head', axis=2, tiled=True)]
  transfers between devices with their start and end apart: 3 -> 3, of which waited for: 3 -> 3; matrix products, arithmetic and copies ran while one was open for 3% -> 4% of each run, Pallas kernels for 0% -> 0%
where the time goes in v1:
time: 271 us; the launch traced here: 270 us
  waiting for transfers between devices  74.9 us (28%)
  matrix products  72.9 us (27%)
  blocking collectives  63 us (23%)
  local copies, waits for them, and re-layouts  21.8 us (8%)
  between operations  15.6 us (6%)
  other arithmetic  14.4 us (5%)
  starting transfers between devices  7.28 us (3%)
    unnamed x2, waiting for transfers between devices  61.4 us
    dot_general x8, matrix products, shards(): jnp.einsum('rhpn,rhn->rhp', fresh_state, c_heads, precision=highest)  41.8 us
    all_gather x1, blocking collectives, shards(): gathered = lax.all_gather(tokens, 'head', axis=1, tiled=True)  32.5 us
    all_gather x1, blocking collectives, shards(): bc_all = lax.all_gather(bc_conv, 'head', axis=2, tiled=True)  30.5 us
    unnamed x114, local copies, waits for them, and re-layouts  16.2 us
    convert_element_type x2, other arithmetic, shards(): ssm_now = fresh_state.astype(jnp.bfloat16)  10.2 us
    dot_general x1, matrix products, shards(): jnp.dot(hidden, weight_down, preferred_element_type=jnp.float32)  8.05 us
    dot_general x1, matrix products, shards(): jnp.dot(normed, weight_xz, preferred_element_type=jnp.float32)  7.21 us
  transfers between devices with their start and end apart: 3, of which 3 were waited for; matrix products, arithmetic and copies ran while one was open for 4% of the time, Pallas kernels for 0%

profile of v1, /device:TPU:0, one launch (start us, length us, event | category | flops | bytes accessed | tf_op | source)
XLA Modules:
  0.0 269.9 jit_solution(17759373759885222538)
XLA Ops:
  7.2 0.8 copy.187
  8.1 32.5 %all_gather.6 = bf16[1,32,2048]{2,0,1:T(2,128)(2,1)S(1)} all-gather(bf16[1,4,2048]{2,0,1:T(2,128)(2,1)S(1)} %copy.187), channel_id=1, replica_groups=mesh['groups'=2,'head'=8,'req'=2] {'head'}, dimensions={1}, use_global_device_ids=true | all-gather | bytes 147456 | tf_op jit(solution)/shard_map/all_gather | solution.py:79
  40.6 0.2 fusion.62
  40.9 0.7 copy.290
  41.6 0.8 fusion.167
  42.4 1.0 convolution_convert_fusion.2
  43.5 0.7 multiply_convert_fusion.2
  44.2 30.5 %all_gather.7 = bf16[4,8,2048]{2,1,0:T(8,128)(2,1)S(1)} all-gather(bf16[4,8,256]{2,1,0:T(8,128)(2,1)S(1)} %multiply_convert_fusion.2), channel_id=1, replica_groups=mesh['groups'=2,'head'=8,'req'=2] {'head'}, dimensions={2}, use_global_device_ids=true | all-gather | bytes 147456 | tf_op jit(solution)/shard_map/all_gather | solution.py:103
  74.7 0.6 slice_reduce_fusion
  75.3 0.2 convolution_bitcast_fusion.7
  75.5 0.8 fusion.118
  76.3 0.2 convolution_bitcast_fusion.6
  76.5 0.8 fusion.117
  77.3 0.2 convolution_bitcast_fusion.5
  77.5 0.8 fusion.116
  78.3 0.2 convolution_bitcast_fusion.4
  78.5 0.8 fusion.115
  79.3 0.8 convolution_bitcast_fusion.3
  80.1 0.8 fusion.114
  80.9 0.8 convolution_bitcast_fusion.2
  81.7 0.8 fusion.113
  82.5 0.8 convolution_bitcast_fusion.1
  83.2 0.8 fusion.112
  84.0 0.8 convolution_bitcast_fusion
  84.8 0.8 fusion.111
  85.6 12.4 %copy.190 = bf16[2048,2048]{0,1:T(8,128)(2,1)} copy(bf16[2048,2048]{1,0:T(8,128)(2,1)} %param.28) | data formatting | bytes 16777216 | tf_op args[6]
  98.0 7.2 %fusion.74 = f32[4,8,16,2,64]{4,1,3,2,0:T(8,128)S(1)} fusion(bf16[16,2,64,2048,1]{3,2,1,0,4:T(8,128)(2,1)} %bitcast.433, bf16[1,32,2048]{2,1,0:T(8,128)(2,1)S(1)} %get-tuple-element.41, f32[2048]{0:T(1024)S(1)} %copy-done.31, f32[32]{0:T(128)S(1)} %add_rsqrt_fusion.2), kind=kOutput, calls=%fused_computation.102 | convolution fusion | flops 268697600 | bytes 8790144 | tf_op jit(solution)/shard_map/dot_general | solution.py:82
  105.4 0.1 convert_element_type.206
  105.8 0.2 reshape.356
  106.1 0.3 multiply_exponential_fusion
  106.5 0.1 fusion.105
  106.7 4.3 %fusion.24 = f32[4,16,1,64]{3,2,1,0:T(1,128)S(1)} fusion(f32[4,16,128,1]{2,3,1,0:T(1,128)} %bitcast.467, bf16[1,4,16,64,128]{4,3,2,1,0:T(8,128)(2,1)S(1)} %copy-done.1, f32[4,16,128]{2,1,0:T(8,128)S(1)} %convolution_bitcast_fusion.7, f32[4,16,64]{2,1,0:T(8,128)S(1)} %get-tuple-element.57, f32[4,16]{1,0:T(4,128)S(1)} %bitcast.496), kind=kOutput, calls=%fused_computation.43 | convolution fusion | flops 8388608 | bytes 1147136 | tf_op jit(solution)/shard_map/rhpn,rhn->rhp/dot_general | solution.py:123
  111.0 5.0 %fusion.22 = f32[4,16,1,64]{3,2,1,0:T(1,128)S(1)} fusion(f32[4,16,128,1]{2,3,1,0:T(1,128)} %bitcast.468, f32[4,16,128]{2,1,0:T(8,128)S(1)} %convolution_bitcast_fusion.6, f32[4,16,64]{2,1,0:T(8,128)S(1)} %get-tuple-element.56, f32[4,16]{1,0:T(4,128)S(1)} %bitcast.491, bf16[1,4,16,64,128]{4,3,2,1,0:T(8,128)(2,1)S(1)} %copy-done.1, ...), kind=kOutput, calls=%fused_computation.41 | convolution fusion | flops 11010048 | bytes 1196544 | tf_op jit(solution)/shard_map/rhpn,rhn->rhp/dot_general | solution.py:123
  116.0 5.3 %fusion.20 = f32[4,16,1,64]{3,2,1,0:T(1,128)S(1)} fusion(f32[4,16,128,1]{2,3,1,0:T(1,128)S(1)} %bitcast.469, f32[4,16,128]{2,1,0:T(8,128)S(1)} %convolution_bitcast_fusion.5, f32[4,16,64]{2,1,0:T(8,128)S(1)} %get-tuple-element.55, f32[4,16]{1,0:T(4,128)S(1)} %bitcast.487, f32[4,16,128]{2,1,0:T(8,128)S(1)} %convolution_bitcast_fusion.6, ...), kind=kOutput, calls=%fused_computation.38 | convolution fusion | flops 13631488 | bytes 1245952 | tf_op jit(solution)/shard_map/rhpn,rhn->rhp/dot_general | solution.py:123
  121.3 3.2 %fusion.17 = bf16[4,16,64,128]{3,2,1,0:T(8,128)(2,1)S(1)} fusion(f32[4,16,128]{2,1,0:T(8,128)S(1)} %convolution_bitcast_fusion.4, f32[4,16,64]{2,1,0:T(8,128)S(1)} %get-tuple-element.54, f32[4,16]{1,0:T(4,128)S(1)} %bitcast.484, f32[4,16,128]{2,1,0:T(8,128)S(1)} %convolution_bitcast_fusion.5, f32[4,16,64]{2,1,0:T(8,128)S(1)} %get-tuple-element.55, ...), kind=kLoop, calls=%fused_computation.34 | loop fusion | flops 10485760 | bytes 2294784 | tf_op jit(solution)/shard_map/convert_element_type | solution.py:126
  124.6 6.9 %fusion.18 = f32[4,16,1,64]{3,2,1,0:T(1,128)S(1)} fusion(f32[4,16,128,1]{2,3,1,0:T(1,128)S(1)} %bitcast.470, f32[4,16,128]{2,1,0:T(8,128)S(1)} %convolution_bitcast_fusion.4, f32[4,16,64]{2,1,0:T(8,128)S(1)} %get-tuple-element.54, f32[4,16]{1,0:T(4,128)S(1)} %bitcast.485, f32[4,16,128]{2,1,0:T(8,128)S(1)} %convolution_bitcast_fusion.5, ...), kind=kOutput, calls=%fused_computation.35 | convolution fusion | flops 16252928 | bytes 1295360 | tf_op jit(solution)/shard_map/rhpn,rhn->rhp/dot_general | solution.py:123
  131.5 3.6 %fusion.16 = f32[4,16,1,64]{3,2,1,0:T(1,128)S(1)} fusion(f32[4,16,128,1]{2,3,1,0:T(1,128)S(1)} %bitcast.471, bf16[4,16,64,128]{3,2,1,0:T(8,128)(2,1)S(1)} %fusion.17, f32[4,16,128]{2,1,0:T(8,128)S(1)} %copy-done.6, f32[4,16,64]{2,1,0:T(8,128)S(1)} %get-tuple-element.53, f32[4,16]{1,0:T(4,128)S(1)} %bitcast.515), kind=kOutput, calls=%fused_computation.32 | convolution fusion | flops 8388608 | bytes 1147136 | tf_op jit(solution)/shard_map/rhpn,rhn->rhp/dot_general | solution.py:123
  135.1 4.7 %fusion.14 = f32[4,16,1,64]{3,2,1,0:T(1,128)S(1)} fusion(f32[4,16,128,1]{2,3,1,0:T(1,128)S(1)} %bitcast.472, f32[4,16,128]{2,1,0:T(8,128)S(1)} %copy-done.8, f32[4,16,64]{2,1,0:T(8,128)S(1)} %get-tuple-element.52, f32[4,16]{1,0:T(4,128)S(1)} %bitcast.511, bf16[4,16,64,128]{3,2,1,0:T(8,128)(2,1)S(1)} %fusion.17, f32[4,16,128]{2,1,0:T(8,128)S(1)} %copy-done.6, ...), kind=kOutput, calls=%fused_computation.29 | convolution fusion | flops 11010048 | bytes 1196544 | tf_op jit(solution)/shard_map/rhpn,rhn->rhp/dot_general | solution.py:123
  139.9 5.3 %fusion.12 = f32[4,16,1,64]{3,2,1,0:T(1,128)S(1)} fusion(f32[4,16,128,1]{2,3,1,0:T(1,128)S(1)} %bitcast.473, f32[4,16,128]{2,1,0:T(8,128)S(1)} %copy-done.10, f32[4,16,64]{2,1,0:T(8,128)S(1)} %get-tuple-element.51, f32[4,16]{1,0:T(4,128)S(1)} %bitcast.508, f32[4,16,128]{2,1,0:T(8,128)S(1)} %copy-done.8, f32[4,16,64]{2,1,0:T(8,128)S(1)} %get-tuple-element.52, ...), kind=kOutput, calls=%fused_computation.26 | convolution fusion | flops 13631488 | bytes 1245952 | tf_op jit(solution)/shard_map/rhpn,rhn->rhp/dot_general | solution.py:123
  145.3 6.7 %fusion.6 = f32[4,16,1,64]{3,2,1,0:T(1,128)S(1)} fusion(f32[4,16,128,1]{2,3,1,0:T(1,128)S(1)} %bitcast.474, f32[4,16,128]{2,1,0:T(8,128)S(1)} %copy-done.12, f32[4,16,64]{2,1,0:T(8,128)S(1)} %get-tuple-element.50, f32[4,16]{1,0:T(4,128)S(1)} %bitcast.506, f32[4,16,128]{2,1,0:T(8,128)S(1)} %copy-done.10, f32[4,16,64]{2,1,0:T(8,128)S(1)} %get-tuple-element.51, ...), kind=kOutput, calls=%fused_computation.19 | convolution fusion | flops 16252928 | bytes 1295360 | tf_op jit(solution)/shard_map/rhpn,rhn->rhp/dot_general | solution.py:123
  152.1 0.4 stack.42
  152.5 0.8 fusion.70
  153.3 0.8 copy.219
  154.2 0.1 mul.830
  154.9 3.7 %fusion.84 = f32[32,2048]{1,0:T(8,128)} fusion(bf16[1024,2048]{1,0:T(8,128)(2,1)} %param.39, f32[32,1024]{1,0:T(8,128)S(1)} %mul.831, f32[32,1024]{1,0:T(8,128)S(1)} %stack.43, f32[32,1024]{1,0:T(8,128)S(1)} %squeeze.121, f32[1024]{0:T(1024)} %param.38), kind=kOutput, calls=%fused_computation.116 | convolution fusion | flops 134479872 | bytes 4853760 | tf_op jit(solution)/shard_map/dot_general | solution.py:135
  158.8 7.0 %add_convert_fusion = bf16[1,4,16,64,128]{4,3,2,1,0:T(8,128)(2,1)} fusion(bf16[1,4,16,64,128]{4,3,2,1,0:T(8,128)(2,1)S(1)} %copy-done.1, f32[4,16,128]{2,1,0:T(8,128)S(1)} %copy-done.13, f32[4,16,64]{2,1,0:T(8,128)S(1)} %get-tuple-element.50, f32[4,16,128]{2,1,0:T(8,128)S(1)} %copy-done.11, f32[4,16,64]{2,1,0:T(8,128)S(1)} %get-tuple-element.51, ...), kind=kLoop, calls=%fused_computation.12 | loop fusion | flops 20971520 | bytes 2492416 | tf_op jit(solution)/shard_map/convert_element_type | solution.py:126
  166.1 0.2 select_reduce_fusion
  166.5 0.6 copy.223
  167.2 0.6 copy.224
  167.8 0.6 dynamic-slice
  169.0 61.4 %all-reduce.3.cloned.1.call-done = f32[32,2048]{1,0:T(8,128)} async-done(((f32[32,2048]{1,0:T(8,128)}), f32[32,2048]{1,0:T(8,128)}) %all-reduce.3.cloned.1.call-update) | async-done | bytes 262160
  230.4 1.0 fusion.89
  231.5 0.1 fusion.168
  231.7 0.1 convolution_convert_fusion
  231.8 0.7 reshape_broadcast_in_dim_reshape.3
  232.5 3.9 %all-to-all-start = ((bf16[8,2,2048]{2,1,0:T(2,128)(2,1)}), bf16[8,2,2048]{2,1,0:T(2,128)(2,1)S(1)}, u32[]{:S(2)}, u32[]{:S(2)}) async-start(bf16[8,2,2048]{2,1,0:T(2,128)(2,1)} %reshape_broadcast_in_dim_reshape.3), calls=%async_computation | async-start | bytes 131072 | tf_op jit(solution)/shard_map/all_to_all | solution.py:152
  236.4 0.2 fusion.119
  236.7 6.6 %all-to-all-done = bf16[8,2,2048]{2,1,0:T(2,128)(2,1)S(1)} async-done(((bf16[8,2,2048]{2,1,0:T(2,128)(2,1)}), bf16[8,2,2048]{2,1,0:T(2,128)(2,1)S(1)}, u32[]{:S(2)}, u32[]{:S(2)}) %all-to-all-start) | async-done | bytes 65568 | tf_op jit(solution)/shard_map/all_to_all | solution.py:152
  243.3 8.0 %convolution_convert_fusion.1 = bf16[16,2048]{1,0:T(8,128)(2,1)S(1)} fusion(bf16[2048,2048]{1,0:T(8,128)(2,1)} %param.43, bf16[16,2048]{1,0:T(8,128)(2,1)S(1)} %reshape.366, bf16[2048,2048]{1,0:T(8,128)(2,1)} %param.42), kind=kOutput, calls=%fused_computation.6 | convolution fusion | flops 268566528 | bytes 16908288 | tf_op jit(solution)/shard_map/dot_general | solution.py:155
  251.4 0.7 convert_element_type.233
  252.1 3.3 %all-to-all-start.1 = ((bf16[8,2,2048]{2,1,0:T(2,128)(2,1)}), bf16[8,2,2048]{2,1,0:T(2,128)(2,1)S(1)}, u32[]{:S(2)}, u32[]{:S(2)}) async-start(bf16[8,2,2048]{2,1,0:T(2,128)(2,1)} %convert_element_type.233), calls=%async_computation.1 | async-start | bytes 131072 | tf_op jit(solution)/shard_map/all_to_all | solution.py:158
  255.5 6.8 %all-to-all-done.1 = bf16[8,2,2048]{2,1,0:T(2,128)(2,1)S(1)} async-done(((bf16[8,2,2048]{2,1,0:T(2,128)(2,1)}), bf16[8,2,2048]{2,1,0:T(2,128)(2,1)S(1)}, u32[]{:S(2)}, u32[]{:S(2)}) %all-to-all-start.1) | async-done | bytes 65568 | tf_op jit(solution)/shard_map/all_to_all | solution.py:158
  262.3 0.1 fusion.26
  262.5 0.6 fusion.106
  (148 shorter events, 2.3 us)
Async XLA Ops:
  7.2 35.3 %copy-start = (bf16[2048,256]{1,0:T(8,128)(2,1)S(1)}, bf16[2048,256]{1,0:T(8,128)(2,1)}, u32[]{:S(2)}) copy-start(bf16[2048,256]{1,0:T(8,128)(2,1)} %param.29) | copy-start | bytes 3145732
  7.2 78.5 %copy-start.46 = (f32[16]{0:T(128)S(1)}, f32[16]{0:T(128)}, u32[]{:S(2)}) copy-start(f32[16]{0:T(128)} %param.32) | copy-start | bytes 196
  7.2 223.2 %all-reduce.3.cloned.1.call-start = ((), (), s32[]{:S(2)}) async-start(), calls=%async_computation.2 | async-start | bytes 524288
  85.6 12.4 %copy-start.31 = (f32[2048]{0:T(1024)S(1)}, f32[2048]{0:T(1024)}, u32[]{:S(2)}) copy-start(f32[2048]{0:T(1024)} %param.27) | copy-start | bytes 24580
  98.0 7.5 %copy-start.21 = (bf16[1,4,3,1024]{3,1,2,0:T(4,128)(2,1)S(1)}, bf16[1,4,3,1024]{3,1,2,0:T(4,128)(2,1)}, u32[]{:S(2)}) copy-start(bf16[1,4,3,1024]{3,1,2,0:T(4,128)(2,1)} %param.24) | copy-start | bytes 73732
  98.0 7.5 %copy-start.30 = (f32[4,1024]{1,0:T(4,128)S(1)}, f32[4,1024]{1,0:T(4,128)}, u32[]{:S(2)}) copy-start(f32[4,1024]{1,0:T(4,128)} %param.34) | copy-start | bytes 49156
  98.0 7.6 %copy-start.41 = (f32[1024]{0:T(1024)S(1)}, f32[1024]{0:T(1024)}, u32[]{:S(2)}) copy-start(f32[1024]{0:T(1024)} %param.35) | copy-start | bytes 12292
  105.3 0.8 copy-start.44
  105.3 0.8 copy-start.47
  105.3 1.4 copy-start.1
  106.4 18.1 %copy-start.22 = (f32[4,1,16]{2,1,0:T(1,128)}, f32[4,1,16]{2,1,0:T(1,128)S(1)}, u32[]{:S(2)}) copy-start(f32[4,1,16]{2,1,0:T(1,128)S(1)} %get-tuple-element.62) | copy-start | bytes 772
  106.4 18.1 %copy-start.24 = (f32[4,1,16]{2,1,0:T(1,128)}, f32[4,1,16]{2,1,0:T(1,128)S(1)}, u32[]{:S(2)}) copy-start(f32[4,1,16]{2,1,0:T(1,128)S(1)} %get-tuple-element.63) | copy-start | bytes 772
  106.4 18.1 %copy-start.26 = (f32[4,1,16]{2,1,0:T(1,128)}, f32[4,1,16]{2,1,0:T(1,128)S(1)}, u32[]{:S(2)}) copy-start(f32[4,1,16]{2,1,0:T(1,128)S(1)} %get-tuple-element.64) | copy-start | bytes 772
  106.4 18.1 %copy-start.28 = (f32[4,1,16]{2,1,0:T(1,128)}, f32[4,1,16]{2,1,0:T(1,128)S(1)}, u32[]{:S(2)}) copy-start(f32[4,1,16]{2,1,0:T(1,128)S(1)} %get-tuple-element.65) | copy-start | bytes 772
  106.5 38.7 %copy-start.32 = (f32[4,1,16]{2,1,0:T(1,128)}, f32[4,1,16]{2,1,0:T(1,128)S(1)}, u32[]{:S(2)}) copy-start(f32[4,1,16]{2,1,0:T(1,128)S(1)} %get-tuple-element.58) | copy-start | bytes 772
  106.5 38.7 %copy-start.34 = (f32[4,1,16]{2,1,0:T(1,128)}, f32[4,1,16]{2,1,0:T(1,128)S(1)}, u32[]{:S(2)}) copy-start(f32[4,1,16]{2,1,0:T(1,128)S(1)} %get-tuple-element.59) | copy-start | bytes 772
  106.5 38.7 %copy-start.36 = (f32[4,1,16]{2,1,0:T(1,128)}, f32[4,1,16]{2,1,0:T(1,128)S(1)}, u32[]{:S(2)}) copy-start(f32[4,1,16]{2,1,0:T(1,128)S(1)} %get-tuple-element.60) | copy-start | bytes 772
  106.5 38.7 %copy-start.38 = (f32[4,1,16]{2,1,0:T(1,128)}, f32[4,1,16]{2,1,0:T(1,128)S(1)}, u32[]{:S(2)}) copy-start(f32[4,1,16]{2,1,0:T(1,128)S(1)} %get-tuple-element.61) | copy-start | bytes 772
  106.6 38.6 %copy-start.2 = (f32[4,16,64]{2,1,0:T(8,128)}, f32[4,16,64]{2,1,0:T(8,128)S(1)}, u32[]{:S(2)}) copy-start(f32[4,16,64]{2,1,0:T(8,128)S(1)} %get-tuple-element.52) | copy-start | bytes 49156
  106.6 38.6 %copy-start.4 = (f32[4,16,64]{2,1,0:T(8,128)}, f32[4,16,64]{2,1,0:T(8,128)S(1)}, u32[]{:S(2)}) copy-start(f32[4,16,64]{2,1,0:T(8,128)S(1)} %get-tuple-element.53) | copy-start | bytes 49156
  111.0 5.0 %copy-start.15 = (f32[16,4,128]{2,0,1:T(8,128)S(1)}, f32[16,4,128]{2,0,1:T(8,128)}, u32[]{:S(2)}) copy-start(f32[16,4,128]{2,0,1:T(8,128)} %fusion.116) | copy-start | bytes 98308
  121.3 3.2 %copy-start.16 = (f32[16,4,128]{2,0,1:T(8,128)S(1)}, f32[16,4,128]{2,0,1:T(8,128)}, u32[]{:S(2)}) copy-start(f32[16,4,128]{2,0,1:T(8,128)} %fusion.115) | copy-start | bytes 98308
  124.6 6.9 %copy-start.6 = (f32[4,16,128]{2,1,0:T(8,128)S(1)}, f32[4,16,128]{2,1,0:T(8,128)}, u32[]{:S(2)}) copy-start(f32[4,16,128]{2,1,0:T(8,128)} %convolution_bitcast_fusion.3) | copy-start | bytes 98308
  124.6 6.9 %copy-start.17 = (f32[16,4,128]{2,0,1:T(8,128)S(1)}, f32[16,4,128]{2,0,1:T(8,128)}, u32[]{:S(2)}) copy-start(f32[16,4,128]{2,0,1:T(8,128)} %fusion.114) | copy-start | bytes 98308
  131.5 3.6 %copy-start.8 = (f32[4,16,128]{2,1,0:T(8,128)S(1)}, f32[4,16,128]{2,1,0:T(8,128)}, u32[]{:S(2)}) copy-start(f32[4,16,128]{2,1,0:T(8,128)} %convolution_bitcast_fusion.2) | copy-start | bytes 98308
  131.5 3.6 %copy-start.18 = (f32[16,4,128]{2,0,1:T(8,128)S(1)}, f32[16,4,128]{2,0,1:T(8,128)}, u32[]{:S(2)}) copy-start(f32[16,4,128]{2,0,1:T(8,128)} %fusion.113) | copy-start | bytes 98308
  135.1 4.7 %copy-start.10 = (f32[4,16,128]{2,1,0:T(8,128)S(1)}, f32[4,16,128]{2,1,0:T(8,128)}, u32[]{:S(2)}) copy-start(f32[4,16,128]{2,1,0:T(8,128)} %convolution_bitcast_fusion.1) | copy-start | bytes 98308
  135.1 4.7 %copy-start.19 = (f32[16,4,128]{2,0,1:T(8,128)S(1)}, f32[16,4,128]{2,0,1:T(8,128)}, u32[]{:S(2)}) copy-start(f32[16,4,128]{2,0,1:T(8,128)} %fusion.112) | copy-start | bytes 98308
  139.8 5.4 %copy-start.12 = (f32[4,16,128]{2,1,0:T(8,128)S(1)}, f32[4,16,128]{2,1,0:T(8,128)}, u32[]{:S(2)}) copy-start(f32[4,16,128]{2,1,0:T(8,128)} %convolution_bitcast_fusion) | copy-start | bytes 98308
  139.8 5.4 %copy-start.20 = (f32[16,4,128]{2,0,1:T(8,128)S(1)}, f32[16,4,128]{2,0,1:T(8,128)}, u32[]{:S(2)}) copy-start(f32[16,4,128]{2,0,1:T(8,128)} %fusion.111) | copy-start | bytes 98308
  145.2 6.7 %copy-start.43 = (f32[16]{0:T(128)S(1)}, f32[16]{0:T(128)}, u32[]{:S(2)}) copy-start(f32[16]{0:T(128)} %param.33) | copy-start | bytes 196
  154.8 3.9 %copy-start.3 = (f32[4,16,64]{2,1,0:T(8,128)S(1)}, f32[4,16,64]{2,1,0:T(8,128)}, u32[]{:S(2)}) copy-start(f32[4,16,64]{2,1,0:T(8,128)} %copy-done.2) | copy-start | bytes 49156
  154.8 3.9 %copy-start.5 = (f32[4,16,64]{2,1,0:T(8,128)S(1)}, f32[4,16,64]{2,1,0:T(8,128)}, u32[]{:S(2)}) copy-start(f32[4,16,64]{2,1,0:T(8,128)} %copy-done.4) | copy-start | bytes 49156
  154.8 3.9 %copy-start.7 = (f32[4,16,128]{2,1,0:T(8,128)S(1)}, f32[4,16,128]{2,1,0:T(8,128)}, u32[]{:S(2)}) copy-start(f32[4,16,128]{2,1,0:T(8,128)} %convolution_bitcast_fusion.3) | copy-start | bytes 98308
  154.8 3.9 %copy-start.9 = (f32[4,16,128]{2,1,0:T(8,128)S(1)}, f32[4,16,128]{2,1,0:T(8,128)}, u32[]{:S(2)}) copy-start(f32[4,16,128]{2,1,0:T(8,128)} %convolution_bitcast_fusion.2) | copy-start | bytes 98308
  154.8 3.9 %copy-start.11 = (f32[4,16,128]{2,1,0:T(8,128)S(1)}, f32[4,16,128]{2,1,0:T(8,128)}, u32[]{:S(2)}) copy-start(f32[4,16,128]{2,1,0:T(8,128)} %convolution_bitcast_fusion.1) | copy-start | bytes 98308
  154.8 3.9 %copy-start.13 = (f32[4,16,128]{2,1,0:T(8,128)S(1)}, f32[4,16,128]{2,1,0:T(8,128)}, u32[]{:S(2)}) copy-start(f32[4,16,128]{2,1,0:T(8,128)} %convolution_bitcast_fusion) | copy-start | bytes 98308
  154.8 3.9 %copy-start.23 = (f32[4,1,16]{2,1,0:T(1,128)S(1)}, f32[4,1,16]{2,1,0:T(1,128)}, u32[]{:S(2)}) copy-start(f32[4,1,16]{2,1,0:T(1,128)} %copy-done.22) | copy-start | bytes 772
  154.8 3.9 %copy-start.25 = (f32[4,1,16]{2,1,0:T(1,128)S(1)}, f32[4,1,16]{2,1,0:T(1,128)}, u32[]{:S(2)}) copy-start(f32[4,1,16]{2,1,0:T(1,128)} %copy-done.24) | copy-start | bytes 772
  154.8 3.9 %copy-start.27 = (f32[4,1,16]{2,1,0:T(1,128)S(1)}, f32[4,1,16]{2,1,0:T(1,128)}, u32[]{:S(2)}) copy-start(f32[4,1,16]{2,1,0:T(1,128)} %copy-done.26) | copy-start | bytes 772
  154.8 3.9 %copy-start.29 = (f32[4,1,16]{2,1,0:T(1,128)S(1)}, f32[4,1,16]{2,1,0:T(1,128)}, u32[]{:S(2)}) copy-start(f32[4,1,16]{2,1,0:T(1,128)} %copy-done.28) | copy-start | bytes 772
  154.9 3.9 %copy-start.33 = (f32[4,1,16]{2,1,0:T(1,128)S(1)}, f32[4,1,16]{2,1,0:T(1,128)}, u32[]{:S(2)}) copy-start(f32[4,1,16]{2,1,0:T(1,128)} %copy-done.32) | copy-start | bytes 772
  154.9 3.9 %copy-start.35 = (f32[4,1,16]{2,1,0:T(1,128)S(1)}, f32[4,1,16]{2,1,0:T(1,128)}, u32[]{:S(2)}) copy-start(f32[4,1,16]{2,1,0:T(1,128)} %copy-done.34) | copy-start | bytes 772
  154.9 3.9 %copy-start.37 = (f32[4,1,16]{2,1,0:T(1,128)S(1)}, f32[4,1,16]{2,1,0:T(1,128)}, u32[]{:S(2)}) copy-start(f32[4,1,16]{2,1,0:T(1,128)} %copy-done.36) | copy-start | bytes 772
  154.9 3.9 %copy-start.39 = (f32[4,1,16]{2,1,0:T(1,128)S(1)}, f32[4,1,16]{2,1,0:T(1,128)}, u32[]{:S(2)}) copy-start(f32[4,1,16]{2,1,0:T(1,128)} %copy-done.38) | copy-start | bytes 772
  158.6 7.2 %copy-start.42 = (s32[1,4,2]{1,2,0:T(2,128)S(1)}, s32[1,4,2]{1,2,0:T(2,128)}, u32[]{:S(2)}) copy-start(s32[1,4,2]{1,2,0:T(2,128)} %param.26) | copy-start | bytes 100
  158.6 9.1 %copy-start.48 = (u32[32]{0:T(128)S(1)}, u32[32]{0:T(128)}, u32[]{:S(2)}) copy-start(u32[32]{0:T(128)} %constant.62) | copy-start | bytes 388
  158.6 71.8 %copy-start.14 = (bf16[1,4,2048]{2,1,0:T(4,128)(2,1)S(1)}, bf16[1,4,2048]{2,1,0:T(4,128)(2,1)}, u32[]{:S(2)}) copy-start(bf16[1,4,2048]{2,1,0:T(4,128)(2,1)} %param.22) | copy-start | bytes 49156
  158.6 72.8 %copy-start.40 = (f32[2048]{0:T(1024)S(1)}, f32[2048]{0:T(1024)}, u32[]{:S(2)}) copy-start(f32[2048]{0:T(1024)} %param.40) | copy-start | bytes 24580
  158.6 72.9 %copy-start.45 = (bf16[2048,8]{0,1:T(8,128)(2,1)S(1)}, bf16[2048,8]{0,1:T(8,128)(2,1)}, u32[]{:S(2)}) copy-start(bf16[2048,8]{0,1:T(8,128)(2,1)} %param.41) | copy-start | bytes 98308
  232.5 10.8 %all-to-all-start = ((bf16[8,2,2048]{2,1,0:T(2,128)(2,1)}), bf16[8,2,2048]{2,1,0:T(2,128)(2,1)S(1)}, u32[]{:S(2)}, u32[]{:S(2)}) async-start(bf16[8,2,2048]{2,1,0:T(2,128)(2,1)} %reshape_broadcast_in_dim_reshape.3), calls=%async_computation | async-start | bytes 131072 | tf_op jit(solution)/shard_map/all_to_all | solution.py:152
  252.1 10.2 %all-to-all-start.1 = ((bf16[8,2,2048]{2,1,0:T(2,128)(2,1)}), bf16[8,2,2048]{2,1,0:T(2,128)(2,1)S(1)}, u32[]{:S(2)}, u32[]{:S(2)}) async-start(bf16[8,2,2048]{2,1,0:T(2,128)(2,1)} %convert_element_type.233), calls=%async_computation.1 | async-start | bytes 131072 | tf_op jit(solution)/shard_map/all_to_all | solution.py:158
Sparse Core Ops, SparseCore 0:
  158.8 71.5 all-reduce.2

commit v2 on v1

--- a/solution.py
+++ b/solution.py
@@ -42,6 +42,11 @@
     return jnp.square(
         jnp.maximum(jnp.dot(rows_in, weight_up, preferred_element_type=jnp.float32), 0.0)
     ).astype(jnp.bfloat16)
+
+
+def broadcast_gather(block, count):
+    copies = jnp.broadcast_to(block[None], (count,) + block.shape)
+    return lax.all_to_all(copies, "head", 0, 0, tiled=True)
 
 
 def shards(
@@ -76,7 +81,7 @@
     heads_local = ssm_state.shape[2]
     head_dim = ssm_state.shape[3]
     state_dim = ssm_state.shape[4]
-    gathered = lax.all_gather(tokens, "head", axis=1, tiled=True)
+    gathered = broadcast_gather(tokens[0], head_count)
     inputs = gathered.reshape(requests * STEPS, width)
     normed = norm_rows(inputs.astype(jnp.float32), mixer_gain).astype(jnp.bfloat16)
     proj_xz = jnp.dot(normed, weight_xz, preferred_element_type=jnp.float32).reshape(
@@ -100,7 +105,9 @@
     x_conv, conv_x_new = causal_conv(conv_x_state[0], x_fresh, conv_x_kernel, conv_x_bias)
     bc_conv, conv_bc_new = causal_conv(conv_bc_state[0], bc_fresh, conv_bc_kernel, conv_bc_bias)
     bc_conv = bc_conv.astype(jnp.bfloat16)
-    bc_all = lax.all_gather(bc_conv, "head", axis=2, tiled=True)
+    bc_all = jnp.moveaxis(broadcast_gather(bc_conv, head_count), 0, 2).reshape(
+        requests, STEPS, -1
+    )
     bc_list = [bc_all[:, step_index] for step_index in range(STEPS)]
     head_global = my_index * heads_local + jnp.arange(heads_local)
     group_pick = (head_global[:, None] // (HEADS // G) == jnp.arange(G)[None, :]).astype(
@@ -131,12 +138,10 @@
         .reshape(requests * STEPS, heads_local * head_dim)
     )
     per_expert = head_count // EXPERTS
-    mixer_out = lax.psum_scatter(
-        jnp.dot(group_normed, weight_out, preferred_element_type=jnp.float32),
-        "head",
-        scatter_dimension=0,
-        tiled=True,
-    )
+    mixer_part = jnp.dot(group_normed, weight_out, preferred_element_type=jnp.float32)
+    mixer_out = lax.all_to_all(
+        mixer_part.reshape(head_count, tok_local, width), "head", 0, 0, tiled=True
+    ).sum(axis=0)
     residual = (tokens[0].astype(jnp.float32) + mixer_out).astype(jnp.bfloat16)
     ffn_in = norm_rows(residual.astype(jnp.float32), ffn_gain).astype(jnp.bfloat16)
     share = route_share(ffn_in, router_weight, expert_ids[0])

time: 271 us -> 151 us (0.56)
  blocking collectives: 63 us -> 0 us
  waiting for transfers between devices: 74.9 us -> 19.4 us
  starting transfers between devices: 7.28 us -> 25 us
  between operations: 15.6 us -> 1.3 us
  matrix products: 72.9 us -> 64.6 us
  local copies, waits for them, and re-layouts: 21.8 us -> 25 us
    all_gather x2 -> x0, blocking collectives: 63 us -> none  [the longest x1 32.5 us: shards(): gathered = lax.all_gather(tokens, 'head', axis=1, tiled=True)]
    unnamed x2 -> x0, waiting for transfers between devices: 61.4 us -> none
    all_to_all x0 -> x3, starting transfers between devices: none -> 16.8 us  [the longest x2 13.3 us: broadcast_gather(): return lax.all_to_all(copies, 'head', 0, 0, tiled=True)]
    all_to_all x0 -> x3, waiting for transfers between devices: none -> 5.98 us  [the longest x2 4.9 us: broadcast_gather(): return lax.all_to_all(copies, 'head', 0, 0, tiled=True)]
    dot_general x8, matrix products: 6.32 us -> 1.51 us  [shards(): jnp.einsum('rgn,hg->rhn', bc_values[:, 1], group_pick, precision=highest)]
    unnamed x114 -> x78, local copies, waits for them, and re-layouts: 16.2 us -> 14.5 us
  transfers between devices with their start and end apart: 3 -> 5, of which waited for: 3 -> 4; matrix products, arithmetic and copies ran while one was open for 4% -> 17% of each run, Pallas kernels for 0% -> 0%
where the time goes in v2:
time: 151 us; the launch traced here: 150 us
  matrix products  64.6 us (43%)
  local copies, waits for them, and re-layouts  25 us (17%)
  starting transfers between devices  25 us (17%)
  waiting for transfers between devices  19.4 us (13%)
  other arithmetic  14.4 us (10%)
    dot_general x8, matrix products, shards(): jnp.einsum('rhpn,rhn->rhp', fresh_state, c_heads, precision=highest)  41.4 us
    unnamed x78, local copies, waits for them, and re-layouts  14.5 us
    all_to_all x2, starting transfers between devices, broadcast_gather(): return lax.all_to_all(copies, 'head', 0, 0, tiled=True)  13.3 us
    convert_element_type x2, other arithmetic, shards(): ssm_now = fresh_state.astype(jnp.bfloat16)  10.2 us
    dot_general x1, matrix products, shards(): jnp.dot(hidden, weight_down, preferred_element_type=jnp.float32)  8.05 us
    dot_general x1, matrix products, shards(): jnp.dot(normed, weight_xz, preferred_element_type=jnp.float32)  7.2 us
    all_to_all x1, waiting for transfers between devices, shards(): lax.all_to_all(computed.astype(jnp.bfloat16), 'head', split_axis=0, conca...  6.81 us
    all_to_all x1, waiting for transfers between devices, shards(): lax.all_to_all(outgoing, 'head', split_axis=0, concat_axis=0, tiled=True)  6.6 us
  transfers between devices with their start and end apart: 5, of which 4 were waited for; matrix products, arithmetic and copies ran while one was open for 17% of the time, Pallas kernels for 0%

profile of v2, /device:TPU:0, one launch (start us, length us, event | category | flops | bytes accessed | tf_op | source)
XLA Modules:
  0.0 149.7 jit_solution(11709592757917096480)
XLA Ops:
  0.6 1.5 %broadcast_in_dim.13 = bf16[8,4,2048]{2,1,0:T(4,128)(2,1)} broadcast(bf16[4,2048]{1,0:T(4,128)(2,1)} %bitcast.432), dimensions={1,2} | broadcast | bytes 147456 | tf_op jit(solution)/shard_map/broadcast_in_dim | solution.py:48
  2.1 7.3 %all-to-all-start = ((bf16[8,4,2048]{2,1,0:T(4,128)(2,1)}), bf16[8,4,2048]{2,1,0:T(4,128)(2,1)S(1)}, u32[]{:S(2)}, u32[]{:S(2)}) async-start(bf16[8,4,2048]{2,1,0:T(4,128)(2,1)} %broadcast_in_dim.13), calls=%async_computation | async-start | bytes 262144 | tf_op jit(solution)/shard_map/all_to_all | solution.py:49
  9.4 0.7 exponential_negate_fusion
  10.1 0.8 fusion.155
  10.9 0.8 copy.180
  11.9 0.2 select_reduce_fusion
  12.2 12.3 %copy.146 = bf16[2048,2048]{0,1:T(8,128)(2,1)} copy(bf16[2048,2048]{1,0:T(8,128)(2,1)} %param.28) | data formatting | bytes 16777216 | tf_op args[6]
  24.6 0.7 copy.179
  25.2 0.6 eq.82
  26.3 7.2 %fusion.75 = f32[4,8,16,2,64]{4,1,3,2,0:T(8,128)S(1)} fusion(bf16[16,2,64,2048,1]{3,2,1,0,4:T(8,128)(2,1)} %bitcast.429, bf16[4,8,2048,1,1]{2,1,0,3,4:T(8,128)(2,1)S(1)} %reshape.387), kind=kOutput, calls=%fused_computation.109 | convolution fusion | flops 268435456 | bytes 8781824 | tf_op jit(solution)/shard_map/dot_general | solution.py:87
  34.1 0.2 reshape.371
  34.3 0.3 convolution_convert_fusion.2
  34.7 0.7 broadcast_in_dim.14
  35.4 6.0 %all-to-all-start.1 = ((bf16[8,4,8,256]{3,2,1,0:T(8,128)(2,1)}), bf16[8,4,8,256]{3,2,1,0:T(8,128)(2,1)S(1)}, u32[]{:S(2)}, u32[]{:S(2)}) async-start(bf16[8,4,8,256]{3,2,1,0:T(8,128)(2,1)} %broadcast_in_dim.14), calls=%async_computation.1 | async-start | bytes 262144 | tf_op jit(solution)/shard_map/all_to_all | solution.py:49
  41.4 0.2 squeeze.121
  41.6 0.6 copy.182
  42.2 0.6 copy.183
  42.8 0.3 multiply_exponential_fusion
  43.1 0.6 fusion.152
  43.8 4.9 %all-to-all-done.1 = bf16[8,4,8,256]{3,2,1,0:T(8,128)(2,1)S(1)} async-done(((bf16[8,4,8,256]{3,2,1,0:T(8,128)(2,1)}), bf16[8,4,8,256]{3,2,1,0:T(8,128)(2,1)S(1)}, u32[]{:S(2)}, u32[]{:S(2)}) %all-to-all-start.1) | async-done | bytes 131104 | tf_op jit(solution)/shard_map/all_to_all | solution.py:49
  48.7 0.6 slice_reduce_fusion
  49.4 0.2 convolution_bitcast_fusion.7
  49.5 0.2 fusion.107
  49.7 0.2 convolution_bitcast_fusion.6
  49.9 0.2 fusion.106
  50.1 0.2 convolution_bitcast_fusion.5
  50.3 0.2 fusion.105
  50.5 0.2 convolution_bitcast_fusion.4
  50.7 0.2 fusion.104
  50.9 0.2 convolution_bitcast_fusion.3
  51.1 0.2 fusion.103
  51.3 0.2 convolution_bitcast_fusion.2
  51.5 0.2 fusion.102
  51.7 0.2 convolution_bitcast_fusion.1
  51.9 0.2 fusion.101
  52.1 0.2 convolution_bitcast_fusion
  52.2 0.2 fusion.100
  52.4 3.6 %fusion.26 = f32[4,16,1,64]{3,2,1,0:T(1,128)S(1)} fusion(f32[4,16,128,1]{2,3,1,0:T(1,128)S(1)} %bitcast.466, bf16[1,4,16,64,128]{4,3,2,1,0:T(8,128)(2,1)S(1)} %copy-done.1, f32[4,16,128]{2,1,0:T(8,128)S(1)} %convolution_bitcast_fusion.7, f32[4,16,64]{2,1,0:T(8,128)S(1)} %get-tuple-element.49, f32[4,16]{1,0:T(4,128)S(1)} %bitcast.495), kind=kOutput, calls=%fused_computation.45 | convolution fusion | flops 8388608 | bytes 1147136 | tf_op jit(solution)/shard_map/rhpn,rhn->rhp/dot_general | solution.py:130
  56.0 4.7 %fusion.24 = f32[4,16,1,64]{3,2,1,0:T(1,128)S(1)} fusion(f32[4,16,128,1]{2,3,1,0:T(1,128)S(1)} %bitcast.467, f32[4,16,128]{2,1,0:T(8,128)S(1)} %convolution_bitcast_fusion.6, f32[4,16,64]{2,1,0:T(8,128)S(1)} %get-tuple-element.48, f32[4,16]{1,0:T(4,128)S(1)} %bitcast.490, bf16[1,4,16,64,128]{4,3,2,1,0:T(8,128)(2,1)S(1)} %copy-done.1, ...), kind=kOutput, calls=%fused_computation.43 | convolution fusion | flops 11010048 | bytes 1196544 | tf_op jit(solution)/shard_map/rhpn,rhn->rhp/dot_general | solution.py:130
  60.7 5.3 %fusion.22 = f32[4,16,1,64]{3,2,1,0:T(1,128)S(1)} fusion(f32[4,16,128,1]{2,3,1,0:T(1,128)S(1)} %bitcast.468, f32[4,16,128]{2,1,0:T(8,128)S(1)} %convolution_bitcast_fusion.5, f32[4,16,64]{2,1,0:T(8,128)S(1)} %get-tuple-element.47, f32[4,16]{1,0:T(4,128)S(1)} %bitcast.486, f32[4,16,128]{2,1,0:T(8,128)S(1)} %convolution_bitcast_fusion.6, ...), kind=kOutput, calls=%fused_computation.40 | convolution fusion | flops 13631488 | bytes 1245952 | tf_op jit(solution)/shard_map/rhpn,rhn->rhp/dot_general | solution.py:130
  66.0 3.2 %fusion.19 = bf16[4,16,64,128]{3,2,1,0:T(8,128)(2,1)S(1)} fusion(f32[4,16,128]{2,1,0:T(8,128)S(1)} %convolution_bitcast_fusion.4, f32[4,16,64]{2,1,0:T(8,128)S(1)} %get-tuple-element.46, f32[4,16]{1,0:T(4,128)S(1)} %bitcast.483, f32[4,16,128]{2,1,0:T(8,128)S(1)} %convolution_bitcast_fusion.5, f32[4,16,64]{2,1,0:T(8,128)S(1)} %get-tuple-element.47, ...), kind=kLoop, calls=%fused_computation.36 | loop fusion | flops 10485760 | bytes 2294784 | tf_op jit(solution)/shard_map/convert_element_type | solution.py:133
  69.2 6.7 %fusion.20 = f32[4,16,1,64]{3,2,1,0:T(1,128)S(1)} fusion(f32[4,16,128,1]{2,3,1,0:T(1,128)S(1)} %bitcast.469, f32[4,16,128]{2,1,0:T(8,128)S(1)} %convolution_bitcast_fusion.4, f32[4,16,64]{2,1,0:T(8,128)S(1)} %get-tuple-element.46, f32[4,16]{1,0:T(4,128)S(1)} %bitcast.484, f32[4,16,128]{2,1,0:T(8,128)S(1)} %convolution_bitcast_fusion.5, ...), kind=kOutput, calls=%fused_computation.37 | convolution fusion | flops 16252928 | bytes 1295360 | tf_op jit(solution)/shard_map/rhpn,rhn->rhp/dot_general | solution.py:130
  75.9 3.6 %fusion.18 = f32[4,16,1,64]{3,2,1,0:T(1,128)S(1)} fusion(f32[4,16,128,1]{2,3,1,0:T(1,128)S(1)} %bitcast.470, bf16[4,16,64,128]{3,2,1,0:T(8,128)(2,1)S(1)} %fusion.19, f32[4,16,128]{2,1,0:T(8,128)S(1)} %convolution_bitcast_fusion.3, f32[4,16,64]{2,1,0:T(8,128)S(1)} %get-tuple-element.45, f32[4,16]{1,0:T(4,128)S(1)} %bitcast.514), kind=kOutput, calls=%fused_computation.34 | convolution fusion | flops 8388608 | bytes 1147136 | tf_op jit(solution)/shard_map/rhpn,rhn->rhp/dot_general | solution.py:130
  79.4 4.7 %fusion.16 = f32[4,16,1,64]{3,2,1,0:T(1,128)S(1)} fusion(f32[4,16,128,1]{2,3,1,0:T(1,128)S(1)} %bitcast.471, f32[4,16,128]{2,1,0:T(8,128)S(1)} %convolution_bitcast_fusion.2, f32[4,16,64]{2,1,0:T(8,128)S(1)} %get-tuple-element.44, f32[4,16]{1,0:T(4,128)S(1)} %bitcast.510, bf16[4,16,64,128]{3,2,1,0:T(8,128)(2,1)S(1)} %fusion.19, ...), kind=kOutput, calls=%fused_computation.31 | convolution fusion | flops 11010048 | bytes 1196544 | tf_op jit(solution)/shard_map/rhpn,rhn->rhp/dot_general | solution.py:130
  84.2 5.3 %fusion.14 = f32[4,16,1,64]{3,2,1,0:T(1,128)S(1)} fusion(f32[4,16,128,1]{2,3,1,0:T(1,128)S(1)} %bitcast.472, f32[4,16,128]{2,1,0:T(8,128)S(1)} %convolution_bitcast_fusion.1, f32[4,16,64]{2,1,0:T(8,128)S(1)} %get-tuple-element.43, f32[4,16]{1,0:T(4,128)S(1)} %bitcast.507, f32[4,16,128]{2,1,0:T(8,128)S(1)} %convolution_bitcast_fusion.2, ...), kind=kOutput, calls=%fused_computation.28 | convolution fusion | flops 13631488 | bytes 1245952 | tf_op jit(solution)/shard_map/rhpn,rhn->rhp/dot_general | solution.py:130
  89.5 7.6 %fusion.8 = f32[4,16,1,64]{3,2,1,0:T(1,128)S(1)} fusion(f32[4,16,128,1]{2,3,1,0:T(1,128)S(1)} %bitcast.473, f32[4,16,128]{2,1,0:T(8,128)S(1)} %convolution_bitcast_fusion, f32[4,16,64]{2,1,0:T(8,128)S(1)} %get-tuple-element.42, f32[4,16]{1,0:T(4,128)S(1)} %bitcast.505, f32[4,16,128]{2,1,0:T(8,128)S(1)} %convolution_bitcast_fusion.1, ...), kind=kOutput, calls=%fused_computation.21 | convolution fusion | flops 16252928 | bytes 1295360 | tf_op jit(solution)/shard_map/rhpn,rhn->rhp/dot_general | solution.py:130
  97.2 0.8 multiply_add_fusion.12
  97.9 1.2 stack.42
  99.2 0.8 fusion.66
  100.0 0.8 copy.176
  101.0 0.2 mul.835
  101.4 3.7 %fusion = f32[8,4,2048]{2,1,0:T(4,128)} fusion(bf16[1024,2048]{1,0:T(8,128)(2,1)} %param.39, f32[8,4,1024]{2,1,0:T(4,128)S(1)} %mul.835, f32[8,4,1024]{2,1,0:T(4,128)S(1)} %stack.43, f32[8,4,1024]{2,1,0:T(4,128)S(1)} %squeeze.121, f32[1024]{0:T(1024)S(1)} %copy-done.6), kind=kOutput, calls=%fused_computation | convolution fusion | flops 134479872 | bytes 4853760 | tf_op jit(solution)/shard_map/dot_general | solution.py:141
  105.1 3.6 %all-to-all-start.2 = ((f32[8,4,2048]{2,1,0:T(4,128)}), f32[8,4,2048]{2,1,0:T(4,128)S(1)}, u32[]{:S(2)}, u32[]{:S(2)}) async-start(f32[8,4,2048]{2,1,0:T(4,128)} %fusion), calls=%async_computation.2 | async-start | bytes 524288 | tf_op jit(solution)/shard_map/all_to_all | solution.py:142
  108.7 7.0 %add_convert_fusion = bf16[1,4,16,64,128]{4,3,2,1,0:T(8,128)(2,1)} fusion(bf16[1,4,16,64,128]{4,3,2,1,0:T(8,128)(2,1)S(1)} %copy-done.1, f32[4,16,128]{2,1,0:T(8,128)S(1)} %convolution_bitcast_fusion, f32[4,16,64]{2,1,0:T(8,128)S(1)} %get-tuple-element.42, f32[4,16,128]{2,1,0:T(8,128)S(1)} %convolution_bitcast_fusion.1, ...), kind=kLoop, calls=%fused_computation.14 | loop fusion | flops 20971520 | bytes 2492416 | tf_op jit(solution)/shard_map/convert_element_type | solution.py:133
  115.7 1.1 all-to-all-done.2
  117.5 0.7 reshape_broadcast_in_dim_reshape.3
  118.1 4.8 %all-to-all-start.3 = ((bf16[8,2,2048]{2,1,0:T(2,128)(2,1)}), bf16[8,2,2048]{2,1,0:T(2,128)(2,1)S(1)}, u32[]{:S(2)}, u32[]{:S(2)}) async-start(bf16[8,2,2048]{2,1,0:T(2,128)(2,1)} %reshape_broadcast_in_dim_reshape.3), calls=%async_computation.3 | async-start | bytes 131072 | tf_op jit(solution)/shard_map/all_to_all | solution.py:157
  123.0 0.2 fusion.108
  123.3 6.6 %all-to-all-done.3 = bf16[8,2,2048]{2,1,0:T(2,128)(2,1)S(1)} async-done(((bf16[8,2,2048]{2,1,0:T(2,128)(2,1)}), bf16[8,2,2048]{2,1,0:T(2,128)(2,1)S(1)}, u32[]{:S(2)}, u32[]{:S(2)}) %all-to-all-start.3) | async-done | bytes 65568 | tf_op jit(solution)/shard_map/all_to_all | solution.py:157
  129.9 8.0 %convolution_convert_fusion.1 = bf16[16,2048]{1,0:T(8,128)(2,1)S(1)} fusion(bf16[2048,2048]{1,0:T(8,128)(2,1)} %param.43, bf16[16,2048]{1,0:T(8,128)(2,1)S(1)} %reshape.382, bf16[2048,2048]{1,0:T(8,128)(2,1)} %param.42), kind=kOutput, calls=%fused_computation.8 | convolution fusion | flops 268566528 | bytes 16908288 | tf_op jit(solution)/shard_map/dot_general | solution.py:160
  138.0 0.7 convert_element_type.243
  138.7 3.3 %all-to-all-start.4 = ((bf16[8,2,2048]{2,1,0:T(2,128)(2,1)}), bf16[8,2,2048]{2,1,0:T(2,128)(2,1)S(1)}, u32[]{:S(2)}, u32[]{:S(2)}) async-start(bf16[8,2,2048]{2,1,0:T(2,128)(2,1)} %convert_element_type.243), calls=%async_computation.4 | async-start | bytes 131072 | tf_op jit(solution)/shard_map/all_to_all | solution.py:163
  142.0 6.8 %all-to-all-done.4 = bf16[8,2,2048]{2,1,0:T(2,128)(2,1)S(1)} async-done(((bf16[8,2,2048]{2,1,0:T(2,128)(2,1)}), bf16[8,2,2048]{2,1,0:T(2,128)(2,1)S(1)}, u32[]{:S(2)}, u32[]{:S(2)}) %all-to-all-start.4) | async-done | bytes 65568 | tf_op jit(solution)/shard_map/all_to_all | solution.py:163
  149.0 0.6 fusion.88
  (120 shorter events, 2.9 us)
Async XLA Ops:
  0.6 33.6 %copy-start = (bf16[2048,256]{1,0:T(8,128)(2,1)S(1)}, bf16[2048,256]{1,0:T(8,128)(2,1)}, u32[]{:S(2)}) copy-start(bf16[2048,256]{1,0:T(8,128)(2,1)} %param.29) | copy-start | bytes 3145732
  2.1 23.7 %all-to-all-start = ((bf16[8,4,2048]{2,1,0:T(4,128)(2,1)}), bf16[8,4,2048]{2,1,0:T(4,128)(2,1)S(1)}, u32[]{:S(2)}, u32[]{:S(2)}) async-start(bf16[8,4,2048]{2,1,0:T(4,128)(2,1)} %broadcast_in_dim.13), calls=%async_computation | async-start | bytes 262144 | tf_op jit(solution)/shard_map/all_to_all | solution.py:49
  12.0 12.5 %copy-start.28 = (s32[8]{0:T(128)}, s32[8]{0:T(128)S(1)}, u32[]{:S(2)}) copy-start(s32[8]{0:T(128)S(1)} %multiply_add_fusion.20) | copy-start | bytes 100
  12.1 12.4 %copy-start.8 = (bf16[1,4,3,1024]{3,1,2,0:T(4,128)(2,1)S(1)}, bf16[1,4,3,1024]{3,1,2,0:T(4,128)(2,1)}, u32[]{:S(2)}) copy-start(bf16[1,4,3,1024]{3,1,2,0:T(4,128)(2,1)} %param.24) | copy-start | bytes 73732
  12.1 12.4 %copy-start.21 = (bf16[1,4,3,256]{3,1,2,0:T(4,128)(2,1)S(1)}, bf16[1,4,3,256]{3,1,2,0:T(4,128)(2,1)}, u32[]{:S(2)}) copy-start(bf16[1,4,3,256]{3,1,2,0:T(4,128)(2,1)} %param.25) | copy-start | bytes 18436
  12.2 12.4 %copy-start.24 = (s32[1,4,2]{1,2,0:T(2,128)S(1)}, s32[1,4,2]{1,2,0:T(2,128)}, u32[]{:S(2)}) copy-start(s32[1,4,2]{1,2,0:T(2,128)} %param.26) | copy-start | bytes 100
  12.2 13.7 %copy-start.11 = (f32[4,1024]{1,0:T(4,128)S(1)}, f32[4,1024]{1,0:T(4,128)}, u32[]{:S(2)}) copy-start(f32[4,1024]{1,0:T(4,128)} %param.34) | copy-start | bytes 49156
  12.2 13.9 %copy-start.5 = (f32[2048]{0:T(1024)S(1)}, f32[2048]{0:T(1024)}, u32[]{:S(2)}) copy-start(f32[2048]{0:T(1024)} %param.27) | copy-start | bytes 24580
  26.3 7.6 %copy-start.23 = (f32[1024]{0:T(1024)S(1)}, f32[1024]{0:T(1024)}, u32[]{:S(2)}) copy-start(f32[1024]{0:T(1024)} %param.35) | copy-start | bytes 12292
  33.5 1.1 copy-start.2
  33.6 1.1 copy-start.26
  34.0 8.8 %copy-start.7 = (bf16[2048,16]{0,1:T(8,128)(2,1)S(1)}, bf16[2048,16]{0,1:T(8,128)(2,1)}, u32[]{:S(2)}) copy-start(bf16[2048,16]{0,1:T(8,128)(2,1)} %param.30) | copy-start | bytes 196612
  34.0 8.8 %copy-start.27 = (f32[16]{0:T(128)S(1)}, f32[16]{0:T(128)}, u32[]{:S(2)}) copy-start(f32[16]{0:T(128)} %param.31) | copy-start | bytes 196
  34.7 17.8 %copy-start.1 = (bf16[1,4,16,64,128]{4,3,2,1,0:T(8,128)(2,1)S(1)}, bf16[1,4,16,64,128]{4,3,2,1,0:T(8,128)(2,1)}, u32[]{:S(2)}) copy-start(bf16[1,4,16,64,128]{4,3,2,1,0:T(8,128)(2,1)} %param.23) | copy-start | bytes 3145732
  35.4 13.3 %all-to-all-start.1 = ((bf16[8,4,8,256]{3,2,1,0:T(8,128)(2,1)}), bf16[8,4,8,256]{3,2,1,0:T(8,128)(2,1)S(1)}, u32[]{:S(2)}, u32[]{:S(2)}) async-start(bf16[8,4,8,256]{3,2,1,0:T(8,128)(2,1)} %broadcast_in_dim.14), calls=%async_computation.1 | async-start | bytes 262144 | tf_op jit(solution)/shard_map/all_to_all | solution.py:49
  43.7 25.5 %copy-start.9 = (f32[4,1,16]{2,1,0:T(1,128)}, f32[4,1,16]{2,1,0:T(1,128)S(1)}, u32[]{:S(2)}) copy-start(f32[4,1,16]{2,1,0:T(1,128)S(1)} %get-tuple-element.57) | copy-start | bytes 772
  43.7 40.5 %copy-start.14 = (f32[4,1,16]{2,1,0:T(1,128)}, f32[4,1,16]{2,1,0:T(1,128)S(1)}, u32[]{:S(2)}) copy-start(f32[4,1,16]{2,1,0:T(1,128)S(1)} %get-tuple-element.51) | copy-start | bytes 772
  43.7 40.5 %copy-start.16 = (f32[4,1,16]{2,1,0:T(1,128)}, f32[4,1,16]{2,1,0:T(1,128)S(1)}, u32[]{:S(2)}) copy-start(f32[4,1,16]{2,1,0:T(1,128)S(1)} %get-tuple-element.52) | copy-start | bytes 772
  43.7 40.5 %copy-start.18 = (f32[4,1,16]{2,1,0:T(1,128)}, f32[4,1,16]{2,1,0:T(1,128)S(1)}, u32[]{:S(2)}) copy-start(f32[4,1,16]{2,1,0:T(1,128)S(1)} %get-tuple-element.53) | copy-start | bytes 772
  84.2 5.3 %copy-start.12 = (f32[4,1,16]{2,1,0:T(1,128)S(1)}, f32[4,1,16]{2,1,0:T(1,128)}, u32[]{:S(2)}) copy-start(f32[4,1,16]{2,1,0:T(1,128)} %get-tuple-element.50) | copy-start | bytes 772
  89.5 7.7 %copy-start.30 = (f32[16]{0:T(128)S(1)}, f32[16]{0:T(128)}, u32[]{:S(2)}) copy-start(f32[16]{0:T(128)} %param.33) | copy-start | bytes 196
  89.5 9.7 %copy-start.3 = (f32[4,8,16,2,64]{4,1,3,2,0:T(8,128)S(1)}, f32[4,8,16,2,64]{4,1,3,2,0:T(8,128)}, u32[]{:S(2)}) copy-start(f32[4,8,16,2,64]{4,1,3,2,0:T(8,128)} %copy-done.2) | copy-start | bytes 786436
  97.1 4.2 %copy-start.6 = (f32[1024]{0:T(1024)S(1)}, f32[1024]{0:T(1024)}, u32[]{:S(2)}) copy-start(f32[1024]{0:T(1024)} %param.38) | copy-start | bytes 12292
  101.3 7.3 %copy-start.10 = (f32[4,1,16]{2,1,0:T(1,128)S(1)}, f32[4,1,16]{2,1,0:T(1,128)}, u32[]{:S(2)}) copy-start(f32[4,1,16]{2,1,0:T(1,128)} %copy-done.9) | copy-start | bytes 772
  101.4 7.3 %copy-start.13 = (f32[4,1,16]{2,1,0:T(1,128)S(1)}, f32[4,1,16]{2,1,0:T(1,128)}, u32[]{:S(2)}) copy-start(f32[4,1,16]{2,1,0:T(1,128)} %get-tuple-element.50) | copy-start | bytes 772
  101.4 7.3 %copy-start.15 = (f32[4,1,16]{2,1,0:T(1,128)S(1)}, f32[4,1,16]{2,1,0:T(1,128)}, u32[]{:S(2)}) copy-start(f32[4,1,16]{2,1,0:T(1,128)} %copy-done.14) | copy-start | bytes 772
  101.4 7.3 %copy-start.17 = (f32[4,1,16]{2,1,0:T(1,128)S(1)}, f32[4,1,16]{2,1,0:T(1,128)}, u32[]{:S(2)}) copy-start(f32[4,1,16]{2,1,0:T(1,128)} %copy-done.16) | copy-start | bytes 772
  101.4 7.3 %copy-start.19 = (f32[4,1,16]{2,1,0:T(1,128)S(1)}, f32[4,1,16]{2,1,0:T(1,128)}, u32[]{:S(2)}) copy-start(f32[4,1,16]{2,1,0:T(1,128)} %copy-done.18) | copy-start | bytes 772
  105.1 11.8 %copy-start.4 = (bf16[1,4,2048]{2,1,0:T(4,128)(2,1)S(1)}, bf16[1,4,2048]{2,1,0:T(4,128)(2,1)}, u32[]{:S(2)}) copy-start(bf16[1,4,2048]{2,1,0:T(4,128)(2,1)} %param.22) | copy-start | bytes 49156
  105.1 11.9 %copy-start.20 = (f32[2048]{0:T(1024)S(1)}, f32[2048]{0:T(1024)}, u32[]{:S(2)}) copy-start(f32[2048]{0:T(1024)} %param.40) | copy-start | bytes 24580
  105.1 12.0 %copy-start.31 = (bf16[2048,8]{0,1:T(8,128)(2,1)S(1)}, bf16[2048,8]{0,1:T(8,128)(2,1)}, u32[]{:S(2)}) copy-start(bf16[2048,8]{0,1:T(8,128)(2,1)} %param.41) | copy-start | bytes 98308
  105.1 12.2 %copy-start.29 = (s32[8]{0:T(128)S(1)}, s32[8]{0:T(128)}, u32[]{:S(2)}) copy-start(s32[8]{0:T(128)} %copy-done.28) | copy-start | bytes 100
  105.1 17.9 %copy-start.25 = (s32[4,2]{1,0:T(4,128)S(1)}, s32[4,2]{1,0:T(4,128)}, u32[]{:S(2)}) copy-start(s32[4,2]{1,0:T(4,128)} %copy.179) | copy-start | bytes 100
  105.1 11.7 %all-to-all-start.2 = ((f32[8,4,2048]{2,1,0:T(4,128)}), f32[8,4,2048]{2,1,0:T(4,128)S(1)}, u32[]{:S(2)}, u32[]{:S(2)}) async-start(f32[8,4,2048]{2,1,0:T(4,128)} %fusion), calls=%async_computation.2 | async-start | bytes 524288 | tf_op jit(solution)/shard_map/all_to_all | solution.py:142
  118.1 11.7 %all-to-all-start.3 = ((bf16[8,2,2048]{2,1,0:T(2,128)(2,1)}), bf16[8,2,2048]{2,1,0:T(2,128)(2,1)S(1)}, u32[]{:S(2)}, u32[]{:S(2)}) async-start(bf16[8,2,2048]{2,1,0:T(2,128)(2,1)} %reshape_broadcast_in_dim_reshape.3), calls=%async_computation.3 | async-start | bytes 131072 | tf_op jit(solution)/shard_map/all_to_all | solution.py:157
  129.9 19.0 %copy-start.22 = (pred[4,2,16]{2,1,0:T(4,128)(4,1)S(1)}, pred[4,2,16]{2,1,0:T(4,128)(4,1)}, u32[]{:S(2)}) copy-start(pred[4,2,16]{2,1,0:T(4,128)(4,1)} %eq.82) | copy-start | bytes 388
  138.7 10.2 %all-to-all-start.4 = ((bf16[8,2,2048]{2,1,0:T(2,128)(2,1)}), bf16[8,2,2048]{2,1,0:T(2,128)(2,1)S(1)}, u32[]{:S(2)}, u32[]{:S(2)}) async-start(bf16[8,2,2048]{2,1,0:T(2,128)(2,1)} %convert_element_type.243), calls=%async_computation.4 | async-start | bytes 131072 | tf_op jit(solution)/shard_map/all_to_all | solution.py:163

commit v3 on v2

--- a/solution.py
+++ b/solution.py
@@ -1,6 +1,7 @@
 import jax
 import jax.numpy as jnp
 from jax import lax
+from jax.experimental import pallas as pl
 from jax.sharding import PartitionSpec as P
 
 HEADS = 128
@@ -42,6 +43,44 @@
     return jnp.square(
         jnp.maximum(jnp.dot(rows_in, weight_up, preferred_element_type=jnp.float32), 0.0)
     ).astype(jnp.bfloat16)
+
+
+def ssm_scan_kernel(s_ref, dec_ref, dx_ref, b_ref, c_ref, s_out_ref, read_ref):
+    tiles = s_ref.shape[1]
+    steps = dec_ref.shape[2]
+
+    def tile(j, carry):
+        state = s_ref[0, j].astype(jnp.float32)
+        b_all = b_ref[0, j]
+        c_all = c_ref[0, j]
+        dec_all = dec_ref[0, j]
+        dx_all = dx_ref[0, j]
+        for t in range(steps):
+            fresh = dec_all[t : t + 1, :] * state + dx_all[t : t + 1, :] * b_all[:, t : t + 1]
+            read_ref[0, j, t : t + 1, :] = jnp.sum(fresh * c_all[:, t : t + 1], axis=0, keepdims=True)
+            state = fresh.astype(jnp.bfloat16).astype(jnp.float32)
+        s_out_ref[0, j] = state.astype(jnp.bfloat16)
+        return carry
+
+    lax.fori_loop(0, tiles, tile, 0)
+
+
+def ssm_scan(state_tiles, decay_tiles, dx_tiles, b_tiles, c_tiles):
+    requests, tiles, state_dim, lanes = state_tiles.shape
+    steps = decay_tiles.shape[2]
+    big = pl.BlockSpec((1, tiles, state_dim, lanes), lambda r: (r, 0, 0, 0))
+    per_step = pl.BlockSpec((1, tiles, steps, lanes), lambda r: (r, 0, 0, 0))
+    columns = pl.BlockSpec((1, tiles, state_dim, steps), lambda r: (r, 0, 0, 0))
+    return pl.pallas_call(
+        ssm_scan_kernel,
+        grid=(requests,),
+        in_specs=[big, per_step, per_step, columns, columns],
+        out_specs=[big, per_step],
+        out_shape=[
+            jax.ShapeDtypeStruct(state_tiles.shape, jnp.bfloat16),
+            jax.ShapeDtypeStruct(decay_tiles.shape, jnp.float32),
+        ],
+    )(state_tiles, decay_tiles, dx_tiles, b_tiles, c_tiles)
 
 
 def broadcast_gather(block, count):
@@ -108,30 +147,38 @@
     bc_all = jnp.moveaxis(broadcast_gather(bc_conv, head_count), 0, 2).reshape(
         requests, STEPS, -1
     )
-    bc_list = [bc_all[:, step_index] for step_index in range(STEPS)]
-    head_global = my_index * heads_local + jnp.arange(heads_local)
-    group_pick = (head_global[:, None] // (HEADS // G) == jnp.arange(G)[None, :]).astype(
-        jnp.float32
-    )
     x_heads = x_conv.reshape(requests, STEPS, heads_local, head_dim)
     decay_rate = jnp.exp(delta * -jnp.exp(decay_log))
-    ssm_now = ssm_state[0]
-    readings = []
-    for step_index in range(STEPS):
-        bc_values = bc_list[step_index].astype(jnp.float32).reshape(requests, 2, G, state_dim)
-        b_heads = jnp.einsum("rgn,hg->rhn", bc_values[:, 0], group_pick, precision=highest)
-        c_heads = jnp.einsum("rgn,hg->rhn", bc_values[:, 1], group_pick, precision=highest)
-        x_step = x_heads[:, step_index]
-        fresh_state = (
-            decay_rate[:, step_index, :, None, None] * ssm_now.astype(jnp.float32)
-            + (delta[:, step_index, :, None] * x_step)[..., None] * b_heads[:, :, None, :]
-        )
-        readings.append(
-            jnp.einsum("rhpn,rhn->rhp", fresh_state, c_heads, precision=highest)
-            + skip_gain[:, None] * x_step
-        )
-        ssm_now = fresh_state.astype(jnp.bfloat16)
-    gated_out = jnp.stack(readings, axis=1) * jax.nn.silu(z_gate)
+    pack = 2 if heads_local % 2 == 0 else 1
+    tiles = heads_local // pack
+    lanes = pack * head_dim
+
+    def to_tiles(per_head):
+        return per_head.reshape(requests, STEPS, tiles, lanes).transpose(0, 2, 1, 3)
+
+    decay_tiles = to_tiles(
+        jnp.broadcast_to(decay_rate[..., None], (requests, STEPS, heads_local, head_dim))
+    )
+    dx_tiles = to_tiles(delta[..., None] * x_heads)
+    tile_group = (my_index * heads_local + jnp.arange(tiles) * pack) // (HEADS // G)
+    bc_values = bc_all.astype(jnp.float32).reshape(requests, STEPS, 2, G, state_dim)
+    b_tiles = jnp.take(bc_values[:, :, 0], tile_group, axis=2).transpose(0, 2, 3, 1)
+    c_tiles = jnp.take(bc_values[:, :, 1], tile_group, axis=2).transpose(0, 2, 3, 1)
+    state_tiles = (
+        ssm_state[0]
+        .reshape(requests, tiles, pack, head_dim, state_dim)
+        .transpose(0, 1, 4, 2, 3)
+        .reshape(requests, tiles, state_dim, lanes)
+    )
+    state_out, read_tiles = ssm_scan(state_tiles, decay_tiles, dx_tiles, b_tiles, c_tiles)
+    ssm_now = (
+        state_out.reshape(requests, tiles, state_dim, pack, head_dim)
+        .transpose(0, 1, 3, 4, 2)
+        .reshape(requests, heads_local, head_dim, state_dim)
+    )
+    scan_read = read_tiles.transpose(0, 2, 1, 3).reshape(requests, STEPS, heads_local, head_dim)
+    readings = scan_read + skip_gain[:, None] * x_heads
+    gated_out = readings * jax.nn.silu(z_gate)
     group_normed = (
         norm_rows(gated_out, gated_gain.reshape(heads_local, head_dim))
         .astype(jnp.bfloat16)

time: 151 us -> 120 us (0.79)
  matrix products: 64.6 us -> 20.3 us
  Pallas kernels: 0 us -> 13.6 us
  other arithmetic: 14.4 us -> 5.34 us
  local copies, waits for them, and re-layouts: 25 us -> 34 us
  waiting for transfers between devices: 19.4 us -> 21.1 us
  starting transfers between devices: 25 us -> 23.4 us
    dot_general x24 -> x0, matrix products: 44.5 us -> none  [the longest x8 41.4 us: shards(): jnp.einsum('rhpn,rhn->rhp', fresh_state, c_heads, precision=highest)]
    pallas_call x0 -> x1, Pallas kernels: none -> 13.6 us  [ssm_scan(): pl.pallas_call(ssm_scan_kernel, grid=(requests,), in_specs=[big, per_step...]
    convert_element_type x2 -> x1, other arithmetic: 10.2 us -> 0.02 us  [shards(): bc_all.astype(jnp.float32).reshape(requests, STEPS, 2, G, state_dim)]
    select_n x0 -> x2, local copies, waits for them, and re-layouts: none -> 3.88 us  [the longest x1 1.94 us: shards(): jnp.take(bc_values[:, :, 0], tile_group, axis=2).transpose(0, 2, 3, 1)]
    reshape x1 -> x5, local copies, waits for them, and re-layouts: 0.01 us -> 2.89 us  [the longest x1 1.31 us: shards(): state_tiles = ssm_state[0].reshape(requests, tiles, pack, head_dim, state...]
    broadcast_in_dim x2, local copies, waits for them, and re-layouts: 0.03 us -> 1.58 us  [shards(): return (layer_out[None], ssm_now[None], conv_x_new[None], conv_bc_new[None])]
    all_to_all x1, waiting for transfers between devices: 1.08 us -> 2.6 us  [shards(): lax.all_to_all(mixer_part.reshape(head_count, tok_local, width), 'head',...]
    unnamed x78 -> x42, local copies, waits for them, and re-layouts: 14.5 us -> 14.4 us
  transfers between devices with their start and end apart: 5 -> 5, of which waited for: 4 -> 4; matrix products, arithmetic and copies ran while one was open for 17% -> 22% of each run, Pallas kernels for 0% -> 0%
where the time goes in v3:
time: 120 us; the launch traced here: 119 us
  local copies, waits for them, and re-layouts  34 us (28%)
  starting transfers between devices  23.4 us (20%)
  waiting for transfers between devices  21.1 us (18%)
  matrix products  20.3 us (17%)
  Pallas kernels  13.6 us (11%)
  other arithmetic  5.34 us (4%)
    unnamed x42, local copies, waits for them, and re-layouts  14.4 us
    pallas_call x1, Pallas kernels, ssm_scan(): pl.pallas_call(ssm_scan_kernel, grid=(requests,), in_specs=[big, per_step...  13.6 us
    all_to_all x2, starting transfers between devices, broadcast_gather(): return lax.all_to_all(copies, 'head', 0, 0, tiled=True)  13.2 us
    dot_general x1, matrix products, shards(): jnp.dot(hidden, weight_down, preferred_element_type=jnp.float32)  8.05 us
    dot_general x1, matrix products, shards(): jnp.dot(normed, weight_xz, preferred_element_type=jnp.float32)  7.23 us
    all_to_all x1, waiting for transfers between devices, shards(): lax.all_to_all(computed.astype(jnp.bfloat16), 'head', split_axis=0, conca...  6.81 us
    all_to_all x1, waiting for transfers between devices, shards(): lax.all_to_all(outgoing, 'head', split_axis=0, concat_axis=0, tiled=True)  6.45 us
    all_to_all x2, waiting for transfers between devices, broadcast_gather(): return lax.all_to_all(copies, 'head', 0, 0, tiled=True)  5.23 us
  transfers between devices with their start and end apart: 5, of which 4 were waited for; matrix products, arithmetic and copies ran while one was open for 22% of the time, Pallas kernels for 0%

profile of v3, /device:TPU:0, one launch (start us, length us, event | category | flops | bytes accessed | tf_op | source)
XLA Modules:
  0.0 118.8 jit_solution(6442054360408591607)
XLA Ops:
  0.6 1.5 %broadcast_in_dim.24 = bf16[8,4,2048]{2,1,0:T(4,128)(2,1)} broadcast(bf16[4,2048]{1,0:T(4,128)(2,1)} %bitcast.144), dimensions={1,2} | broadcast | bytes 147456 | tf_op jit(solution)/shard_map/broadcast_in_dim | solution.py:87
  2.1 7.3 %all-to-all-start = ((bf16[8,4,2048]{2,1,0:T(4,128)(2,1)}), bf16[8,4,2048]{2,1,0:T(4,128)(2,1)S(1)}, u32[]{:S(2)}, u32[]{:S(2)}) async-start(bf16[8,4,2048]{2,1,0:T(4,128)(2,1)} %broadcast_in_dim.24), calls=%async_computation | async-start | bytes 262144 | tf_op jit(solution)/shard_map/all_to_all | solution.py:88
  9.4 0.7 exponential_negate_fusion
  10.0 0.8 fusion.48
  10.9 0.8 copy.146
  11.9 0.2 select_reduce_fusion
  12.1 0.5 multiply_add_fusion
  12.7 12.3 %copy.126 = bf16[2048,2048]{0,1:T(8,128)(2,1)} copy(bf16[2048,2048]{1,0:T(8,128)(2,1)} %param.30) | data formatting | bytes 16777216 | tf_op args[6]
  25.0 1.3 %copy.136.s_ref = bf16[4,8,128,128]{3,2,1,0:T(8,128)(2,1)} copy(bf16[4,8,128,128]{2,3,1,0:T(8,128)(2,1)S(1)} %bitcast.141) | data formatting | bytes 2097152 | tf_op jit(solution)/shard_map/reshape | solution.py:171
  26.4 0.7 mul.295
  27.1 0.2 multiply_reduce_fusion
  27.3 0.1 multiply_convert_fusion
  27.5 7.2 %fusion.19 = f32[4,8,16,2,64]{4,1,3,2,0:T(8,128)S(1)} fusion(bf16[16,2,64,2048,1]{3,2,1,0,4:T(8,128)(2,1)} %bitcast.138, bf16[4,8,2048,1,1]{2,1,0,3,4:T(8,128)(2,1)S(1)} %reshape.262), kind=kOutput, calls=%fused_computation.45 | convolution fusion | flops 268435456 | bytes 8781824 | tf_op jit(solution)/shard_map/dot_general | solution.py:126
  34.9 0.3 multiply_exponential_fusion
  35.1 0.1 mul.259
  35.3 0.1 mul.260
  35.4 0.1 convert_element_type.115
  35.6 0.3 convolution_convert_fusion.2
  36.0 0.7 broadcast_in_dim.26
  36.6 6.0 %all-to-all-start.1 = ((bf16[8,4,8,256]{3,2,1,0:T(8,128)(2,1)}), bf16[8,4,8,256]{3,2,1,0:T(8,128)(2,1)S(1)}, u32[]{:S(2)}, u32[]{:S(2)}) async-start(bf16[8,4,8,256]{3,2,1,0:T(8,128)(2,1)} %broadcast_in_dim.26), calls=%async_computation.1 | async-start | bytes 262144 | tf_op jit(solution)/shard_map/all_to_all | solution.py:88
  42.7 0.8 fusion.18
  43.5 0.1 reshape.232
  43.6 0.1 broadcast_in_dim.25
  43.8 0.1 reshape.227
  43.9 0.7 copy.176
  44.6 0.2 squeeze.24
  44.8 5.2 %all-to-all-done.1 = bf16[8,4,8,256]{3,2,1,0:T(8,128)(2,1)S(1)} async-done(((bf16[8,4,8,256]{3,2,1,0:T(8,128)(2,1)}), bf16[8,4,8,256]{3,2,1,0:T(8,128)(2,1)S(1)}, u32[]{:S(2)}, u32[]{:S(2)}) %all-to-all-start.1) | async-done | bytes 131104 | tf_op jit(solution)/shard_map/all_to_all | solution.py:88
  50.0 0.2 copy.131
  50.3 0.6 gather_fusion.1
  50.9 0.6 gather_fusion
  51.4 0.1 broadcast_select_fusion
  51.5 1.9 %copy.133 = f32[8,4,8,128]{2,3,0,1:T(8,128)} copy(f32[8,4,8,128]{3,2,1,0:T(8,128)S(1)} %get-tuple-element.44) | data formatting | bytes 262144 | tf_op jit(solution)/shard_map/jit(_take)/select_n | solution.py:165
  53.5 1.9 %copy.135 = f32[8,4,8,128]{2,3,0,1:T(8,128)} copy(f32[8,4,8,128]{3,2,1,0:T(8,128)S(1)} %get-tuple-element.43) | data formatting | bytes 262144 | tf_op jit(solution)/shard_map/jit(_take)/select_n | solution.py:166
  55.4 13.6 %shard_map.237 = (bf16[4,8,128,128]{3,2,1,0:T(8,128)(2,1)}, f32[4,8,8,128]{3,2,1,0:T(8,128)}) custom-call(bf16[4,8,128,128]{3,2,1,0:T(8,128)(2,1)} %copy.136.s_ref, f32[4,8,8,128]{3,2,1,0:T(8,128)} %bitcast.143, f32[4,8,8,128]{3,2,1,0:T(8,128)} %get-tuple-element.31.dx_ref, f32[4,8,128,8]{3,2,1,0:T(8,128)} %bitcast.139, f32[4,8,128,8]{3,2,1,0:T(8,128)} %bitcast.140), custom_call_target="tpu_custom_call" | custom-call | tf_op jit(solution)/shard_map/pallas_call | solution.py:74
  69.0 1.0 copy.137
  70.0 0.1 reshape.231
  70.1 0.7 reshape.229
  70.8 1.0 fusion.11
  71.9 0.1 mul.305
  72.0 0.2 mul.306
  72.2 3.8 %fusion = f32[8,4,2048]{2,1,0:T(4,128)} fusion(bf16[1024,2048]{1,0:T(8,128)(2,1)} %param.41, f32[8,4,1024]{2,1,0:T(4,128)S(1)} %mul.306, f32[8,4,1024]{2,1,0:T(4,128)S(1)} %squeeze.24, f32[8,4,1024]{2,1,0:T(4,128)} %reshape.229, f32[8,4,1024]{2,1,0:T(4,128)S(1)} %reshape.230, f32[1024]{0:T(1024)} %param.40, f32[1024]{0:T(1024)} %mul.295), kind=kOutput, calls=%fused_computation.2 | convolution fusion | flops 134545408 | bytes 4988928 | tf_op jit(solution)/shard_map/dot_general | solution.py:188
  76.1 3.4 %all-to-all-start.2 = ((f32[8,4,2048]{2,1,0:T(4,128)}), f32[8,4,2048]{2,1,0:T(4,128)S(1)}, u32[]{:S(2)}, u32[]{:S(2)}) async-start(f32[8,4,2048]{2,1,0:T(4,128)} %fusion), calls=%async_computation.2 | async-start | bytes 524288 | tf_op jit(solution)/shard_map/all_to_all | solution.py:189
  79.5 0.7 iota_compare_fusion.3
  80.1 0.8 copy.145
  80.9 0.9 slice_bitcast_fusion
  81.8 0.6 copy.149
  82.4 0.7 slice_bitcast_fusion.1
  83.1 0.6 copy.150
  83.7 1.3 %copy.148 = bf16[4,8,128,128]{2,3,1,0:T(8,128)(2,1)} copy(bf16[4,8,128,128]{3,2,1,0:T(8,128)(2,1)S(1)} %copy-done.2) | data formatting | bytes 2097152 | tf_op jit(solution)/shard_map/pallas_call | solution.py:74
  85.0 2.6 %all-to-all-done.2 = f32[8,4,2048]{2,1,0:T(4,128)S(1)} async-done(((f32[8,4,2048]{2,1,0:T(4,128)}), f32[8,4,2048]{2,1,0:T(4,128)S(1)}, u32[]{:S(2)}, u32[]{:S(2)}) %all-to-all-start.2) | async-done | bytes 262176 | tf_op jit(solution)/shard_map/all_to_all | solution.py:189
  87.7 0.1 fusion.26
  88.0 0.1 convolution_convert_fusion
  88.1 0.7 reshape_broadcast_in_dim_reshape.3
  88.8 3.3 %all-to-all-start.3 = ((bf16[8,2,2048]{2,1,0:T(2,128)(2,1)}), bf16[8,2,2048]{2,1,0:T(2,128)(2,1)S(1)}, u32[]{:S(2)}, u32[]{:S(2)}) async-start(bf16[8,2,2048]{2,1,0:T(2,128)(2,1)} %reshape_broadcast_in_dim_reshape.3), calls=%async_computation.3 | async-start | bytes 131072 | tf_op jit(solution)/shard_map/all_to_all | solution.py:204
  92.2 0.1 fusion.49
  92.3 0.2 fusion.37
  92.5 0.1 copy.155
  92.6 6.4 %all-to-all-done.3 = bf16[8,2,2048]{2,1,0:T(2,128)(2,1)S(1)} async-done(((bf16[8,2,2048]{2,1,0:T(2,128)(2,1)}), bf16[8,2,2048]{2,1,0:T(2,128)(2,1)S(1)}, u32[]{:S(2)}, u32[]{:S(2)}) %all-to-all-start.3) | async-done | bytes 65568 | tf_op jit(solution)/shard_map/all_to_all | solution.py:204
  99.1 8.0 %convolution_convert_fusion.1 = bf16[16,2048]{1,0:T(8,128)(2,1)S(1)} fusion(bf16[2048,2048]{1,0:T(8,128)(2,1)} %param.45, bf16[16,2048]{1,0:T(8,128)(2,1)S(1)} %reshape.234, bf16[2048,2048]{1,0:T(8,128)(2,1)} %param.44), kind=kOutput, calls=%fused_computation.8 | convolution fusion | flops 268566528 | bytes 16908288 | tf_op jit(solution)/shard_map/dot_general | solution.py:207
  107.1 0.7 convert_element_type.134
  107.8 3.3 %all-to-all-start.4 = ((bf16[8,2,2048]{2,1,0:T(2,128)(2,1)}), bf16[8,2,2048]{2,1,0:T(2,128)(2,1)S(1)}, u32[]{:S(2)}, u32[]{:S(2)}) async-start(bf16[8,2,2048]{2,1,0:T(2,128)(2,1)} %convert_element_type.134), calls=%async_computation.4 | async-start | bytes 131072 | tf_op jit(solution)/shard_map/all_to_all | solution.py:210
  111.2 6.8 %all-to-all-done.4 = bf16[8,2,2048]{2,1,0:T(2,128)(2,1)S(1)} async-done(((bf16[8,2,2048]{2,1,0:T(2,128)(2,1)}), bf16[8,2,2048]{2,1,0:T(2,128)(2,1)S(1)}, u32[]{:S(2)}, u32[]{:S(2)}) %all-to-all-start.4) | async-done | bytes 65568 | tf_op jit(solution)/shard_map/all_to_all | solution.py:210
  118.0 0.1 fusion.4
  118.2 0.6 fusion.33
  (75 shorter events, 1.3 us)
Async XLA Ops:
  0.6 34.9 %copy-start = (bf16[2048,256]{1,0:T(8,128)(2,1)S(1)}, bf16[2048,256]{1,0:T(8,128)(2,1)}, u32[]{:S(2)}) copy-start(bf16[2048,256]{1,0:T(8,128)(2,1)} %param.31) | copy-start | bytes 3145732
  2.1 24.9 %all-to-all-start = ((bf16[8,4,2048]{2,1,0:T(4,128)(2,1)}), bf16[8,4,2048]{2,1,0:T(4,128)(2,1)S(1)}, u32[]{:S(2)}, u32[]{:S(2)}) async-start(bf16[8,4,2048]{2,1,0:T(4,128)(2,1)} %broadcast_in_dim.24), calls=%async_computation | async-start | bytes 262144 | tf_op jit(solution)/shard_map/all_to_all | solution.py:88
  12.6 12.3 %copy-start.8 = (bf16[1,4,3,1024]{3,1,2,0:T(4,128)(2,1)S(1)}, bf16[1,4,3,1024]{3,1,2,0:T(4,128)(2,1)}, u32[]{:S(2)}) copy-start(bf16[1,4,3,1024]{3,1,2,0:T(4,128)(2,1)} %param.26) | copy-start | bytes 73732
  12.6 12.4 %copy-start.1 = (bf16[1,4,16,64,128]{4,3,2,1,0:T(8,128)(2,1)S(1)}, bf16[1,4,16,64,128]{4,3,2,1,0:T(8,128)(2,1)}, u32[]{:S(2)}) copy-start(bf16[1,4,16,64,128]{4,3,2,1,0:T(8,128)(2,1)} %param.25) | copy-start | bytes 3145732
  12.6 13.7 %copy-start.11 = (bf16[1,4,3,256]{3,1,2,0:T(4,128)(2,1)S(1)}, bf16[1,4,3,256]{3,1,2,0:T(4,128)(2,1)}, u32[]{:S(2)}) copy-start(bf16[1,4,3,256]{3,1,2,0:T(4,128)(2,1)} %param.27) | copy-start | bytes 18436
  12.6 13.7 %copy-start.13 = (f32[16]{0:T(128)S(1)}, f32[16]{0:T(128)}, u32[]{:S(2)}) copy-start(f32[16]{0:T(128)} %param.35) | copy-start | bytes 196
  12.6 14.4 %copy-start.9 = (f32[4,1024]{1,0:T(4,128)S(1)}, f32[4,1024]{1,0:T(4,128)}, u32[]{:S(2)}) copy-start(f32[4,1024]{1,0:T(4,128)} %param.36) | copy-start | bytes 49156
  12.6 14.7 %copy-start.6 = (f32[2048]{0:T(1024)S(1)}, f32[2048]{0:T(1024)}, u32[]{:S(2)}) copy-start(f32[2048]{0:T(1024)} %param.29) | copy-start | bytes 24580
  27.5 7.4 %copy-start.7 = (bf16[2048,16]{0,1:T(8,128)(2,1)S(1)}, bf16[2048,16]{0,1:T(8,128)(2,1)}, u32[]{:S(2)}) copy-start(bf16[2048,16]{0,1:T(8,128)(2,1)} %param.32) | copy-start | bytes 196612
  27.5 7.4 %copy-start.15 = (f32[16]{0:T(128)S(1)}, f32[16]{0:T(128)}, u32[]{:S(2)}) copy-start(f32[16]{0:T(128)} %param.33) | copy-start | bytes 196
  27.5 8.4 %copy-start.14 = (f32[256]{0:T(256)S(1)}, f32[256]{0:T(256)}, u32[]{:S(2)}) copy-start(f32[256]{0:T(256)} %param.39) | copy-start | bytes 3076
  27.5 15.2 %copy-start.12 = (f32[1024]{0:T(1024)S(1)}, f32[1024]{0:T(1024)}, u32[]{:S(2)}) copy-start(f32[1024]{0:T(1024)} %param.37) | copy-start | bytes 12292
  35.6 14.7 %copy-start.3 = (bf16[4,8,1024]{2,1,0:T(8,128)(2,1)}, bf16[4,8,1024]{2,1,0:T(8,128)(2,1)S(1)}, u32[]{:S(2)}) copy-start(bf16[4,8,1024]{2,1,0:T(8,128)(2,1)S(1)} %convert_element_type.115) | copy-start | bytes 196612
  35.9 14.3 %copy-start.5 = (bf16[4,8,256]{2,1,0:T(8,128)(2,1)}, bf16[4,8,256]{2,1,0:T(8,128)(2,1)S(1)}, u32[]{:S(2)}) copy-start(bf16[4,8,256]{2,1,0:T(8,128)(2,1)S(1)} %convolution_convert_fusion.2) | copy-start | bytes 49156
  36.6 13.3 %all-to-all-start.1 = ((bf16[8,4,8,256]{3,2,1,0:T(8,128)(2,1)}), bf16[8,4,8,256]{3,2,1,0:T(8,128)(2,1)S(1)}, u32[]{:S(2)}, u32[]{:S(2)}) async-start(bf16[8,4,8,256]{3,2,1,0:T(8,128)(2,1)} %broadcast_in_dim.26), calls=%async_computation.1 | async-start | bytes 262144 | tf_op jit(solution)/shard_map/all_to_all | solution.py:88
  55.4 32.3 %copy-start.4 = (bf16[1,4,2048]{2,1,0:T(4,128)(2,1)S(1)}, bf16[1,4,2048]{2,1,0:T(4,128)(2,1)}, u32[]{:S(2)}) copy-start(bf16[1,4,2048]{2,1,0:T(4,128)(2,1)} %param.24) | copy-start | bytes 49156
  69.0 14.7 %copy-start.2 = (bf16[4,8,128,128]{3,2,1,0:T(8,128)(2,1)S(1)}, bf16[4,8,128,128]{3,2,1,0:T(8,128)(2,1)}, u32[]{:S(2)}) copy-start(bf16[4,8,128,128]{3,2,1,0:T(8,128)(2,1)} %get-tuple-element.8) | copy-start | bytes 3145732
  71.8 16.0 %copy-start.10 = (f32[2048]{0:T(1024)S(1)}, f32[2048]{0:T(1024)}, u32[]{:S(2)}) copy-start(f32[2048]{0:T(1024)} %param.42) | copy-start | bytes 24580
  71.8 16.2 %copy-start.16 = (s32[8]{0:T(128)S(1)}, s32[8]{0:T(128)}, u32[]{:S(2)}) copy-start(s32[8]{0:T(128)} %multiply_add_fusion) | copy-start | bytes 100
  71.8 20.4 %copy-start.17 = (bf16[2048,8]{0,1:T(8,128)(2,1)S(1)}, bf16[2048,8]{0,1:T(8,128)(2,1)}, u32[]{:S(2)}) copy-start(bf16[2048,8]{0,1:T(8,128)(2,1)} %param.43) | copy-start | bytes 98308
  76.1 11.6 %all-to-all-start.2 = ((f32[8,4,2048]{2,1,0:T(4,128)}), f32[8,4,2048]{2,1,0:T(4,128)S(1)}, u32[]{:S(2)}, u32[]{:S(2)}) async-start(f32[8,4,2048]{2,1,0:T(4,128)} %fusion), calls=%async_computation.2 | async-start | bytes 524288 | tf_op jit(solution)/shard_map/all_to_all | solution.py:189
  88.8 10.2 %all-to-all-start.3 = ((bf16[8,2,2048]{2,1,0:T(2,128)(2,1)}), bf16[8,2,2048]{2,1,0:T(2,128)(2,1)S(1)}, u32[]{:S(2)}, u32[]{:S(2)}) async-start(bf16[8,2,2048]{2,1,0:T(2,128)(2,1)} %reshape_broadcast_in_dim_reshape.3), calls=%async_computation.3 | async-start | bytes 131072 | tf_op jit(solution)/shard_map/all_to_all | solution.py:204
  107.8 10.2 %all-to-all-start.4 = ((bf16[8,2,2048]{2,1,0:T(2,128)(2,1)}), bf16[8,2,2048]{2,1,0:T(2,128)(2,1)S(1)}, u32[]{:S(2)}, u32[]{:S(2)}) async-start(bf16[8,2,2048]{2,1,0:T(2,128)(2,1)} %convert_element_type.134), calls=%async_computation.4 | async-start | bytes 131072 | tf_op jit(solution)/shard_map/all_to_all | solution.py:210

commit v4 on v3

--- a/solution.py
+++ b/solution.py
@@ -43,6 +43,26 @@
     return jnp.square(
         jnp.maximum(jnp.dot(rows_in, weight_up, preferred_element_type=jnp.float32), 0.0)
     ).astype(jnp.bfloat16)
+
+
+def column_matmul_kernel(a_ref, w_ref, o_ref):
+    o_ref[...] = jnp.dot(a_ref[...], w_ref[...], preferred_element_type=jnp.float32)
+
+
+def column_matmul(rows, weight):
+    m, k = rows.shape
+    cols = weight.shape[1]
+    block = min(512, cols)
+    return pl.pallas_call(
+        column_matmul_kernel,
+        grid=(cols // block,),
+        in_specs=[
+            pl.BlockSpec((m, k), lambda j: (0, 0)),
+            pl.BlockSpec((k, block), lambda j: (0, j)),
+        ],
+        out_specs=pl.BlockSpec((m, block), lambda j: (0, j)),
+        out_shape=jax.ShapeDtypeStruct((m, cols), jnp.float32),
+    )(rows, weight)
 
 
 def ssm_scan_kernel(s_ref, dec_ref, dx_ref, b_ref, c_ref, s_out_ref, read_ref):
@@ -123,7 +143,7 @@
     gathered = broadcast_gather(tokens[0], head_count)
     inputs = gathered.reshape(requests * STEPS, width)
     normed = norm_rows(inputs.astype(jnp.float32), mixer_gain).astype(jnp.bfloat16)
-    proj_xz = jnp.dot(normed, weight_xz, preferred_element_type=jnp.float32).reshape(
+    proj_xz = column_matmul(normed, weight_xz).reshape(
         requests, STEPS, heads_local, 2, head_dim
     )
     x_fresh = (

time: 120 us -> 110 us (0.917)
  local copies, waits for them, and re-layouts: 34 us -> 23.8 us
  matrix products: 20.3 us -> 13 us
  Pallas kernels: 13.6 us -> 19.2 us
  waiting for transfers between devices: 21.1 us -> 23.4 us
    unnamed x42 -> x32, local copies, waits for them, and re-layouts: 14.4 us -> 3.53 us
    dot_general x1 -> x0, matrix products: 7.23 us -> none  [shards(): jnp.dot(normed, weight_xz, preferred_element_type=jnp.float32)]
    pallas_call x0 -> x1, Pallas kernels: none -> 5.61 us  [column_matmul(): pl.pallas_call(column_matmul_kernel, grid=(cols // block,), in_specs=[pl....]
    all_to_all x1, waiting for transfers between devices: 2.6 us -> 5.41 us  [shards(): lax.all_to_all(mixer_part.reshape(head_count, tok_local, width), 'head',...]
    broadcast_in_dim x2, local copies, waits for them, and re-layouts: 1.58 us -> 0.03 us  [shards(): return (layer_out[None], ssm_now[None], conv_x_new[None], conv_bc_new[None])]
    reshape x0 -> x1, local copies, waits for them, and re-layouts: none -> 1.33 us  [shards(): column_matmul(normed, weight_xz)]
    convert_element_type x1, other arithmetic: 0.13 us -> 1.44 us  [shards(): norm_rows(inputs.astype(jnp.float32), mixer_gain).astype(jnp.bfloat16)]
  transfers between devices with their start and end apart: 5 -> 5, of which waited for: 4 -> 4; matrix products, arithmetic and copies ran while one was open for 22% -> 13% of each run, Pallas kernels for 0% -> 0%
where the time goes in v4:
time: 110 us; the launch traced here: 109 us
  local copies, waits for them, and re-layouts  23.8 us (22%)
  starting transfers between devices  23.4 us (21%)
  waiting for transfers between devices  23.4 us (21%)
  Pallas kernels  19.2 us (17%)
  matrix products  13 us (12%)
  other arithmetic  4.77 us (4%)
    pallas_call x1, Pallas kernels, ssm_scan(): pl.pallas_call(ssm_scan_kernel, grid=(requests,), in_specs=[big, per_step...  13.6 us
    all_to_all x2, starting transfers between devices, broadcast_gather(): return lax.all_to_all(copies, 'head', 0, 0, tiled=True)  13.2 us
    dot_general x1, matrix products, shards(): jnp.dot(hidden, weight_down, preferred_element_type=jnp.float32)  8.05 us
    all_to_all x1, waiting for transfers between devices, shards(): lax.all_to_all(computed.astype(jnp.bfloat16), 'head', split_axis=0, conca...  6.81 us
    all_to_all x1, waiting for transfers between devices, shards(): lax.all_to_all(outgoing, 'head', split_axis=0, concat_axis=0, tiled=True)  6.55 us
    pallas_call x1, Pallas kernels, column_matmul(): pl.pallas_call(column_matmul_kernel, grid=(cols // block,), in_specs=[pl....  5.61 us
    all_to_all x1, waiting for transfers between devices, shards(): lax.all_to_all(mixer_part.reshape(head_count, tok_local, width), 'head',...  5.41 us
    all_to_all x2, waiting for transfers between devices, broadcast_gather(): return lax.all_to_all(copies, 'head', 0, 0, tiled=True)  4.61 us
  transfers between devices with their start and end apart: 5, of which 4 were waited for; matrix products, arithmetic and copies ran while one was open for 13% of the time, Pallas kernels for 0%

profile of v4, /device:TPU:0, one launch (start us, length us, event | category | flops | bytes accessed | tf_op | source)
XLA Modules:
  0.0 108.5 jit_solution(2635195425639896648)
XLA Ops:
  0.7 1.5 %broadcast_in_dim.24 = bf16[8,4,2048]{2,1,0:T(4,128)(2,1)} broadcast(bf16[4,2048]{1,0:T(4,128)(2,1)} %bitcast.136), dimensions={1,2} | broadcast | bytes 147456 | tf_op jit(solution)/shard_map/broadcast_in_dim | solution.py:107
  2.2 7.3 %all-to-all-start = ((bf16[8,4,2048]{2,1,0:T(4,128)(2,1)}), bf16[8,4,2048]{2,1,0:T(4,128)(2,1)S(1)}, u32[]{:S(2)}, u32[]{:S(2)}) async-start(bf16[8,4,2048]{2,1,0:T(4,128)(2,1)} %broadcast_in_dim.24), calls=%async_computation | async-start | bytes 262144 | tf_op jit(solution)/shard_map/all_to_all | solution.py:108
  9.4 0.8 fusion.46
  10.3 0.7 exponential_negate_fusion
  10.9 0.8 copy.157
  11.9 0.2 select_reduce_fusion
  12.1 0.7 copy.183
  12.8 0.8 copy.182
  13.6 2.3 %copy.150.s_ref = bf16[4,8,128,128]{3,2,1,0:T(8,128)(2,1)} copy(bf16[4,8,128,128]{2,3,1,0:T(8,128)(2,1)} %bitcast.133) | data formatting | bytes 2097152 | tf_op jit(solution)/shard_map/reshape | solution.py:191
  15.8 0.7 mul.282
  16.7 0.9 fusion.45
  17.6 0.2 multiply_reduce_fusion
  17.9 1.4 %multiply_convert_fusion.a_ref = bf16[32,2048]{1,0:T(8,128)(2,1)} fusion(f32[32,2048]{1,0:T(8,128)S(1)} %reshape.225, f32[2048]{0:T(1024)} %param.29, f32[32]{0:T(128)S(1)} %rsqrt.33), kind=kLoop, calls=%fused_computation.23 | loop fusion | flops 196608 | bytes 401536 | tf_op jit(solution)/shard_map/convert_element_type | solution.py:145
  19.3 5.6 %shard_map.237 = f32[32,2048]{1,0:T(8,128)} custom-call(bf16[32,2048]{1,0:T(8,128)(2,1)} %multiply_convert_fusion.a_ref, bf16[2048,2048]{1,0:T(8,128)(2,1)} %w_ref.1), custom_call_target="tpu_custom_call" | custom-call | tf_op jit(solution)/shard_map/pallas_call | solution.py:56
  25.0 1.3 %reshape.214 = f32[4,8,16,2,64]{4,3,2,1,0:T(2,128)S(1)} reshape(f32[32,2048]{1,0:T(8,128)} %shard_map.237) | data formatting | bytes 524288 | tf_op jit(solution)/shard_map/reshape | solution.py:146
  26.3 0.2 slice.101
  26.5 0.3 slice.112
  26.8 0.3 convolution_convert_fusion.2
  27.2 0.6 broadcast_in_dim.26
  27.9 6.0 %all-to-all-start.1 = ((bf16[8,4,8,256]{3,2,1,0:T(8,128)(2,1)}), bf16[8,4,8,256]{3,2,1,0:T(8,128)(2,1)S(1)}, u32[]{:S(2)}, u32[]{:S(2)}) async-start(bf16[8,4,8,256]{3,2,1,0:T(8,128)(2,1)} %broadcast_in_dim.26), calls=%async_computation.1 | async-start | bytes 262144 | tf_op jit(solution)/shard_map/all_to_all | solution.py:108
  33.9 0.3 multiply_exponential_fusion
  34.1 0.1 mul.247
  34.3 0.1 mul.248
  34.4 0.1 convert_element_type.105
  34.6 0.8 fusion.18
  35.4 0.1 reshape.219
  35.5 0.1 broadcast_in_dim.25
  35.6 0.1 reshape.213
  35.8 0.7 copy.181
  36.4 0.2 squeeze.24
  36.6 4.6 %all-to-all-done.1 = bf16[8,4,8,256]{3,2,1,0:T(8,128)(2,1)S(1)} async-done(((bf16[8,4,8,256]{3,2,1,0:T(8,128)(2,1)}), bf16[8,4,8,256]{3,2,1,0:T(8,128)(2,1)S(1)}, u32[]{:S(2)}, u32[]{:S(2)}) %all-to-all-start.1) | async-done | bytes 131104 | tf_op jit(solution)/shard_map/all_to_all | solution.py:108
  41.2 0.2 copy.145
  41.5 0.6 gather_fusion
  42.1 0.6 gather_fusion.1
  42.6 0.1 broadcast_select_fusion
  42.7 1.9 %copy.147 = f32[8,4,8,128]{2,3,0,1:T(8,128)} copy(f32[8,4,8,128]{3,2,1,0:T(8,128)S(1)} %get-tuple-element.48) | data formatting | bytes 262144 | tf_op jit(solution)/shard_map/jit(_take)/select_n | solution.py:185
  44.7 1.9 %copy.149 = f32[8,4,8,128]{2,3,0,1:T(8,128)} copy(f32[8,4,8,128]{3,2,1,0:T(8,128)S(1)} %get-tuple-element.47) | data formatting | bytes 262144 | tf_op jit(solution)/shard_map/jit(_take)/select_n | solution.py:186
  46.6 13.6 %shard_map.238 = (bf16[4,8,128,128]{3,2,1,0:T(8,128)(2,1)}, f32[4,8,8,128]{3,2,1,0:T(8,128)}) custom-call(bf16[4,8,128,128]{3,2,1,0:T(8,128)(2,1)} %copy.150.s_ref, f32[4,8,8,128]{3,2,1,0:T(8,128)} %bitcast.135, f32[4,8,8,128]{3,2,1,0:T(8,128)} %get-tuple-element.35.dx_ref, f32[4,8,128,8]{3,2,1,0:T(8,128)} %bitcast.130, f32[4,8,128,8]{3,2,1,0:T(8,128)} %bitcast.131), custom_call_target="tpu_custom_call" | custom-call | tf_op jit(solution)/shard_map/pallas_call | solution.py:94
  60.2 1.0 copy.151
  61.2 0.1 reshape.218
  61.4 0.2 fusion.11
  61.6 0.1 mul.293
  61.8 0.2 mul.294
  61.9 3.8 %fusion = f32[8,4,2048]{2,1,0:T(4,128)} fusion(bf16[1024,2048]{1,0:T(8,128)(2,1)} %param.41, f32[8,4,1024]{2,1,0:T(4,128)S(1)} %mul.294, f32[8,4,1024]{2,1,0:T(4,128)S(1)} %squeeze.24, f32[8,4,1024]{2,1,0:T(4,128)S(1)} %reshape.216, f32[8,4,1024]{2,1,0:T(4,128)S(1)} %reshape.217, f32[1024]{0:T(1024)S(1)} %copy-done.4, f32[1024]{0:T(1024)S(1)} %mul.283), kind=kOutput, calls=%fused_computation.2 | convolution fusion | flops 134545408 | bytes 4988928 | tf_op jit(solution)/shard_map/dot_general | solution.py:208
  65.7 3.4 %all-to-all-start.2 = ((f32[8,4,2048]{2,1,0:T(4,128)}), f32[8,4,2048]{2,1,0:T(4,128)S(1)}, u32[]{:S(2)}, u32[]{:S(2)}) async-start(f32[8,4,2048]{2,1,0:T(4,128)} %fusion), calls=%async_computation.2 | async-start | bytes 524288 | tf_op jit(solution)/shard_map/all_to_all | solution.py:209
  69.2 0.1 copy.156
  69.3 0.6 copy.161
  69.9 0.6 copy.160
  70.5 1.3 %copy.159 = bf16[4,8,128,128]{2,3,1,0:T(8,128)(2,1)} copy(bf16[4,8,128,128]{3,2,1,0:T(8,128)(2,1)S(1)} %copy-done.1) | data formatting | bytes 2097152 | tf_op jit(solution)/shard_map/pallas_call | solution.py:94
  71.8 5.4 %all-to-all-done.2 = f32[8,4,2048]{2,1,0:T(4,128)S(1)} async-done(((f32[8,4,2048]{2,1,0:T(4,128)}), f32[8,4,2048]{2,1,0:T(4,128)S(1)}, u32[]{:S(2)}, u32[]{:S(2)}) %all-to-all-start.2) | async-done | bytes 262176 | tf_op jit(solution)/shard_map/all_to_all | solution.py:209
  77.3 0.1 fusion.24
  77.6 0.1 fusion.47
  77.7 0.1 convolution_convert_fusion
  77.9 0.7 reshape_broadcast_in_dim_reshape.3
  78.6 3.3 %all-to-all-start.3 = ((bf16[8,2,2048]{2,1,0:T(2,128)(2,1)}), bf16[8,2,2048]{2,1,0:T(2,128)(2,1)S(1)}, u32[]{:S(2)}, u32[]{:S(2)}) async-start(bf16[8,2,2048]{2,1,0:T(2,128)(2,1)} %reshape_broadcast_in_dim_reshape.3), calls=%async_computation.3 | async-start | bytes 131072 | tf_op jit(solution)/shard_map/all_to_all | solution.py:224
  81.9 0.2 fusion.35
  82.1 0.1 copy.165
  82.2 6.5 %all-to-all-done.3 = bf16[8,2,2048]{2,1,0:T(2,128)(2,1)S(1)} async-done(((bf16[8,2,2048]{2,1,0:T(2,128)(2,1)}), bf16[8,2,2048]{2,1,0:T(2,128)(2,1)S(1)}, u32[]{:S(2)}, u32[]{:S(2)}) %all-to-all-start.3) | async-done | bytes 65568 | tf_op jit(solution)/shard_map/all_to_all | solution.py:224
  88.8 8.0 %convolution_convert_fusion.1 = bf16[16,2048]{1,0:T(8,128)(2,1)S(1)} fusion(bf16[2048,2048]{1,0:T(8,128)(2,1)} %param.45, bf16[16,2048]{1,0:T(8,128)(2,1)S(1)} %reshape.221, bf16[2048,2048]{1,0:T(8,128)(2,1)} %param.44), kind=kOutput, calls=%fused_computation.8 | convolution fusion | flops 268566528 | bytes 16908288 | tf_op jit(solution)/shard_map/dot_general | solution.py:227
  96.8 0.7 convert_element_type.124
  97.5 3.3 %all-to-all-start.4 = ((bf16[8,2,2048]{2,1,0:T(2,128)(2,1)}), bf16[8,2,2048]{2,1,0:T(2,128)(2,1)S(1)}, u32[]{:S(2)}, u32[]{:S(2)}) async-start(bf16[8,2,2048]{2,1,0:T(2,128)(2,1)} %convert_element_type.124), calls=%async_computation.4 | async-start | bytes 131072 | tf_op jit(solution)/shard_map/all_to_all | solution.py:230
  100.9 6.8 %all-to-all-done.4 = bf16[8,2,2048]{2,1,0:T(2,128)(2,1)S(1)} async-done(((bf16[8,2,2048]{2,1,0:T(2,128)(2,1)}), bf16[8,2,2048]{2,1,0:T(2,128)(2,1)S(1)}, u32[]{:S(2)}, u32[]{:S(2)}) %all-to-all-start.4) | async-done | bytes 65568 | tf_op jit(solution)/shard_map/all_to_all | solution.py:230
  107.8 0.1 fusion.4
  107.9 0.6 fusion.31
  (64 shorter events, 1.3 us)
Async XLA Ops:
  0.6 26.2 %copy-start = (bf16[2048,256]{1,0:T(8,128)(2,1)S(1)}, bf16[2048,256]{1,0:T(8,128)(2,1)}, u32[]{:S(2)}) copy-start(bf16[2048,256]{1,0:T(8,128)(2,1)} %param.31) | copy-start | bytes 3145732
  0.6 26.2 %copy-start.3 = (f32[2048]{0:T(1024)S(1)}, f32[2048]{0:T(1024)}, u32[]{:S(2)}) copy-start(f32[2048]{0:T(1024)} %param.29) | copy-start | bytes 24580
  0.7 26.5 %copy-start.10 = (f32[256]{0:T(256)S(1)}, f32[256]{0:T(256)}, u32[]{:S(2)}) copy-start(f32[256]{0:T(256)} %param.39) | copy-start | bytes 3076
  0.7 33.2 %copy-start.5 = (bf16[2048,16]{0,1:T(8,128)(2,1)S(1)}, bf16[2048,16]{0,1:T(8,128)(2,1)}, u32[]{:S(2)}) copy-start(bf16[2048,16]{0,1:T(8,128)(2,1)} %param.32) | copy-start | bytes 196612
  0.7 33.2 %copy-start.11 = (f32[16]{0:T(128)S(1)}, f32[16]{0:T(128)}, u32[]{:S(2)}) copy-start(f32[16]{0:T(128)} %param.33) | copy-start | bytes 196
  2.2 15.4 %all-to-all-start = ((bf16[8,4,2048]{2,1,0:T(4,128)(2,1)}), bf16[8,4,2048]{2,1,0:T(4,128)(2,1)S(1)}, u32[]{:S(2)}, u32[]{:S(2)}) async-start(bf16[8,4,2048]{2,1,0:T(4,128)(2,1)} %broadcast_in_dim.24), calls=%async_computation | async-start | bytes 262144 | tf_op jit(solution)/shard_map/all_to_all | solution.py:108
  15.8 18.8 %copy-start.7 = (f32[1024]{0:T(1024)S(1)}, f32[1024]{0:T(1024)}, u32[]{:S(2)}) copy-start(f32[1024]{0:T(1024)} %param.37) | copy-start | bytes 12292
  27.9 13.3 %all-to-all-start.1 = ((bf16[8,4,8,256]{3,2,1,0:T(8,128)(2,1)}), bf16[8,4,8,256]{3,2,1,0:T(8,128)(2,1)S(1)}, u32[]{:S(2)}, u32[]{:S(2)}) async-start(bf16[8,4,8,256]{3,2,1,0:T(8,128)(2,1)} %broadcast_in_dim.26), calls=%async_computation.1 | async-start | bytes 262144 | tf_op jit(solution)/shard_map/all_to_all | solution.py:108
  35.4 26.0 %copy-start.9 = (f32[16]{0:T(128)S(1)}, f32[16]{0:T(128)}, u32[]{:S(2)}) copy-start(f32[16]{0:T(128)} %param.35) | copy-start | bytes 196
  35.7 26.2 %copy-start.4 = (f32[1024]{0:T(1024)S(1)}, f32[1024]{0:T(1024)}, u32[]{:S(2)}) copy-start(f32[1024]{0:T(1024)} %param.40) | copy-start | bytes 12292
  44.7 24.5 %copy-start.8 = (s32[1,4,2]{1,2,0:T(2,128)S(1)}, s32[1,4,2]{1,2,0:T(2,128)}, u32[]{:S(2)}) copy-start(s32[1,4,2]{1,2,0:T(2,128)} %param.28) | copy-start | bytes 100
  46.6 30.7 %copy-start.2 = (bf16[1,4,2048]{2,1,0:T(4,128)(2,1)S(1)}, bf16[1,4,2048]{2,1,0:T(4,128)(2,1)}, u32[]{:S(2)}) copy-start(bf16[1,4,2048]{2,1,0:T(4,128)(2,1)} %param.24) | copy-start | bytes 49156
  46.6 30.9 %copy-start.6 = (f32[2048]{0:T(1024)S(1)}, f32[2048]{0:T(1024)}, u32[]{:S(2)}) copy-start(f32[2048]{0:T(1024)} %param.42) | copy-start | bytes 24580
  60.2 10.4 %copy-start.1 = (bf16[4,8,128,128]{3,2,1,0:T(8,128)(2,1)S(1)}, bf16[4,8,128,128]{3,2,1,0:T(8,128)(2,1)}, u32[]{:S(2)}) copy-start(bf16[4,8,128,128]{3,2,1,0:T(8,128)(2,1)} %get-tuple-element.8) | copy-start | bytes 3145732
  61.6 16.0 %copy-start.12 = (bf16[2048,8]{0,1:T(8,128)(2,1)S(1)}, bf16[2048,8]{0,1:T(8,128)(2,1)}, u32[]{:S(2)}) copy-start(bf16[2048,8]{0,1:T(8,128)(2,1)} %param.43) | copy-start | bytes 98308
  65.7 11.6 %all-to-all-start.2 = ((f32[8,4,2048]{2,1,0:T(4,128)}), f32[8,4,2048]{2,1,0:T(4,128)S(1)}, u32[]{:S(2)}, u32[]{:S(2)}) async-start(f32[8,4,2048]{2,1,0:T(4,128)} %fusion), calls=%async_computation.2 | async-start | bytes 524288 | tf_op jit(solution)/shard_map/all_to_all | solution.py:209
  78.6 10.2 %all-to-all-start.3 = ((bf16[8,2,2048]{2,1,0:T(2,128)(2,1)}), bf16[8,2,2048]{2,1,0:T(2,128)(2,1)S(1)}, u32[]{:S(2)}, u32[]{:S(2)}) async-start(bf16[8,2,2048]{2,1,0:T(2,128)(2,1)} %reshape_broadcast_in_dim_reshape.3), calls=%async_computation.3 | async-start | bytes 131072 | tf_op jit(solution)/shard_map/all_to_all | solution.py:224
  97.5 10.2 %all-to-all-start.4 = ((bf16[8,2,2048]{2,1,0:T(2,128)(2,1)}), bf16[8,2,2048]{2,1,0:T(2,128)(2,1)S(1)}, u32[]{:S(2)}, u32[]{:S(2)}) async-start(bf16[8,2,2048]{2,1,0:T(2,128)(2,1)} %convert_element_type.124), calls=%async_computation.4 | async-start | bytes 131072 | tf_op jit(solution)/shard_map/all_to_all | solution.py:230

commit v5 on v4

--- a/solution.py
+++ b/solution.py
@@ -140,7 +140,19 @@
     heads_local = ssm_state.shape[2]
     head_dim = ssm_state.shape[3]
     state_dim = ssm_state.shape[4]
-    gathered = broadcast_gather(tokens[0], head_count)
+    top = expert_ids.shape[2]
+    broadcast_sum = head_count * requests * STEPS * width * 4 <= (8 << 20)
+    if broadcast_sum:
+        id_cols = jnp.zeros((tok_local, 128), jnp.bfloat16).at[:, :top].set(
+            expert_ids[0].astype(jnp.bfloat16)
+        )
+        gathered_all = broadcast_gather(jnp.concatenate([tokens[0], id_cols], axis=1), head_count)
+        gathered = gathered_all[..., :width]
+        ids_all = (
+            gathered_all[..., width : width + top].astype(jnp.int32).reshape(requests * STEPS, top)
+        )
+    else:
+        gathered = broadcast_gather(tokens[0], head_count)
     inputs = gathered.reshape(requests * STEPS, width)
     normed = norm_rows(inputs.astype(jnp.float32), mixer_gain).astype(jnp.bfloat16)
     proj_xz = column_matmul(normed, weight_xz).reshape(
@@ -206,6 +218,22 @@
     )
     per_expert = head_count // EXPERTS
     mixer_part = jnp.dot(group_normed, weight_out, preferred_element_type=jnp.float32)
+    if broadcast_sum:
+        mixer_all = broadcast_gather(mixer_part, head_count).sum(axis=0)
+        residual_all = (inputs.astype(jnp.float32) + mixer_all).astype(jnp.bfloat16)
+        ffn_all = norm_rows(residual_all.astype(jnp.float32), ffn_gain).astype(jnp.bfloat16)
+        share_all = route_share(ffn_all, router_weight, ids_all)
+        my_expert = my_index // per_expert
+        row_weight = jnp.sum(share_all * (ids_all == my_expert).astype(jnp.float32), axis=1)
+        hidden = expert_hidden(ffn_all, weight_up)
+        computed = jnp.dot(hidden, weight_down, preferred_element_type=jnp.float32)
+        contrib = row_weight[:, None] * computed
+        combined = lax.all_to_all(
+            contrib.reshape(head_count, tok_local, width), "head", 0, 0, tiled=True
+        ).sum(axis=0)
+        residual = lax.dynamic_slice_in_dim(residual_all, my_index * tok_local, tok_local, axis=0)
+        layer_out = (residual.astype(jnp.float32) + combined).astype(jnp.bfloat16)
+        return (layer_out[None], ssm_now[None], conv_x_new[None], conv_bc_new[None])
     mixer_out = lax.all_to_all(
         mixer_part.reshape(head_count, tok_local, width), "head", 0, 0, tiled=True
     ).sum(axis=0)

time: 110 us -> 149 us (1.35)
  waiting for transfers between devices: 23.4 us -> 54.7 us
  other arithmetic: 4.77 us -> 11.1 us
  local copies, waits for them, and re-layouts: 23.8 us -> 27.8 us
  starting transfers between devices: 23.4 us -> 19.9 us
    all_to_all x2 -> x3, waiting for transfers between devices: 4.61 us -> 48.2 us  [broadcast_gather(): return lax.all_to_all(copies, 'head', 0, 0, tiled=True)]
    all_to_all x3 -> x1, waiting for transfers between devices: 18.8 us -> 6.52 us  [shards(): lax.all_to_all(contrib.reshape(head_count, tok_local, width), 'head', 0,...]
    all_to_all x3 -> x1, starting transfers between devices: 10.1 us -> 3.45 us  [shards(): lax.all_to_all(contrib.reshape(head_count, tok_local, width), 'head', 0,...]
    all_to_all x2 -> x3, starting transfers between devices: 13.2 us -> 16.5 us  [broadcast_gather(): return lax.all_to_all(copies, 'head', 0, 0, tiled=True)]
    another operation x2, other arithmetic: 0.04 us -> 1.97 us  [the longest x1 0.03 us: shards(): earlier = jnp.cumsum(onehot, axis=0) - onehot]
    unnamed x32 -> x35, local copies, waits for them, and re-layouts: 3.53 us -> 3.86 us
    dot_general x5 -> x1, matrix products: 8.66 us -> 8.93 us  [shards(): computed = jnp.dot(hidden, weight_down, preferred_element_type=jnp.float32)]
  transfers between devices with their start and end apart: 5 -> 4, of which waited for: 4 -> 4; matrix products, arithmetic and copies ran while one was open for 13% -> 11% of each run, Pallas kernels for 0% -> 0%
where the time goes in v5:
time: 149 us; the launch traced here: 147 us
  waiting for transfers between devices  54.7 us (37%)
  local copies, waits for them, and re-layouts  27.8 us (19%)
  starting transfers between devices  19.9 us (13%)
  Pallas kernels  19.2 us (13%)
  matrix products  13.6 us (9%)
  other arithmetic  11.1 us (7%)
    all_to_all x3, waiting for transfers between devices, broadcast_gather(): return lax.all_to_all(copies, 'head', 0, 0, tiled=True)  48.2 us
    all_to_all x3, starting transfers between devices, broadcast_gather(): return lax.all_to_all(copies, 'head', 0, 0, tiled=True)  16.5 us
    pallas_call x1, Pallas kernels, ssm_scan(): pl.pallas_call(ssm_scan_kernel, grid=(requests,), in_specs=[big, per_step...  13.6 us
    dot_general x1, matrix products, shards(): computed = jnp.dot(hidden, weight_down, preferred_element_type=jnp.float32)  8.93 us
    all_to_all x1, waiting for transfers between devices, shards(): lax.all_to_all(contrib.reshape(head_count, tok_local, width), 'head', 0,...  6.52 us
    pallas_call x1, Pallas kernels, column_matmul(): pl.pallas_call(column_matmul_kernel, grid=(cols // block,), in_specs=[pl....  5.59 us
    unnamed x35, local copies, waits for them, and re-layouts  3.86 us
    all_to_all x1, starting transfers between devices, shards(): lax.all_to_all(contrib.reshape(head_count, tok_local, width), 'head', 0,...  3.45 us
  transfers between devices with their start and end apart: 4, of which 4 were waited for; matrix products, arithmetic and copies ran while one was open for 11% of the time, Pallas kernels for 0%

profile of v5, /device:TPU:0, one launch (start us, length us, event | category | flops | bytes accessed | tf_op | source)
XLA Modules:
  0.0 147.3 jit_solution(6116921250661991806)
XLA Ops:
  0.7 0.6 compare_reduce_fusion
  1.3 1.3 fusion.37
  2.7 0.7 fusion.32
  3.5 0.7 broadcast_in_dim.20
  4.2 7.3 %all-to-all-start = ((bf16[8,4,2176]{2,1,0:T(4,128)(2,1)}), bf16[8,4,2176]{2,1,0:T(4,128)(2,1)S(1)}, u32[]{:S(2)}, u32[]{:S(2)}) async-start(bf16[8,4,2176]{2,1,0:T(4,128)(2,1)} %broadcast_in_dim.20), calls=%async_computation | async-start | bytes 278528 | tf_op jit(solution)/shard_map/all_to_all | solution.py:108
  11.4 0.8 fusion.44
  12.3 0.7 exponential_negate_fusion
  13.0 0.7 copy.183
  13.7 0.8 copy.182
  14.5 2.3 %copy.149.s_ref = bf16[4,8,128,128]{3,2,1,0:T(8,128)(2,1)} copy(bf16[4,8,128,128]{2,3,1,0:T(8,128)(2,1)} %bitcast.131) | data formatting | bytes 2097152 | tf_op jit(solution)/shard_map/reshape | solution.py:203
  16.8 0.7 mul.276
  17.5 0.9 fusion.43
  18.4 0.4 all-to-all-done
  19.1 0.2 multiply_reduce_fusion.1
  19.4 1.4 multiply_convert_fusion.1.a_ref
  20.8 5.6 %shard_map.237 = f32[32,2048]{1,0:T(8,128)} custom-call(bf16[32,2048]{1,0:T(8,128)(2,1)} %multiply_convert_fusion.1.a_ref, bf16[2048,2048]{1,0:T(8,128)(2,1)} %w_ref.1), custom_call_target="tpu_custom_call" | custom-call | tf_op jit(solution)/shard_map/pallas_call | solution.py:56
  26.4 1.3 reshape.199
  27.8 0.2 slice.126
  27.9 0.3 slice.137
  28.2 0.3 convolution_convert_fusion
  28.7 0.6 broadcast_in_dim.22
  29.3 5.6 %all-to-all-start.1 = ((bf16[8,4,8,256]{3,2,1,0:T(8,128)(2,1)}), bf16[8,4,8,256]{3,2,1,0:T(8,128)(2,1)S(1)}, u32[]{:S(2)}, u32[]{:S(2)}) async-start(bf16[8,4,8,256]{3,2,1,0:T(8,128)(2,1)} %broadcast_in_dim.22), calls=%async_computation.1 | async-start | bytes 262144 | tf_op jit(solution)/shard_map/all_to_all | solution.py:108
  34.9 0.1 convert_element_type.94
  35.1 0.3 multiply_exponential_fusion
  35.4 0.1 mul.241
  35.6 0.1 broadcast_in_dim.21
  35.9 0.7 copy.181
  36.6 0.8 fusion.17
  37.5 0.1 squeeze.28
  37.6 4.7 %all-to-all-done.1 = bf16[8,4,8,256]{3,2,1,0:T(8,128)(2,1)S(1)} async-done(((bf16[8,4,8,256]{3,2,1,0:T(8,128)(2,1)}), bf16[8,4,8,256]{3,2,1,0:T(8,128)(2,1)S(1)}, u32[]{:S(2)}, u32[]{:S(2)}) %all-to-all-start.1) | async-done | bytes 131104 | tf_op jit(solution)/shard_map/all_to_all | solution.py:108
  42.3 0.2 copy.144
  42.6 0.6 gather_fusion
  43.1 0.6 gather_fusion.1
  43.8 2.0 %copy.146 = f32[8,4,8,128]{2,3,0,1:T(8,128)} copy(f32[8,4,8,128]{3,2,1,0:T(8,128)S(1)} %get-tuple-element.62) | data formatting | bytes 262144 | tf_op jit(solution)/shard_map/jit(_take)/select_n | solution.py:197
  45.8 1.9 %copy.148 = f32[8,4,8,128]{2,3,0,1:T(8,128)} copy(f32[8,4,8,128]{3,2,1,0:T(8,128)S(1)} %get-tuple-element.61) | data formatting | bytes 262144 | tf_op jit(solution)/shard_map/jit(_take)/select_n | solution.py:198
  47.7 13.6 %shard_map.238 = (bf16[4,8,128,128]{3,2,1,0:T(8,128)(2,1)}, f32[4,8,8,128]{3,2,1,0:T(8,128)}) custom-call(bf16[4,8,128,128]{3,2,1,0:T(8,128)(2,1)} %copy.149.s_ref, f32[4,8,8,128]{3,2,1,0:T(8,128)} %bitcast.133, f32[4,8,8,128]{3,2,1,0:T(8,128)} %get-tuple-element.47.dx_ref, f32[4,8,128,8]{3,2,1,0:T(8,128)} %bitcast.128, f32[4,8,128,8]{3,2,1,0:T(8,128)} %bitcast.129), custom_call_target="tpu_custom_call" | custom-call | tf_op jit(solution)/shard_map/pallas_call | solution.py:94
  61.2 0.9 copy.151
  62.3 0.2 fusion.8
  62.5 0.1 mul.287
  62.7 0.1 mul.288
  62.8 3.1 %fusion.19 = f32[32,2048]{1,0:T(8,128)S(1)} fusion(bf16[1024,2048]{1,0:T(8,128)(2,1)} %param.43, f32[32,1024]{1,0:T(8,128)S(1)} %mul.288, f32[4,8,8,128]{3,2,1,0:T(8,128)} %get-tuple-element.19, f32[4,8,1024]{2,1,0:T(8,128)S(1)} %get-tuple-element.48, f32[32,1024]{1,0:T(8,128)S(1)} %squeeze.28, f32[1024]{0:T(1024)S(1)} %copy-done.9, f32[1024]{0:T(1024)S(1)} %mul.277), kind=kOutput, calls=%fused_computation.49 | convolution fusion | flops 134545408 | bytes 4988928 | tf_op jit(solution)/shard_map/dot_general | solution.py:220
  65.9 1.6 %broadcast_in_dim.26 = f32[8,32,2048]{2,1,0:T(8,128)} broadcast(f32[32,2048]{1,0:T(8,128)S(1)} %fusion.19), dimensions={1,2} | broadcast | bytes 2359296 | tf_op jit(solution)/shard_map/broadcast_in_dim | solution.py:107
  67.5 3.6 %all-to-all-start.2 = ((f32[8,32,2048]{2,1,0:T(8,128)}), f32[8,32,2048]{2,1,0:T(8,128)S(1)}, u32[]{:S(2)}, u32[]{:S(2)}) async-start(f32[8,32,2048]{2,1,0:T(8,128)} %broadcast_in_dim.26), calls=%async_computation.2 | async-start | bytes 4194304 | tf_op jit(solution)/shard_map/all_to_all | solution.py:108
  71.1 0.6 slice.138
  71.7 0.8 copy.165
  72.5 0.6 convert_element_type.105
  73.1 1.4 copy.162
  74.5 43.1 %all-to-all-done.2 = f32[8,32,2048]{2,1,0:T(8,128)S(1)} async-done(((f32[8,32,2048]{2,1,0:T(8,128)}), f32[8,32,2048]{2,1,0:T(8,128)S(1)}, u32[]{:S(2)}, u32[]{:S(2)}) %all-to-all-start.2) | async-done | bytes 2097184 | tf_op jit(solution)/shard_map/all_to_all | solution.py:108
  117.6 0.8 reduce_sum.58
  118.5 1.0 reduce_sum.59
  119.5 1.0 add_convert_fusion.1
  120.5 0.2 multiply_reduce_fusion
  120.7 1.0 fusion.26
  121.7 0.9 fusion.27
  122.9 0.5 broadcast.246
  123.4 0.7 fusion.40
  124.4 8.9 %convolution_multiply_fusion = f32[32,2048]{1,0:T(8,128)S(1)} fusion(bf16[2048,2048]{1,0:T(8,128)(2,1)} %param.47, bf16[2048,2048]{1,0:T(8,128)(2,1)} %param.46, f32[32]{0:T(128)S(1)} %mul.299, bf16[32,2048]{1,0:T(8,128)(2,1)S(1)} %add_convert_fusion.1, f32[2048]{0:T(1024)} %param.44, f32[32]{0:T(128)S(1)} %rsqrt.39), kind=kOutput, calls=%fused_computation.2 | convolution fusion | flops 537395200 | bytes 17178880 | tf_op jit(solution)/shard_map/dot_general | solution.py:229
  133.3 0.8 reshape.205
  134.1 3.4 %all-to-all-start.3 = ((f32[8,4,2048]{2,1,0:T(4,128)}), f32[8,4,2048]{2,1,0:T(4,128)S(1)}, u32[]{:S(2)}, u32[]{:S(2)}) async-start(f32[8,4,2048]{2,1,0:T(4,128)} %reshape.205), calls=%async_computation.3 | async-start | bytes 524288 | tf_op jit(solution)/shard_map/all_to_all | solution.py:231
  137.5 0.6 copy.155
  138.2 0.6 copy.156
  138.8 1.3 copy.154
  140.1 6.5 %all-to-all-done.3 = f32[8,4,2048]{2,1,0:T(4,128)S(1)} async-done(((f32[8,4,2048]{2,1,0:T(4,128)}), f32[8,4,2048]{2,1,0:T(4,128)S(1)}, u32[]{:S(2)}, u32[]{:S(2)}) %all-to-all-start.3) | async-done | bytes 262176 | tf_op jit(solution)/shard_map/all_to_all | solution.py:231
  146.7 0.6 fusion.33
  (63 shorter events, 2.0 us)
Async XLA Ops:
  0.6 27.6 %copy-start = (bf16[2048,256]{1,0:T(8,128)(2,1)S(1)}, bf16[2048,256]{1,0:T(8,128)(2,1)}, u32[]{:S(2)}) copy-start(bf16[2048,256]{1,0:T(8,128)(2,1)} %param.33) | copy-start | bytes 3145732
  0.6 27.6 %copy-start.6 = (f32[2048]{0:T(1024)S(1)}, f32[2048]{0:T(1024)}, u32[]{:S(2)}) copy-start(f32[2048]{0:T(1024)} %param.31) | copy-start | bytes 24580
  2.7 25.9 %copy-start.11 = (f32[256]{0:T(256)S(1)}, f32[256]{0:T(256)}, u32[]{:S(2)}) copy-start(f32[256]{0:T(256)} %param.41) | copy-start | bytes 3076
  4.2 14.7 %all-to-all-start = ((bf16[8,4,2176]{2,1,0:T(4,128)(2,1)}), bf16[8,4,2176]{2,1,0:T(4,128)(2,1)S(1)}, u32[]{:S(2)}, u32[]{:S(2)}) async-start(bf16[8,4,2176]{2,1,0:T(4,128)(2,1)} %broadcast_in_dim.20), calls=%async_computation | async-start | bytes 278528 | tf_op jit(solution)/shard_map/all_to_all | solution.py:108
  14.4 20.7 %copy-start.7 = (bf16[2048,16]{0,1:T(8,128)(2,1)S(1)}, bf16[2048,16]{0,1:T(8,128)(2,1)}, u32[]{:S(2)}) copy-start(bf16[2048,16]{0,1:T(8,128)(2,1)} %param.34) | copy-start | bytes 196612
  14.4 20.7 %copy-start.12 = (f32[16]{0:T(128)S(1)}, f32[16]{0:T(128)}, u32[]{:S(2)}) copy-start(f32[16]{0:T(128)} %param.35) | copy-start | bytes 196
  18.9 17.6 %copy-start.8 = (f32[1024]{0:T(1024)S(1)}, f32[1024]{0:T(1024)}, u32[]{:S(2)}) copy-start(f32[1024]{0:T(1024)} %param.39) | copy-start | bytes 12292
  28.6 0.7 copy-start.4
  29.3 13.0 %all-to-all-start.1 = ((bf16[8,4,8,256]{3,2,1,0:T(8,128)(2,1)}), bf16[8,4,8,256]{3,2,1,0:T(8,128)(2,1)S(1)}, u32[]{:S(2)}, u32[]{:S(2)}) async-start(bf16[8,4,8,256]{3,2,1,0:T(8,128)(2,1)} %broadcast_in_dim.22), calls=%async_computation.1 | async-start | bytes 262144 | tf_op jit(solution)/shard_map/all_to_all | solution.py:108
  35.1 2.2 %copy-start.2 = (bf16[4,8,1024]{2,1,0:T(8,128)(2,1)}, bf16[4,8,1024]{2,1,0:T(8,128)(2,1)S(1)}, u32[]{:S(2)}) copy-start(bf16[4,8,1024]{2,1,0:T(8,128)(2,1)S(1)} %convert_element_type.94) | copy-start | bytes 196612
  35.8 26.5 %copy-start.10 = (f32[16]{0:T(128)S(1)}, f32[16]{0:T(128)}, u32[]{:S(2)}) copy-start(f32[16]{0:T(128)} %param.37) | copy-start | bytes 196
  37.4 25.4 %copy-start.9 = (f32[1024]{0:T(1024)S(1)}, f32[1024]{0:T(1024)}, u32[]{:S(2)}) copy-start(f32[1024]{0:T(1024)} %param.42) | copy-start | bytes 12292
  67.5 50.2 %all-to-all-start.2 = ((f32[8,32,2048]{2,1,0:T(8,128)}), f32[8,32,2048]{2,1,0:T(8,128)S(1)}, u32[]{:S(2)}, u32[]{:S(2)}) async-start(f32[8,32,2048]{2,1,0:T(8,128)} %broadcast_in_dim.26), calls=%async_computation.2 | async-start | bytes 4194304 | tf_op jit(solution)/shard_map/all_to_all | solution.py:108
  124.3 13.2 %copy-start.3 = (bf16[4,8,1024]{2,1,0:T(8,128)(2,1)S(1)}, bf16[4,8,1024]{2,1,0:T(8,128)(2,1)}, u32[]{:S(2)}) copy-start(bf16[4,8,1024]{2,1,0:T(8,128)(2,1)} %copy-done.2) | copy-start | bytes 196612
  124.3 13.8 %copy-start.5 = (bf16[4,8,256]{2,1,0:T(8,128)(2,1)S(1)}, bf16[4,8,256]{2,1,0:T(8,128)(2,1)}, u32[]{:S(2)}) copy-start(bf16[4,8,256]{2,1,0:T(8,128)(2,1)} %copy-done.4) | copy-start | bytes 49156
  124.3 14.4 %copy-start.1 = (bf16[4,8,128,128]{3,2,1,0:T(8,128)(2,1)S(1)}, bf16[4,8,128,128]{3,2,1,0:T(8,128)(2,1)}, u32[]{:S(2)}) copy-start(bf16[4,8,128,128]{3,2,1,0:T(8,128)(2,1)} %get-tuple-element.20) | copy-start | bytes 3145732
  134.1 12.5 %all-to-all-start.3 = ((f32[8,4,2048]{2,1,0:T(4,128)}), f32[8,4,2048]{2,1,0:T(4,128)S(1)}, u32[]{:S(2)}, u32[]{:S(2)}) async-start(f32[8,4,2048]{2,1,0:T(4,128)} %reshape.205), calls=%async_computation.3 | async-start | bytes 524288 | tf_op jit(solution)/shard_map/all_to_all | solution.py:231

commit v6 on v4

--- a/solution.py
+++ b/solution.py
@@ -67,40 +67,38 @@
 
 def ssm_scan_kernel(s_ref, dec_ref, dx_ref, b_ref, c_ref, s_out_ref, read_ref):
     tiles = s_ref.shape[1]
-    steps = dec_ref.shape[2]
-
-    def tile(j, carry):
+    lanes = s_ref.shape[3]
+    steps = dec_ref.shape[1]
+    for j in range(tiles):
+        cols = slice(j * lanes, (j + 1) * lanes)
         state = s_ref[0, j].astype(jnp.float32)
-        b_all = b_ref[0, j]
-        c_all = c_ref[0, j]
-        dec_all = dec_ref[0, j]
-        dx_all = dx_ref[0, j]
+        b_all = b_ref[0, j].T
+        c_all = c_ref[0, j].T
+        dec_all = dec_ref[0, :, cols]
+        dx_all = dx_ref[0, :, cols]
         for t in range(steps):
             fresh = dec_all[t : t + 1, :] * state + dx_all[t : t + 1, :] * b_all[:, t : t + 1]
-            read_ref[0, j, t : t + 1, :] = jnp.sum(fresh * c_all[:, t : t + 1], axis=0, keepdims=True)
+            read_ref[0, t : t + 1, cols] = jnp.sum(fresh * c_all[:, t : t + 1], axis=0, keepdims=True)
             state = fresh.astype(jnp.bfloat16).astype(jnp.float32)
         s_out_ref[0, j] = state.astype(jnp.bfloat16)
-        return carry
-
-    lax.fori_loop(0, tiles, tile, 0)
-
-
-def ssm_scan(state_tiles, decay_tiles, dx_tiles, b_tiles, c_tiles):
+
+
+def ssm_scan(state_tiles, decay_rows, dx_rows, b_rows, c_rows):
     requests, tiles, state_dim, lanes = state_tiles.shape
-    steps = decay_tiles.shape[2]
+    steps = decay_rows.shape[1]
     big = pl.BlockSpec((1, tiles, state_dim, lanes), lambda r: (r, 0, 0, 0))
-    per_step = pl.BlockSpec((1, tiles, steps, lanes), lambda r: (r, 0, 0, 0))
-    columns = pl.BlockSpec((1, tiles, state_dim, steps), lambda r: (r, 0, 0, 0))
+    per_step = pl.BlockSpec((1, steps, tiles * lanes), lambda r: (r, 0, 0))
+    rows = pl.BlockSpec((1, tiles, steps, state_dim), lambda r: (r, 0, 0, 0))
     return pl.pallas_call(
         ssm_scan_kernel,
         grid=(requests,),
-        in_specs=[big, per_step, per_step, columns, columns],
+        in_specs=[big, per_step, per_step, rows, rows],
         out_specs=[big, per_step],
         out_shape=[
             jax.ShapeDtypeStruct(state_tiles.shape, jnp.bfloat16),
-            jax.ShapeDtypeStruct(decay_tiles.shape, jnp.float32),
+            jax.ShapeDtypeStruct(decay_rows.shape, jnp.float32),
         ],
-    )(state_tiles, decay_tiles, dx_tiles, b_tiles, c_tiles)
+    )(state_tiles, decay_rows, dx_rows, b_rows, c_rows)
 
 
 def broadcast_gather(block, count):
@@ -173,30 +171,27 @@
     tiles = heads_local // pack
     lanes = pack * head_dim
 
-    def to_tiles(per_head):
-        return per_head.reshape(requests, STEPS, tiles, lanes).transpose(0, 2, 1, 3)
-
-    decay_tiles = to_tiles(
-        jnp.broadcast_to(decay_rate[..., None], (requests, STEPS, heads_local, head_dim))
-    )
-    dx_tiles = to_tiles(delta[..., None] * x_heads)
+    decay_rows = jnp.broadcast_to(
+        decay_rate[..., None], (requests, STEPS, heads_local, head_dim)
+    ).reshape(requests, STEPS, heads_local * head_dim)
+    dx_rows = (delta[..., None] * x_heads).reshape(requests, STEPS, heads_local * head_dim)
     tile_group = (my_index * heads_local + jnp.arange(tiles) * pack) // (HEADS // G)
     bc_values = bc_all.astype(jnp.float32).reshape(requests, STEPS, 2, G, state_dim)
-    b_tiles = jnp.take(bc_values[:, :, 0], tile_group, axis=2).transpose(0, 2, 3, 1)
-    c_tiles = jnp.take(bc_values[:, :, 1], tile_group, axis=2).transpose(0, 2, 3, 1)
+    b_rows = jnp.take(bc_values[:, :, 0], tile_group, axis=2).transpose(0, 2, 1, 3)
+    c_rows = jnp.take(bc_values[:, :, 1], tile_group, axis=2).transpose(0, 2, 1, 3)
     state_tiles = (
         ssm_state[0]
         .reshape(requests, tiles, pack, head_dim, state_dim)
         .transpose(0, 1, 4, 2, 3)
         .reshape(requests, tiles, state_dim, lanes)
     )
-    state_out, read_tiles = ssm_scan(state_tiles, decay_tiles, dx_tiles, b_tiles, c_tiles)
+    state_out, read_rows = ssm_scan(state_tiles, decay_rows, dx_rows, b_rows, c_rows)
     ssm_now = (
         state_out.reshape(requests, tiles, state_dim, pack, head_dim)
         .transpose(0, 1, 3, 4, 2)
         .reshape(requests, heads_local, head_dim, state_dim)
     )
-    scan_read = read_tiles.transpose(0, 2, 1, 3).reshape(requests, STEPS, heads_local, head_dim)
+    scan_read = read_rows.reshape(requests, STEPS, heads_local, head_dim)
     readings = scan_read + skip_gain[:, None] * x_heads
     gated_out = readings * jax.nn.silu(z_gate)
     group_normed = (

time: 110 us -> 106 us (0.964)
  local copies, waits for them, and re-layouts: 23.8 us -> 20.8 us
    select_n x2 -> x0, local copies, waits for them, and re-layouts: 3.87 us -> none  [the longest x1 1.94 us: shards(): jnp.take(bc_values[:, :, 0], tile_group, axis=2).transpose(0, 2, 3, 1)]
    reshape x4 -> x3, local copies, waits for them, and re-layouts: 0.92 us -> 2.8 us  [the longest x2 2.04 us: shards(): scan_read = read_rows.reshape(requests, STEPS, heads_local, head_dim)]
where the time goes in v6:
time: 106 us; the launch traced here: 105 us
  starting transfers between devices  23.4 us (22%)
  waiting for transfers between devices  23.4 us (22%)
  local copies, waits for them, and re-layouts  20.8 us (20%)
  Pallas kernels  18.1 us (17%)
  matrix products  13 us (12%)
  other arithmetic  5.47 us (5%)
  between operations  1.06 us (1%)
    all_to_all x2, starting transfers between devices, broadcast_gather(): return lax.all_to_all(copies, 'head', 0, 0, tiled=True)  13.2 us
    pallas_call x1, Pallas kernels, ssm_scan(): pl.pallas_call(ssm_scan_kernel, grid=(requests,), in_specs=[big, per_step...  12.5 us
    dot_general x1, matrix products, shards(): jnp.dot(hidden, weight_down, preferred_element_type=jnp.float32)  8.05 us
    all_to_all x1, waiting for transfers between devices, shards(): lax.all_to_all(computed.astype(jnp.bfloat16), 'head', split_axis=0, conca...  6.81 us
    all_to_all x1, waiting for transfers between devices, shards(): lax.all_to_all(outgoing, 'head', split_axis=0, concat_axis=0, tiled=True)  6.55 us
    pallas_call x1, Pallas kernels, column_matmul(): pl.pallas_call(column_matmul_kernel, grid=(cols // block,), in_specs=[pl....  5.61 us
    all_to_all x1, waiting for transfers between devices, shards(): lax.all_to_all(mixer_part.reshape(head_count, tok_local, width), 'head',...  5.41 us
    all_to_all x2, waiting for transfers between devices, broadcast_gather(): return lax.all_to_all(copies, 'head', 0, 0, tiled=True)  4.59 us
  transfers between devices with their start and end apart: 5, of which 4 were waited for; matrix products, arithmetic and copies ran while one was open for 13% of the time, Pallas kernels for 0%

profile of v6, /device:TPU:0, one launch (start us, length us, event | category | flops | bytes accessed | tf_op | source)
XLA Modules:
  0.0 105.2 jit_solution(802085469125099382)
XLA Ops:
  0.7 1.5 %broadcast_in_dim.24 = bf16[8,4,2048]{2,1,0:T(4,128)(2,1)} broadcast(bf16[4,2048]{1,0:T(4,128)(2,1)} %bitcast.121), dimensions={1,2} | broadcast | bytes 147456 | tf_op jit(solution)/shard_map/broadcast_in_dim | solution.py:105
  2.2 7.3 %all-to-all-start = ((bf16[8,4,2048]{2,1,0:T(4,128)(2,1)}), bf16[8,4,2048]{2,1,0:T(4,128)(2,1)S(1)}, u32[]{:S(2)}, u32[]{:S(2)}) async-start(bf16[8,4,2048]{2,1,0:T(4,128)(2,1)} %broadcast_in_dim.24), calls=%async_computation | async-start | bytes 262144 | tf_op jit(solution)/shard_map/all_to_all | solution.py:106
  9.4 0.8 fusion.48
  10.3 0.7 exponential_negate_fusion
  10.9 0.8 copy.86
  11.7 0.1 reshape_squeeze.8
  11.9 0.2 select_reduce_fusion
  12.1 0.7 copy.115
  12.8 0.8 copy.114
  13.6 2.3 %copy.81.s_ref = bf16[4,8,128,128]{3,2,1,0:T(8,128)(2,1)} copy(bf16[4,8,128,128]{2,3,1,0:T(8,128)(2,1)} %bitcast.119) | data formatting | bytes 2097152 | tf_op jit(solution)/shard_map/reshape | solution.py:186
  15.8 0.7 mul.282
  16.7 0.9 fusion.47
  17.6 0.2 multiply_reduce_fusion
  17.7 0.1 rsqrt.32
  17.9 1.4 %multiply_convert_fusion.a_ref = bf16[32,2048]{1,0:T(8,128)(2,1)} fusion(f32[32,2048]{1,0:T(8,128)S(1)} %reshape.221, f32[2048]{0:T(1024)} %param.29, f32[32]{0:T(128)S(1)} %rsqrt.33), kind=kLoop, calls=%fused_computation.23 | loop fusion | flops 196608 | bytes 401536 | tf_op jit(solution)/shard_map/convert_element_type | solution.py:143
  19.3 5.6 %shard_map.237 = f32[32,2048]{1,0:T(8,128)} custom-call(bf16[32,2048]{1,0:T(8,128)(2,1)} %multiply_convert_fusion.a_ref, bf16[2048,2048]{1,0:T(8,128)(2,1)} %w_ref.1), custom_call_target="tpu_custom_call" | custom-call | tf_op jit(solution)/shard_map/pallas_call | solution.py:56
  25.0 1.4 %reshape.211 = f32[4,8,16,2,64]{4,3,2,1,0:T(2,128)S(1)} reshape(f32[32,2048]{1,0:T(8,128)} %shard_map.237) | data formatting | bytes 524288 | tf_op jit(solution)/shard_map/reshape | solution.py:144
  26.3 0.2 slice.101
  26.5 0.3 slice.112
  26.8 0.3 convolution_convert_fusion.2
  27.2 0.6 broadcast_in_dim.26
  27.9 6.0 %all-to-all-start.1 = ((bf16[8,4,8,256]{3,2,1,0:T(8,128)(2,1)}), bf16[8,4,8,256]{3,2,1,0:T(8,128)(2,1)S(1)}, u32[]{:S(2)}, u32[]{:S(2)}) async-start(bf16[8,4,8,256]{3,2,1,0:T(8,128)(2,1)} %broadcast_in_dim.26), calls=%async_computation.1 | async-start | bytes 262144 | tf_op jit(solution)/shard_map/all_to_all | solution.py:106
  33.9 0.3 multiply_exponential_fusion
  34.2 0.1 mul.247
  34.3 0.1 mul.248
  34.5 0.1 convert_element_type.105
  34.7 0.8 fusion.45
  35.4 0.1 reshape.215
  35.6 0.1 broadcast_in_dim.25
  35.7 0.8 reshape.210.dec_ref
  36.5 0.2 squeeze.24
  36.6 4.6 %all-to-all-done.1 = bf16[8,4,8,256]{3,2,1,0:T(8,128)(2,1)S(1)} async-done(((bf16[8,4,8,256]{3,2,1,0:T(8,128)(2,1)}), bf16[8,4,8,256]{3,2,1,0:T(8,128)(2,1)S(1)}, u32[]{:S(2)}, u32[]{:S(2)}) %all-to-all-start.1) | async-done | bytes 131104 | tf_op jit(solution)/shard_map/all_to_all | solution.py:106
  41.3 0.2 copy.76
  41.5 0.6 gather_fusion
  42.1 0.6 gather_fusion.1
  42.7 0.8 fusion.18
  43.5 12.5 %shard_map.238 = (bf16[4,8,128,128]{3,2,1,0:T(8,128)(2,1)}, f32[4,8,1024]{2,1,0:T(8,128)}) custom-call(bf16[4,8,128,128]{3,2,1,0:T(8,128)(2,1)} %copy.81.s_ref, f32[4,8,1024]{2,1,0:T(8,128)} %reshape.210.dec_ref, f32[4,8,1024]{2,1,0:T(8,128)} %get-tuple-element.27.dx_ref, f32[4,8,8,128]{3,2,1,0:T(8,128)} %get-tuple-element.40.b_ref, ...), custom_call_target="tpu_custom_call" | custom-call | tf_op jit(solution)/shard_map/pallas_call | solution.py:92
  56.0 1.1 %reshape.214 = f32[4,8,16,64]{3,2,1,0:T(8,128)S(1)} reshape(f32[4,8,1024]{2,1,0:T(8,128)} %get-tuple-element.7) | data formatting | bytes 262144 | tf_op jit(solution)/shard_map/reshape | solution.py:194
  57.1 0.9 reshape.212
  58.0 0.2 fusion.11
  58.3 0.1 mul.293
  58.4 0.2 mul.294
  58.6 3.8 %fusion = f32[8,4,2048]{2,1,0:T(4,128)} fusion(bf16[1024,2048]{1,0:T(8,128)(2,1)} %param.41, f32[8,4,1024]{2,1,0:T(4,128)S(1)} %mul.294, f32[8,4,1024]{2,1,0:T(4,128)S(1)} %squeeze.24, f32[8,4,1024]{2,1,0:T(4,128)S(1)} %reshape.212, f32[8,4,1024]{2,1,0:T(4,128)S(1)} %reshape.213, f32[1024]{0:T(1024)S(1)} %copy-done.4, f32[1024]{0:T(1024)S(1)} %mul.283), kind=kOutput, calls=%fused_computation.2 | convolution fusion | flops 134545408 | bytes 4988928 | tf_op jit(solution)/shard_map/dot_general | solution.py:203
  62.3 3.4 %all-to-all-start.2 = ((f32[8,4,2048]{2,1,0:T(4,128)}), f32[8,4,2048]{2,1,0:T(4,128)S(1)}, u32[]{:S(2)}, u32[]{:S(2)}) async-start(f32[8,4,2048]{2,1,0:T(4,128)} %fusion), calls=%async_computation.2 | async-start | bytes 524288 | tf_op jit(solution)/shard_map/all_to_all | solution.py:204
  65.8 0.1 copy.85
  65.9 0.6 copy.90
  66.6 0.6 copy.89
  67.2 1.3 %copy.88 = bf16[4,8,128,128]{2,3,1,0:T(8,128)(2,1)} copy(bf16[4,8,128,128]{3,2,1,0:T(8,128)(2,1)S(1)} %copy-done.1) | data formatting | bytes 2097152 | tf_op jit(solution)/shard_map/pallas_call | solution.py:92
  68.5 5.4 %all-to-all-done.2 = f32[8,4,2048]{2,1,0:T(4,128)S(1)} async-done(((f32[8,4,2048]{2,1,0:T(4,128)}), f32[8,4,2048]{2,1,0:T(4,128)S(1)}, u32[]{:S(2)}, u32[]{:S(2)}) %all-to-all-start.2) | async-done | bytes 262176 | tf_op jit(solution)/shard_map/all_to_all | solution.py:204
  74.0 0.1 fusion.25
  74.1 0.1 fusion.27
  74.2 0.1 fusion.49
  74.4 0.1 convolution_convert_fusion
  74.5 0.7 reshape_broadcast_in_dim_reshape.3
  75.2 3.3 %all-to-all-start.3 = ((bf16[8,2,2048]{2,1,0:T(2,128)(2,1)}), bf16[8,2,2048]{2,1,0:T(2,128)(2,1)S(1)}, u32[]{:S(2)}, u32[]{:S(2)}) async-start(bf16[8,2,2048]{2,1,0:T(2,128)(2,1)} %reshape_broadcast_in_dim_reshape.3), calls=%async_computation.3 | async-start | bytes 131072 | tf_op jit(solution)/shard_map/all_to_all | solution.py:219
  78.6 0.2 fusion.36
  78.8 0.1 copy.94
  78.9 6.5 %all-to-all-done.3 = bf16[8,2,2048]{2,1,0:T(2,128)(2,1)S(1)} async-done(((bf16[8,2,2048]{2,1,0:T(2,128)(2,1)}), bf16[8,2,2048]{2,1,0:T(2,128)(2,1)S(1)}, u32[]{:S(2)}, u32[]{:S(2)}) %all-to-all-start.3) | async-done | bytes 65568 | tf_op jit(solution)/shard_map/all_to_all | solution.py:219
  85.4 8.0 %convolution_convert_fusion.1 = bf16[16,2048]{1,0:T(8,128)(2,1)S(1)} fusion(bf16[2048,2048]{1,0:T(8,128)(2,1)} %param.45, bf16[16,2048]{1,0:T(8,128)(2,1)S(1)} %reshape.217, bf16[2048,2048]{1,0:T(8,128)(2,1)} %param.44), kind=kOutput, calls=%fused_computation.8 | convolution fusion | flops 268566528 | bytes 16908288 | tf_op jit(solution)/shard_map/dot_general | solution.py:222
  93.5 0.7 convert_element_type.124
  94.2 3.3 %all-to-all-start.4 = ((bf16[8,2,2048]{2,1,0:T(2,128)(2,1)}), bf16[8,2,2048]{2,1,0:T(2,128)(2,1)S(1)}, u32[]{:S(2)}, u32[]{:S(2)}) async-start(bf16[8,2,2048]{2,1,0:T(2,128)(2,1)} %convert_element_type.124), calls=%async_computation.4 | async-start | bytes 131072 | tf_op jit(solution)/shard_map/all_to_all | solution.py:225
  97.6 6.8 %all-to-all-done.4 = bf16[8,2,2048]{2,1,0:T(2,128)(2,1)S(1)} async-done(((bf16[8,2,2048]{2,1,0:T(2,128)(2,1)}), bf16[8,2,2048]{2,1,0:T(2,128)(2,1)S(1)}, u32[]{:S(2)}, u32[]{:S(2)}) %all-to-all-start.4) | async-done | bytes 65568 | tf_op jit(solution)/shard_map/all_to_all | solution.py:225
  104.4 0.1 fusion.4
  104.5 0.6 fusion.32
  (60 shorter events, 1.0 us)
Async XLA Ops:
  0.6 26.2 %copy-start = (bf16[2048,256]{1,0:T(8,128)(2,1)S(1)}, bf16[2048,256]{1,0:T(8,128)(2,1)}, u32[]{:S(2)}) copy-start(bf16[2048,256]{1,0:T(8,128)(2,1)} %param.31) | copy-start | bytes 3145732
  0.6 26.2 %copy-start.3 = (f32[2048]{0:T(1024)S(1)}, f32[2048]{0:T(1024)}, u32[]{:S(2)}) copy-start(f32[2048]{0:T(1024)} %param.29) | copy-start | bytes 24580
  0.7 26.5 %copy-start.10 = (f32[256]{0:T(256)S(1)}, f32[256]{0:T(256)}, u32[]{:S(2)}) copy-start(f32[256]{0:T(256)} %param.39) | copy-start | bytes 3076
  0.7 33.2 %copy-start.5 = (bf16[2048,16]{0,1:T(8,128)(2,1)S(1)}, bf16[2048,16]{0,1:T(8,128)(2,1)}, u32[]{:S(2)}) copy-start(bf16[2048,16]{0,1:T(8,128)(2,1)} %param.32) | copy-start | bytes 196612
  0.7 33.2 %copy-start.11 = (f32[16]{0:T(128)S(1)}, f32[16]{0:T(128)}, u32[]{:S(2)}) copy-start(f32[16]{0:T(128)} %param.33) | copy-start | bytes 196
  2.2 15.4 %all-to-all-start = ((bf16[8,4,2048]{2,1,0:T(4,128)(2,1)}), bf16[8,4,2048]{2,1,0:T(4,128)(2,1)S(1)}, u32[]{:S(2)}, u32[]{:S(2)}) async-start(bf16[8,4,2048]{2,1,0:T(4,128)(2,1)} %broadcast_in_dim.24), calls=%async_computation | async-start | bytes 262144 | tf_op jit(solution)/shard_map/all_to_all | solution.py:106
  15.8 18.8 %copy-start.7 = (f32[1024]{0:T(1024)S(1)}, f32[1024]{0:T(1024)}, u32[]{:S(2)}) copy-start(f32[1024]{0:T(1024)} %param.37) | copy-start | bytes 12292
  25.0 33.1 %copy-start.9 = (f32[16]{0:T(128)S(1)}, f32[16]{0:T(128)}, u32[]{:S(2)}) copy-start(f32[16]{0:T(128)} %param.35) | copy-start | bytes 196
  25.0 33.6 %copy-start.4 = (f32[1024]{0:T(1024)S(1)}, f32[1024]{0:T(1024)}, u32[]{:S(2)}) copy-start(f32[1024]{0:T(1024)} %param.40) | copy-start | bytes 12292
  27.9 13.3 %all-to-all-start.1 = ((bf16[8,4,8,256]{3,2,1,0:T(8,128)(2,1)}), bf16[8,4,8,256]{3,2,1,0:T(8,128)(2,1)S(1)}, u32[]{:S(2)}, u32[]{:S(2)}) async-start(bf16[8,4,8,256]{3,2,1,0:T(8,128)(2,1)} %broadcast_in_dim.26), calls=%async_computation.1 | async-start | bytes 262144 | tf_op jit(solution)/shard_map/all_to_all | solution.py:106
  34.6 31.2 %copy-start.8 = (s32[1,4,2]{1,2,0:T(2,128)S(1)}, s32[1,4,2]{1,2,0:T(2,128)}, u32[]{:S(2)}) copy-start(s32[1,4,2]{1,2,0:T(2,128)} %param.28) | copy-start | bytes 100
  36.5 37.5 %copy-start.2 = (bf16[1,4,2048]{2,1,0:T(4,128)(2,1)S(1)}, bf16[1,4,2048]{2,1,0:T(4,128)(2,1)}, u32[]{:S(2)}) copy-start(bf16[1,4,2048]{2,1,0:T(4,128)(2,1)} %param.24) | copy-start | bytes 49156
  36.6 37.5 %copy-start.6 = (f32[2048]{0:T(1024)S(1)}, f32[2048]{0:T(1024)}, u32[]{:S(2)}) copy-start(f32[2048]{0:T(1024)} %param.42) | copy-start | bytes 24580
  36.6 37.6 %copy-start.12 = (bf16[2048,8]{0,1:T(8,128)(2,1)S(1)}, bf16[2048,8]{0,1:T(8,128)(2,1)}, u32[]{:S(2)}) copy-start(bf16[2048,8]{0,1:T(8,128)(2,1)} %param.43) | copy-start | bytes 98308
  56.0 11.2 %copy-start.1 = (bf16[4,8,128,128]{3,2,1,0:T(8,128)(2,1)S(1)}, bf16[4,8,128,128]{3,2,1,0:T(8,128)(2,1)}, u32[]{:S(2)}) copy-start(bf16[4,8,128,128]{3,2,1,0:T(8,128)(2,1)} %get-tuple-element.8) | copy-start | bytes 3145732
  62.3 11.6 %all-to-all-start.2 = ((f32[8,4,2048]{2,1,0:T(4,128)}), f32[8,4,2048]{2,1,0:T(4,128)S(1)}, u32[]{:S(2)}, u32[]{:S(2)}) async-start(f32[8,4,2048]{2,1,0:T(4,128)} %fusion), calls=%async_computation.2 | async-start | bytes 524288 | tf_op jit(solution)/shard_map/all_to_all | solution.py:204
  75.2 10.2 %all-to-all-start.3 = ((bf16[8,2,2048]{2,1,0:T(2,128)(2,1)}), bf16[8,2,2048]{2,1,0:T(2,128)(2,1)S(1)}, u32[]{:S(2)}, u32[]{:S(2)}) async-start(bf16[8,2,2048]{2,1,0:T(2,128)(2,1)} %reshape_broadcast_in_dim_reshape.3), calls=%async_computation.3 | async-start | bytes 131072 | tf_op jit(solution)/shard_map/all_to_all | solution.py:219
  94.2 10.2 %all-to-all-start.4 = ((bf16[8,2,2048]{2,1,0:T(2,128)(2,1)}), bf16[8,2,2048]{2,1,0:T(2,128)(2,1)S(1)}, u32[]{:S(2)}, u32[]{:S(2)}) async-start(bf16[8,2,2048]{2,1,0:T(2,128)(2,1)} %convert_element_type.124), calls=%async_computation.4 | async-start | bytes 131072 | tf_op jit(solution)/shard_map/all_to_all | solution.py:225

commit v7 on v6

--- a/solution.py
+++ b/solution.py
@@ -62,6 +62,11 @@
         ],
         out_specs=pl.BlockSpec((m, block), lambda j: (0, j)),
         out_shape=jax.ShapeDtypeStruct((m, cols), jnp.float32),
+        cost_estimate=pl.CostEstimate(
+            flops=2 * m * k * cols,
+            transcendentals=0,
+            bytes_accessed=2 * (m * k + k * cols) + 4 * m * cols,
+        ),
     )(rows, weight)
 
 
@@ -141,18 +146,23 @@
     gathered = broadcast_gather(tokens[0], head_count)
     inputs = gathered.reshape(requests * STEPS, width)
     normed = norm_rows(inputs.astype(jnp.float32), mixer_gain).astype(jnp.bfloat16)
-    proj_xz = column_matmul(normed, weight_xz).reshape(
-        requests, STEPS, heads_local, 2, head_dim
-    )
-    x_fresh = (
-        proj_xz[:, :, :, 0, :].reshape(requests, STEPS, heads_local * head_dim).astype(jnp.bfloat16)
-    )
-    z_gate = proj_xz[:, :, :, 1, :]
     bc_fresh = (
         jnp.dot(normed, weight_bc, preferred_element_type=jnp.float32)
         .reshape(requests, STEPS, -1)
         .astype(jnp.bfloat16)
     )
+    bc_conv, conv_bc_new = causal_conv(conv_bc_state[0], bc_fresh, conv_bc_kernel, conv_bc_bias)
+    bc_conv = bc_conv.astype(jnp.bfloat16)
+    bc_all = jnp.moveaxis(broadcast_gather(bc_conv, head_count), 0, 2).reshape(
+        requests, STEPS, -1
+    )
+    proj_xz = column_matmul(normed, weight_xz).reshape(
+        requests, STEPS, heads_local, 2 * head_dim
+    )
+    x_fresh = (
+        proj_xz[..., :head_dim].reshape(requests, STEPS, heads_local * head_dim).astype(jnp.bfloat16)
+    )
+    z_gate = proj_xz[..., head_dim:]
     delta = jax.nn.softplus(
         jnp.dot(normed, weight_delta, preferred_element_type=jnp.float32).reshape(
             requests, STEPS, heads_local
@@ -160,11 +170,6 @@
         + delta_bias
     )
     x_conv, conv_x_new = causal_conv(conv_x_state[0], x_fresh, conv_x_kernel, conv_x_bias)
-    bc_conv, conv_bc_new = causal_conv(conv_bc_state[0], bc_fresh, conv_bc_kernel, conv_bc_bias)
-    bc_conv = bc_conv.astype(jnp.bfloat16)
-    bc_all = jnp.moveaxis(broadcast_gather(bc_conv, head_count), 0, 2).reshape(
-        requests, STEPS, -1
-    )
     x_heads = x_conv.reshape(requests, STEPS, heads_local, head_dim)
     decay_rate = jnp.exp(delta * -jnp.exp(decay_log))
     pack = 2 if heads_local % 2 == 0 else 1

time: 106 us -> 105 us (level)
  local copies, waits for them, and re-layouts: 20.8 us -> 19.7 us
    slice x2, local copies, waits for them, and re-layouts: 0.46 us -> 2.06 us  [the longest x1 1.07 us: shards(): z_gate = proj_xz[..., head_dim:]]
    reshape x1 -> x0, local copies, waits for them, and re-layouts: 1.36 us -> none  [shards(): column_matmul(normed, weight_xz)]
    unnamed x32 -> x30, local copies, waits for them, and re-layouts: 3.53 us -> 3.53 us
where the time goes in v7:
time: 105 us; the launch traced here: 104 us
  waiting for transfers between devices  23.6 us (22%)
  starting transfers between devices  23.4 us (22%)
  local copies, waits for them, and re-layouts  19.7 us (19%)
  Pallas kernels  18.1 us (17%)
  matrix products  12.9 us (12%)
  other arithmetic  5.6 us (5%)
    all_to_all x2, starting transfers between devices, broadcast_gather(): return lax.all_to_all(copies, 'head', 0, 0, tiled=True)  13.3 us
    pallas_call x1, Pallas kernels, ssm_scan(): pl.pallas_call(ssm_scan_kernel, grid=(requests,), in_specs=[big, per_step...  12.5 us
    dot_general x1, matrix products, shards(): jnp.dot(hidden, weight_down, preferred_element_type=jnp.float32)  8.05 us
    all_to_all x1, waiting for transfers between devices, shards(): lax.all_to_all(computed.astype(jnp.bfloat16), 'head', split_axis=0, conca...  6.81 us
    all_to_all x1, waiting for transfers between devices, shards(): lax.all_to_all(outgoing, 'head', split_axis=0, concat_axis=0, tiled=True)  6.55 us
    pallas_call x1, Pallas kernels, column_matmul(): pl.pallas_call(column_matmul_kernel, grid=(cols // block,), in_specs=[pl....  5.61 us
    all_to_all x1, waiting for transfers between devices, shards(): lax.all_to_all(mixer_part.reshape(head_count, tok_local, width), 'head',...  5.41 us
    all_to_all x2, waiting for transfers between devices, broadcast_gather(): return lax.all_to_all(copies, 'head', 0, 0, tiled=True)  4.8 us
  transfers between devices with their start and end apart: 5, of which 4 were waited for; matrix products, arithmetic and copies ran while one was open for 13% of the time, Pallas kernels for 0%

profile of v7, /device:TPU:0, one launch (start us, length us, event | category | flops | bytes accessed | tf_op | source)
XLA Modules:
  0.0 104.3 jit_solution(8673514070053376592)
XLA Ops:
  0.7 1.5 %broadcast_in_dim.24 = bf16[8,4,2048]{2,1,0:T(4,128)(2,1)} broadcast(bf16[4,2048]{1,0:T(4,128)(2,1)} %bitcast.100), dimensions={1,2} | broadcast | bytes 147456 | tf_op jit(solution)/shard_map/broadcast_in_dim | solution.py:110
  2.2 7.3 %all-to-all-start = ((bf16[8,4,2048]{2,1,0:T(4,128)(2,1)}), bf16[8,4,2048]{2,1,0:T(4,128)(2,1)S(1)}, u32[]{:S(2)}, u32[]{:S(2)}) async-start(bf16[8,4,2048]{2,1,0:T(4,128)(2,1)} %broadcast_in_dim.24), calls=%async_computation | async-start | bytes 262144 | tf_op jit(solution)/shard_map/all_to_all | solution.py:111
  9.4 0.8 fusion.36
  10.3 0.7 exponential_negate_fusion
  10.9 0.8 copy.84
  11.7 0.1 reshape_squeeze.7
  11.8 0.1 fusion.28
  11.9 0.2 select_reduce_fusion
  12.1 0.7 copy.114
  12.8 0.8 copy.113
  13.6 2.3 %copy.79.s_ref = bf16[4,8,128,128]{3,2,1,0:T(8,128)(2,1)} copy(bf16[4,8,128,128]{2,3,1,0:T(8,128)(2,1)} %bitcast.98) | data formatting | bytes 2097152 | tf_op jit(solution)/shard_map/reshape | solution.py:191
  15.9 0.8 mul.267
  16.6 0.9 fusion.35
  17.5 0.2 multiply_reduce_fusion.1
  17.7 0.1 rsqrt.32
  17.7 0.1 rsqrt.33
  17.9 1.4 %multiply_convert_fusion.1.a_ref = bf16[32,2048]{1,0:T(8,128)(2,1)} fusion(f32[32,2048]{1,0:T(8,128)S(1)} %reshape.196, f32[2048]{0:T(1024)} %param.29, f32[32]{0:T(128)S(1)} %rsqrt.33), kind=kLoop, calls=%fused_computation.19 | loop fusion | flops 196608 | bytes 401536 | tf_op jit(solution)/shard_map/convert_element_type | solution.py:148
  19.3 5.6 %shard_map.237 = f32[32,2048]{1,0:T(8,128)} custom-call(bf16[32,2048]{1,0:T(8,128)(2,1)} %multiply_convert_fusion.1.a_ref, bf16[2048,2048]{1,0:T(8,128)(2,1)} %w_ref.1), custom_call_target="tpu_custom_call" | custom-call | flops 268435456 | bytes 8781824 | tf_op jit(solution)/shard_map/pallas_call | solution.py:56
  24.9 1.0 slice.101
  25.9 1.1 %slice.112 = f32[4,8,16,64]{3,1,2,0:T(8,128)S(1)} slice(f32[4,8,16,128]{3,1,2,0:T(8,128)} %bitcast.97), slice={[0:4], [0:8], [0:16], [64:128]} | slice | bytes 262144 | tf_op jit(solution)/shard_map/slice | solution.py:165
  27.0 0.3 convolution_convert_fusion.2
  27.4 0.6 broadcast_in_dim.26
  28.1 6.0 %all-to-all-start.1 = ((bf16[8,4,8,256]{3,2,1,0:T(8,128)(2,1)}), bf16[8,4,8,256]{3,2,1,0:T(8,128)(2,1)S(1)}, u32[]{:S(2)}, u32[]{:S(2)}) async-start(bf16[8,4,8,256]{3,2,1,0:T(8,128)(2,1)} %broadcast_in_dim.26), calls=%async_computation.1 | async-start | bytes 262144 | tf_op jit(solution)/shard_map/all_to_all | solution.py:111
  34.1 0.3 multiply_exponential_fusion
  34.4 0.1 mul.225
  34.5 0.1 mul.226
  34.6 0.1 convert_element_type.103
  34.8 0.1 broadcast_in_dim.25
  34.9 0.8 reshape.187.dec_ref
  35.7 0.8 fusion.33
  36.5 0.1 reshape.190
  36.6 4.8 %all-to-all-done.1 = bf16[8,4,8,256]{3,2,1,0:T(8,128)(2,1)S(1)} async-done(((bf16[8,4,8,256]{3,2,1,0:T(8,128)(2,1)}), bf16[8,4,8,256]{3,2,1,0:T(8,128)(2,1)S(1)}, u32[]{:S(2)}, u32[]{:S(2)}) %all-to-all-start.1) | async-done | bytes 131104 | tf_op jit(solution)/shard_map/all_to_all | solution.py:111
  41.4 0.2 copy.74
  41.7 0.6 gather_fusion
  42.3 0.6 gather_fusion.1
  42.8 0.8 fusion.10
  43.6 12.5 %shard_map.238 = (bf16[4,8,128,128]{3,2,1,0:T(8,128)(2,1)}, f32[4,8,1024]{2,1,0:T(8,128)}) custom-call(bf16[4,8,128,128]{3,2,1,0:T(8,128)(2,1)} %copy.79.s_ref, f32[4,8,1024]{2,1,0:T(8,128)} %reshape.187.dec_ref, f32[4,8,1024]{2,1,0:T(8,128)} %get-tuple-element.29.dx_ref, f32[4,8,8,128]{3,2,1,0:T(8,128)} %get-tuple-element.42.b_ref, ...), custom_call_target="tpu_custom_call" | custom-call | tf_op jit(solution)/shard_map/pallas_call | solution.py:97
  56.1 1.1 %reshape.189 = f32[4,8,16,64]{3,2,1,0:T(8,128)S(1)} reshape(f32[4,8,1024]{2,1,0:T(8,128)} %get-tuple-element.7) | data formatting | bytes 262144 | tf_op jit(solution)/shard_map/reshape | solution.py:199
  57.3 0.2 multiply_reduce_fusion
  57.5 0.1 multiply_convert_fusion
  57.6 0.1 dot_general.31
  57.8 3.7 %fusion = f32[8,4,2048]{2,1,0:T(4,128)} fusion(bf16[8,4,1024]{2,1,0:T(4,128)(2,1)S(1)} %dot_general.31, bf16[1024,2048]{1,0:T(8,128)(2,1)} %param.41), kind=kOutput, calls=%fused_computation.2 | convolution fusion | flops 134217728 | bytes 4521984 | tf_op jit(solution)/shard_map/dot_general | solution.py:208
  61.5 3.4 %all-to-all-start.2 = ((f32[8,4,2048]{2,1,0:T(4,128)}), f32[8,4,2048]{2,1,0:T(4,128)S(1)}, u32[]{:S(2)}, u32[]{:S(2)}) async-start(f32[8,4,2048]{2,1,0:T(4,128)} %fusion), calls=%async_computation.2 | async-start | bytes 524288 | tf_op jit(solution)/shard_map/all_to_all | solution.py:209
  64.9 0.1 iota_compare_fusion.3
  65.0 0.1 copy.83
  65.1 0.6 copy.88
  65.7 0.6 copy.87
  66.3 1.3 %copy.86 = bf16[4,8,128,128]{2,3,1,0:T(8,128)(2,1)} copy(bf16[4,8,128,128]{3,2,1,0:T(8,128)(2,1)S(1)} %copy-done.1) | data formatting | bytes 2097152 | tf_op jit(solution)/shard_map/pallas_call | solution.py:97
  67.6 5.4 %all-to-all-done.2 = f32[8,4,2048]{2,1,0:T(4,128)S(1)} async-done(((f32[8,4,2048]{2,1,0:T(4,128)}), f32[8,4,2048]{2,1,0:T(4,128)S(1)}, u32[]{:S(2)}, u32[]{:S(2)}) %all-to-all-start.2) | async-done | bytes 262176 | tf_op jit(solution)/shard_map/all_to_all | solution.py:209
  73.1 0.1 fusion.14
  73.3 0.1 fusion.16
  73.4 0.1 fusion.37
  73.5 0.1 convolution_convert_fusion
  73.7 0.7 reshape_broadcast_in_dim_reshape.3
  74.4 3.3 %all-to-all-start.3 = ((bf16[8,2,2048]{2,1,0:T(2,128)(2,1)}), bf16[8,2,2048]{2,1,0:T(2,128)(2,1)S(1)}, u32[]{:S(2)}, u32[]{:S(2)}) async-start(bf16[8,2,2048]{2,1,0:T(2,128)(2,1)} %reshape_broadcast_in_dim_reshape.3), calls=%async_computation.3 | async-start | bytes 131072 | tf_op jit(solution)/shard_map/all_to_all | solution.py:224
  77.7 0.2 fusion.25
  77.9 0.1 copy.92
  78.0 6.5 %all-to-all-done.3 = bf16[8,2,2048]{2,1,0:T(2,128)(2,1)S(1)} async-done(((bf16[8,2,2048]{2,1,0:T(2,128)(2,1)}), bf16[8,2,2048]{2,1,0:T(2,128)(2,1)S(1)}, u32[]{:S(2)}, u32[]{:S(2)}) %all-to-all-start.3) | async-done | bytes 65568 | tf_op jit(solution)/shard_map/all_to_all | solution.py:224
  84.6 8.0 %convolution_convert_fusion.1 = bf16[16,2048]{1,0:T(8,128)(2,1)S(1)} fusion(bf16[2048,2048]{1,0:T(8,128)(2,1)} %param.45, bf16[16,2048]{1,0:T(8,128)(2,1)S(1)} %reshape.192, bf16[2048,2048]{1,0:T(8,128)(2,1)} %param.44), kind=kOutput, calls=%fused_computation.8 | convolution fusion | flops 268566528 | bytes 16908288 | tf_op jit(solution)/shard_map/dot_general | solution.py:227
  92.6 0.7 convert_element_type.122
  93.3 3.3 %all-to-all-start.4 = ((bf16[8,2,2048]{2,1,0:T(2,128)(2,1)}), bf16[8,2,2048]{2,1,0:T(2,128)(2,1)S(1)}, u32[]{:S(2)}, u32[]{:S(2)}) async-start(bf16[8,2,2048]{2,1,0:T(2,128)(2,1)} %convert_element_type.122), calls=%async_computation.4 | async-start | bytes 131072 | tf_op jit(solution)/shard_map/all_to_all | solution.py:230
  96.7 6.8 %all-to-all-done.4 = bf16[8,2,2048]{2,1,0:T(2,128)(2,1)S(1)} async-done(((bf16[8,2,2048]{2,1,0:T(2,128)(2,1)}), bf16[8,2,2048]{2,1,0:T(2,128)(2,1)S(1)}, u32[]{:S(2)}, u32[]{:S(2)}) %all-to-all-start.4) | async-done | bytes 65568 | tf_op jit(solution)/shard_map/all_to_all | solution.py:230
  103.6 0.1 fusion.4
  103.7 0.6 fusion.21
  (53 shorter events, 0.6 us)
Async XLA Ops:
  0.6 26.4 %copy-start = (bf16[2048,256]{1,0:T(8,128)(2,1)S(1)}, bf16[2048,256]{1,0:T(8,128)(2,1)}, u32[]{:S(2)}) copy-start(bf16[2048,256]{1,0:T(8,128)(2,1)} %param.31) | copy-start | bytes 3145732
  0.6 26.4 %copy-start.3 = (f32[2048]{0:T(1024)S(1)}, f32[2048]{0:T(1024)}, u32[]{:S(2)}) copy-start(f32[2048]{0:T(1024)} %param.29) | copy-start | bytes 24580
  0.7 26.7 %copy-start.8 = (f32[256]{0:T(256)S(1)}, f32[256]{0:T(256)}, u32[]{:S(2)}) copy-start(f32[256]{0:T(256)} %param.39) | copy-start | bytes 3076
  0.7 33.4 %copy-start.4 = (bf16[2048,16]{0,1:T(8,128)(2,1)S(1)}, bf16[2048,16]{0,1:T(8,128)(2,1)}, u32[]{:S(2)}) copy-start(bf16[2048,16]{0,1:T(8,128)(2,1)} %param.32) | copy-start | bytes 196612
  0.7 33.4 %copy-start.9 = (f32[16]{0:T(128)S(1)}, f32[16]{0:T(128)}, u32[]{:S(2)}) copy-start(f32[16]{0:T(128)} %param.33) | copy-start | bytes 196
  2.2 15.3 %all-to-all-start = ((bf16[8,4,2048]{2,1,0:T(4,128)(2,1)}), bf16[8,4,2048]{2,1,0:T(4,128)(2,1)S(1)}, u32[]{:S(2)}, u32[]{:S(2)}) async-start(bf16[8,4,2048]{2,1,0:T(4,128)(2,1)} %broadcast_in_dim.24), calls=%async_computation | async-start | bytes 262144 | tf_op jit(solution)/shard_map/all_to_all | solution.py:111
  13.6 22.2 %copy-start.6 = (f32[1024]{0:T(1024)S(1)}, f32[1024]{0:T(1024)}, u32[]{:S(2)}) copy-start(f32[1024]{0:T(1024)} %param.37) | copy-start | bytes 12292
  24.9 32.3 %copy-start.10 = (f32[16]{0:T(128)S(1)}, f32[16]{0:T(128)}, u32[]{:S(2)}) copy-start(f32[16]{0:T(128)} %param.35) | copy-start | bytes 196
  28.1 13.3 %all-to-all-start.1 = ((bf16[8,4,8,256]{3,2,1,0:T(8,128)(2,1)}), bf16[8,4,8,256]{3,2,1,0:T(8,128)(2,1)S(1)}, u32[]{:S(2)}, u32[]{:S(2)}) async-start(bf16[8,4,8,256]{3,2,1,0:T(8,128)(2,1)} %broadcast_in_dim.26), calls=%async_computation.1 | async-start | bytes 262144 | tf_op jit(solution)/shard_map/all_to_all | solution.py:111
  34.3 30.6 %copy-start.7 = (s32[1,4,2]{1,2,0:T(2,128)S(1)}, s32[1,4,2]{1,2,0:T(2,128)}, u32[]{:S(2)}) copy-start(s32[1,4,2]{1,2,0:T(2,128)} %param.28) | copy-start | bytes 100
  35.7 37.4 %copy-start.2 = (bf16[1,4,2048]{2,1,0:T(4,128)(2,1)S(1)}, bf16[1,4,2048]{2,1,0:T(4,128)(2,1)}, u32[]{:S(2)}) copy-start(bf16[1,4,2048]{2,1,0:T(4,128)(2,1)} %param.24) | copy-start | bytes 49156
  36.5 36.8 %copy-start.5 = (f32[2048]{0:T(1024)S(1)}, f32[2048]{0:T(1024)}, u32[]{:S(2)}) copy-start(f32[2048]{0:T(1024)} %param.42) | copy-start | bytes 24580
  36.5 36.8 %copy-start.11 = (bf16[2048,8]{0,1:T(8,128)(2,1)S(1)}, bf16[2048,8]{0,1:T(8,128)(2,1)}, u32[]{:S(2)}) copy-start(bf16[2048,8]{0,1:T(8,128)(2,1)} %param.43) | copy-start | bytes 98308
  56.1 10.2 %copy-start.1 = (bf16[4,8,128,128]{3,2,1,0:T(8,128)(2,1)S(1)}, bf16[4,8,128,128]{3,2,1,0:T(8,128)(2,1)}, u32[]{:S(2)}) copy-start(bf16[4,8,128,128]{3,2,1,0:T(8,128)(2,1)} %get-tuple-element.8) | copy-start | bytes 3145732
  61.5 11.6 %all-to-all-start.2 = ((f32[8,4,2048]{2,1,0:T(4,128)}), f32[8,4,2048]{2,1,0:T(4,128)S(1)}, u32[]{:S(2)}, u32[]{:S(2)}) async-start(f32[8,4,2048]{2,1,0:T(4,128)} %fusion), calls=%async_computation.2 | async-start | bytes 524288 | tf_op jit(solution)/shard_map/all_to_all | solution.py:209
  74.4 10.2 %all-to-all-start.3 = ((bf16[8,2,2048]{2,1,0:T(2,128)(2,1)}), bf16[8,2,2048]{2,1,0:T(2,128)(2,1)S(1)}, u32[]{:S(2)}, u32[]{:S(2)}) async-start(bf16[8,2,2048]{2,1,0:T(2,128)(2,1)} %reshape_broadcast_in_dim_reshape.3), calls=%async_computation.3 | async-start | bytes 131072 | tf_op jit(solution)/shard_map/all_to_all | solution.py:224
  93.3 10.2 %all-to-all-start.4 = ((bf16[8,2,2048]{2,1,0:T(2,128)(2,1)}), bf16[8,2,2048]{2,1,0:T(2,128)(2,1)S(1)}, u32[]{:S(2)}, u32[]{:S(2)}) async-start(bf16[8,2,2048]{2,1,0:T(2,128)(2,1)} %convert_element_type.122), calls=%async_computation.4 | async-start | bytes 131072 | tf_op jit(solution)/shard_map/all_to_all | solution.py:230

commit v8 on v7

--- a/solution.py
+++ b/solution.py
@@ -2,6 +2,7 @@
 import jax.numpy as jnp
 from jax import lax
 from jax.experimental import pallas as pl
+from jax.experimental.pallas import tpu as pltpu
 from jax.sharding import PartitionSpec as P
 
 HEADS = 128
@@ -68,6 +69,48 @@
             bytes_accessed=2 * (m * k + k * cols) + 4 * m * cols,
         ),
     )(rows, weight)
+
+
+def expert_ffn_kernel(x_ref, up_ref, down_ref, o_ref, acc_ref):
+    j = pl.program_id(0)
+    hidden = jnp.dot(x_ref[...], up_ref[...], preferred_element_type=jnp.float32)
+    hidden = jnp.square(jnp.maximum(hidden, 0.0)).astype(jnp.bfloat16)
+    part = jnp.dot(hidden, down_ref[...], preferred_element_type=jnp.float32)
+
+    @pl.when(j == 0)
+    def _():
+        acc_ref[...] = part
+
+    @pl.when(j > 0)
+    def _():
+        acc_ref[...] += part
+
+    @pl.when(j == pl.num_programs(0) - 1)
+    def _():
+        o_ref[...] = acc_ref[...].astype(o_ref.dtype)
+
+
+def expert_ffn(rows, weight_up, weight_down):
+    m, width = rows.shape
+    hidden_units = weight_up.shape[1]
+    block = min(512, hidden_units)
+    return pl.pallas_call(
+        expert_ffn_kernel,
+        grid=(hidden_units // block,),
+        in_specs=[
+            pl.BlockSpec((m, width), lambda j: (0, 0)),
+            pl.BlockSpec((width, block), lambda j: (0, j)),
+            pl.BlockSpec((block, width), lambda j: (j, 0)),
+        ],
+        out_specs=pl.BlockSpec((m, width), lambda j: (0, 0)),
+        out_shape=jax.ShapeDtypeStruct((m, width), jnp.bfloat16),
+        scratch_shapes=[pltpu.VMEM((m, width), jnp.float32)],
+        cost_estimate=pl.CostEstimate(
+            flops=4 * m * width * hidden_units,
+            transcendentals=0,
+            bytes_accessed=4 * width * hidden_units + 4 * m * width,
+        ),
+    )(rows, weight_up, weight_down)
 
 
 def ssm_scan_kernel(s_ref, dec_ref, dx_ref, b_ref, c_ref, s_out_ref, read_ref):
@@ -205,7 +248,7 @@
         .reshape(requests * STEPS, heads_local * head_dim)
     )
     per_expert = head_count // EXPERTS
-    mixer_part = jnp.dot(group_normed, weight_out, preferred_element_type=jnp.float32)
+    mixer_part = column_matmul(group_normed, weight_out)
     mixer_out = lax.all_to_all(
         mixer_part.reshape(head_count, tok_local, width), "head", 0, 0, tiled=True
     ).sum(axis=0)
@@ -223,13 +266,12 @@
     outgoing = jnp.repeat(packed.reshape(EXPERTS, CAP, width), per_expert, axis=0)
     received = lax.all_to_all(outgoing, "head", split_axis=0, concat_axis=0, tiled=True)
     flat_rows = received.reshape(-1, width)
-    hidden = expert_hidden(flat_rows, weight_up)
-    computed = jnp.dot(hidden, weight_down, preferred_element_type=jnp.float32).reshape(
+    computed = expert_ffn(flat_rows, weight_up, weight_down).reshape(
         received.shape[0], received.shape[1], width
     )
     returned = lax.all_to_all(
-        computed.astype(jnp.bfloat16), "head", split_axis=0, concat_axis=0, tiled=True
-    ).astype(computed.dtype)
+        computed, "head", split_axis=0, concat_axis=0, tiled=True
+    ).astype(jnp.float32)
     summed = (
         returned.reshape(EXPERTS, per_expert, CAP, width).sum(axis=1).reshape(EXPERTS * CAP, width)
     )

time: 105 us -> 110 us (1.048)
  Pallas kernels: 18.1 us -> 31 us
  matrix products: 12.9 us -> 1.18 us
  local copies, waits for them, and re-layouts: 19.7 us -> 23.5 us
    dot_general x2 -> x0, matrix products: 11.8 us -> none  [the longest x1 8.05 us: shards(): jnp.dot(hidden, weight_down, preferred_element_type=jnp.float32)]
    pallas_call x0 -> x1, Pallas kernels: none -> 8.52 us  [expert_ffn(): pl.pallas_call(expert_ffn_kernel, grid=(hidden_units // block,), in_specs...]
    pallas_call x1 -> x2, Pallas kernels: 5.61 us -> 9.97 us  [column_matmul(): pl.pallas_call(column_matmul_kernel, grid=(cols // block,), in_specs=[pl....]
    reshape x0 -> x3, local copies, waits for them, and re-layouts: none -> 4 us  [the longest x1 1.73 us: shards(): mixer_part.reshape(head_count, tok_local, width)]
  transfers between devices with their start and end apart: 5 -> 5, of which waited for: 4 -> 4; matrix products, arithmetic and copies ran while one was open for 13% -> 12% of each run, Pallas kernels for 0% -> 0%
where the time goes in v8:
time: 110 us; the launch traced here: 109 us
  Pallas kernels  31 us (28%)
  local copies, waits for them, and re-layouts  23.5 us (21%)
  waiting for transfers between devices  23.5 us (21%)
  starting transfers between devices  23.4 us (21%)
  other arithmetic  5.6 us (5%)
  matrix products  1.18 us (1%)
    all_to_all x2, starting transfers between devices, broadcast_gather(): return lax.all_to_all(copies, 'head', 0, 0, tiled=True)  13.3 us
    pallas_call x1, Pallas kernels, ssm_scan(): pl.pallas_call(ssm_scan_kernel, grid=(requests,), in_specs=[big, per_step...  12.5 us
    pallas_call x2, Pallas kernels, column_matmul(): pl.pallas_call(column_matmul_kernel, grid=(cols // block,), in_specs=[pl....  9.97 us
    pallas_call x1, Pallas kernels, expert_ffn(): pl.pallas_call(expert_ffn_kernel, grid=(hidden_units // block,), in_specs...  8.52 us
    all_to_all x1, waiting for transfers between devices, shards(): lax.all_to_all(computed, 'head', split_axis=0, concat_axis=0, tiled=True)  6.81 us
    all_to_all x1, waiting for transfers between devices, shards(): lax.all_to_all(outgoing, 'head', split_axis=0, concat_axis=0, tiled=True)  6.55 us
    all_to_all x1, waiting for transfers between devices, shards(): lax.all_to_all(mixer_part.reshape(head_count, tok_local, width), 'head',...  5.41 us
    all_to_all x2, waiting for transfers between devices, broadcast_gather(): return lax.all_to_all(copies, 'head', 0, 0, tiled=True)  4.78 us
  transfers between devices with their start and end apart: 5, of which 4 were waited for; matrix products, arithmetic and copies ran while one was open for 12% of the time, Pallas kernels for 0%

profile of v8, /device:TPU:0, one launch (start us, length us, event | category | flops | bytes accessed | tf_op | source)
XLA Modules:
  0.0 109.2 jit_solution(1193031353002375962)
XLA Ops:
  0.7 1.5 %broadcast_in_dim.24 = bf16[8,4,2048]{2,1,0:T(4,128)(2,1)} broadcast(bf16[4,2048]{1,0:T(4,128)(2,1)} %bitcast.93), dimensions={1,2} | broadcast | bytes 147456 | tf_op jit(solution)/shard_map/broadcast_in_dim | solution.py:153
  2.2 7.3 %all-to-all-start = ((bf16[8,4,2048]{2,1,0:T(4,128)(2,1)}), bf16[8,4,2048]{2,1,0:T(4,128)(2,1)S(1)}, u32[]{:S(2)}, u32[]{:S(2)}) async-start(bf16[8,4,2048]{2,1,0:T(4,128)(2,1)} %broadcast_in_dim.24), calls=%async_computation | async-start | bytes 262144 | tf_op jit(solution)/shard_map/all_to_all | solution.py:154
  9.4 0.8 fusion.30
  10.3 0.7 exponential_negate_fusion
  10.9 0.8 copy.79
  11.7 0.1 reshape_squeeze.7
  11.9 0.2 select_reduce_fusion
  12.1 0.7 copy.107
  12.8 0.8 copy.106
  13.6 2.3 %copy.76.s_ref = bf16[4,8,128,128]{3,2,1,0:T(8,128)(2,1)} copy(bf16[4,8,128,128]{2,3,1,0:T(8,128)(2,1)} %bitcast.91) | data formatting | bytes 2097152 | tf_op jit(solution)/shard_map/reshape | solution.py:234
  15.9 0.8 mul.267
  16.6 0.9 fusion.29
  17.5 0.2 multiply_reduce_fusion.1
  17.7 0.1 rsqrt.32
  17.7 0.1 rsqrt.33
  17.9 1.4 %multiply_convert_fusion.1.a_ref = bf16[32,2048]{1,0:T(8,128)(2,1)} fusion(f32[32,2048]{1,0:T(8,128)S(1)} %reshape.202, f32[2048]{0:T(1024)} %param.29, f32[32]{0:T(128)S(1)} %rsqrt.33), kind=kLoop, calls=%fused_computation.13 | loop fusion | flops 196608 | bytes 401536 | tf_op jit(solution)/shard_map/convert_element_type | solution.py:191
  19.3 5.6 %shard_map.237 = f32[32,2048]{1,0:T(8,128)} custom-call(bf16[32,2048]{1,0:T(8,128)(2,1)} %multiply_convert_fusion.1.a_ref, bf16[2048,2048]{1,0:T(8,128)(2,1)} %w_ref.2), custom_call_target="tpu_custom_call" | custom-call | flops 268435456 | bytes 8781824 | tf_op jit(solution)/shard_map/pallas_call | solution.py:57
  24.9 1.0 slice.101
  25.9 1.1 slice.112
  27.0 0.3 convolution_convert_fusion.1
  27.4 0.6 broadcast_in_dim.26
  28.1 6.0 %all-to-all-start.1 = ((bf16[8,4,8,256]{3,2,1,0:T(8,128)(2,1)}), bf16[8,4,8,256]{3,2,1,0:T(8,128)(2,1)S(1)}, u32[]{:S(2)}, u32[]{:S(2)}) async-start(bf16[8,4,8,256]{3,2,1,0:T(8,128)(2,1)} %broadcast_in_dim.26), calls=%async_computation.1 | async-start | bytes 262144 | tf_op jit(solution)/shard_map/all_to_all | solution.py:154
  34.1 0.3 multiply_exponential_fusion
  34.4 0.1 mul.225
  34.5 0.1 mul.226
  34.6 0.1 convert_element_type.94
  34.8 0.1 broadcast_in_dim.25
  34.9 0.8 reshape.190.dec_ref
  35.8 0.8 fusion.27
  36.5 0.1 reshape.193
  36.6 4.8 %all-to-all-done.1 = bf16[8,4,8,256]{3,2,1,0:T(8,128)(2,1)S(1)} async-done(((bf16[8,4,8,256]{3,2,1,0:T(8,128)(2,1)}), bf16[8,4,8,256]{3,2,1,0:T(8,128)(2,1)S(1)}, u32[]{:S(2)}, u32[]{:S(2)}) %all-to-all-start.1) | async-done | bytes 131104 | tf_op jit(solution)/shard_map/all_to_all | solution.py:154
  41.4 0.2 copy.71
  41.7 0.6 gather_fusion
  42.3 0.6 gather_fusion.1
  42.8 0.8 fusion.6
  43.6 12.5 %shard_map.238 = (bf16[4,8,128,128]{3,2,1,0:T(8,128)(2,1)}, f32[4,8,1024]{2,1,0:T(8,128)}) custom-call(bf16[4,8,128,128]{3,2,1,0:T(8,128)(2,1)} %copy.76.s_ref, f32[4,8,1024]{2,1,0:T(8,128)} %reshape.190.dec_ref, f32[4,8,1024]{2,1,0:T(8,128)} %get-tuple-element.29.dx_ref, f32[4,8,8,128]{3,2,1,0:T(8,128)} %get-tuple-element.42.b_ref, ...), custom_call_target="tpu_custom_call" | custom-call | tf_op jit(solution)/shard_map/pallas_call | solution.py:140
  56.1 1.1 %reshape.192 = f32[4,8,16,64]{3,2,1,0:T(8,128)S(1)} reshape(f32[4,8,1024]{2,1,0:T(8,128)} %get-tuple-element.7) | data formatting | bytes 262144 | tf_op jit(solution)/shard_map/reshape | solution.py:242
  57.3 0.2 multiply_reduce_fusion
  57.5 0.1 multiply_convert_fusion
  57.6 0.8 reshape.194.a_ref
  58.4 4.4 %shard_map.239 = f32[32,2048]{1,0:T(8,128)} custom-call(bf16[32,1024]{1,0:T(8,128)(2,1)} %reshape.194.a_ref, bf16[1024,2048]{1,0:T(8,128)(2,1)} %w_ref.3), custom_call_target="tpu_custom_call" | custom-call | flops 134217728 | bytes 4521984 | tf_op jit(solution)/shard_map/pallas_call | solution.py:57
  62.8 1.7 %reshape.195 = f32[8,4,2048]{2,1,0:T(4,128)} reshape(f32[32,2048]{1,0:T(8,128)} %shard_map.239) | data formatting | bytes 524288 | tf_op jit(solution)/shard_map/reshape | solution.py:253
  64.5 3.4 %all-to-all-start.2 = ((f32[8,4,2048]{2,1,0:T(4,128)}), f32[8,4,2048]{2,1,0:T(4,128)S(1)}, u32[]{:S(2)}, u32[]{:S(2)}) async-start(f32[8,4,2048]{2,1,0:T(4,128)} %reshape.195), calls=%async_computation.2 | async-start | bytes 524288 | tf_op jit(solution)/shard_map/all_to_all | solution.py:252
  68.0 0.1 copy.78
  68.1 0.6 copy.83
  68.7 0.6 copy.82
  69.3 1.3 %copy.81 = bf16[4,8,128,128]{2,3,1,0:T(8,128)(2,1)} copy(bf16[4,8,128,128]{3,2,1,0:T(8,128)(2,1)S(1)} %copy-done.1) | data formatting | bytes 2097152 | tf_op jit(solution)/shard_map/pallas_call | solution.py:140
  70.7 5.4 %all-to-all-done.2 = f32[8,4,2048]{2,1,0:T(4,128)S(1)} async-done(((f32[8,4,2048]{2,1,0:T(4,128)}), f32[8,4,2048]{2,1,0:T(4,128)S(1)}, u32[]{:S(2)}, u32[]{:S(2)}) %all-to-all-start.2) | async-done | bytes 262176 | tf_op jit(solution)/shard_map/all_to_all | solution.py:252
  76.1 0.1 fusion.9
  76.3 0.1 fusion.11
  76.4 0.1 fusion.31
  76.5 0.1 convolution_convert_fusion
  76.7 0.7 reshape_broadcast_in_dim_reshape.3
  77.4 3.3 %all-to-all-start.3 = ((bf16[8,2,2048]{2,1,0:T(2,128)(2,1)}), bf16[8,2,2048]{2,1,0:T(2,128)(2,1)S(1)}, u32[]{:S(2)}, u32[]{:S(2)}) async-start(bf16[8,2,2048]{2,1,0:T(2,128)(2,1)} %reshape_broadcast_in_dim_reshape.3), calls=%async_computation.3 | async-start | bytes 131072 | tf_op jit(solution)/shard_map/all_to_all | solution.py:267
  80.7 0.2 fusion.20
  80.9 0.1 copy.85
  81.0 6.5 %all-to-all-done.3 = bf16[8,2,2048]{2,1,0:T(2,128)(2,1)S(1)} async-done(((bf16[8,2,2048]{2,1,0:T(2,128)(2,1)}), bf16[8,2,2048]{2,1,0:T(2,128)(2,1)S(1)}, u32[]{:S(2)}, u32[]{:S(2)}) %all-to-all-start.3) | async-done | bytes 65568 | tf_op jit(solution)/shard_map/all_to_all | solution.py:267
  87.6 0.6 reshape.197.x_ref
  88.2 8.5 %shard_map.240 = bf16[16,2048]{1,0:T(8,128)(2,1)} custom-call(bf16[16,2048]{1,0:T(8,128)(2,1)} %reshape.197.x_ref, bf16[2048,2048]{1,0:T(8,128)(2,1)} %up_ref.1, bf16[2048,2048]{1,0:T(8,128)(2,1)} %down_ref.1), custom_call_target="tpu_custom_call" | custom-call | flops 268435456 | bytes 16908288 | tf_op jit(solution)/shard_map/pallas_call | solution.py:97
  96.7 1.5 %reshape.198 = bf16[8,2,2048]{2,1,0:T(2,128)(2,1)} reshape(bf16[16,2048]{1,0:T(8,128)(2,1)} %shard_map.240) | data formatting | bytes 131072 | tf_op jit(solution)/shard_map/reshape | solution.py:269
  98.2 3.3 %all-to-all-start.4 = ((bf16[8,2,2048]{2,1,0:T(2,128)(2,1)}), bf16[8,2,2048]{2,1,0:T(2,128)(2,1)S(1)}, u32[]{:S(2)}, u32[]{:S(2)}) async-start(bf16[8,2,2048]{2,1,0:T(2,128)(2,1)} %reshape.198), calls=%async_computation.4 | async-start | bytes 131072 | tf_op jit(solution)/shard_map/all_to_all | solution.py:272
  101.6 6.8 %all-to-all-done.4 = bf16[8,2,2048]{2,1,0:T(2,128)(2,1)S(1)} async-done(((bf16[8,2,2048]{2,1,0:T(2,128)(2,1)}), bf16[8,2,2048]{2,1,0:T(2,128)(2,1)S(1)}, u32[]{:S(2)}, u32[]{:S(2)}) %all-to-all-start.4) | async-done | bytes 65568 | tf_op jit(solution)/shard_map/all_to_all | solution.py:272
  108.5 0.1 fusion
  108.6 0.6 fusion.16
  (54 shorter events, 0.8 us)
Async XLA Ops:
  0.6 26.4 %copy-start = (bf16[2048,256]{1,0:T(8,128)(2,1)S(1)}, bf16[2048,256]{1,0:T(8,128)(2,1)}, u32[]{:S(2)}) copy-start(bf16[2048,256]{1,0:T(8,128)(2,1)} %param.31) | copy-start | bytes 3145732
  0.6 26.4 %copy-start.3 = (f32[2048]{0:T(1024)S(1)}, f32[2048]{0:T(1024)}, u32[]{:S(2)}) copy-start(f32[2048]{0:T(1024)} %param.29) | copy-start | bytes 24580
  0.7 26.7 %copy-start.8 = (f32[256]{0:T(256)S(1)}, f32[256]{0:T(256)}, u32[]{:S(2)}) copy-start(f32[256]{0:T(256)} %param.39) | copy-start | bytes 3076
  0.7 33.4 %copy-start.4 = (bf16[2048,16]{0,1:T(8,128)(2,1)S(1)}, bf16[2048,16]{0,1:T(8,128)(2,1)}, u32[]{:S(2)}) copy-start(bf16[2048,16]{0,1:T(8,128)(2,1)} %param.32) | copy-start | bytes 196612
  0.7 33.4 %copy-start.9 = (f32[16]{0:T(128)S(1)}, f32[16]{0:T(128)}, u32[]{:S(2)}) copy-start(f32[16]{0:T(128)} %param.33) | copy-start | bytes 196
  2.2 15.3 %all-to-all-start = ((bf16[8,4,2048]{2,1,0:T(4,128)(2,1)}), bf16[8,4,2048]{2,1,0:T(4,128)(2,1)S(1)}, u32[]{:S(2)}, u32[]{:S(2)}) async-start(bf16[8,4,2048]{2,1,0:T(4,128)(2,1)} %broadcast_in_dim.24), calls=%async_computation | async-start | bytes 262144 | tf_op jit(solution)/shard_map/all_to_all | solution.py:154
  13.6 22.2 %copy-start.6 = (f32[1024]{0:T(1024)S(1)}, f32[1024]{0:T(1024)}, u32[]{:S(2)}) copy-start(f32[1024]{0:T(1024)} %param.37) | copy-start | bytes 12292
  24.9 32.3 %copy-start.10 = (f32[16]{0:T(128)S(1)}, f32[16]{0:T(128)}, u32[]{:S(2)}) copy-start(f32[16]{0:T(128)} %param.35) | copy-start | bytes 196
  28.1 13.3 %all-to-all-start.1 = ((bf16[8,4,8,256]{3,2,1,0:T(8,128)(2,1)}), bf16[8,4,8,256]{3,2,1,0:T(8,128)(2,1)S(1)}, u32[]{:S(2)}, u32[]{:S(2)}) async-start(bf16[8,4,8,256]{3,2,1,0:T(8,128)(2,1)} %broadcast_in_dim.26), calls=%async_computation.1 | async-start | bytes 262144 | tf_op jit(solution)/shard_map/all_to_all | solution.py:154
  34.1 33.9 %copy-start.7 = (s32[1,4,2]{1,2,0:T(2,128)S(1)}, s32[1,4,2]{1,2,0:T(2,128)}, u32[]{:S(2)}) copy-start(s32[1,4,2]{1,2,0:T(2,128)} %param.28) | copy-start | bytes 100
  35.7 40.4 %copy-start.2 = (bf16[1,4,2048]{2,1,0:T(4,128)(2,1)S(1)}, bf16[1,4,2048]{2,1,0:T(4,128)(2,1)}, u32[]{:S(2)}) copy-start(bf16[1,4,2048]{2,1,0:T(4,128)(2,1)} %param.24) | copy-start | bytes 49156
  35.7 40.5 %copy-start.5 = (f32[2048]{0:T(1024)S(1)}, f32[2048]{0:T(1024)}, u32[]{:S(2)}) copy-start(f32[2048]{0:T(1024)} %param.42) | copy-start | bytes 24580
  35.8 40.6 %copy-start.11 = (bf16[2048,8]{0,1:T(8,128)(2,1)S(1)}, bf16[2048,8]{0,1:T(8,128)(2,1)}, u32[]{:S(2)}) copy-start(bf16[2048,8]{0,1:T(8,128)(2,1)} %param.43) | copy-start | bytes 98308
  56.1 13.2 %copy-start.1 = (bf16[4,8,128,128]{3,2,1,0:T(8,128)(2,1)S(1)}, bf16[4,8,128,128]{3,2,1,0:T(8,128)(2,1)}, u32[]{:S(2)}) copy-start(bf16[4,8,128,128]{3,2,1,0:T(8,128)(2,1)} %get-tuple-element.8) | copy-start | bytes 3145732
  64.5 11.6 %all-to-all-start.2 = ((f32[8,4,2048]{2,1,0:T(4,128)}), f32[8,4,2048]{2,1,0:T(4,128)S(1)}, u32[]{:S(2)}, u32[]{:S(2)}) async-start(f32[8,4,2048]{2,1,0:T(4,128)} %reshape.195), calls=%async_computation.2 | async-start | bytes 524288 | tf_op jit(solution)/shard_map/all_to_all | solution.py:252
  77.4 10.2 %all-to-all-start.3 = ((bf16[8,2,2048]{2,1,0:T(2,128)(2,1)}), bf16[8,2,2048]{2,1,0:T(2,128)(2,1)S(1)}, u32[]{:S(2)}, u32[]{:S(2)}) async-start(bf16[8,2,2048]{2,1,0:T(2,128)(2,1)} %reshape_broadcast_in_dim_reshape.3), calls=%async_computation.3 | async-start | bytes 131072 | tf_op jit(solution)/shard_map/all_to_all | solution.py:267
  98.2 10.2 %all-to-all-start.4 = ((bf16[8,2,2048]{2,1,0:T(2,128)(2,1)}), bf16[8,2,2048]{2,1,0:T(2,128)(2,1)S(1)}, u32[]{:S(2)}, u32[]{:S(2)}) async-start(bf16[8,2,2048]{2,1,0:T(2,128)(2,1)} %reshape.198), calls=%async_computation.4 | async-start | bytes 131072 | tf_op jit(solution)/shard_map/all_to_all | solution.py:272

commit v9 on v7

--- a/solution.py
+++ b/solution.py
@@ -2,6 +2,7 @@
 import jax.numpy as jnp
 from jax import lax
 from jax.experimental import pallas as pl
+from jax.experimental.pallas import tpu as pltpu
 from jax.sharding import PartitionSpec as P
 
 HEADS = 128
@@ -70,20 +71,32 @@
     )(rows, weight)
 
 
-def ssm_scan_kernel(s_ref, dec_ref, dx_ref, b_ref, c_ref, s_out_ref, read_ref):
+def ssm_scan_kernel(s_ref, dec_ref, dx_ref, b_ref, c_ref, s_out_ref, read_ref, bb_ref, cb_ref):
     tiles = s_ref.shape[1]
+    state_dim = s_ref.shape[2]
     lanes = s_ref.shape[3]
     steps = dec_ref.shape[1]
+    shared = b_ref.shape[1] == 1
+
+    def fill(jb):
+        b_cols = b_ref[0, jb].T
+        c_cols = c_ref[0, jb].T
+        for t in range(steps):
+            bb_ref[t] = jnp.broadcast_to(b_cols[:, t : t + 1], (state_dim, lanes))
+            cb_ref[t] = jnp.broadcast_to(c_cols[:, t : t + 1], (state_dim, lanes))
+
+    if shared:
+        fill(0)
     for j in range(tiles):
+        if not shared:
+            fill(j)
         cols = slice(j * lanes, (j + 1) * lanes)
         state = s_ref[0, j].astype(jnp.float32)
-        b_all = b_ref[0, j].T
-        c_all = c_ref[0, j].T
         dec_all = dec_ref[0, :, cols]
         dx_all = dx_ref[0, :, cols]
         for t in range(steps):
-            fresh = dec_all[t : t + 1, :] * state + dx_all[t : t + 1, :] * b_all[:, t : t + 1]
-            read_ref[0, t : t + 1, cols] = jnp.sum(fresh * c_all[:, t : t + 1], axis=0, keepdims=True)
+            fresh = dec_all[t : t + 1, :] * state + dx_all[t : t + 1, :] * bb_ref[t]
+            read_ref[0, t : t + 1, cols] = jnp.sum(fresh * cb_ref[t], axis=0, keepdims=True)
             state = fresh.astype(jnp.bfloat16).astype(jnp.float32)
         s_out_ref[0, j] = state.astype(jnp.bfloat16)
 
@@ -93,7 +106,7 @@
     steps = decay_rows.shape[1]
     big = pl.BlockSpec((1, tiles, state_dim, lanes), lambda r: (r, 0, 0, 0))
     per_step = pl.BlockSpec((1, steps, tiles * lanes), lambda r: (r, 0, 0))
-    rows = pl.BlockSpec((1, tiles, steps, state_dim), lambda r: (r, 0, 0, 0))
+    rows = pl.BlockSpec((1,) + b_rows.shape[1:], lambda r: (r, 0, 0, 0))
     return pl.pallas_call(
         ssm_scan_kernel,
         grid=(requests,),
@@ -102,6 +115,10 @@
         out_shape=[
             jax.ShapeDtypeStruct(state_tiles.shape, jnp.bfloat16),
             jax.ShapeDtypeStruct(decay_rows.shape, jnp.float32),
+        ],
+        scratch_shapes=[
+            pltpu.VMEM((steps, state_dim, lanes), jnp.float32),
+            pltpu.VMEM((steps, state_dim, lanes), jnp.float32),
         ],
     )(state_tiles, decay_rows, dx_rows, b_rows, c_rows)
 
@@ -180,7 +197,10 @@
         decay_rate[..., None], (requests, STEPS, heads_local, head_dim)
     ).reshape(requests, STEPS, heads_local * head_dim)
     dx_rows = (delta[..., None] * x_heads).reshape(requests, STEPS, heads_local * head_dim)
-    tile_group = (my_index * heads_local + jnp.arange(tiles) * pack) // (HEADS // G)
+    shared_group = (HEADS // G) % heads_local == 0
+    tile_group = (my_index * heads_local + jnp.arange(1 if shared_group else tiles) * pack) // (
+        HEADS // G
+    )
     bc_values = bc_all.astype(jnp.float32).reshape(requests, STEPS, 2, G, state_dim)
     b_rows = jnp.take(bc_values[:, :, 0], tile_group, axis=2).transpose(0, 2, 1, 3)
     c_rows = jnp.take(bc_values[:, :, 1], tile_group, axis=2).transpose(0, 2, 1, 3)

time: 105 us -> 98.7 us (0.940)
  Pallas kernels: 18.1 us -> 12.1 us
  local copies, waits for them, and re-layouts: 19.7 us -> 18.6 us
    pallas_call x1, Pallas kernels: 12.5 us -> 6.48 us  [ssm_scan(): pl.pallas_call(ssm_scan_kernel, grid=(requests,), in_specs=[big, per_step...]
    gather x2 -> x0, local copies, waits for them, and re-layouts: 1.13 us -> none  [the longest x1 0.56 us: shards(): jnp.take(bc_values[:, :, 0], tile_group, axis=2).transpose(0, 2, 1, 3)]
  transfers between devices with their start and end apart: 5 -> 5, of which waited for: 4 -> 4; matrix products, arithmetic and copies ran while one was open for 13% -> 14% of each run, Pallas kernels for 0% -> 0%
where the time goes in v9:
time: 98.7 us; the launch traced here: 97.6 us
  waiting for transfers between devices  23.5 us (24%)
  starting transfers between devices  23.4 us (24%)
  local copies, waits for them, and re-layouts  18.6 us (19%)
  matrix products  12.9 us (13%)
  Pallas kernels  12.1 us (12%)
  other arithmetic  6.01 us (6%)
  between operations  1.03 us (1%)
    all_to_all x2, starting transfers between devices, broadcast_gather(): return lax.all_to_all(copies, 'head', 0, 0, tiled=True)  13.3 us
    dot_general x1, matrix products, shards(): jnp.dot(hidden, weight_down, preferred_element_type=jnp.float32)  8.05 us
    all_to_all x1, waiting for transfers between devices, shards(): lax.all_to_all(computed.astype(jnp.bfloat16), 'head', split_axis=0, conca...  6.81 us
    all_to_all x1, waiting for transfers between devices, shards(): lax.all_to_all(outgoing, 'head', split_axis=0, concat_axis=0, tiled=True)  6.55 us
    pallas_call x1, Pallas kernels, ssm_scan(): pl.pallas_call(ssm_scan_kernel, grid=(requests,), in_specs=[big, per_step...  6.48 us
    pallas_call x1, Pallas kernels, column_matmul(): pl.pallas_call(column_matmul_kernel, grid=(cols // block,), in_specs=[pl....  5.63 us
    all_to_all x1, waiting for transfers between devices, shards(): lax.all_to_all(mixer_part.reshape(head_count, tok_local, width), 'head',...  5.41 us
    all_to_all x2, waiting for transfers between devices, broadcast_gather(): return lax.all_to_all(copies, 'head', 0, 0, tiled=True)  4.76 us
  transfers between devices with their start and end apart: 5, of which 4 were waited for; matrix products, arithmetic and copies ran while one was open for 14% of the time, Pallas kernels for 0%

profile of v9, /device:TPU:0, one launch (start us, length us, event | category | flops | bytes accessed | tf_op | source)
XLA Modules:
  0.0 97.6 jit_solution(5034544831645789456)
XLA Ops:
  0.7 1.5 %broadcast_in_dim.24 = bf16[8,4,2048]{2,1,0:T(4,128)(2,1)} broadcast(bf16[4,2048]{1,0:T(4,128)(2,1)} %bitcast.101), dimensions={1,2} | broadcast | bytes 147456 | tf_op jit(solution)/shard_map/broadcast_in_dim | solution.py:127
  2.2 7.3 %all-to-all-start = ((bf16[8,4,2048]{2,1,0:T(4,128)(2,1)}), bf16[8,4,2048]{2,1,0:T(4,128)(2,1)S(1)}, u32[]{:S(2)}, u32[]{:S(2)}) async-start(bf16[8,4,2048]{2,1,0:T(4,128)(2,1)} %broadcast_in_dim.24), calls=%async_computation | async-start | bytes 262144 | tf_op jit(solution)/shard_map/all_to_all | solution.py:128
  9.4 0.8 fusion.34
  10.3 0.8 copy.79
  11.0 0.1 reshape_squeeze.7
  11.1 0.1 fusion.26
  11.2 0.2 select_reduce_fusion
  11.4 0.7 exponential_negate_fusion
  12.1 0.7 copy.103
  12.8 0.8 copy.102
  13.5 2.3 %copy.74.s_ref = bf16[4,8,128,128]{3,2,1,0:T(8,128)(2,1)} copy(bf16[4,8,128,128]{2,3,1,0:T(8,128)(2,1)} %bitcast.99) | data formatting | bytes 2097152 | tf_op jit(solution)/shard_map/reshape | solution.py:211
  15.8 0.8 mul.263
  16.6 0.9 fusion.33
  17.5 0.2 multiply_reduce_fusion.1
  17.6 0.1 rsqrt.32
  17.7 0.1 rsqrt.33
  17.8 1.4 %multiply_convert_fusion.1.a_ref = bf16[32,2048]{1,0:T(8,128)(2,1)} fusion(f32[32,2048]{1,0:T(8,128)S(1)} %reshape.241, f32[2048]{0:T(1024)} %param.29, f32[32]{0:T(128)S(1)} %rsqrt.33), kind=kLoop, calls=%fused_computation.17 | loop fusion | flops 196608 | bytes 401536 | tf_op jit(solution)/shard_map/convert_element_type | solution.py:165
  19.3 5.6 %shard_map.237 = f32[32,2048]{1,0:T(8,128)} custom-call(bf16[32,2048]{1,0:T(8,128)(2,1)} %multiply_convert_fusion.1.a_ref, bf16[2048,2048]{1,0:T(8,128)(2,1)} %w_ref.1), custom_call_target="tpu_custom_call" | custom-call | flops 268435456 | bytes 8781824 | tf_op jit(solution)/shard_map/pallas_call | solution.py:57
  24.9 1.0 slice.108
  25.9 1.1 %slice.119 = f32[4,8,16,64]{3,1,2,0:T(8,128)S(1)} slice(f32[4,8,16,128]{3,1,2,0:T(8,128)} %bitcast.98), slice={[0:4], [0:8], [0:16], [64:128]} | slice | bytes 262144 | tf_op jit(solution)/shard_map/slice | solution.py:182
  27.0 0.3 convolution_convert_fusion.2
  27.4 0.7 broadcast_in_dim.26
  28.0 6.0 %all-to-all-start.1 = ((bf16[8,4,8,256]{3,2,1,0:T(8,128)(2,1)}), bf16[8,4,8,256]{3,2,1,0:T(8,128)(2,1)S(1)}, u32[]{:S(2)}, u32[]{:S(2)}) async-start(bf16[8,4,8,256]{3,2,1,0:T(8,128)(2,1)} %broadcast_in_dim.26), calls=%async_computation.1 | async-start | bytes 262144 | tf_op jit(solution)/shard_map/all_to_all | solution.py:128
  34.1 0.3 multiply_exponential_fusion
  34.3 0.1 mul.222
  34.5 0.1 mul.223
  34.6 0.1 convert_element_type.103
  34.8 0.1 broadcast_in_dim.25
  34.9 0.8 reshape.197.dec_ref
  35.8 0.8 fusion.31
  36.5 0.1 reshape.200
  36.6 4.8 %all-to-all-done.1 = bf16[8,4,8,256]{3,2,1,0:T(8,128)(2,1)S(1)} async-done(((bf16[8,4,8,256]{3,2,1,0:T(8,128)(2,1)}), bf16[8,4,8,256]{3,2,1,0:T(8,128)(2,1)S(1)}, u32[]{:S(2)}, u32[]{:S(2)}) %all-to-all-start.1) | async-done | bytes 131104 | tf_op jit(solution)/shard_map/all_to_all | solution.py:128
  41.4 0.2 copy.71
  41.6 0.1 copy_bitcast_fusion
  41.7 0.6 select_bitcast_fusion.c_ref
  42.3 0.6 select_bitcast_fusion.1.b_ref
  42.9 6.5 %shard_map.238 = (bf16[4,8,128,128]{3,2,1,0:T(8,128)(2,1)}, f32[4,8,1024]{2,1,0:T(8,128)}) custom-call(bf16[4,8,128,128]{3,2,1,0:T(8,128)(2,1)} %copy.74.s_ref, f32[4,8,1024]{2,1,0:T(8,128)} %reshape.197.dec_ref, f32[4,8,1024]{2,1,0:T(8,128)} %get-tuple-element.40.dx_ref, f32[4,1,8,128]{3,2,1,0:T(8,128)} %select_bitcast_fusion.1.b_ref, ...), custom_call_target="tpu_custom_call" | custom-call | tf_op jit(solution)/shard_map/pallas_call | solution.py:110
  49.4 1.1 %reshape.199 = f32[4,8,16,64]{3,2,1,0:T(8,128)S(1)} reshape(f32[4,8,1024]{2,1,0:T(8,128)} %get-tuple-element.7) | data formatting | bytes 262144 | tf_op jit(solution)/shard_map/reshape | solution.py:219
  50.5 0.2 multiply_reduce_fusion
  50.8 0.1 multiply_convert_fusion
  50.9 0.1 dot_general.31
  51.0 3.7 %fusion = f32[8,4,2048]{2,1,0:T(4,128)} fusion(bf16[8,4,1024]{2,1,0:T(4,128)(2,1)S(1)} %dot_general.31, bf16[1024,2048]{1,0:T(8,128)(2,1)} %param.41), kind=kOutput, calls=%fused_computation | convolution fusion | flops 134217728 | bytes 4521984 | tf_op jit(solution)/shard_map/dot_general | solution.py:228
  54.7 3.4 %all-to-all-start.2 = ((f32[8,4,2048]{2,1,0:T(4,128)}), f32[8,4,2048]{2,1,0:T(4,128)S(1)}, u32[]{:S(2)}, u32[]{:S(2)}) async-start(f32[8,4,2048]{2,1,0:T(4,128)} %fusion), calls=%async_computation.2 | async-start | bytes 524288 | tf_op jit(solution)/shard_map/all_to_all | solution.py:229
  58.2 0.1 iota_compare_fusion.3
  58.2 0.1 copy.78
  58.3 0.6 copy.83
  59.0 0.6 copy.82
  59.6 1.3 %copy.81 = bf16[4,8,128,128]{2,3,1,0:T(8,128)(2,1)} copy(bf16[4,8,128,128]{3,2,1,0:T(8,128)(2,1)S(1)} %copy-done.1) | data formatting | bytes 2097152 | tf_op jit(solution)/shard_map/pallas_call | solution.py:110
  60.9 5.4 %all-to-all-done.2 = f32[8,4,2048]{2,1,0:T(4,128)S(1)} async-done(((f32[8,4,2048]{2,1,0:T(4,128)}), f32[8,4,2048]{2,1,0:T(4,128)S(1)}, u32[]{:S(2)}, u32[]{:S(2)}) %all-to-all-start.2) | async-done | bytes 262176 | tf_op jit(solution)/shard_map/all_to_all | solution.py:229
  66.4 0.1 fusion.12
  66.5 0.1 fusion.14
  66.6 0.1 fusion.35
  66.8 0.1 convolution_convert_fusion
  66.9 0.7 reshape_broadcast_in_dim_reshape.3
  67.6 3.3 %all-to-all-start.3 = ((bf16[8,2,2048]{2,1,0:T(2,128)(2,1)}), bf16[8,2,2048]{2,1,0:T(2,128)(2,1)S(1)}, u32[]{:S(2)}, u32[]{:S(2)}) async-start(bf16[8,2,2048]{2,1,0:T(2,128)(2,1)} %reshape_broadcast_in_dim_reshape.3), calls=%async_computation.3 | async-start | bytes 131072 | tf_op jit(solution)/shard_map/all_to_all | solution.py:244
  71.0 0.2 fusion.23
  71.2 0.1 copy.87
  71.3 6.5 %all-to-all-done.3 = bf16[8,2,2048]{2,1,0:T(2,128)(2,1)S(1)} async-done(((bf16[8,2,2048]{2,1,0:T(2,128)(2,1)}), bf16[8,2,2048]{2,1,0:T(2,128)(2,1)S(1)}, u32[]{:S(2)}, u32[]{:S(2)}) %all-to-all-start.3) | async-done | bytes 65568 | tf_op jit(solution)/shard_map/all_to_all | solution.py:244
  77.9 8.0 %convolution_convert_fusion.1 = bf16[16,2048]{1,0:T(8,128)(2,1)S(1)} fusion(bf16[2048,2048]{1,0:T(8,128)(2,1)} %param.45, bf16[16,2048]{1,0:T(8,128)(2,1)S(1)} %reshape.202, bf16[2048,2048]{1,0:T(8,128)(2,1)} %param.44), kind=kOutput, calls=%fused_computation.6 | convolution fusion | flops 268566528 | bytes 16908288 | tf_op jit(solution)/shard_map/dot_general | solution.py:247
  85.9 0.7 convert_element_type.122
  86.6 3.3 %all-to-all-start.4 = ((bf16[8,2,2048]{2,1,0:T(2,128)(2,1)}), bf16[8,2,2048]{2,1,0:T(2,128)(2,1)S(1)}, u32[]{:S(2)}, u32[]{:S(2)}) async-start(bf16[8,2,2048]{2,1,0:T(2,128)(2,1)} %convert_element_type.122), calls=%async_computation.4 | async-start | bytes 131072 | tf_op jit(solution)/shard_map/all_to_all | solution.py:250
  90.0 6.8 %all-to-all-done.4 = bf16[8,2,2048]{2,1,0:T(2,128)(2,1)S(1)} async-done(((bf16[8,2,2048]{2,1,0:T(2,128)(2,1)}), bf16[8,2,2048]{2,1,0:T(2,128)(2,1)S(1)}, u32[]{:S(2)}, u32[]{:S(2)}) %all-to-all-start.4) | async-done | bytes 65568 | tf_op jit(solution)/shard_map/all_to_all | solution.py:250
  96.8 0.1 fusion.4
  97.0 0.6 fusion.19
  (49 shorter events, 0.6 us)
Async XLA Ops:
  0.6 26.3 %copy-start = (bf16[2048,256]{1,0:T(8,128)(2,1)S(1)}, bf16[2048,256]{1,0:T(8,128)(2,1)}, u32[]{:S(2)}) copy-start(bf16[2048,256]{1,0:T(8,128)(2,1)} %param.31) | copy-start | bytes 3145732
  0.6 26.3 %copy-start.3 = (f32[2048]{0:T(1024)S(1)}, f32[2048]{0:T(1024)}, u32[]{:S(2)}) copy-start(f32[2048]{0:T(1024)} %param.29) | copy-start | bytes 24580
  0.7 26.7 %copy-start.8 = (f32[256]{0:T(256)S(1)}, f32[256]{0:T(256)}, u32[]{:S(2)}) copy-start(f32[256]{0:T(256)} %param.39) | copy-start | bytes 3076
  0.7 33.4 %copy-start.4 = (bf16[2048,16]{0,1:T(8,128)(2,1)S(1)}, bf16[2048,16]{0,1:T(8,128)(2,1)}, u32[]{:S(2)}) copy-start(bf16[2048,16]{0,1:T(8,128)(2,1)} %param.32) | copy-start | bytes 196612
  0.7 33.4 %copy-start.9 = (f32[16]{0:T(128)S(1)}, f32[16]{0:T(128)}, u32[]{:S(2)}) copy-start(f32[16]{0:T(128)} %param.33) | copy-start | bytes 196
  2.2 15.3 %all-to-all-start = ((bf16[8,4,2048]{2,1,0:T(4,128)(2,1)}), bf16[8,4,2048]{2,1,0:T(4,128)(2,1)S(1)}, u32[]{:S(2)}, u32[]{:S(2)}) async-start(bf16[8,4,2048]{2,1,0:T(4,128)(2,1)} %broadcast_in_dim.24), calls=%async_computation | async-start | bytes 262144 | tf_op jit(solution)/shard_map/all_to_all | solution.py:128
  13.5 22.2 %copy-start.6 = (f32[1024]{0:T(1024)S(1)}, f32[1024]{0:T(1024)}, u32[]{:S(2)}) copy-start(f32[1024]{0:T(1024)} %param.37) | copy-start | bytes 12292
  19.3 31.2 %copy-start.10 = (f32[16]{0:T(128)S(1)}, f32[16]{0:T(128)}, u32[]{:S(2)}) copy-start(f32[16]{0:T(128)} %param.35) | copy-start | bytes 196
  27.3 30.9 %copy-start.7 = (s32[1,4,2]{1,2,0:T(2,128)S(1)}, s32[1,4,2]{1,2,0:T(2,128)}, u32[]{:S(2)}) copy-start(s32[1,4,2]{1,2,0:T(2,128)} %param.28) | copy-start | bytes 100
  28.0 13.3 %all-to-all-start.1 = ((bf16[8,4,8,256]{3,2,1,0:T(8,128)(2,1)}), bf16[8,4,8,256]{3,2,1,0:T(8,128)(2,1)S(1)}, u32[]{:S(2)}, u32[]{:S(2)}) async-start(bf16[8,4,8,256]{3,2,1,0:T(8,128)(2,1)} %broadcast_in_dim.26), calls=%async_computation.1 | async-start | bytes 262144 | tf_op jit(solution)/shard_map/all_to_all | solution.py:128
  34.9 31.5 %copy-start.2 = (bf16[1,4,2048]{2,1,0:T(4,128)(2,1)S(1)}, bf16[1,4,2048]{2,1,0:T(4,128)(2,1)}, u32[]{:S(2)}) copy-start(bf16[1,4,2048]{2,1,0:T(4,128)(2,1)} %param.24) | copy-start | bytes 49156
  34.9 31.6 %copy-start.5 = (f32[2048]{0:T(1024)S(1)}, f32[2048]{0:T(1024)}, u32[]{:S(2)}) copy-start(f32[2048]{0:T(1024)} %param.42) | copy-start | bytes 24580
  34.9 31.7 %copy-start.11 = (bf16[2048,8]{0,1:T(8,128)(2,1)S(1)}, bf16[2048,8]{0,1:T(8,128)(2,1)}, u32[]{:S(2)}) copy-start(bf16[2048,8]{0,1:T(8,128)(2,1)} %param.43) | copy-start | bytes 98308
  49.4 10.2 %copy-start.1 = (bf16[4,8,128,128]{3,2,1,0:T(8,128)(2,1)S(1)}, bf16[4,8,128,128]{3,2,1,0:T(8,128)(2,1)}, u32[]{:S(2)}) copy-start(bf16[4,8,128,128]{3,2,1,0:T(8,128)(2,1)} %get-tuple-element.8) | copy-start | bytes 3145732
  54.7 11.6 %all-to-all-start.2 = ((f32[8,4,2048]{2,1,0:T(4,128)}), f32[8,4,2048]{2,1,0:T(4,128)S(1)}, u32[]{:S(2)}, u32[]{:S(2)}) async-start(f32[8,4,2048]{2,1,0:T(4,128)} %fusion), calls=%async_computation.2 | async-start | bytes 524288 | tf_op jit(solution)/shard_map/all_to_all | solution.py:229
  67.6 10.2 %all-to-all-start.3 = ((bf16[8,2,2048]{2,1,0:T(2,128)(2,1)}), bf16[8,2,2048]{2,1,0:T(2,128)(2,1)S(1)}, u32[]{:S(2)}, u32[]{:S(2)}) async-start(bf16[8,2,2048]{2,1,0:T(2,128)(2,1)} %reshape_broadcast_in_dim_reshape.3), calls=%async_computation.3 | async-start | bytes 131072 | tf_op jit(solution)/shard_map/all_to_all | solution.py:244
  86.6 10.2 %all-to-all-start.4 = ((bf16[8,2,2048]{2,1,0:T(2,128)(2,1)}), bf16[8,2,2048]{2,1,0:T(2,128)(2,1)S(1)}, u32[]{:S(2)}, u32[]{:S(2)}) async-start(bf16[8,2,2048]{2,1,0:T(2,128)(2,1)} %convert_element_type.122), calls=%async_computation.4 | async-start | bytes 131072 | tf_op jit(solution)/shard_map/all_to_all | solution.py:250

commit v10 on v9

--- a/solution.py
+++ b/solution.py
@@ -1,3 +1,5 @@
+import functools
+
 import jax
 import jax.numpy as jnp
 from jax import lax
@@ -67,6 +69,45 @@
             flops=2 * m * k * cols,
             transcendentals=0,
             bytes_accessed=2 * (m * k + k * cols) + 4 * m * cols,
+        ),
+    )(rows, weight)
+
+
+def xz_matmul_kernel(head_dim, a_ref, w_ref, x_ref, z_ref):
+    product = jnp.dot(a_ref[...], w_ref[...], preferred_element_type=jnp.float32)
+    width = z_ref.shape[1]
+    for h in range(width // head_dim):
+        x_ref[:, h * head_dim : (h + 1) * head_dim] = product[
+            :, 2 * h * head_dim : (2 * h + 1) * head_dim
+        ].astype(x_ref.dtype)
+        z_ref[:, h * head_dim : (h + 1) * head_dim] = product[
+            :, (2 * h + 1) * head_dim : (2 * h + 2) * head_dim
+        ]
+
+
+def xz_matmul(rows, weight, head_dim):
+    m, k = rows.shape
+    cols = weight.shape[1]
+    block = min(512, cols)
+    return pl.pallas_call(
+        functools.partial(xz_matmul_kernel, head_dim),
+        grid=(cols // block,),
+        in_specs=[
+            pl.BlockSpec((m, k), lambda j: (0, 0)),
+            pl.BlockSpec((k, block), lambda j: (0, j)),
+        ],
+        out_specs=[
+            pl.BlockSpec((m, block // 2), lambda j: (0, j)),
+            pl.BlockSpec((m, block // 2), lambda j: (0, j)),
+        ],
+        out_shape=[
+            jax.ShapeDtypeStruct((m, cols // 2), jnp.bfloat16),
+            jax.ShapeDtypeStruct((m, cols // 2), jnp.float32),
+        ],
+        cost_estimate=pl.CostEstimate(
+            flops=2 * m * k * cols,
+            transcendentals=0,
+            bytes_accessed=2 * (m * k + k * cols) + 3 * m * cols,
         ),
     )(rows, weight)
 
@@ -173,13 +214,9 @@
     bc_all = jnp.moveaxis(broadcast_gather(bc_conv, head_count), 0, 2).reshape(
         requests, STEPS, -1
     )
-    proj_xz = column_matmul(normed, weight_xz).reshape(
-        requests, STEPS, heads_local, 2 * head_dim
-    )
-    x_fresh = (
-        proj_xz[..., :head_dim].reshape(requests, STEPS, heads_local * head_dim).astype(jnp.bfloat16)
-    )
-    z_gate = proj_xz[..., head_dim:]
+    x_rows, z_rows = xz_matmul(normed, weight_xz, head_dim)
+    x_fresh = x_rows.reshape(requests, STEPS, heads_local * head_dim)
+    z_gate = z_rows.reshape(requests, STEPS, heads_local, head_dim)
     delta = jax.nn.softplus(
         jnp.dot(normed, weight_delta, preferred_element_type=jnp.float32).reshape(
             requests, STEPS, heads_local

time: 98.7 us -> 99.8 us (1.011)
  waiting for transfers between devices: 23.5 us -> 18.8 us
  other arithmetic: 6.01 us -> 8.51 us
  starting transfers between devices: 23.4 us -> 25.9 us
  matrix products: 12.9 us -> 14.5 us
  local copies, waits for them, and re-layouts: 18.6 us -> 17.6 us
    all_to_all x2, waiting for transfers between devices: 4.76 us -> 0.01 us  [broadcast_gather(): return lax.all_to_all(copies, 'head', 0, 0, tiled=True)]
    all_to_all x1, starting transfers between devices: 3.41 us -> 6 us  [shards(): lax.all_to_all(mixer_part.reshape(head_count, tok_local, width), 'head',...]
    slice x2 -> x0, local copies, waits for them, and re-layouts: 2.04 us -> none  [the longest x1 1.07 us: shards(): z_gate = proj_xz[..., head_dim:]]
    reshape x0 -> x1, local copies, waits for them, and re-layouts: none -> 1.01 us  [shards(): z_gate = z_rows.reshape(requests, STEPS, heads_local, head_dim)]
    unnamed x30 -> x25, local copies, waits for them, and re-layouts: 3.53 us -> 3.5 us
  transfers between devices with their start and end apart: 5 -> 5, of which waited for: 4 -> 3; matrix products, arithmetic and copies ran while one was open for 14% -> 18% of each run, Pallas kernels for 0% -> 6%
where the time goes in v10:
time: 99.8 us; the launch traced here: 98.6 us
  starting transfers between devices  25.9 us (26%)
  waiting for transfers between devices  18.8 us (19%)
  local copies, waits for them, and re-layouts  17.6 us (18%)
  matrix products  14.5 us (15%)
  Pallas kernels  12.2 us (12%)
  other arithmetic  8.51 us (9%)
    all_to_all x2, starting transfers between devices, broadcast_gather(): return lax.all_to_all(copies, 'head', 0, 0, tiled=True)  13.3 us
    dot_general x1, matrix products, shards(): jnp.dot(hidden, weight_down, preferred_element_type=jnp.float32)  8.05 us
    all_to_all x1, waiting for transfers between devices, shards(): lax.all_to_all(computed.astype(jnp.bfloat16), 'head', split_axis=0, conca...  6.81 us
    all_to_all x1, waiting for transfers between devices, shards(): lax.all_to_all(outgoing, 'head', split_axis=0, concat_axis=0, tiled=True)  6.55 us
    pallas_call x1, Pallas kernels, ssm_scan(): pl.pallas_call(ssm_scan_kernel, grid=(requests,), in_specs=[big, per_step...  6.49 us
    all_to_all x1, starting transfers between devices, shards(): lax.all_to_all(mixer_part.reshape(head_count, tok_local, width), 'head',...  6 us
    pallas_call x1, Pallas kernels, xz_matmul(): pl.pallas_call(functools.partial(xz_matmul_kernel, head_dim), grid=(cols...  5.76 us
    all_to_all x1, waiting for transfers between devices, shards(): lax.all_to_all(mixer_part.reshape(head_count, tok_local, width), 'head',...  5.48 us
  transfers between devices with their start and end apart: 5, of which 3 were waited for; matrix products, arithmetic and copies ran while one was open for 18% of the time, Pallas kernels for 6%

profile of v10, /device:TPU:0, one launch (start us, length us, event | category | flops | bytes accessed | tf_op | source)
XLA Modules:
  0.0 98.6 jit_solution(12371666832910049087)
XLA Ops:
  0.7 1.5 %broadcast_in_dim.24 = bf16[8,4,2048]{2,1,0:T(4,128)(2,1)} broadcast(bf16[4,2048]{1,0:T(4,128)(2,1)} %bitcast.111), dimensions={1,2} | broadcast | bytes 147456 | tf_op jit(solution)/shard_map/broadcast_in_dim | solution.py:168
  2.1 7.3 %all-to-all-start = ((bf16[8,4,2048]{2,1,0:T(4,128)(2,1)}), bf16[8,4,2048]{2,1,0:T(4,128)(2,1)S(1)}, u32[]{:S(2)}, u32[]{:S(2)}) async-start(bf16[8,4,2048]{2,1,0:T(4,128)(2,1)} %broadcast_in_dim.24), calls=%async_computation | async-start | bytes 262144 | tf_op jit(solution)/shard_map/all_to_all | solution.py:169
  9.4 0.8 fusion.39
  10.2 0.8 copy.72
  11.0 0.1 reshape_squeeze.7
  11.1 0.1 fusion.31
  11.2 0.2 select_reduce_fusion
  11.4 0.7 exponential_negate_fusion
  12.0 0.7 copy.90
  12.7 0.8 copy.89
  13.5 2.3 %copy.68.s_ref = bf16[4,8,128,128]{3,2,1,0:T(8,128)(2,1)} copy(bf16[4,8,128,128]{2,3,1,0:T(8,128)(2,1)} %bitcast.109) | data formatting | bytes 2097152 | tf_op jit(solution)/shard_map/reshape | solution.py:248
  15.8 0.7 mul.273
  16.5 0.1 mul.274
  16.6 0.9 fusion.38
  17.5 0.2 multiply_reduce_fusion.1
  17.6 0.1 rsqrt.32
  17.7 0.1 rsqrt.33
  17.8 1.0 %convolution_convert_fusion.2 = bf16[4,8,256]{2,1,0:T(8,128)(2,1)S(1)} fusion(bf16[2048,256]{1,0:T(8,128)(2,1)S(1)} %copy-done, f32[4,8,2048]{2,1,0:T(8,128)S(1)} %reshape.253, f32[2048]{0:T(1024)} %param.29, f32[4,8]{1,0:T(4,128)S(1)} %rsqrt.32), kind=kOutput, calls=%fused_computation.9 | convolution fusion | flops 33759232 | bytes 1335424 | tf_op jit(solution)/shard_map/dot_general | solution.py:208
  18.9 0.7 multiply_convert_fusion.2
  19.6 0.7 broadcast_in_dim.26
  20.3 6.0 %all-to-all-start.1 = ((bf16[8,4,8,256]{3,2,1,0:T(8,128)(2,1)}), bf16[8,4,8,256]{3,2,1,0:T(8,128)(2,1)S(1)}, u32[]{:S(2)}, u32[]{:S(2)}) async-start(bf16[8,4,8,256]{3,2,1,0:T(8,128)(2,1)} %broadcast_in_dim.26), calls=%async_computation.1 | async-start | bytes 262144 | tf_op jit(solution)/shard_map/all_to_all | solution.py:169
  26.3 1.1 %multiply_exponential_fusion = (f32[4,8,16]{2,1,0:T(8,128)S(1)}, f32[4,8,16]{2,1,0:T(8,128)S(1)}) fusion(f32[16]{0:T(128)S(1)} %exponential_negate_fusion, f32[16]{0:T(128)} %param.33, bf16[2048,16]{0,1:T(8,128)(2,1)} %param.32, f32[4,8,2048]{2,1,0:T(8,128)S(1)} %reshape.253, f32[2048]{0:T(1024)} %param.29, f32[4,8]{1,0:T(4,128)S(1)} %rsqrt.32), kind=kOutput, calls=%fused_computation.63 | convolution fusion | flops 2297856 | bytes 340224 | tf_op jit(solution)/shard_map/dot_general | solution.py:221
  27.4 0.1 mul.239
  27.5 0.1 mul.240
  27.6 0.1 broadcast_in_dim.25
  27.7 0.8 reshape.207.dec_ref
  28.6 1.5 %multiply_convert_fusion.a_ref = bf16[32,2048]{1,0:T(8,128)(2,1)} fusion(f32[32,2048]{1,0:T(8,128)S(1)} %reshape.254, f32[2048]{0:T(1024)} %param.29, f32[32]{0:T(128)S(1)} %rsqrt.33), kind=kLoop, calls=%fused_computation.14 | loop fusion | flops 196608 | bytes 401536 | tf_op jit(solution)/shard_map/convert_element_type | solution.py:206
  30.0 5.8 %shard_map.237 = (bf16[32,1024]{1,0:T(8,128)(2,1)}, f32[32,1024]{1,0:T(8,128)}) custom-call(bf16[32,2048]{1,0:T(8,128)(2,1)} %multiply_convert_fusion.a_ref, bf16[2048,2048]{1,0:T(8,128)(2,1)} %w_ref.1), custom_call_target="tpu_custom_call" | custom-call | flops 268435456 | bytes 8716288 | tf_op jit(solution)/shard_map/pallas_call | solution.py:92
  35.8 0.9 maximum_convert_fusion
  36.8 0.8 fusion.36
  37.6 0.1 reshape.212
  37.7 1.0 %reshape.213 = f32[4,8,16,64]{3,2,1,0:T(8,128)S(1)} reshape(f32[32,1024]{1,0:T(8,128)} %get-tuple-element.11) | data formatting | bytes 262144 | tf_op jit(solution)/shard_map/reshape | solution.py:219
  38.7 0.2 copy.65
  39.0 0.6 select_bitcast_fusion.c_ref
  39.6 0.6 select_bitcast_fusion.1.b_ref
  40.2 6.5 %shard_map.238 = (bf16[4,8,128,128]{3,2,1,0:T(8,128)(2,1)}, f32[4,8,1024]{2,1,0:T(8,128)}) custom-call(bf16[4,8,128,128]{3,2,1,0:T(8,128)(2,1)} %copy.68.s_ref, f32[4,8,1024]{2,1,0:T(8,128)} %reshape.207.dec_ref, f32[4,8,1024]{2,1,0:T(8,128)} %get-tuple-element.42.dx_ref, f32[4,1,8,128]{3,2,1,0:T(8,128)} %select_bitcast_fusion.1.b_ref, ...), custom_call_target="tpu_custom_call" | custom-call | tf_op jit(solution)/shard_map/pallas_call | solution.py:151
  46.7 1.1 %reshape.211 = f32[4,8,16,64]{3,2,1,0:T(8,128)S(1)} reshape(f32[4,8,1024]{2,1,0:T(8,128)} %get-tuple-element.10) | data formatting | bytes 262144 | tf_op jit(solution)/shard_map/reshape | solution.py:256
  47.8 0.2 multiply_reduce_fusion
  48.0 0.1 mul.284
  48.2 0.1 mul.285
  48.3 1.0 %fusion.14 = bf16[32,1024]{1,0:T(8,128)(2,1)S(1)} fusion(f32[32,1024]{1,0:T(8,128)S(1)} %mul.285, f32[4,8,1024]{2,1,0:T(8,128)S(1)} %get-tuple-element.43, f32[4,8,1024]{2,1,0:T(8,128)} %get-tuple-element.10, f32[32,1024]{1,0:T(8,128)} %get-tuple-element.11, f32[1024]{0:T(1024)S(1)} %copy-done.6, f32[1024]{0:T(1024)S(1)} %mul.274), kind=kLoop, calls=%fused_computation.33 | loop fusion | flops 327680 | bytes 598016 | tf_op jit(solution)/shard_map/convert_element_type | solution.py:261
  49.4 3.7 %fusion = f32[8,4,2048]{2,1,0:T(4,128)} fusion(bf16[8,4,1024]{2,1,0:T(4,128)(2,1)S(1)} %dot_general.31, bf16[1024,2048]{1,0:T(8,128)(2,1)} %param.41), kind=kOutput, calls=%fused_computation | convolution fusion | flops 134217728 | bytes 4521984 | tf_op jit(solution)/shard_map/dot_general | solution.py:265
  53.1 6.0 %all-to-all-start.2 = ((f32[8,4,2048]{2,1,0:T(4,128)}), f32[8,4,2048]{2,1,0:T(4,128)S(1)}, u32[]{:S(2)}, u32[]{:S(2)}) async-start(f32[8,4,2048]{2,1,0:T(4,128)} %fusion), calls=%async_computation.2 | async-start | bytes 524288 | tf_op jit(solution)/shard_map/all_to_all | solution.py:266
  59.1 0.1 iota_compare_fusion.3
  59.2 0.1 copy.71
  59.3 0.6 copy.76
  59.9 0.6 copy.75
  60.5 1.3 %copy.74 = bf16[4,8,128,128]{2,3,1,0:T(8,128)(2,1)} copy(bf16[4,8,128,128]{3,2,1,0:T(8,128)(2,1)S(1)} %copy-done.1) | data formatting | bytes 2097152 | tf_op jit(solution)/shard_map/pallas_call | solution.py:151
  61.8 5.5 %all-to-all-done.2 = f32[8,4,2048]{2,1,0:T(4,128)S(1)} async-done(((f32[8,4,2048]{2,1,0:T(4,128)}), f32[8,4,2048]{2,1,0:T(4,128)S(1)}, u32[]{:S(2)}, u32[]{:S(2)}) %all-to-all-start.2) | async-done | bytes 262176 | tf_op jit(solution)/shard_map/all_to_all | solution.py:266
  67.4 0.1 fusion.17
  67.5 0.1 fusion.19
  67.6 0.1 fusion.40
  67.8 0.1 convolution_convert_fusion
  67.9 0.7 reshape_broadcast_in_dim_reshape.3
  68.6 3.3 %all-to-all-start.3 = ((bf16[8,2,2048]{2,1,0:T(2,128)(2,1)}), bf16[8,2,2048]{2,1,0:T(2,128)(2,1)S(1)}, u32[]{:S(2)}, u32[]{:S(2)}) async-start(bf16[8,2,2048]{2,1,0:T(2,128)(2,1)} %reshape_broadcast_in_dim_reshape.3), calls=%async_computation.3 | async-start | bytes 131072 | tf_op jit(solution)/shard_map/all_to_all | solution.py:281
  72.0 0.2 fusion.28
  72.2 0.1 copy.80
  72.3 6.5 %all-to-all-done.3 = bf16[8,2,2048]{2,1,0:T(2,128)(2,1)S(1)} async-done(((bf16[8,2,2048]{2,1,0:T(2,128)(2,1)}), bf16[8,2,2048]{2,1,0:T(2,128)(2,1)S(1)}, u32[]{:S(2)}, u32[]{:S(2)}) %all-to-all-start.3) | async-done | bytes 65568 | tf_op jit(solution)/shard_map/all_to_all | solution.py:281
  78.9 8.0 %convolution_convert_fusion.1 = bf16[16,2048]{1,0:T(8,128)(2,1)S(1)} fusion(bf16[2048,2048]{1,0:T(8,128)(2,1)} %param.45, bf16[16,2048]{1,0:T(8,128)(2,1)S(1)} %reshape.215, bf16[2048,2048]{1,0:T(8,128)(2,1)} %param.44), kind=kOutput, calls=%fused_computation.6 | convolution fusion | flops 268566528 | bytes 16908288 | tf_op jit(solution)/shard_map/dot_general | solution.py:284
  86.9 0.7 convert_element_type.118
  87.6 3.3 %all-to-all-start.4 = ((bf16[8,2,2048]{2,1,0:T(2,128)(2,1)}), bf16[8,2,2048]{2,1,0:T(2,128)(2,1)S(1)}, u32[]{:S(2)}, u32[]{:S(2)}) async-start(bf16[8,2,2048]{2,1,0:T(2,128)(2,1)} %convert_element_type.118), calls=%async_computation.4 | async-start | bytes 131072 | tf_op jit(solution)/shard_map/all_to_all | solution.py:287
  91.0 6.8 %all-to-all-done.4 = bf16[8,2,2048]{2,1,0:T(2,128)(2,1)S(1)} async-done(((bf16[8,2,2048]{2,1,0:T(2,128)(2,1)}), bf16[8,2,2048]{2,1,0:T(2,128)(2,1)S(1)}, u32[]{:S(2)}, u32[]{:S(2)}) %all-to-all-start.4) | async-done | bytes 65568 | tf_op jit(solution)/shard_map/all_to_all | solution.py:287
  97.8 0.1 fusion.4
  98.0 0.6 fusion.24
  (45 shorter events, 0.5 us)
Async XLA Ops:
  0.6 17.2 %copy-start = (bf16[2048,256]{1,0:T(8,128)(2,1)S(1)}, bf16[2048,256]{1,0:T(8,128)(2,1)}, u32[]{:S(2)}) copy-start(bf16[2048,256]{1,0:T(8,128)(2,1)} %param.31) | copy-start | bytes 3145732
  0.6 36.1 %copy-start.5 = (f32[1024]{0:T(1024)S(1)}, f32[1024]{0:T(1024)}, u32[]{:S(2)}) copy-start(f32[1024]{0:T(1024)} %param.37) | copy-start | bytes 12292
  2.1 15.3 %all-to-all-start = ((bf16[8,4,2048]{2,1,0:T(4,128)(2,1)}), bf16[8,4,2048]{2,1,0:T(4,128)(2,1)S(1)}, u32[]{:S(2)}, u32[]{:S(2)}) async-start(bf16[8,4,2048]{2,1,0:T(4,128)(2,1)} %broadcast_in_dim.24), calls=%async_computation | async-start | bytes 262144 | tf_op jit(solution)/shard_map/all_to_all | solution.py:169
  20.3 18.4 %all-to-all-start.1 = ((bf16[8,4,8,256]{3,2,1,0:T(8,128)(2,1)}), bf16[8,4,8,256]{3,2,1,0:T(8,128)(2,1)S(1)}, u32[]{:S(2)}, u32[]{:S(2)}) async-start(bf16[8,4,8,256]{3,2,1,0:T(8,128)(2,1)} %broadcast_in_dim.26), calls=%async_computation.1 | async-start | bytes 262144 | tf_op jit(solution)/shard_map/all_to_all | solution.py:169
  27.5 20.3 %copy-start.8 = (f32[16]{0:T(128)S(1)}, f32[16]{0:T(128)}, u32[]{:S(2)}) copy-start(f32[16]{0:T(128)} %param.35) | copy-start | bytes 196
  28.6 19.8 %copy-start.6 = (f32[1024]{0:T(1024)S(1)}, f32[1024]{0:T(1024)}, u32[]{:S(2)}) copy-start(f32[1024]{0:T(1024)} %param.40) | copy-start | bytes 12292
  35.8 23.4 %copy-start.7 = (s32[1,4,2]{1,2,0:T(2,128)S(1)}, s32[1,4,2]{1,2,0:T(2,128)}, u32[]{:S(2)}) copy-start(s32[1,4,2]{1,2,0:T(2,128)} %param.28) | copy-start | bytes 100
  35.8 24.1 %copy-start.3 = (bf16[32,1024]{1,0:T(8,128)(2,1)S(1)}, bf16[32,1024]{1,0:T(8,128)(2,1)}, u32[]{:S(2)}) copy-start(bf16[32,1024]{1,0:T(8,128)(2,1)} %get-tuple-element.9) | copy-start | bytes 196612
  36.7 30.6 %copy-start.2 = (bf16[1,4,2048]{2,1,0:T(4,128)(2,1)S(1)}, bf16[1,4,2048]{2,1,0:T(4,128)(2,1)}, u32[]{:S(2)}) copy-start(bf16[1,4,2048]{2,1,0:T(4,128)(2,1)} %param.24) | copy-start | bytes 49156
  36.8 30.8 %copy-start.4 = (f32[2048]{0:T(1024)S(1)}, f32[2048]{0:T(1024)}, u32[]{:S(2)}) copy-start(f32[2048]{0:T(1024)} %param.42) | copy-start | bytes 24580
  36.8 30.8 %copy-start.9 = (bf16[2048,8]{0,1:T(8,128)(2,1)S(1)}, bf16[2048,8]{0,1:T(8,128)(2,1)}, u32[]{:S(2)}) copy-start(bf16[2048,8]{0,1:T(8,128)(2,1)} %param.43) | copy-start | bytes 98308
  46.7 13.8 %copy-start.1 = (bf16[4,8,128,128]{3,2,1,0:T(8,128)(2,1)S(1)}, bf16[4,8,128,128]{3,2,1,0:T(8,128)(2,1)}, u32[]{:S(2)}) copy-start(bf16[4,8,128,128]{3,2,1,0:T(8,128)(2,1)} %get-tuple-element.12) | copy-start | bytes 3145732
  53.1 14.2 %all-to-all-start.2 = ((f32[8,4,2048]{2,1,0:T(4,128)}), f32[8,4,2048]{2,1,0:T(4,128)S(1)}, u32[]{:S(2)}, u32[]{:S(2)}) async-start(f32[8,4,2048]{2,1,0:T(4,128)} %fusion), calls=%async_computation.2 | async-start | bytes 524288 | tf_op jit(solution)/shard_map/all_to_all | solution.py:266
  68.6 10.2 %all-to-all-start.3 = ((bf16[8,2,2048]{2,1,0:T(2,128)(2,1)}), bf16[8,2,2048]{2,1,0:T(2,128)(2,1)S(1)}, u32[]{:S(2)}, u32[]{:S(2)}) async-start(bf16[8,2,2048]{2,1,0:T(2,128)(2,1)} %reshape_broadcast_in_dim_reshape.3), calls=%async_computation.3 | async-start | bytes 131072 | tf_op jit(solution)/shard_map/all_to_all | solution.py:281
  87.6 10.2 %all-to-all-start.4 = ((bf16[8,2,2048]{2,1,0:T(2,128)(2,1)}), bf16[8,2,2048]{2,1,0:T(2,128)(2,1)S(1)}, u32[]{:S(2)}, u32[]{:S(2)}) async-start(bf16[8,2,2048]{2,1,0:T(2,128)(2,1)} %convert_element_type.118), calls=%async_computation.4 | async-start | bytes 131072 | tf_op jit(solution)/shard_map/all_to_all | solution.py:287

commit v11 on v9

--- a/solution.py
+++ b/solution.py
@@ -247,9 +247,7 @@
     computed = jnp.dot(hidden, weight_down, preferred_element_type=jnp.float32).reshape(
         received.shape[0], received.shape[1], width
     )
-    returned = lax.all_to_all(
-        computed.astype(jnp.bfloat16), "head", split_axis=0, concat_axis=0, tiled=True
-    ).astype(computed.dtype)
+    returned = lax.all_to_all(computed, "head", split_axis=0, concat_axis=0, tiled=True)
     summed = (
         returned.reshape(EXPERTS, per_expert, CAP, width).sum(axis=1).reshape(EXPERTS * CAP, width)
     )

time: 98.7 us -> 99.3 us (level)
  no operation moved by 1% of the time
where the time goes in v11:
time: 99.3 us; the launch traced here: 98.2 us
  waiting for transfers between devices  24 us (24%)
  starting transfers between devices  23.4 us (24%)
  local copies, waits for them, and re-layouts  18.7 us (19%)
  matrix products  13 us (13%)
  Pallas kernels  12.1 us (12%)
  other arithmetic  6.01 us (6%)
  between operations  1.02 us (1%)
    all_to_all x2, starting transfers between devices, broadcast_gather(): return lax.all_to_all(copies, 'head', 0, 0, tiled=True)  13.3 us
    dot_general x1, matrix products, shards(): jnp.dot(hidden, weight_down, preferred_element_type=jnp.float32)  8.05 us
    all_to_all x1, waiting for transfers between devices, shards(): lax.all_to_all(computed, 'head', split_axis=0, concat_axis=0, tiled=True)  7.25 us
    all_to_all x1, waiting for transfers between devices, shards(): lax.all_to_all(outgoing, 'head', split_axis=0, concat_axis=0, tiled=True)  6.55 us
    pallas_call x1, Pallas kernels, ssm_scan(): pl.pallas_call(ssm_scan_kernel, grid=(requests,), in_specs=[big, per_step...  6.48 us
    pallas_call x1, Pallas kernels, column_matmul(): pl.pallas_call(column_matmul_kernel, grid=(cols // block,), in_specs=[pl....  5.63 us
    all_to_all x1, waiting for transfers between devices, shards(): lax.all_to_all(mixer_part.reshape(head_count, tok_local, width), 'head',...  5.41 us
    all_to_all x2, waiting for transfers between devices, broadcast_gather(): return lax.all_to_all(copies, 'head', 0, 0, tiled=True)  4.76 us
  transfers between devices with their start and end apart: 5, of which 4 were waited for; matrix products, arithmetic and copies ran while one was open for 14% of the time, Pallas kernels for 0%

profile of v11, /device:TPU:0, one launch (start us, length us, event | category | flops | bytes accessed | tf_op | source)
XLA Modules:
  0.0 98.2 jit_solution(15163861869805959379)
XLA Ops:
  0.7 1.5 %broadcast_in_dim.24 = bf16[8,4,2048]{2,1,0:T(4,128)(2,1)} broadcast(bf16[4,2048]{1,0:T(4,128)(2,1)} %bitcast.101), dimensions={1,2} | broadcast | bytes 147456 | tf_op jit(solution)/shard_map/broadcast_in_dim | solution.py:127
  2.2 7.3 %all-to-all-start = ((bf16[8,4,2048]{2,1,0:T(4,128)(2,1)}), bf16[8,4,2048]{2,1,0:T(4,128)(2,1)S(1)}, u32[]{:S(2)}, u32[]{:S(2)}) async-start(bf16[8,4,2048]{2,1,0:T(4,128)(2,1)} %broadcast_in_dim.24), calls=%async_computation | async-start | bytes 262144 | tf_op jit(solution)/shard_map/all_to_all | solution.py:128
  9.4 0.8 fusion.35
  10.3 0.8 copy.79
  11.0 0.1 reshape_squeeze.7
  11.1 0.1 fusion.27
  11.2 0.2 select_reduce_fusion
  11.4 0.7 exponential_negate_fusion
  12.1 0.7 copy.103
  12.8 0.8 copy.102
  13.5 2.3 %copy.74.s_ref = bf16[4,8,128,128]{3,2,1,0:T(8,128)(2,1)} copy(bf16[4,8,128,128]{2,3,1,0:T(8,128)(2,1)} %bitcast.99) | data formatting | bytes 2097152 | tf_op jit(solution)/shard_map/reshape | solution.py:211
  15.8 0.8 mul.263
  16.6 0.9 fusion.34
  17.5 0.2 multiply_reduce_fusion.1
  17.6 0.1 rsqrt.32
  17.7 0.1 rsqrt.33
  17.8 1.4 %multiply_convert_fusion.1.a_ref = bf16[32,2048]{1,0:T(8,128)(2,1)} fusion(f32[32,2048]{1,0:T(8,128)S(1)} %reshape.243, f32[2048]{0:T(1024)} %param.29, f32[32]{0:T(128)S(1)} %rsqrt.33), kind=kLoop, calls=%fused_computation.17 | loop fusion | flops 196608 | bytes 401536 | tf_op jit(solution)/shard_map/convert_element_type | solution.py:165
  19.3 5.6 %shard_map.237 = f32[32,2048]{1,0:T(8,128)} custom-call(bf16[32,2048]{1,0:T(8,128)(2,1)} %multiply_convert_fusion.1.a_ref, bf16[2048,2048]{1,0:T(8,128)(2,1)} %w_ref.1), custom_call_target="tpu_custom_call" | custom-call | flops 268435456 | bytes 8781824 | tf_op jit(solution)/shard_map/pallas_call | solution.py:57
  24.9 1.0 slice.108
  25.9 1.1 %slice.119 = f32[4,8,16,64]{3,1,2,0:T(8,128)S(1)} slice(f32[4,8,16,128]{3,1,2,0:T(8,128)} %bitcast.98), slice={[0:4], [0:8], [0:16], [64:128]} | slice | bytes 262144 | tf_op jit(solution)/shard_map/slice | solution.py:182
  27.0 0.3 convolution_convert_fusion.1
  27.4 0.7 broadcast_in_dim.26
  28.0 6.0 %all-to-all-start.1 = ((bf16[8,4,8,256]{3,2,1,0:T(8,128)(2,1)}), bf16[8,4,8,256]{3,2,1,0:T(8,128)(2,1)S(1)}, u32[]{:S(2)}, u32[]{:S(2)}) async-start(bf16[8,4,8,256]{3,2,1,0:T(8,128)(2,1)} %broadcast_in_dim.26), calls=%async_computation.1 | async-start | bytes 262144 | tf_op jit(solution)/shard_map/all_to_all | solution.py:128
  34.1 0.3 multiply_exponential_fusion
  34.3 0.1 mul.222
  34.5 0.1 mul.223
  34.6 0.1 convert_element_type.96
  34.8 0.1 broadcast_in_dim.25
  34.9 0.8 reshape.198.dec_ref
  35.8 0.8 fusion.32
  36.5 0.1 reshape.201
  36.6 4.8 %all-to-all-done.1 = bf16[8,4,8,256]{3,2,1,0:T(8,128)(2,1)S(1)} async-done(((bf16[8,4,8,256]{3,2,1,0:T(8,128)(2,1)}), bf16[8,4,8,256]{3,2,1,0:T(8,128)(2,1)S(1)}, u32[]{:S(2)}, u32[]{:S(2)}) %all-to-all-start.1) | async-done | bytes 131104 | tf_op jit(solution)/shard_map/all_to_all | solution.py:128
  41.4 0.2 copy.71
  41.7 0.6 select_bitcast_fusion.c_ref
  42.3 0.6 select_bitcast_fusion.1.b_ref
  42.9 6.5 %shard_map.238 = (bf16[4,8,128,128]{3,2,1,0:T(8,128)(2,1)}, f32[4,8,1024]{2,1,0:T(8,128)}) custom-call(bf16[4,8,128,128]{3,2,1,0:T(8,128)(2,1)} %copy.74.s_ref, f32[4,8,1024]{2,1,0:T(8,128)} %reshape.198.dec_ref, f32[4,8,1024]{2,1,0:T(8,128)} %get-tuple-element.40.dx_ref, f32[4,1,8,128]{3,2,1,0:T(8,128)} %select_bitcast_fusion.1.b_ref, ...), custom_call_target="tpu_custom_call" | custom-call | tf_op jit(solution)/shard_map/pallas_call | solution.py:110
  49.4 1.1 %reshape.200 = f32[4,8,16,64]{3,2,1,0:T(8,128)S(1)} reshape(f32[4,8,1024]{2,1,0:T(8,128)} %get-tuple-element.7) | data formatting | bytes 262144 | tf_op jit(solution)/shard_map/reshape | solution.py:219
  50.5 0.2 multiply_reduce_fusion
  50.8 0.1 multiply_convert_fusion
  50.9 0.1 dot_general.31
  51.0 3.7 %fusion = f32[8,4,2048]{2,1,0:T(4,128)} fusion(bf16[8,4,1024]{2,1,0:T(4,128)(2,1)S(1)} %dot_general.31, bf16[1024,2048]{1,0:T(8,128)(2,1)} %param.41), kind=kOutput, calls=%fused_computation | convolution fusion | flops 134217728 | bytes 4521984 | tf_op jit(solution)/shard_map/dot_general | solution.py:228
  54.7 3.4 %all-to-all-start.2 = ((f32[8,4,2048]{2,1,0:T(4,128)}), f32[8,4,2048]{2,1,0:T(4,128)S(1)}, u32[]{:S(2)}, u32[]{:S(2)}) async-start(f32[8,4,2048]{2,1,0:T(4,128)} %fusion), calls=%async_computation.2 | async-start | bytes 524288 | tf_op jit(solution)/shard_map/all_to_all | solution.py:229
  58.2 0.1 iota_compare_fusion.3
  58.2 0.1 copy.78
  58.3 0.6 copy.83
  59.0 0.6 copy.82
  59.6 1.3 %copy.81 = bf16[4,8,128,128]{2,3,1,0:T(8,128)(2,1)} copy(bf16[4,8,128,128]{3,2,1,0:T(8,128)(2,1)S(1)} %copy-done.1) | data formatting | bytes 2097152 | tf_op jit(solution)/shard_map/pallas_call | solution.py:110
  60.9 5.4 %all-to-all-done.2 = f32[8,4,2048]{2,1,0:T(4,128)S(1)} async-done(((f32[8,4,2048]{2,1,0:T(4,128)}), f32[8,4,2048]{2,1,0:T(4,128)S(1)}, u32[]{:S(2)}, u32[]{:S(2)}) %all-to-all-start.2) | async-done | bytes 262176 | tf_op jit(solution)/shard_map/all_to_all | solution.py:229
  66.4 0.1 fusion.13
  66.5 0.1 fusion.15
  66.6 0.1 fusion.36
  66.8 0.1 convolution_convert_fusion
  66.9 0.7 reshape_broadcast_in_dim_reshape.3
  67.6 3.3 %all-to-all-start.3 = ((bf16[8,2,2048]{2,1,0:T(2,128)(2,1)}), bf16[8,2,2048]{2,1,0:T(2,128)(2,1)S(1)}, u32[]{:S(2)}, u32[]{:S(2)}) async-start(bf16[8,2,2048]{2,1,0:T(2,128)(2,1)} %reshape_broadcast_in_dim_reshape.3), calls=%async_computation.3 | async-start | bytes 131072 | tf_op jit(solution)/shard_map/all_to_all | solution.py:244
  71.0 0.2 fusion.24
  71.2 0.1 copy.87
  71.3 6.5 %all-to-all-done.3 = bf16[8,2,2048]{2,1,0:T(2,128)(2,1)S(1)} async-done(((bf16[8,2,2048]{2,1,0:T(2,128)(2,1)}), bf16[8,2,2048]{2,1,0:T(2,128)(2,1)S(1)}, u32[]{:S(2)}, u32[]{:S(2)}) %all-to-all-start.3) | async-done | bytes 65568 | tf_op jit(solution)/shard_map/all_to_all | solution.py:244
  77.9 8.0 %fusion.6 = f32[16,2048]{1,0:T(8,128)S(1)} fusion(bf16[2048,2048]{1,0:T(8,128)(2,1)} %param.45, bf16[16,2048]{1,0:T(8,128)(2,1)S(1)} %reshape.203, bf16[2048,2048]{1,0:T(8,128)(2,1)} %param.44), kind=kOutput, calls=%fused_computation.11 | convolution fusion | flops 268533760 | bytes 16973824 | tf_op jit(solution)/shard_map/dot_general | solution.py:247
  85.9 0.7 reshape.204
  86.6 3.4 %all-to-all-start.4 = ((f32[8,2,2048]{2,1,0:T(2,128)}), f32[8,2,2048]{2,1,0:T(2,128)S(1)}, u32[]{:S(2)}, u32[]{:S(2)}) async-start(f32[8,2,2048]{2,1,0:T(2,128)} %reshape.204), calls=%async_computation.4 | async-start | bytes 262144 | tf_op jit(solution)/shard_map/all_to_all | solution.py:250
  90.0 7.2 %all-to-all-done.4 = f32[8,2,2048]{2,1,0:T(2,128)S(1)} async-done(((f32[8,2,2048]{2,1,0:T(2,128)}), f32[8,2,2048]{2,1,0:T(2,128)S(1)}, u32[]{:S(2)}, u32[]{:S(2)}) %all-to-all-start.4) | async-done | bytes 131104 | tf_op jit(solution)/shard_map/all_to_all | solution.py:250
  97.3 0.1 reshape.274
  97.4 0.2 fusion.4
  97.6 0.6 fusion.20
  (49 shorter events, 0.6 us)
Async XLA Ops:
  0.6 26.3 %copy-start = (bf16[2048,256]{1,0:T(8,128)(2,1)S(1)}, bf16[2048,256]{1,0:T(8,128)(2,1)}, u32[]{:S(2)}) copy-start(bf16[2048,256]{1,0:T(8,128)(2,1)} %param.31) | copy-start | bytes 3145732
  0.6 26.3 %copy-start.3 = (f32[2048]{0:T(1024)S(1)}, f32[2048]{0:T(1024)}, u32[]{:S(2)}) copy-start(f32[2048]{0:T(1024)} %param.29) | copy-start | bytes 24580
  0.7 26.7 %copy-start.8 = (f32[256]{0:T(256)S(1)}, f32[256]{0:T(256)}, u32[]{:S(2)}) copy-start(f32[256]{0:T(256)} %param.39) | copy-start | bytes 3076
  0.7 33.4 %copy-start.4 = (bf16[2048,16]{0,1:T(8,128)(2,1)S(1)}, bf16[2048,16]{0,1:T(8,128)(2,1)}, u32[]{:S(2)}) copy-start(bf16[2048,16]{0,1:T(8,128)(2,1)} %param.32) | copy-start | bytes 196612
  0.7 33.4 %copy-start.9 = (f32[16]{0:T(128)S(1)}, f32[16]{0:T(128)}, u32[]{:S(2)}) copy-start(f32[16]{0:T(128)} %param.33) | copy-start | bytes 196
  2.2 15.3 %all-to-all-start = ((bf16[8,4,2048]{2,1,0:T(4,128)(2,1)}), bf16[8,4,2048]{2,1,0:T(4,128)(2,1)S(1)}, u32[]{:S(2)}, u32[]{:S(2)}) async-start(bf16[8,4,2048]{2,1,0:T(4,128)(2,1)} %broadcast_in_dim.24), calls=%async_computation | async-start | bytes 262144 | tf_op jit(solution)/shard_map/all_to_all | solution.py:128
  13.5 22.2 %copy-start.6 = (f32[1024]{0:T(1024)S(1)}, f32[1024]{0:T(1024)}, u32[]{:S(2)}) copy-start(f32[1024]{0:T(1024)} %param.37) | copy-start | bytes 12292
  19.3 31.2 %copy-start.10 = (f32[16]{0:T(128)S(1)}, f32[16]{0:T(128)}, u32[]{:S(2)}) copy-start(f32[16]{0:T(128)} %param.35) | copy-start | bytes 196
  27.3 30.9 %copy-start.7 = (s32[1,4,2]{1,2,0:T(2,128)S(1)}, s32[1,4,2]{1,2,0:T(2,128)}, u32[]{:S(2)}) copy-start(s32[1,4,2]{1,2,0:T(2,128)} %param.28) | copy-start | bytes 100
  28.0 13.3 %all-to-all-start.1 = ((bf16[8,4,8,256]{3,2,1,0:T(8,128)(2,1)}), bf16[8,4,8,256]{3,2,1,0:T(8,128)(2,1)S(1)}, u32[]{:S(2)}, u32[]{:S(2)}) async-start(bf16[8,4,8,256]{3,2,1,0:T(8,128)(2,1)} %broadcast_in_dim.26), calls=%async_computation.1 | async-start | bytes 262144 | tf_op jit(solution)/shard_map/all_to_all | solution.py:128
  34.9 31.5 %copy-start.2 = (bf16[1,4,2048]{2,1,0:T(4,128)(2,1)S(1)}, bf16[1,4,2048]{2,1,0:T(4,128)(2,1)}, u32[]{:S(2)}) copy-start(bf16[1,4,2048]{2,1,0:T(4,128)(2,1)} %param.24) | copy-start | bytes 49156
  34.9 31.6 %copy-start.5 = (f32[2048]{0:T(1024)S(1)}, f32[2048]{0:T(1024)}, u32[]{:S(2)}) copy-start(f32[2048]{0:T(1024)} %param.42) | copy-start | bytes 24580
  34.9 31.7 %copy-start.11 = (bf16[2048,8]{0,1:T(8,128)(2,1)S(1)}, bf16[2048,8]{0,1:T(8,128)(2,1)}, u32[]{:S(2)}) copy-start(bf16[2048,8]{0,1:T(8,128)(2,1)} %param.43) | copy-start | bytes 98308
  49.4 10.2 %copy-start.1 = (bf16[4,8,128,128]{3,2,1,0:T(8,128)(2,1)S(1)}, bf16[4,8,128,128]{3,2,1,0:T(8,128)(2,1)}, u32[]{:S(2)}) copy-start(bf16[4,8,128,128]{3,2,1,0:T(8,128)(2,1)} %get-tuple-element.8) | copy-start | bytes 3145732
  54.7 11.6 %all-to-all-start.2 = ((f32[8,4,2048]{2,1,0:T(4,128)}), f32[8,4,2048]{2,1,0:T(4,128)S(1)}, u32[]{:S(2)}, u32[]{:S(2)}) async-start(f32[8,4,2048]{2,1,0:T(4,128)} %fusion), calls=%async_computation.2 | async-start | bytes 524288 | tf_op jit(solution)/shard_map/all_to_all | solution.py:229
  67.6 10.2 %all-to-all-start.3 = ((bf16[8,2,2048]{2,1,0:T(2,128)(2,1)}), bf16[8,2,2048]{2,1,0:T(2,128)(2,1)S(1)}, u32[]{:S(2)}, u32[]{:S(2)}) async-start(bf16[8,2,2048]{2,1,0:T(2,128)(2,1)} %reshape_broadcast_in_dim_reshape.3), calls=%async_computation.3 | async-start | bytes 131072 | tf_op jit(solution)/shard_map/all_to_all | solution.py:244
  86.6 10.7 %all-to-all-start.4 = ((f32[8,2,2048]{2,1,0:T(2,128)}), f32[8,2,2048]{2,1,0:T(2,128)S(1)}, u32[]{:S(2)}, u32[]{:S(2)}) async-start(f32[8,2,2048]{2,1,0:T(2,128)} %reshape.204), calls=%async_computation.4 | async-start | bytes 262144 | tf_op jit(solution)/shard_map/all_to_all | solution.py:250

commit v12 on v9

--- a/solution.py
+++ b/solution.py
@@ -79,8 +79,8 @@
     shared = b_ref.shape[1] == 1
 
     def fill(jb):
-        b_cols = b_ref[0, jb].T
-        c_cols = c_ref[0, jb].T
+        b_cols = b_ref[0, jb].astype(jnp.float32).T
+        c_cols = c_ref[0, jb].astype(jnp.float32).T
         for t in range(steps):
             bb_ref[t] = jnp.broadcast_to(b_cols[:, t : t + 1], (state_dim, lanes))
             cb_ref[t] = jnp.broadcast_to(c_cols[:, t : t + 1], (state_dim, lanes))
@@ -121,6 +121,51 @@
             pltpu.VMEM((steps, state_dim, lanes), jnp.float32),
         ],
     )(state_tiles, decay_rows, dx_rows, b_rows, c_rows)
+
+
+def ssm_scan_direct_kernel(group_ref, *refs):
+    ssm_scan_kernel(*refs)
+
+
+def ssm_scan_direct(state_tiles, decay_rows, dx_rows, bc_blocks, group, group_count):
+    requests, tiles, state_dim, lanes = state_tiles.shape
+    steps = decay_rows.shape[1]
+    cols_local = bc_blocks.shape[3]
+    c_start = group_count * state_dim
+
+    def b_map(r, g):
+        first = g[0] * state_dim
+        return (first // cols_local, r, 0, (first % cols_local) // state_dim)
+
+    def c_map(r, g):
+        first = c_start + g[0] * state_dim
+        return (first // cols_local, r, 0, (first % cols_local) // state_dim)
+
+    big = pl.BlockSpec((1, tiles, state_dim, lanes), lambda r, g: (r, 0, 0, 0))
+    per_step = pl.BlockSpec((1, steps, tiles * lanes), lambda r, g: (r, 0, 0))
+    return pl.pallas_call(
+        ssm_scan_direct_kernel,
+        grid_spec=pltpu.PrefetchScalarGridSpec(
+            num_scalar_prefetch=1,
+            grid=(requests,),
+            in_specs=[
+                big,
+                per_step,
+                per_step,
+                pl.BlockSpec((1, 1, steps, state_dim), b_map),
+                pl.BlockSpec((1, 1, steps, state_dim), c_map),
+            ],
+            out_specs=[big, per_step],
+            scratch_shapes=[
+                pltpu.VMEM((steps, state_dim, lanes), jnp.float32),
+                pltpu.VMEM((steps, state_dim, lanes), jnp.float32),
+            ],
+        ),
+        out_shape=[
+            jax.ShapeDtypeStruct(state_tiles.shape, jnp.bfloat16),
+            jax.ShapeDtypeStruct(decay_rows.shape, jnp.float32),
+        ],
+    )(group, state_tiles, decay_rows, dx_rows, bc_blocks, bc_blocks)
 
 
 def broadcast_gather(block, count):
@@ -170,9 +215,7 @@
     )
     bc_conv, conv_bc_new = causal_conv(conv_bc_state[0], bc_fresh, conv_bc_kernel, conv_bc_bias)
     bc_conv = bc_conv.astype(jnp.bfloat16)
-    bc_all = jnp.moveaxis(broadcast_gather(bc_conv, head_count), 0, 2).reshape(
-        requests, STEPS, -1
-    )
+    bc_blocks = broadcast_gather(bc_conv, head_count)
     proj_xz = column_matmul(normed, weight_xz).reshape(
         requests, STEPS, heads_local, 2 * head_dim
     )
@@ -201,16 +244,22 @@
     tile_group = (my_index * heads_local + jnp.arange(1 if shared_group else tiles) * pack) // (
         HEADS // G
     )
-    bc_values = bc_all.astype(jnp.float32).reshape(requests, STEPS, 2, G, state_dim)
-    b_rows = jnp.take(bc_values[:, :, 0], tile_group, axis=2).transpose(0, 2, 1, 3)
-    c_rows = jnp.take(bc_values[:, :, 1], tile_group, axis=2).transpose(0, 2, 1, 3)
     state_tiles = (
         ssm_state[0]
         .reshape(requests, tiles, pack, head_dim, state_dim)
         .transpose(0, 1, 4, 2, 3)
         .reshape(requests, tiles, state_dim, lanes)
     )
-    state_out, read_rows = ssm_scan(state_tiles, decay_rows, dx_rows, b_rows, c_rows)
+    if shared_group and bc_blocks.shape[3] % state_dim == 0:
+        state_out, read_rows = ssm_scan_direct(
+            state_tiles, decay_rows, dx_rows, bc_blocks, tile_group.astype(jnp.int32), G
+        )
+    else:
+        bc_all = jnp.moveaxis(bc_blocks, 0, 2).reshape(requests, STEPS, -1)
+        bc_values = bc_all.astype(jnp.float32).reshape(requests, STEPS, 2, G, state_dim)
+        b_rows = jnp.take(bc_values[:, :, 0], tile_group, axis=2).transpose(0, 2, 1, 3)
+        c_rows = jnp.take(bc_values[:, :, 1], tile_group, axis=2).transpose(0, 2, 1, 3)
+        state_out, read_rows = ssm_scan(state_tiles, decay_rows, dx_rows, b_rows, c_rows)
     ssm_now = (
         state_out.reshape(requests, tiles, state_dim, pack, head_dim)
         .transpose(0, 1, 3, 4, 2)

time: 98.7 us -> 98.4 us (level)
  other arithmetic: 6.01 us -> 4.75 us
    transpose x2 -> x0, other arithmetic: 1.22 us -> none  [the longest x1 0.62 us: shards(): jnp.take(bc_values[:, :, 1], tile_group, axis=2).transpose(0, 2, 1, 3)]
    unnamed x30 -> x32, local copies, waits for them, and re-layouts: 3.53 us -> 4.17 us
  transfers between devices with their start and end apart: 5 -> 5, of which waited for: 4 -> 4; matrix products, arithmetic and copies ran while one was open for 14% -> 13% of each run, Pallas kernels for 0% -> 0%
where the time goes in v12:
time: 98.4 us; the launch traced here: 97.4 us
  waiting for transfers between devices  24.3 us (25%)
  starting transfers between devices  23.4 us (24%)
  local copies, waits for them, and re-layouts  19 us (19%)
  matrix products  12.9 us (13%)
  Pallas kernels  12 us (12%)
  other arithmetic  4.75 us (5%)
    all_to_all x2, starting transfers between devices, broadcast_gather(): return lax.all_to_all(copies, 'head', 0, 0, tiled=True)  13.2 us
    dot_general x1, matrix products, shards(): jnp.dot(hidden, weight_down, preferred_element_type=jnp.float32)  8.05 us
    all_to_all x1, waiting for transfers between devices, shards(): lax.all_to_all(computed.astype(jnp.bfloat16), 'head', split_axis=0, conca...  6.81 us
    all_to_all x1, waiting for transfers between devices, shards(): lax.all_to_all(outgoing, 'head', split_axis=0, concat_axis=0, tiled=True)  6.55 us
    pallas_call x1, Pallas kernels, ssm_scan_direct(): pl.pallas_call(ssm_scan_direct_kernel, grid_spec=pltpu.PrefetchScalarGrid...  6.44 us
    pallas_call x1, Pallas kernels, column_matmul(): pl.pallas_call(column_matmul_kernel, grid=(cols // block,), in_specs=[pl....  5.6 us
    all_to_all x2, waiting for transfers between devices, broadcast_gather(): return lax.all_to_all(copies, 'head', 0, 0, tiled=True)  5.51 us
    all_to_all x1, waiting for transfers between devices, shards(): lax.all_to_all(mixer_part.reshape(head_count, tok_local, width), 'head',...  5.41 us
  transfers between devices with their start and end apart: 5, of which 4 were waited for; matrix products, arithmetic and copies ran while one was open for 13% of the time, Pallas kernels for 0%

profile of v12, /device:TPU:0, one launch (start us, length us, event | category | flops | bytes accessed | tf_op | source)
XLA Modules:
  0.0 97.4 jit_solution(6548612406833073803)
XLA Ops:
  0.6 0.0 copy-start
  0.7 1.5 %broadcast_in_dim.15 = bf16[8,4,2048]{2,1,0:T(4,128)(2,1)} broadcast(bf16[4,2048]{1,0:T(4,128)(2,1)} %bitcast.85), dimensions={1,2} | broadcast | bytes 147456 | tf_op jit(solution)/shard_map/broadcast_in_dim | solution.py:172
  2.2 7.3 %all-to-all-start = ((bf16[8,4,2048]{2,1,0:T(4,128)(2,1)}), bf16[8,4,2048]{2,1,0:T(4,128)(2,1)S(1)}, u32[]{:S(2)}, u32[]{:S(2)}) async-start(bf16[8,4,2048]{2,1,0:T(4,128)(2,1)} %broadcast_in_dim.15), calls=%async_computation | async-start | bytes 262144 | tf_op jit(solution)/shard_map/all_to_all | solution.py:173
  9.4 0.8 fusion.33
  10.3 0.8 copy.70
  11.0 0.1 reshape_squeeze.7
  11.1 0.1 fusion.26
  11.2 0.2 select_reduce_fusion
  11.4 0.7 exponential_negate_fusion
  12.1 0.8 copy.89
  12.8 0.7 copy.90
  13.5 2.3 %copy.65.refs_0_ = bf16[4,8,128,128]{3,2,1,0:T(8,128)(2,1)} copy(bf16[4,8,128,128]{2,3,1,0:T(8,128)(2,1)} %bitcast.83) | data formatting | bytes 2097152 | tf_op jit(solution)/shard_map/reshape | solution.py:251
  15.8 0.8 mul.263
  16.6 0.9 fusion.32
  17.5 0.2 multiply_reduce_fusion.1
  17.6 0.1 rsqrt.32
  17.7 0.1 rsqrt.33
  17.8 1.4 %multiply_convert_fusion.1.a_ref = bf16[32,2048]{1,0:T(8,128)(2,1)} fusion(f32[32,2048]{1,0:T(8,128)S(1)} %reshape.190, f32[2048]{0:T(1024)} %param.27, f32[32]{0:T(128)S(1)} %rsqrt.33), kind=kLoop, calls=%fused_computation.16 | loop fusion | flops 196608 | bytes 401536 | tf_op jit(solution)/shard_map/convert_element_type | solution.py:210
  19.2 5.6 %shard_map.237 = f32[32,2048]{1,0:T(8,128)} custom-call(bf16[32,2048]{1,0:T(8,128)(2,1)} %multiply_convert_fusion.1.a_ref, bf16[2048,2048]{1,0:T(8,128)(2,1)} %w_ref.1), custom_call_target="tpu_custom_call" | custom-call | flops 268435456 | bytes 8781824 | tf_op jit(solution)/shard_map/pallas_call | solution.py:57
  24.9 1.0 %slice.89 = bf16[4,8,16,64]{3,1,2,0:T(8,128)(2,1)S(1)} slice(f32[4,8,16,128]{3,1,2,0:T(8,128)} %bitcast.81), slice={[0:4], [0:8], [0:16], [0:64]} | slice | bytes 131072 | tf_op jit(solution)/shard_map/slice | solution.py:223
  25.8 1.1 %slice.98 = f32[4,8,16,64]{3,1,2,0:T(8,128)S(1)} slice(f32[4,8,16,128]{3,1,2,0:T(8,128)} %bitcast.82), slice={[0:4], [0:8], [0:16], [64:128]} | slice | bytes 262144 | tf_op jit(solution)/shard_map/slice | solution.py:225
  27.0 0.3 multiply_exponential_fusion
  27.2 0.1 mul.223
  27.4 0.1 mul.224
  27.5 0.1 convert_element_type.93
  27.7 0.0 copy-start.6
  27.7 0.0 copy-start.12
  27.7 0.3 convolution_convert_fusion.2
  28.1 0.7 broadcast_in_dim.17
  28.8 6.0 %all-to-all-start.1 = ((bf16[8,4,8,256]{3,2,1,0:T(8,128)(2,1)}), bf16[8,4,8,256]{3,2,1,0:T(8,128)(2,1)S(1)}, u32[]{:S(2)}, u32[]{:S(2)}) async-start(bf16[8,4,8,256]{3,2,1,0:T(8,128)(2,1)} %broadcast_in_dim.17), calls=%async_computation.1 | async-start | bytes 262144 | tf_op jit(solution)/shard_map/all_to_all | solution.py:173
  34.8 0.1 broadcast_in_dim.16
  34.9 0.8 reshape.181.refs_1_
  35.7 0.8 fusion.31
  36.5 0.1 reshape.184
  36.6 5.5 %all-to-all-done.1.refs_3_.refs_4_ = bf16[8,4,8,256]{3,2,1,0:T(8,128)(2,1)S(1)} async-done(((bf16[8,4,8,256]{3,2,1,0:T(8,128)(2,1)}), bf16[8,4,8,256]{3,2,1,0:T(8,128)(2,1)S(1)}, u32[]{:S(2)}, u32[]{:S(2)}) %all-to-all-start.1) | async-done | bytes 131104 | tf_op jit(solution)/shard_map/all_to_all | solution.py:173
  42.1 0.6 copy-done.1
  42.8 6.4 %shard_map.238 = (bf16[4,8,128,128]{3,2,1,0:T(8,128)(2,1)}, f32[4,8,1024]{2,1,0:T(8,128)}) custom-call(s32[1]{0:T(128)S(6)} %select_n.9.group_ref, bf16[4,8,128,128]{3,2,1,0:T(8,128)(2,1)} %copy.65.refs_0_, f32[4,8,1024]{2,1,0:T(8,128)} %reshape.181.refs_1_, f32[4,8,1024]{2,1,0:T(8,128)} %get-tuple-element.28.refs_2_, bf16[8,4,8,256]{3,2,1,0:T(8,128)(2,1)} %copy-done.1, ...), custom_call_target="tpu_custom_call" | custom-call | tf_op jit(solution)/shard_map/pallas_call | solution.py:146
  49.2 1.1 %reshape.183 = f32[4,8,16,64]{3,2,1,0:T(8,128)S(1)} reshape(f32[4,8,1024]{2,1,0:T(8,128)} %get-tuple-element.6) | data formatting | bytes 262144 | tf_op jit(solution)/shard_map/reshape | solution.py:268
  50.3 0.2 multiply_reduce_fusion
  50.6 0.1 multiply_convert_fusion
  50.7 0.1 dot_general.31
  50.8 3.7 %fusion = f32[8,4,2048]{2,1,0:T(4,128)} fusion(bf16[8,4,1024]{2,1,0:T(4,128)(2,1)S(1)} %dot_general.31, bf16[1024,2048]{1,0:T(8,128)(2,1)} %param.39), kind=kOutput, calls=%fused_computation | convolution fusion | flops 134217728 | bytes 4521984 | tf_op jit(solution)/shard_map/dot_general | solution.py:277
  54.5 3.4 %all-to-all-start.2 = ((f32[8,4,2048]{2,1,0:T(4,128)}), f32[8,4,2048]{2,1,0:T(4,128)S(1)}, u32[]{:S(2)}, u32[]{:S(2)}) async-start(f32[8,4,2048]{2,1,0:T(4,128)} %fusion), calls=%async_computation.2 | async-start | bytes 524288 | tf_op jit(solution)/shard_map/all_to_all | solution.py:278
  58.0 0.1 iota_compare_fusion.3
  58.0 0.1 copy.69
  58.2 0.6 copy.74
  58.8 0.6 copy.73
  59.4 1.3 %copy.72 = bf16[4,8,128,128]{2,3,1,0:T(8,128)(2,1)} copy(bf16[4,8,128,128]{3,2,1,0:T(8,128)(2,1)S(1)} %copy-done.2) | data formatting | bytes 2097152 | tf_op jit(solution)/shard_map/pallas_call | solution.py:146
  60.7 5.4 %all-to-all-done.2 = f32[8,4,2048]{2,1,0:T(4,128)S(1)} async-done(((f32[8,4,2048]{2,1,0:T(4,128)}), f32[8,4,2048]{2,1,0:T(4,128)S(1)}, u32[]{:S(2)}, u32[]{:S(2)}) %all-to-all-start.2) | async-done | bytes 262176 | tf_op jit(solution)/shard_map/all_to_all | solution.py:278
  66.2 0.1 fusion.12
  66.3 0.1 fusion.14
  66.4 0.1 fusion.34
  66.6 0.1 convolution_convert_fusion
  66.7 0.7 reshape_broadcast_in_dim_reshape.3
  67.4 3.3 %all-to-all-start.3 = ((bf16[8,2,2048]{2,1,0:T(2,128)(2,1)}), bf16[8,2,2048]{2,1,0:T(2,128)(2,1)S(1)}, u32[]{:S(2)}, u32[]{:S(2)}) async-start(bf16[8,2,2048]{2,1,0:T(2,128)(2,1)} %reshape_broadcast_in_dim_reshape.3), calls=%async_computation.3 | async-start | bytes 131072 | tf_op jit(solution)/shard_map/all_to_all | solution.py:293
  70.8 0.2 fusion.23
  71.0 0.1 copy.78
  71.1 6.5 %all-to-all-done.3 = bf16[8,2,2048]{2,1,0:T(2,128)(2,1)S(1)} async-done(((bf16[8,2,2048]{2,1,0:T(2,128)(2,1)}), bf16[8,2,2048]{2,1,0:T(2,128)(2,1)S(1)}, u32[]{:S(2)}, u32[]{:S(2)}) %all-to-all-start.3) | async-done | bytes 65568 | tf_op jit(solution)/shard_map/all_to_all | solution.py:293
  77.7 8.0 %convolution_convert_fusion.1 = bf16[16,2048]{1,0:T(8,128)(2,1)S(1)} fusion(bf16[2048,2048]{1,0:T(8,128)(2,1)} %param.43, bf16[16,2048]{1,0:T(8,128)(2,1)S(1)} %reshape.186, bf16[2048,2048]{1,0:T(8,128)(2,1)} %param.42), kind=kOutput, calls=%fused_computation.6 | convolution fusion | flops 268566528 | bytes 16908288 | tf_op jit(solution)/shard_map/dot_general | solution.py:296
  85.7 0.7 convert_element_type.109
  86.4 3.3 %all-to-all-start.4 = ((bf16[8,2,2048]{2,1,0:T(2,128)(2,1)}), bf16[8,2,2048]{2,1,0:T(2,128)(2,1)S(1)}, u32[]{:S(2)}, u32[]{:S(2)}) async-start(bf16[8,2,2048]{2,1,0:T(2,128)(2,1)} %convert_element_type.109), calls=%async_computation.4 | async-start | bytes 131072 | tf_op jit(solution)/shard_map/all_to_all | solution.py:299
  89.8 6.8 %all-to-all-done.4 = bf16[8,2,2048]{2,1,0:T(2,128)(2,1)S(1)} async-done(((bf16[8,2,2048]{2,1,0:T(2,128)(2,1)}), bf16[8,2,2048]{2,1,0:T(2,128)(2,1)S(1)}, u32[]{:S(2)}, u32[]{:S(2)}) %all-to-all-start.4) | async-done | bytes 65568 | tf_op jit(solution)/shard_map/all_to_all | solution.py:299
  96.6 0.1 fusion.4
  96.8 0.6 fusion.19
  (44 shorter events, 0.5 us)
Async XLA Ops:
  0.6 27.0 %copy-start = (bf16[2048,256]{1,0:T(8,128)(2,1)S(1)}, bf16[2048,256]{1,0:T(8,128)(2,1)}, u32[]{:S(2)}) copy-start(bf16[2048,256]{1,0:T(8,128)(2,1)} %param.29) | copy-start | bytes 3145732
  0.6 26.3 %copy-start.4 = (f32[2048]{0:T(1024)S(1)}, f32[2048]{0:T(1024)}, u32[]{:S(2)}) copy-start(f32[2048]{0:T(1024)} %param.27) | copy-start | bytes 24580
  0.7 26.3 %copy-start.5 = (bf16[2048,16]{0,1:T(8,128)(2,1)S(1)}, bf16[2048,16]{0,1:T(8,128)(2,1)}, u32[]{:S(2)}) copy-start(bf16[2048,16]{0,1:T(8,128)(2,1)} %param.30) | copy-start | bytes 196612
  0.7 26.3 %copy-start.10 = (f32[16]{0:T(128)S(1)}, f32[16]{0:T(128)}, u32[]{:S(2)}) copy-start(f32[16]{0:T(128)} %param.31) | copy-start | bytes 196
  0.7 27.4 %copy-start.9 = (f32[256]{0:T(256)S(1)}, f32[256]{0:T(256)}, u32[]{:S(2)}) copy-start(f32[256]{0:T(256)} %param.37) | copy-start | bytes 3076
  2.2 15.3 %all-to-all-start = ((bf16[8,4,2048]{2,1,0:T(4,128)(2,1)}), bf16[8,4,2048]{2,1,0:T(4,128)(2,1)S(1)}, u32[]{:S(2)}, u32[]{:S(2)}) async-start(bf16[8,4,2048]{2,1,0:T(4,128)(2,1)} %broadcast_in_dim.15), calls=%async_computation | async-start | bytes 262144 | tf_op jit(solution)/shard_map/all_to_all | solution.py:173
  13.5 22.2 %copy-start.7 = (f32[1024]{0:T(1024)S(1)}, f32[1024]{0:T(1024)}, u32[]{:S(2)}) copy-start(f32[1024]{0:T(1024)} %param.35) | copy-start | bytes 12292
  19.2 31.1 %copy-start.11 = (f32[16]{0:T(128)S(1)}, f32[16]{0:T(128)}, u32[]{:S(2)}) copy-start(f32[16]{0:T(128)} %param.33) | copy-start | bytes 196
  24.9 33.2 %copy-start.8 = (s32[1,4,2]{1,2,0:T(2,128)S(1)}, s32[1,4,2]{1,2,0:T(2,128)}, u32[]{:S(2)}) copy-start(s32[1,4,2]{1,2,0:T(2,128)} %param.26) | copy-start | bytes 100
  27.7 38.5 %copy-start.3 = (bf16[1,4,2048]{2,1,0:T(4,128)(2,1)S(1)}, bf16[1,4,2048]{2,1,0:T(4,128)(2,1)}, u32[]{:S(2)}) copy-start(bf16[1,4,2048]{2,1,0:T(4,128)(2,1)} %param.22) | copy-start | bytes 49156
  27.7 38.6 %copy-start.6 = (f32[2048]{0:T(1024)S(1)}, f32[2048]{0:T(1024)}, u32[]{:S(2)}) copy-start(f32[2048]{0:T(1024)} %param.40) | copy-start | bytes 24580
  27.7 38.7 %copy-start.12 = (bf16[2048,8]{0,1:T(8,128)(2,1)S(1)}, bf16[2048,8]{0,1:T(8,128)(2,1)}, u32[]{:S(2)}) copy-start(bf16[2048,8]{0,1:T(8,128)(2,1)} %param.41) | copy-start | bytes 98308
  28.8 13.3 %all-to-all-start.1 = ((bf16[8,4,8,256]{3,2,1,0:T(8,128)(2,1)}), bf16[8,4,8,256]{3,2,1,0:T(8,128)(2,1)S(1)}, u32[]{:S(2)}, u32[]{:S(2)}) async-start(bf16[8,4,8,256]{3,2,1,0:T(8,128)(2,1)} %broadcast_in_dim.17), calls=%async_computation.1 | async-start | bytes 262144 | tf_op jit(solution)/shard_map/all_to_all | solution.py:173
  42.1 0.6 copy-start.1
  49.2 10.2 %copy-start.2 = (bf16[4,8,128,128]{3,2,1,0:T(8,128)(2,1)S(1)}, bf16[4,8,128,128]{3,2,1,0:T(8,128)(2,1)}, u32[]{:S(2)}) copy-start(bf16[4,8,128,128]{3,2,1,0:T(8,128)(2,1)} %get-tuple-element.7) | copy-start | bytes 3145732
  54.5 11.6 %all-to-all-start.2 = ((f32[8,4,2048]{2,1,0:T(4,128)}), f32[8,4,2048]{2,1,0:T(4,128)S(1)}, u32[]{:S(2)}, u32[]{:S(2)}) async-start(f32[8,4,2048]{2,1,0:T(4,128)} %fusion), calls=%async_computation.2 | async-start | bytes 524288 | tf_op jit(solution)/shard_map/all_to_all | solution.py:278
  67.4 10.2 %all-to-all-start.3 = ((bf16[8,2,2048]{2,1,0:T(2,128)(2,1)}), bf16[8,2,2048]{2,1,0:T(2,128)(2,1)S(1)}, u32[]{:S(2)}, u32[]{:S(2)}) async-start(bf16[8,2,2048]{2,1,0:T(2,128)(2,1)} %reshape_broadcast_in_dim_reshape.3), calls=%async_computation.3 | async-start | bytes 131072 | tf_op jit(solution)/shard_map/all_to_all | solution.py:293
  86.4 10.2 %all-to-all-start.4 = ((bf16[8,2,2048]{2,1,0:T(2,128)(2,1)}), bf16[8,2,2048]{2,1,0:T(2,128)(2,1)S(1)}, u32[]{:S(2)}, u32[]{:S(2)}) async-start(bf16[8,2,2048]{2,1,0:T(2,128)(2,1)} %convert_element_type.109), calls=%async_computation.4 | async-start | bytes 131072 | tf_op jit(solution)/shard_map/all_to_all | solution.py:299

commit v13 on v12

--- a/solution.py
+++ b/solution.py
@@ -53,7 +53,7 @@
 def column_matmul(rows, weight):
     m, k = rows.shape
     cols = weight.shape[1]
-    block = min(512, cols)
+    block = min(1024, cols)
     return pl.pallas_call(
         column_matmul_kernel,
         grid=(cols // block,),

time: 98.4 us -> 97.8 us (level)
  no operation moved by 1% of the time
where the time goes in v13:
time: 97.8 us; the launch traced here: 96.8 us
  waiting for transfers between devices  24.3 us (25%)
  starting transfers between devices  23.4 us (24%)
  local copies, waits for them, and re-layouts  19 us (19%)
  matrix products  12.9 us (13%)
  Pallas kernels  11.4 us (12%)
  other arithmetic  4.75 us (5%)
  between operations  0.98 us (1%)
    all_to_all x2, starting transfers between devices, broadcast_gather(): return lax.all_to_all(copies, 'head', 0, 0, tiled=True)  13.2 us
    dot_general x1, matrix products, shards(): jnp.dot(hidden, weight_down, preferred_element_type=jnp.float32)  8.05 us
    all_to_all x1, waiting for transfers between devices, shards(): lax.all_to_all(computed.astype(jnp.bfloat16), 'head', split_axis=0, conca...  6.81 us
    all_to_all x1, waiting for transfers between devices, shards(): lax.all_to_all(outgoing, 'head', split_axis=0, concat_axis=0, tiled=True)  6.55 us
    pallas_call x1, Pallas kernels, ssm_scan_direct(): pl.pallas_call(ssm_scan_direct_kernel, grid_spec=pltpu.PrefetchScalarGrid...  6.44 us
    all_to_all x2, waiting for transfers between devices, broadcast_gather(): return lax.all_to_all(copies, 'head', 0, 0, tiled=True)  5.51 us
    all_to_all x1, waiting for transfers between devices, shards(): lax.all_to_all(mixer_part.reshape(head_count, tok_local, width), 'head',...  5.41 us
    pallas_call x1, Pallas kernels, column_matmul(): pl.pallas_call(column_matmul_kernel, grid=(cols // block,), in_specs=[pl....  4.98 us
  transfers between devices with their start and end apart: 5, of which 4 were waited for; matrix products, arithmetic and copies ran while one was open for 13% of the time, Pallas kernels for 0%

profile of v13, /device:TPU:0, one launch (start us, length us, event | category | flops | bytes accessed | tf_op | source)
XLA Modules:
  0.0 96.8 jit_solution(17599872461319797435)
XLA Ops:
  0.6 0.0 copy-start
  0.6 0.0 copy-start.4
  0.7 1.5 %broadcast_in_dim.15 = bf16[8,4,2048]{2,1,0:T(4,128)(2,1)} broadcast(bf16[4,2048]{1,0:T(4,128)(2,1)} %bitcast.85), dimensions={1,2} | broadcast | bytes 147456 | tf_op jit(solution)/shard_map/broadcast_in_dim | solution.py:172
  2.2 7.3 %all-to-all-start = ((bf16[8,4,2048]{2,1,0:T(4,128)(2,1)}), bf16[8,4,2048]{2,1,0:T(4,128)(2,1)S(1)}, u32[]{:S(2)}, u32[]{:S(2)}) async-start(bf16[8,4,2048]{2,1,0:T(4,128)(2,1)} %broadcast_in_dim.15), calls=%async_computation | async-start | bytes 262144 | tf_op jit(solution)/shard_map/all_to_all | solution.py:173
  9.4 0.8 fusion.33
  10.3 0.8 copy.70
  11.0 0.1 reshape_squeeze.7
  11.1 0.1 fusion.26
  11.2 0.2 select_reduce_fusion
  11.4 0.7 exponential_negate_fusion
  12.1 0.8 copy.89
  12.8 0.7 copy.90
  13.5 2.3 %copy.65.refs_0_ = bf16[4,8,128,128]{3,2,1,0:T(8,128)(2,1)} copy(bf16[4,8,128,128]{2,3,1,0:T(8,128)(2,1)} %bitcast.83) | data formatting | bytes 2097152 | tf_op jit(solution)/shard_map/reshape | solution.py:251
  15.8 0.8 mul.263
  16.6 0.9 fusion.32
  17.5 0.2 multiply_reduce_fusion.1
  17.6 0.1 rsqrt.32
  17.7 0.1 rsqrt.33
  17.8 1.4 %multiply_convert_fusion.1.a_ref = bf16[32,2048]{1,0:T(8,128)(2,1)} fusion(f32[32,2048]{1,0:T(8,128)S(1)} %reshape.190, f32[2048]{0:T(1024)} %param.27, f32[32]{0:T(128)S(1)} %rsqrt.33), kind=kLoop, calls=%fused_computation.16 | loop fusion | flops 196608 | bytes 401536 | tf_op jit(solution)/shard_map/convert_element_type | solution.py:210
  19.2 5.0 %shard_map.237 = f32[32,2048]{1,0:T(8,128)} custom-call(bf16[32,2048]{1,0:T(8,128)(2,1)} %multiply_convert_fusion.1.a_ref, bf16[2048,2048]{1,0:T(8,128)(2,1)} %w_ref.1), custom_call_target="tpu_custom_call" | custom-call | flops 268435456 | bytes 8781824 | tf_op jit(solution)/shard_map/pallas_call | solution.py:57
  24.2 1.0 %slice.89 = bf16[4,8,16,64]{3,1,2,0:T(8,128)(2,1)S(1)} slice(f32[4,8,16,128]{3,1,2,0:T(8,128)} %bitcast.81), slice={[0:4], [0:8], [0:16], [0:64]} | slice | bytes 131072 | tf_op jit(solution)/shard_map/slice | solution.py:223
  25.2 1.1 %slice.98 = f32[4,8,16,64]{3,1,2,0:T(8,128)S(1)} slice(f32[4,8,16,128]{3,1,2,0:T(8,128)} %bitcast.82), slice={[0:4], [0:8], [0:16], [64:128]} | slice | bytes 262144 | tf_op jit(solution)/shard_map/slice | solution.py:225
  26.4 0.3 multiply_exponential_fusion
  26.6 0.1 mul.223
  26.7 0.1 mul.224
  26.9 0.1 convert_element_type.93
  27.1 0.0 copy-start.6
  27.1 0.3 convolution_convert_fusion.2
  27.5 0.7 broadcast_in_dim.17
  28.1 6.0 %all-to-all-start.1 = ((bf16[8,4,8,256]{3,2,1,0:T(8,128)(2,1)}), bf16[8,4,8,256]{3,2,1,0:T(8,128)(2,1)S(1)}, u32[]{:S(2)}, u32[]{:S(2)}) async-start(bf16[8,4,8,256]{3,2,1,0:T(8,128)(2,1)} %broadcast_in_dim.17), calls=%async_computation.1 | async-start | bytes 262144 | tf_op jit(solution)/shard_map/all_to_all | solution.py:173
  34.1 0.1 broadcast_in_dim.16
  34.3 0.8 reshape.181.refs_1_
  35.1 0.8 fusion.31
  35.9 0.1 reshape.184
  36.0 5.5 %all-to-all-done.1.refs_3_.refs_4_ = bf16[8,4,8,256]{3,2,1,0:T(8,128)(2,1)S(1)} async-done(((bf16[8,4,8,256]{3,2,1,0:T(8,128)(2,1)}), bf16[8,4,8,256]{3,2,1,0:T(8,128)(2,1)S(1)}, u32[]{:S(2)}, u32[]{:S(2)}) %all-to-all-start.1) | async-done | bytes 131104 | tf_op jit(solution)/shard_map/all_to_all | solution.py:173
  41.5 0.6 copy-done.1
  42.1 6.4 %shard_map.238 = (bf16[4,8,128,128]{3,2,1,0:T(8,128)(2,1)}, f32[4,8,1024]{2,1,0:T(8,128)}) custom-call(s32[1]{0:T(128)S(6)} %select_n.9.group_ref, bf16[4,8,128,128]{3,2,1,0:T(8,128)(2,1)} %copy.65.refs_0_, f32[4,8,1024]{2,1,0:T(8,128)} %reshape.181.refs_1_, f32[4,8,1024]{2,1,0:T(8,128)} %get-tuple-element.28.refs_2_, bf16[8,4,8,256]{3,2,1,0:T(8,128)(2,1)} %copy-done.1, ...), custom_call_target="tpu_custom_call" | custom-call | tf_op jit(solution)/shard_map/pallas_call | solution.py:146
  48.6 1.1 %reshape.183 = f32[4,8,16,64]{3,2,1,0:T(8,128)S(1)} reshape(f32[4,8,1024]{2,1,0:T(8,128)} %get-tuple-element.6) | data formatting | bytes 262144 | tf_op jit(solution)/shard_map/reshape | solution.py:268
  49.7 0.2 multiply_reduce_fusion
  49.9 0.1 multiply_convert_fusion
  50.1 0.1 dot_general.31
  50.2 3.7 %fusion = f32[8,4,2048]{2,1,0:T(4,128)} fusion(bf16[8,4,1024]{2,1,0:T(4,128)(2,1)S(1)} %dot_general.31, bf16[1024,2048]{1,0:T(8,128)(2,1)} %param.39), kind=kOutput, calls=%fused_computation | convolution fusion | flops 134217728 | bytes 4521984 | tf_op jit(solution)/shard_map/dot_general | solution.py:277
  53.9 3.4 %all-to-all-start.2 = ((f32[8,4,2048]{2,1,0:T(4,128)}), f32[8,4,2048]{2,1,0:T(4,128)S(1)}, u32[]{:S(2)}, u32[]{:S(2)}) async-start(f32[8,4,2048]{2,1,0:T(4,128)} %fusion), calls=%async_computation.2 | async-start | bytes 524288 | tf_op jit(solution)/shard_map/all_to_all | solution.py:278
  57.3 0.1 iota_compare_fusion.3
  57.4 0.1 copy.69
  57.5 0.6 copy.74
  58.2 0.6 copy.73
  58.8 1.3 %copy.72 = bf16[4,8,128,128]{2,3,1,0:T(8,128)(2,1)} copy(bf16[4,8,128,128]{3,2,1,0:T(8,128)(2,1)S(1)} %copy-done.2) | data formatting | bytes 2097152 | tf_op jit(solution)/shard_map/pallas_call | solution.py:146
  60.1 5.4 %all-to-all-done.2 = f32[8,4,2048]{2,1,0:T(4,128)S(1)} async-done(((f32[8,4,2048]{2,1,0:T(4,128)}), f32[8,4,2048]{2,1,0:T(4,128)S(1)}, u32[]{:S(2)}, u32[]{:S(2)}) %all-to-all-start.2) | async-done | bytes 262176 | tf_op jit(solution)/shard_map/all_to_all | solution.py:278
  65.6 0.1 fusion.12
  65.7 0.1 fusion.14
  65.8 0.1 fusion.34
  66.0 0.1 convolution_convert_fusion
  66.1 0.7 reshape_broadcast_in_dim_reshape.3
  66.8 3.3 %all-to-all-start.3 = ((bf16[8,2,2048]{2,1,0:T(2,128)(2,1)}), bf16[8,2,2048]{2,1,0:T(2,128)(2,1)S(1)}, u32[]{:S(2)}, u32[]{:S(2)}) async-start(bf16[8,2,2048]{2,1,0:T(2,128)(2,1)} %reshape_broadcast_in_dim_reshape.3), calls=%async_computation.3 | async-start | bytes 131072 | tf_op jit(solution)/shard_map/all_to_all | solution.py:293
  70.2 0.2 fusion.23
  70.4 0.1 copy.78
  70.5 6.5 %all-to-all-done.3 = bf16[8,2,2048]{2,1,0:T(2,128)(2,1)S(1)} async-done(((bf16[8,2,2048]{2,1,0:T(2,128)(2,1)}), bf16[8,2,2048]{2,1,0:T(2,128)(2,1)S(1)}, u32[]{:S(2)}, u32[]{:S(2)}) %all-to-all-start.3) | async-done | bytes 65568 | tf_op jit(solution)/shard_map/all_to_all | solution.py:293
  77.0 8.0 %convolution_convert_fusion.1 = bf16[16,2048]{1,0:T(8,128)(2,1)S(1)} fusion(bf16[2048,2048]{1,0:T(8,128)(2,1)} %param.43, bf16[16,2048]{1,0:T(8,128)(2,1)S(1)} %reshape.186, bf16[2048,2048]{1,0:T(8,128)(2,1)} %param.42), kind=kOutput, calls=%fused_computation.6 | convolution fusion | flops 268566528 | bytes 16908288 | tf_op jit(solution)/shard_map/dot_general | solution.py:296
  85.1 0.7 convert_element_type.109
  85.8 3.3 %all-to-all-start.4 = ((bf16[8,2,2048]{2,1,0:T(2,128)(2,1)}), bf16[8,2,2048]{2,1,0:T(2,128)(2,1)S(1)}, u32[]{:S(2)}, u32[]{:S(2)}) async-start(bf16[8,2,2048]{2,1,0:T(2,128)(2,1)} %convert_element_type.109), calls=%async_computation.4 | async-start | bytes 131072 | tf_op jit(solution)/shard_map/all_to_all | solution.py:299
  89.1 6.8 %all-to-all-done.4 = bf16[8,2,2048]{2,1,0:T(2,128)(2,1)S(1)} async-done(((bf16[8,2,2048]{2,1,0:T(2,128)(2,1)}), bf16[8,2,2048]{2,1,0:T(2,128)(2,1)S(1)}, u32[]{:S(2)}, u32[]{:S(2)}) %all-to-all-start.4) | async-done | bytes 65568 | tf_op jit(solution)/shard_map/all_to_all | solution.py:299
  96.0 0.1 fusion.4
  96.1 0.6 fusion.19
  (44 shorter events, 0.5 us)
Async XLA Ops:
  0.6 26.4 %copy-start = (bf16[2048,256]{1,0:T(8,128)(2,1)S(1)}, bf16[2048,256]{1,0:T(8,128)(2,1)}, u32[]{:S(2)}) copy-start(bf16[2048,256]{1,0:T(8,128)(2,1)} %param.29) | copy-start | bytes 3145732
  0.6 25.7 %copy-start.4 = (f32[2048]{0:T(1024)S(1)}, f32[2048]{0:T(1024)}, u32[]{:S(2)}) copy-start(f32[2048]{0:T(1024)} %param.27) | copy-start | bytes 24580
  0.7 25.7 %copy-start.5 = (bf16[2048,16]{0,1:T(8,128)(2,1)S(1)}, bf16[2048,16]{0,1:T(8,128)(2,1)}, u32[]{:S(2)}) copy-start(bf16[2048,16]{0,1:T(8,128)(2,1)} %param.30) | copy-start | bytes 196612
  0.7 25.7 %copy-start.10 = (f32[16]{0:T(128)S(1)}, f32[16]{0:T(128)}, u32[]{:S(2)}) copy-start(f32[16]{0:T(128)} %param.31) | copy-start | bytes 196
  0.7 26.8 %copy-start.9 = (f32[256]{0:T(256)S(1)}, f32[256]{0:T(256)}, u32[]{:S(2)}) copy-start(f32[256]{0:T(256)} %param.37) | copy-start | bytes 3076
  2.2 15.3 %all-to-all-start = ((bf16[8,4,2048]{2,1,0:T(4,128)(2,1)}), bf16[8,4,2048]{2,1,0:T(4,128)(2,1)S(1)}, u32[]{:S(2)}, u32[]{:S(2)}) async-start(bf16[8,4,2048]{2,1,0:T(4,128)(2,1)} %broadcast_in_dim.15), calls=%async_computation | async-start | bytes 262144 | tf_op jit(solution)/shard_map/all_to_all | solution.py:173
  13.5 21.6 %copy-start.7 = (f32[1024]{0:T(1024)S(1)}, f32[1024]{0:T(1024)}, u32[]{:S(2)}) copy-start(f32[1024]{0:T(1024)} %param.35) | copy-start | bytes 12292
  19.2 30.4 %copy-start.11 = (f32[16]{0:T(128)S(1)}, f32[16]{0:T(128)}, u32[]{:S(2)}) copy-start(f32[16]{0:T(128)} %param.33) | copy-start | bytes 196
  24.2 33.2 %copy-start.8 = (s32[1,4,2]{1,2,0:T(2,128)S(1)}, s32[1,4,2]{1,2,0:T(2,128)}, u32[]{:S(2)}) copy-start(s32[1,4,2]{1,2,0:T(2,128)} %param.26) | copy-start | bytes 100
  27.1 38.5 %copy-start.3 = (bf16[1,4,2048]{2,1,0:T(4,128)(2,1)S(1)}, bf16[1,4,2048]{2,1,0:T(4,128)(2,1)}, u32[]{:S(2)}) copy-start(bf16[1,4,2048]{2,1,0:T(4,128)(2,1)} %param.22) | copy-start | bytes 49156
  27.1 38.6 %copy-start.6 = (f32[2048]{0:T(1024)S(1)}, f32[2048]{0:T(1024)}, u32[]{:S(2)}) copy-start(f32[2048]{0:T(1024)} %param.40) | copy-start | bytes 24580
  27.1 38.7 %copy-start.12 = (bf16[2048,8]{0,1:T(8,128)(2,1)S(1)}, bf16[2048,8]{0,1:T(8,128)(2,1)}, u32[]{:S(2)}) copy-start(bf16[2048,8]{0,1:T(8,128)(2,1)} %param.41) | copy-start | bytes 98308
  28.1 13.3 %all-to-all-start.1 = ((bf16[8,4,8,256]{3,2,1,0:T(8,128)(2,1)}), bf16[8,4,8,256]{3,2,1,0:T(8,128)(2,1)S(1)}, u32[]{:S(2)}, u32[]{:S(2)}) async-start(bf16[8,4,8,256]{3,2,1,0:T(8,128)(2,1)} %broadcast_in_dim.17), calls=%async_computation.1 | async-start | bytes 262144 | tf_op jit(solution)/shard_map/all_to_all | solution.py:173
  41.5 0.6 copy-start.1
  48.6 10.2 %copy-start.2 = (bf16[4,8,128,128]{3,2,1,0:T(8,128)(2,1)S(1)}, bf16[4,8,128,128]{3,2,1,0:T(8,128)(2,1)}, u32[]{:S(2)}) copy-start(bf16[4,8,128,128]{3,2,1,0:T(8,128)(2,1)} %get-tuple-element.7) | copy-start | bytes 3145732
  53.9 11.6 %all-to-all-start.2 = ((f32[8,4,2048]{2,1,0:T(4,128)}), f32[8,4,2048]{2,1,0:T(4,128)S(1)}, u32[]{:S(2)}, u32[]{:S(2)}) async-start(f32[8,4,2048]{2,1,0:T(4,128)} %fusion), calls=%async_computation.2 | async-start | bytes 524288 | tf_op jit(solution)/shard_map/all_to_all | solution.py:278
  66.8 10.2 %all-to-all-start.3 = ((bf16[8,2,2048]{2,1,0:T(2,128)(2,1)}), bf16[8,2,2048]{2,1,0:T(2,128)(2,1)S(1)}, u32[]{:S(2)}, u32[]{:S(2)}) async-start(bf16[8,2,2048]{2,1,0:T(2,128)(2,1)} %reshape_broadcast_in_dim_reshape.3), calls=%async_computation.3 | async-start | bytes 131072 | tf_op jit(solution)/shard_map/all_to_all | solution.py:293
  85.8 10.2 %all-to-all-start.4 = ((bf16[8,2,2048]{2,1,0:T(2,128)(2,1)}), bf16[8,2,2048]{2,1,0:T(2,128)(2,1)S(1)}, u32[]{:S(2)}, u32[]{:S(2)}) async-start(bf16[8,2,2048]{2,1,0:T(2,128)(2,1)} %convert_element_type.109), calls=%async_computation.4 | async-start | bytes 131072 | tf_op jit(solution)/shard_map/all_to_all | solution.py:299

commit v14 on v13

--- a/solution.py
+++ b/solution.py
@@ -1,3 +1,5 @@
+import functools
+
 import jax
 import jax.numpy as jnp
 from jax import lax
@@ -123,11 +125,27 @@
     )(state_tiles, decay_rows, dx_rows, b_rows, c_rows)
 
 
-def ssm_scan_direct_kernel(group_ref, *refs):
-    ssm_scan_kernel(*refs)
-
-
-def ssm_scan_direct(state_tiles, decay_rows, dx_rows, bc_blocks, group, group_count):
+def ssm_scan_direct_kernel(
+    head_dim, group_ref, s_ref, dec_ref, dx_ref, b_ref, c_ref, z_ref, sx_ref, gain_ref,
+    s_out_ref, read_ref, gn_ref, bb_ref, cb_ref,
+):
+    ssm_scan_kernel(s_ref, dec_ref, dx_ref, b_ref, c_ref, s_out_ref, read_ref, bb_ref, cb_ref)
+    reading = read_ref[0] + sx_ref[0]
+    z = z_ref[0]
+    gated = reading * (z * jax.nn.sigmoid(z))
+    steps, width = gated.shape
+    lane = lax.broadcasted_iota(jnp.int32, (steps, width), 1)
+    scale = jnp.zeros_like(gated)
+    for h in range(width // head_dim):
+        inside = (lane >= h * head_dim) & (lane < (h + 1) * head_dim)
+        square_sum = jnp.sum(jnp.where(inside, gated * gated, 0.0), axis=1, keepdims=True)
+        scale = jnp.where(inside, lax.rsqrt(square_sum * (1.0 / head_dim) + eps), scale)
+    gn_ref[0] = (gated * scale * gain_ref[...]).astype(gn_ref.dtype)
+
+
+def ssm_scan_direct(
+    state_tiles, decay_rows, dx_rows, bc_blocks, group, group_count, z_rows, skip_rows, gain_row, head_dim
+):
     requests, tiles, state_dim, lanes = state_tiles.shape
     steps = decay_rows.shape[1]
     cols_local = bc_blocks.shape[3]
@@ -144,7 +162,7 @@
     big = pl.BlockSpec((1, tiles, state_dim, lanes), lambda r, g: (r, 0, 0, 0))
     per_step = pl.BlockSpec((1, steps, tiles * lanes), lambda r, g: (r, 0, 0))
     return pl.pallas_call(
-        ssm_scan_direct_kernel,
+        functools.partial(ssm_scan_direct_kernel, head_dim),
         grid_spec=pltpu.PrefetchScalarGridSpec(
             num_scalar_prefetch=1,
             grid=(requests,),
@@ -154,8 +172,11 @@
                 per_step,
                 pl.BlockSpec((1, 1, steps, state_dim), b_map),
                 pl.BlockSpec((1, 1, steps, state_dim), c_map),
+                per_step,
+                per_step,
+                pl.BlockSpec((1, tiles * lanes), lambda r, g: (0, 0)),
             ],
-            out_specs=[big, per_step],
+            out_specs=[big, per_step, per_step],
             scratch_shapes=[
                 pltpu.VMEM((steps, state_dim, lanes), jnp.float32),
                 pltpu.VMEM((steps, state_dim, lanes), jnp.float32),
@@ -164,8 +185,9 @@
         out_shape=[
             jax.ShapeDtypeStruct(state_tiles.shape, jnp.bfloat16),
             jax.ShapeDtypeStruct(decay_rows.shape, jnp.float32),
+            jax.ShapeDtypeStruct(decay_rows.shape, jnp.bfloat16),
         ],
-    )(group, state_tiles, decay_rows, dx_rows, bc_blocks, bc_blocks)
+    )(group, state_tiles, decay_rows, dx_rows, bc_blocks, bc_blocks, z_rows, skip_rows, gain_row)
 
 
 def broadcast_gather(block, count):
@@ -250,9 +272,20 @@
         .transpose(0, 1, 4, 2, 3)
         .reshape(requests, tiles, state_dim, lanes)
     )
-    if shared_group and bc_blocks.shape[3] % state_dim == 0:
-        state_out, read_rows = ssm_scan_direct(
-            state_tiles, decay_rows, dx_rows, bc_blocks, tile_group.astype(jnp.int32), G
+    fused_gate = shared_group and bc_blocks.shape[3] % state_dim == 0
+    if fused_gate:
+        skip_rows = (skip_gain[:, None] * x_heads).reshape(requests, STEPS, heads_local * head_dim)
+        state_out, read_rows, gn_rows = ssm_scan_direct(
+            state_tiles,
+            decay_rows,
+            dx_rows,
+            bc_blocks,
+            tile_group.astype(jnp.int32),
+            G,
+            z_gate.reshape(requests, STEPS, heads_local * head_dim),
+            skip_rows,
+            gated_gain.reshape(1, heads_local * head_dim),
+            head_dim,
         )
     else:
         bc_all = jnp.moveaxis(bc_blocks, 0, 2).reshape(requests, STEPS, -1)
@@ -265,14 +298,17 @@
         .transpose(0, 1, 3, 4, 2)
         .reshape(requests, heads_local, head_dim, state_dim)
     )
-    scan_read = read_rows.reshape(requests, STEPS, heads_local, head_dim)
-    readings = scan_read + skip_gain[:, None] * x_heads
-    gated_out = readings * jax.nn.silu(z_gate)
-    group_normed = (
-        norm_rows(gated_out, gated_gain.reshape(heads_local, head_dim))
-        .astype(jnp.bfloat16)
-        .reshape(requests * STEPS, heads_local * head_dim)
-    )
+    if fused_gate:
+        group_normed = gn_rows.reshape(requests * STEPS, heads_local * head_dim)
+    else:
+        scan_read = read_rows.reshape(requests, STEPS, heads_local, head_dim)
+        readings = scan_read + skip_gain[:, None] * x_heads
+        gated_out = readings * jax.nn.silu(z_gate)
+        group_normed = (
+            norm_rows(gated_out, gated_gain.reshape(heads_local, head_dim))
+            .astype(jnp.bfloat16)
+            .reshape(requests * STEPS, heads_local * head_dim)
+        )
     per_expert = head_count // EXPERTS
     mixer_part = jnp.dot(group_normed, weight_out, preferred_element_type=jnp.float32)
     mixer_out = lax.all_to_all(

time: 97.8 us -> 97 us (level)
  waiting for transfers between devices: 24.3 us -> 21.2 us
  local copies, waits for them, and re-layouts: 19 us -> 20.4 us
    all_to_all x2, waiting for transfers between devices: 5.51 us -> 3.4 us  [broadcast_gather(): return lax.all_to_all(copies, 'head', 0, 0, tiled=True)]
    unnamed x32 -> x29, local copies, waits for them, and re-layouts: 4.17 us -> 4.22 us
  transfers between devices with their start and end apart: 5 -> 5, of which waited for: 4 -> 4; matrix products, arithmetic and copies ran while one was open for 13% -> 17% of each run, Pallas kernels for 0% -> 0%
where the time goes in v14:
time: 97 us; the launch traced here: 95.9 us
  starting transfers between devices  23.5 us (24%)
  waiting for transfers between devices  21.2 us (22%)
  local copies, waits for them, and re-layouts  20.4 us (21%)
  matrix products  12.9 us (13%)
  Pallas kernels  11.8 us (12%)
  other arithmetic  5.05 us (5%)
    all_to_all x2, starting transfers between devices, broadcast_gather(): return lax.all_to_all(copies, 'head', 0, 0, tiled=True)  13.4 us
    dot_general x1, matrix products, shards(): jnp.dot(hidden, weight_down, preferred_element_type=jnp.float32)  8.05 us
    pallas_call x1, Pallas kernels, ssm_scan_direct(): pl.pallas_call(functools.partial(ssm_scan_direct_kernel, head_dim), grid_...  6.88 us
    all_to_all x1, waiting for transfers between devices, shards(): lax.all_to_all(computed.astype(jnp.bfloat16), 'head', split_axis=0, conca...  6.81 us
    all_to_all x1, waiting for transfers between devices, shards(): lax.all_to_all(outgoing, 'head', split_axis=0, concat_axis=0, tiled=True)  6.55 us
    pallas_call x1, Pallas kernels, column_matmul(): pl.pallas_call(column_matmul_kernel, grid=(cols // block,), in_specs=[pl....  4.97 us
    all_to_all x1, waiting for transfers between devices, shards(): lax.all_to_all(mixer_part.reshape(head_count, tok_local, width), 'head',...  4.46 us
    unnamed x29, local copies, waits for them, and re-layouts  4.22 us
  transfers between devices with their start and end apart: 5, of which 4 were waited for; matrix products, arithmetic and copies ran while one was open for 17% of the time, Pallas kernels for 0%

profile of v14, /device:TPU:0, one launch (start us, length us, event | category | flops | bytes accessed | tf_op | source)
XLA Modules:
  0.0 95.9 jit_solution(11808291736979673395)
XLA Ops:
  0.6 0.0 copy-start
  0.6 0.0 copy-start.3
  0.7 1.5 %broadcast_in_dim.15 = bf16[8,4,2048]{2,1,0:T(4,128)(2,1)} broadcast(bf16[4,2048]{1,0:T(4,128)(2,1)} %bitcast.86), dimensions={1,2} | broadcast | bytes 147456 | tf_op jit(solution)/shard_map/broadcast_in_dim | solution.py:194
  2.2 7.4 %all-to-all-start = ((bf16[8,4,2048]{2,1,0:T(4,128)(2,1)}), bf16[8,4,2048]{2,1,0:T(4,128)(2,1)S(1)}, u32[]{:S(2)}, u32[]{:S(2)}) async-start(bf16[8,4,2048]{2,1,0:T(4,128)(2,1)} %broadcast_in_dim.15), calls=%async_computation | async-start | bytes 262144 | tf_op jit(solution)/shard_map/all_to_all | solution.py:195
  9.5 0.8 copy.71
  10.3 0.1 reshape_squeeze.7
  10.4 0.1 fusion.26
  10.5 0.2 select_reduce_fusion
  10.7 0.8 fusion.32
  11.5 0.7 exponential_negate_fusion
  12.2 0.7 copy.89
  12.9 0.7 mul.233
  13.6 0.1 mul.234
  13.7 0.8 copy.88
  14.4 2.3 %copy.67.s_ref = bf16[4,8,128,128]{3,2,1,0:T(8,128)(2,1)} copy(bf16[4,8,128,128]{2,3,1,0:T(8,128)(2,1)} %bitcast.84) | data formatting | bytes 2097152 | tf_op jit(solution)/shard_map/reshape | solution.py:273
  16.7 0.9 fusion.31
  17.6 0.2 multiply_reduce_fusion
  17.8 0.1 rsqrt.25
  17.9 0.1 rsqrt.24
  18.0 1.4 %multiply_convert_fusion.a_ref = bf16[32,2048]{1,0:T(8,128)(2,1)} fusion(f32[32,2048]{1,0:T(8,128)S(1)} %reshape.184, f32[2048]{0:T(1024)} %param.27, f32[32]{0:T(128)S(1)} %rsqrt.25), kind=kLoop, calls=%fused_computation.13 | loop fusion | flops 196608 | bytes 401536 | tf_op jit(solution)/shard_map/convert_element_type | solution.py:232
  19.4 5.0 %shard_map.237 = f32[32,2048]{1,0:T(8,128)} custom-call(bf16[32,2048]{1,0:T(8,128)(2,1)} %multiply_convert_fusion.a_ref, bf16[2048,2048]{1,0:T(8,128)(2,1)} %w_ref.1), custom_call_target="tpu_custom_call" | custom-call | flops 268435456 | bytes 8781824 | tf_op jit(solution)/shard_map/pallas_call | solution.py:59
  24.4 1.0 %slice.89 = bf16[4,8,16,64]{3,1,2,0:T(8,128)(2,1)S(1)} slice(f32[4,8,16,128]{3,1,2,0:T(8,128)} %bitcast.82), slice={[0:4], [0:8], [0:16], [0:64]} | slice | bytes 131072 | tf_op jit(solution)/shard_map/slice | solution.py:245
  25.4 1.1 %slice.98 = f32[4,8,16,64]{3,1,2,0:T(8,128)S(1)} slice(f32[4,8,16,128]{3,1,2,0:T(8,128)} %bitcast.83), slice={[0:4], [0:8], [0:16], [64:128]} | slice | bytes 262144 | tf_op jit(solution)/shard_map/slice | solution.py:247
  26.5 0.0 copy-start.5
  26.5 0.3 convolution_convert_fusion.2
  26.8 0.0 copy-start.10
  26.9 0.7 broadcast_in_dim.17
  27.6 6.0 %all-to-all-start.1 = ((bf16[8,4,8,256]{3,2,1,0:T(8,128)(2,1)}), bf16[8,4,8,256]{3,2,1,0:T(8,128)(2,1)S(1)}, u32[]{:S(2)}, u32[]{:S(2)}) async-start(bf16[8,4,8,256]{3,2,1,0:T(8,128)(2,1)} %broadcast_in_dim.17), calls=%async_computation.1 | async-start | bytes 262144 | tf_op jit(solution)/shard_map/all_to_all | solution.py:195
  33.6 0.8 reshape.177.z_ref
  34.4 0.1 convert_element_type.90
  34.6 0.3 multiply_exponential_fusion
  34.8 0.1 broadcast_in_dim.16
  35.0 0.8 reshape.175.dec_ref
  35.8 0.1 mul.200
  35.9 0.1 mul.201
  36.1 0.8 broadcast_multiply_fusion
  36.8 0.7 mul.219.dx_ref
  37.5 3.4 %all-to-all-done.1.b_ref.c_ref = bf16[8,4,8,256]{3,2,1,0:T(8,128)(2,1)S(1)} async-done(((bf16[8,4,8,256]{3,2,1,0:T(8,128)(2,1)}), bf16[8,4,8,256]{3,2,1,0:T(8,128)(2,1)S(1)}, u32[]{:S(2)}, u32[]{:S(2)}) %all-to-all-start.1) | async-done | bytes 131104 | tf_op jit(solution)/shard_map/all_to_all | solution.py:195
  40.9 0.7 copy-done.1
  41.6 6.9 %shard_map.238 = (bf16[4,8,128,128]{3,2,1,0:T(8,128)(2,1)}, f32[4,8,1024]{2,1,0:T(8,128)}, bf16[4,8,1024]{2,1,0:T(8,128)(2,1)}) custom-call(s32[1]{0:T(128)S(6)} %select_n.9.group_ref, bf16[4,8,128,128]{3,2,1,0:T(8,128)(2,1)} %copy.67.s_ref, f32[4,8,1024]{2,1,0:T(8,128)} %reshape.175.dec_ref, f32[4,8,1024]{2,1,0:T(8,128)} %mul.219.dx_ref, ...), custom_call_target="tpu_custom_call" | custom-call | tf_op jit(solution)/shard_map/pallas_call | solution.py:164
  48.4 0.9 dot_general.31
  49.3 3.7 %fusion = f32[8,4,2048]{2,1,0:T(4,128)} fusion(bf16[8,4,1024]{2,1,0:T(4,128)(2,1)S(1)} %dot_general.31, bf16[1024,2048]{1,0:T(8,128)(2,1)} %param.39), kind=kOutput, calls=%fused_computation | convolution fusion | flops 134217728 | bytes 4521984 | tf_op jit(solution)/shard_map/dot_general | solution.py:313
  53.0 3.4 %all-to-all-start.2 = ((f32[8,4,2048]{2,1,0:T(4,128)}), f32[8,4,2048]{2,1,0:T(4,128)S(1)}, u32[]{:S(2)}, u32[]{:S(2)}) async-start(f32[8,4,2048]{2,1,0:T(4,128)} %fusion), calls=%async_computation.2 | async-start | bytes 524288 | tf_op jit(solution)/shard_map/all_to_all | solution.py:314
  56.4 0.1 iota_compare_fusion.3
  56.5 0.1 copy.70
  56.6 0.6 copy.75
  57.3 0.6 copy.74
  57.9 2.3 %copy.73 = bf16[4,8,128,128]{2,3,1,0:T(8,128)(2,1)} copy(bf16[4,8,128,128]{3,2,1,0:T(8,128)(2,1)} %get-tuple-element.7) | data formatting | bytes 2097152 | tf_op jit(solution)/shard_map/pallas_call | solution.py:164
  60.1 4.5 %all-to-all-done.2 = f32[8,4,2048]{2,1,0:T(4,128)S(1)} async-done(((f32[8,4,2048]{2,1,0:T(4,128)}), f32[8,4,2048]{2,1,0:T(4,128)S(1)}, u32[]{:S(2)}, u32[]{:S(2)}) %all-to-all-start.2) | async-done | bytes 262176 | tf_op jit(solution)/shard_map/all_to_all | solution.py:314
  64.7 0.1 fusion.12
  64.8 0.1 fusion.14
  64.9 0.1 fusion.33
  65.1 0.1 convolution_convert_fusion
  65.2 0.7 reshape_broadcast_in_dim_reshape.3
  65.9 3.3 %all-to-all-start.3 = ((bf16[8,2,2048]{2,1,0:T(2,128)(2,1)}), bf16[8,2,2048]{2,1,0:T(2,128)(2,1)S(1)}, u32[]{:S(2)}, u32[]{:S(2)}) async-start(bf16[8,2,2048]{2,1,0:T(2,128)(2,1)} %reshape_broadcast_in_dim_reshape.3), calls=%async_computation.3 | async-start | bytes 131072 | tf_op jit(solution)/shard_map/all_to_all | solution.py:329
  69.3 0.2 fusion.23
  69.5 0.1 copy.79
  69.6 6.5 %all-to-all-done.3 = bf16[8,2,2048]{2,1,0:T(2,128)(2,1)S(1)} async-done(((bf16[8,2,2048]{2,1,0:T(2,128)(2,1)}), bf16[8,2,2048]{2,1,0:T(2,128)(2,1)S(1)}, u32[]{:S(2)}, u32[]{:S(2)}) %all-to-all-start.3) | async-done | bytes 65568 | tf_op jit(solution)/shard_map/all_to_all | solution.py:329
  76.1 8.0 %convolution_convert_fusion.1 = bf16[16,2048]{1,0:T(8,128)(2,1)S(1)} fusion(bf16[2048,2048]{1,0:T(8,128)(2,1)} %param.43, bf16[16,2048]{1,0:T(8,128)(2,1)S(1)} %reshape.180, bf16[2048,2048]{1,0:T(8,128)(2,1)} %param.42), kind=kOutput, calls=%fused_computation.6 | convolution fusion | flops 268566528 | bytes 16908288 | tf_op jit(solution)/shard_map/dot_general | solution.py:332
  84.2 0.7 convert_element_type.105
  84.9 3.3 %all-to-all-start.4 = ((bf16[8,2,2048]{2,1,0:T(2,128)(2,1)}), bf16[8,2,2048]{2,1,0:T(2,128)(2,1)S(1)}, u32[]{:S(2)}, u32[]{:S(2)}) async-start(bf16[8,2,2048]{2,1,0:T(2,128)(2,1)} %convert_element_type.105), calls=%async_computation.4 | async-start | bytes 131072 | tf_op jit(solution)/shard_map/all_to_all | solution.py:335
  88.3 6.8 %all-to-all-done.4 = bf16[8,2,2048]{2,1,0:T(2,128)(2,1)S(1)} async-done(((bf16[8,2,2048]{2,1,0:T(2,128)(2,1)}), bf16[8,2,2048]{2,1,0:T(2,128)(2,1)S(1)}, u32[]{:S(2)}, u32[]{:S(2)}) %all-to-all-start.4) | async-done | bytes 65568 | tf_op jit(solution)/shard_map/all_to_all | solution.py:335
  95.1 0.1 fusion.4
  95.3 0.6 fusion.19
  (39 shorter events, 0.5 us)
Async XLA Ops:
  0.6 25.8 %copy-start = (bf16[2048,256]{1,0:T(8,128)(2,1)S(1)}, bf16[2048,256]{1,0:T(8,128)(2,1)}, u32[]{:S(2)}) copy-start(bf16[2048,256]{1,0:T(8,128)(2,1)} %param.29) | copy-start | bytes 3145732
  0.6 25.8 %copy-start.3 = (f32[2048]{0:T(1024)S(1)}, f32[2048]{0:T(1024)}, u32[]{:S(2)}) copy-start(f32[2048]{0:T(1024)} %param.27) | copy-start | bytes 24580
  0.7 26.2 %copy-start.8 = (f32[256]{0:T(256)S(1)}, f32[256]{0:T(256)}, u32[]{:S(2)}) copy-start(f32[256]{0:T(256)} %param.37) | copy-start | bytes 3076
  2.2 32.4 %copy-start.4 = (bf16[2048,16]{0,1:T(8,128)(2,1)S(1)}, bf16[2048,16]{0,1:T(8,128)(2,1)}, u32[]{:S(2)}) copy-start(bf16[2048,16]{0,1:T(8,128)(2,1)} %param.30) | copy-start | bytes 196612
  2.2 32.4 %copy-start.9 = (f32[16]{0:T(128)S(1)}, f32[16]{0:T(128)}, u32[]{:S(2)}) copy-start(f32[16]{0:T(128)} %param.31) | copy-start | bytes 196
  2.2 15.4 %all-to-all-start = ((bf16[8,4,2048]{2,1,0:T(4,128)(2,1)}), bf16[8,4,2048]{2,1,0:T(4,128)(2,1)S(1)}, u32[]{:S(2)}, u32[]{:S(2)}) async-start(bf16[8,4,2048]{2,1,0:T(4,128)(2,1)} %broadcast_in_dim.15), calls=%async_computation | async-start | bytes 262144 | tf_op jit(solution)/shard_map/all_to_all | solution.py:195
  16.7 19.4 %copy-start.6 = (f32[1024]{0:T(1024)S(1)}, f32[1024]{0:T(1024)}, u32[]{:S(2)}) copy-start(f32[1024]{0:T(1024)} %param.35) | copy-start | bytes 12292
  24.4 32.2 %copy-start.7 = (s32[1,4,2]{1,2,0:T(2,128)S(1)}, s32[1,4,2]{1,2,0:T(2,128)}, u32[]{:S(2)}) copy-start(s32[1,4,2]{1,2,0:T(2,128)} %param.26) | copy-start | bytes 100
  26.5 38.2 %copy-start.2 = (bf16[1,4,2048]{2,1,0:T(4,128)(2,1)S(1)}, bf16[1,4,2048]{2,1,0:T(4,128)(2,1)}, u32[]{:S(2)}) copy-start(bf16[1,4,2048]{2,1,0:T(4,128)(2,1)} %param.22) | copy-start | bytes 49156
  26.5 38.3 %copy-start.5 = (f32[2048]{0:T(1024)S(1)}, f32[2048]{0:T(1024)}, u32[]{:S(2)}) copy-start(f32[2048]{0:T(1024)} %param.40) | copy-start | bytes 24580
  26.8 38.1 %copy-start.10 = (bf16[2048,8]{0,1:T(8,128)(2,1)S(1)}, bf16[2048,8]{0,1:T(8,128)(2,1)}, u32[]{:S(2)}) copy-start(bf16[2048,8]{0,1:T(8,128)(2,1)} %param.41) | copy-start | bytes 98308
  27.6 13.3 %all-to-all-start.1 = ((bf16[8,4,8,256]{3,2,1,0:T(8,128)(2,1)}), bf16[8,4,8,256]{3,2,1,0:T(8,128)(2,1)S(1)}, u32[]{:S(2)}, u32[]{:S(2)}) async-start(bf16[8,4,8,256]{3,2,1,0:T(8,128)(2,1)} %broadcast_in_dim.17), calls=%async_computation.1 | async-start | bytes 262144 | tf_op jit(solution)/shard_map/all_to_all | solution.py:195
  40.9 0.7 copy-start.1
  53.0 11.6 %all-to-all-start.2 = ((f32[8,4,2048]{2,1,0:T(4,128)}), f32[8,4,2048]{2,1,0:T(4,128)S(1)}, u32[]{:S(2)}, u32[]{:S(2)}) async-start(f32[8,4,2048]{2,1,0:T(4,128)} %fusion), calls=%async_computation.2 | async-start | bytes 524288 | tf_op jit(solution)/shard_map/all_to_all | solution.py:314
  65.9 10.2 %all-to-all-start.3 = ((bf16[8,2,2048]{2,1,0:T(2,128)(2,1)}), bf16[8,2,2048]{2,1,0:T(2,128)(2,1)S(1)}, u32[]{:S(2)}, u32[]{:S(2)}) async-start(bf16[8,2,2048]{2,1,0:T(2,128)(2,1)} %reshape_broadcast_in_dim_reshape.3), calls=%async_computation.3 | async-start | bytes 131072 | tf_op jit(solution)/shard_map/all_to_all | solution.py:329
  84.9 10.2 %all-to-all-start.4 = ((bf16[8,2,2048]{2,1,0:T(2,128)(2,1)}), bf16[8,2,2048]{2,1,0:T(2,128)(2,1)S(1)}, u32[]{:S(2)}, u32[]{:S(2)}) async-start(bf16[8,2,2048]{2,1,0:T(2,128)(2,1)} %convert_element_type.105), calls=%async_computation.4 | async-start | bytes 131072 | tf_op jit(solution)/shard_map/all_to_all | solution.py:335

commit v15 on v14

--- a/solution.py
+++ b/solution.py
@@ -69,6 +69,45 @@
             flops=2 * m * k * cols,
             transcendentals=0,
             bytes_accessed=2 * (m * k + k * cols) + 4 * m * cols,
+        ),
+    )(rows, weight)
+
+
+def xz_matmul_kernel(head_dim, a_ref, w_ref, x_ref, z_ref):
+    product = jnp.dot(a_ref[...], w_ref[...], preferred_element_type=jnp.float32)
+    width = z_ref.shape[1]
+    for h in range(width // head_dim):
+        x_ref[:, h * head_dim : (h + 1) * head_dim] = product[
+            :, 2 * h * head_dim : (2 * h + 1) * head_dim
+        ].astype(x_ref.dtype)
+        z_ref[:, h * head_dim : (h + 1) * head_dim] = product[
+            :, (2 * h + 1) * head_dim : (2 * h + 2) * head_dim
+        ]
+
+
+def xz_matmul(rows, weight, head_dim):
+    m, k = rows.shape
+    cols = weight.shape[1]
+    block = min(512, cols)
+    return pl.pallas_call(
+        functools.partial(xz_matmul_kernel, head_dim),
+        grid=(cols // block,),
+        in_specs=[
+            pl.BlockSpec((m, k), lambda j: (0, 0)),
+            pl.BlockSpec((k, block), lambda j: (0, j)),
+        ],
+        out_specs=[
+            pl.BlockSpec((m, block // 2), lambda j: (0, j)),
+            pl.BlockSpec((m, block // 2), lambda j: (0, j)),
+        ],
+        out_shape=[
+            jax.ShapeDtypeStruct((m, cols // 2), jnp.bfloat16),
+            jax.ShapeDtypeStruct((m, cols // 2), jnp.float32),
+        ],
+        cost_estimate=pl.CostEstimate(
+            flops=2 * m * k * cols,
+            transcendentals=0,
+            bytes_accessed=2 * (m * k + k * cols) + 3 * m * cols,
         ),
     )(rows, weight)
 
@@ -236,15 +275,11 @@
         .astype(jnp.bfloat16)
     )
     bc_conv, conv_bc_new = causal_conv(conv_bc_state[0], bc_fresh, conv_bc_kernel, conv_bc_bias)
-    bc_conv = bc_conv.astype(jnp.bfloat16)
+    x_rows, z_rows = xz_matmul(normed, weight_xz, head_dim)
+    bc_conv, x_rows, z_rows = lax.optimization_barrier((bc_conv.astype(jnp.bfloat16), x_rows, z_rows))
     bc_blocks = broadcast_gather(bc_conv, head_count)
-    proj_xz = column_matmul(normed, weight_xz).reshape(
-        requests, STEPS, heads_local, 2 * head_dim
-    )
-    x_fresh = (
-        proj_xz[..., :head_dim].reshape(requests, STEPS, heads_local * head_dim).astype(jnp.bfloat16)
-    )
-    z_gate = proj_xz[..., head_dim:]
+    x_fresh = x_rows.reshape(requests, STEPS, heads_local * head_dim)
+    z_gate = z_rows.reshape(requests, STEPS, heads_local, head_dim)
     delta = jax.nn.softplus(
         jnp.dot(normed, weight_delta, preferred_element_type=jnp.float32).reshape(
             requests, STEPS, heads_local

time: 97 us -> 96.3 us (level)
  local copies, waits for them, and re-layouts: 20.4 us -> 17.3 us
    slice x2 -> x0, local copies, waits for them, and re-layouts: 2.06 us -> none  [the longest x1 1.07 us: shards(): z_gate = proj_xz[..., head_dim:]]
where the time goes in v15:
time: 96.3 us; the launch traced here: 95.2 us
  starting transfers between devices  23.4 us (24%)
  waiting for transfers between devices  21.4 us (22%)
  local copies, waits for them, and re-layouts  17.3 us (18%)
  matrix products  13.6 us (14%)
  Pallas kernels  12.7 us (13%)
  other arithmetic  5.88 us (6%)
    all_to_all x2, starting transfers between devices, broadcast_gather(): return lax.all_to_all(copies, 'head', 0, 0, tiled=True)  13.3 us
    dot_general x1, matrix products, shards(): jnp.dot(hidden, weight_down, preferred_element_type=jnp.float32)  8.05 us
    pallas_call x1, Pallas kernels, ssm_scan_direct(): pl.pallas_call(functools.partial(ssm_scan_direct_kernel, head_dim), grid_...  6.88 us
    all_to_all x1, waiting for transfers between devices, shards(): lax.all_to_all(computed.astype(jnp.bfloat16), 'head', split_axis=0, conca...  6.81 us
    all_to_all x1, waiting for transfers between devices, shards(): lax.all_to_all(outgoing, 'head', split_axis=0, concat_axis=0, tiled=True)  6.55 us
    pallas_call x1, Pallas kernels, xz_matmul(): pl.pallas_call(functools.partial(xz_matmul_kernel, head_dim), grid=(cols...  5.78 us
    all_to_all x1, waiting for transfers between devices, shards(): lax.all_to_all(mixer_part.reshape(head_count, tok_local, width), 'head',...  4.45 us
    unnamed x29, local copies, waits for them, and re-layouts  4.16 us
  transfers between devices with their start and end apart: 5, of which 4 were waited for; matrix products, arithmetic and copies ran while one was open for 17% of the time, Pallas kernels for 0%

profile of v15, /device:TPU:0, one launch (start us, length us, event | category | flops | bytes accessed | tf_op | source)
XLA Modules:
  0.0 95.2 jit_solution(14211615854168775492)
XLA Ops:
  0.6 0.0 copy-start
  0.6 0.0 copy-start.4
  0.7 1.5 %broadcast_in_dim.15 = bf16[8,4,2048]{2,1,0:T(4,128)(2,1)} broadcast(bf16[4,2048]{1,0:T(4,128)(2,1)} %bitcast.81), dimensions={1,2} | broadcast | bytes 147456 | tf_op jit(solution)/shard_map/broadcast_in_dim | solution.py:233
  2.2 7.3 %all-to-all-start = ((bf16[8,4,2048]{2,1,0:T(4,128)(2,1)}), bf16[8,4,2048]{2,1,0:T(4,128)(2,1)S(1)}, u32[]{:S(2)}, u32[]{:S(2)}) async-start(bf16[8,4,2048]{2,1,0:T(4,128)(2,1)} %broadcast_in_dim.15), calls=%async_computation | async-start | bytes 262144 | tf_op jit(solution)/shard_map/all_to_all | solution.py:234
  9.4 0.8 copy.63
  10.2 0.1 reshape_squeeze.7
  10.3 0.1 fusion.26
  10.4 0.2 select_reduce_fusion
  10.6 0.8 fusion.32
  11.4 0.7 exponential_negate_fusion
  12.1 0.7 copy.77
  12.8 0.7 mul.233
  13.5 0.1 mul.234
  13.6 0.8 copy.76
  14.3 2.3 %copy.59.s_ref = bf16[4,8,128,128]{3,2,1,0:T(8,128)(2,1)} copy(bf16[4,8,128,128]{2,3,1,0:T(8,128)(2,1)} %bitcast.79) | data formatting | bytes 2097152 | tf_op jit(solution)/shard_map/reshape | solution.py:308
  16.6 0.9 fusion.31
  17.5 0.0 all-to-all-done
  17.5 0.2 multiply_reduce_fusion
  17.7 0.1 rsqrt.25
  17.7 0.1 rsqrt.24
  17.9 1.0 %convolution_convert_fusion.2 = bf16[4,8,256]{2,1,0:T(8,128)(2,1)S(1)} fusion(bf16[2048,256]{1,0:T(8,128)(2,1)S(1)} %copy-done, f32[4,8,2048]{2,1,0:T(8,128)S(1)} %reshape.177, f32[2048]{0:T(1024)} %param.27, f32[4,8]{1,0:T(4,128)S(1)} %rsqrt.24), kind=kOutput, calls=%fused_computation.9 | convolution fusion | flops 33759232 | bytes 1335424 | tf_op jit(solution)/shard_map/dot_general | solution.py:273
  18.9 1.4 %multiply_convert_fusion.a_ref = bf16[32,2048]{1,0:T(8,128)(2,1)} fusion(f32[32,2048]{1,0:T(8,128)S(1)} %reshape.178, f32[2048]{0:T(1024)} %param.27, f32[32]{0:T(128)S(1)} %rsqrt.25), kind=kLoop, calls=%fused_computation.12 | loop fusion | flops 196608 | bytes 401536 | tf_op jit(solution)/shard_map/convert_element_type | solution.py:271
  20.4 5.8 %shard_map.237 = (bf16[32,1024]{1,0:T(8,128)(2,1)}, f32[32,1024]{1,0:T(8,128)}) custom-call(bf16[32,2048]{1,0:T(8,128)(2,1)} %multiply_convert_fusion.a_ref, bf16[2048,2048]{1,0:T(8,128)(2,1)} %w_ref.1), custom_call_target="tpu_custom_call" | custom-call | flops 268435456 | bytes 8716288 | tf_op jit(solution)/shard_map/pallas_call | solution.py:92
  26.1 0.0 copy-start.6
  26.2 0.0 copy-start.11
  26.2 0.6 broadcast_in_dim.17
  26.9 6.0 %all-to-all-start.1 = ((bf16[8,4,8,256]{3,2,1,0:T(8,128)(2,1)}), bf16[8,4,8,256]{3,2,1,0:T(8,128)(2,1)S(1)}, u32[]{:S(2)}, u32[]{:S(2)}) async-start(bf16[8,4,8,256]{3,2,1,0:T(8,128)(2,1)} %broadcast_in_dim.17), calls=%async_computation.1 | async-start | bytes 262144 | tf_op jit(solution)/shard_map/all_to_all | solution.py:234
  32.9 0.0 copy-done.10
  32.9 0.0 copy-done.5
  32.9 0.3 multiply_exponential_fusion
  33.2 0.1 broadcast_in_dim.16
  33.3 0.8 reshape.170.dec_ref
  34.1 0.1 mul.200
  34.2 0.1 mul.201
  34.3 0.9 maximum_convert_fusion
  35.2 0.8 broadcast_multiply_fusion
  36.0 0.7 mul.232.dx_ref
  36.6 3.6 %all-to-all-done.1.b_ref.c_ref = bf16[8,4,8,256]{3,2,1,0:T(8,128)(2,1)S(1)} async-done(((bf16[8,4,8,256]{3,2,1,0:T(8,128)(2,1)}), bf16[8,4,8,256]{3,2,1,0:T(8,128)(2,1)S(1)}, u32[]{:S(2)}, u32[]{:S(2)}) %all-to-all-start.1) | async-done | bytes 131104 | tf_op jit(solution)/shard_map/all_to_all | solution.py:234
  40.2 0.7 copy-done.1
  40.9 6.9 %shard_map.238 = (bf16[4,8,128,128]{3,2,1,0:T(8,128)(2,1)}, f32[4,8,1024]{2,1,0:T(8,128)}, bf16[4,8,1024]{2,1,0:T(8,128)(2,1)}) custom-call(s32[1]{0:T(128)S(6)} %select_n.9.group_ref, bf16[4,8,128,128]{3,2,1,0:T(8,128)(2,1)} %copy.59.s_ref, f32[4,8,1024]{2,1,0:T(8,128)} %reshape.170.dec_ref, f32[4,8,1024]{2,1,0:T(8,128)} %mul.232.dx_ref, ...), custom_call_target="tpu_custom_call" | custom-call | tf_op jit(solution)/shard_map/pallas_call | solution.py:203
  47.8 0.9 dot_general.31
  48.6 3.7 %fusion = f32[8,4,2048]{2,1,0:T(4,128)} fusion(bf16[8,4,1024]{2,1,0:T(4,128)(2,1)S(1)} %dot_general.31, bf16[1024,2048]{1,0:T(8,128)(2,1)} %param.39), kind=kOutput, calls=%fused_computation | convolution fusion | flops 134217728 | bytes 4521984 | tf_op jit(solution)/shard_map/dot_general | solution.py:348
  52.3 3.4 %all-to-all-start.2 = ((f32[8,4,2048]{2,1,0:T(4,128)}), f32[8,4,2048]{2,1,0:T(4,128)S(1)}, u32[]{:S(2)}, u32[]{:S(2)}) async-start(f32[8,4,2048]{2,1,0:T(4,128)} %fusion), calls=%async_computation.2 | async-start | bytes 524288 | tf_op jit(solution)/shard_map/all_to_all | solution.py:349
  55.8 0.1 iota_compare_fusion.3
  55.8 0.1 copy.62
  55.9 0.6 copy.67
  56.6 0.6 copy.66
  57.2 2.3 %copy.65 = bf16[4,8,128,128]{2,3,1,0:T(8,128)(2,1)} copy(bf16[4,8,128,128]{3,2,1,0:T(8,128)(2,1)} %get-tuple-element.17) | data formatting | bytes 2097152 | tf_op jit(solution)/shard_map/pallas_call | solution.py:203
  59.5 4.5 %all-to-all-done.2 = f32[8,4,2048]{2,1,0:T(4,128)S(1)} async-done(((f32[8,4,2048]{2,1,0:T(4,128)}), f32[8,4,2048]{2,1,0:T(4,128)S(1)}, u32[]{:S(2)}, u32[]{:S(2)}) %all-to-all-start.2) | async-done | bytes 262176 | tf_op jit(solution)/shard_map/all_to_all | solution.py:349
  64.0 0.1 fusion.12
  64.1 0.1 fusion.14
  64.2 0.1 fusion.33
  64.4 0.1 convolution_convert_fusion
  64.5 0.7 reshape_broadcast_in_dim_reshape.3
  65.2 3.3 %all-to-all-start.3 = ((bf16[8,2,2048]{2,1,0:T(2,128)(2,1)}), bf16[8,2,2048]{2,1,0:T(2,128)(2,1)S(1)}, u32[]{:S(2)}, u32[]{:S(2)}) async-start(bf16[8,2,2048]{2,1,0:T(2,128)(2,1)} %reshape_broadcast_in_dim_reshape.3), calls=%async_computation.3 | async-start | bytes 131072 | tf_op jit(solution)/shard_map/all_to_all | solution.py:364
  68.6 0.2 fusion.23
  68.8 0.1 copy.71
  68.9 6.5 %all-to-all-done.3 = bf16[8,2,2048]{2,1,0:T(2,128)(2,1)S(1)} async-done(((bf16[8,2,2048]{2,1,0:T(2,128)(2,1)}), bf16[8,2,2048]{2,1,0:T(2,128)(2,1)S(1)}, u32[]{:S(2)}, u32[]{:S(2)}) %all-to-all-start.3) | async-done | bytes 65568 | tf_op jit(solution)/shard_map/all_to_all | solution.py:364
  75.4 8.0 %convolution_convert_fusion.1 = bf16[16,2048]{1,0:T(8,128)(2,1)S(1)} fusion(bf16[2048,2048]{1,0:T(8,128)(2,1)} %param.43, bf16[16,2048]{1,0:T(8,128)(2,1)S(1)} %reshape.174, bf16[2048,2048]{1,0:T(8,128)(2,1)} %param.42), kind=kOutput, calls=%fused_computation.6 | convolution fusion | flops 268566528 | bytes 16908288 | tf_op jit(solution)/shard_map/dot_general | solution.py:367
  83.5 0.7 convert_element_type.100
  84.2 3.3 %all-to-all-start.4 = ((bf16[8,2,2048]{2,1,0:T(2,128)(2,1)}), bf16[8,2,2048]{2,1,0:T(2,128)(2,1)S(1)}, u32[]{:S(2)}, u32[]{:S(2)}) async-start(bf16[8,2,2048]{2,1,0:T(2,128)(2,1)} %convert_element_type.100), calls=%async_computation.4 | async-start | bytes 131072 | tf_op jit(solution)/shard_map/all_to_all | solution.py:370
  87.6 6.8 %all-to-all-done.4 = bf16[8,2,2048]{2,1,0:T(2,128)(2,1)S(1)} async-done(((bf16[8,2,2048]{2,1,0:T(2,128)(2,1)}), bf16[8,2,2048]{2,1,0:T(2,128)(2,1)S(1)}, u32[]{:S(2)}, u32[]{:S(2)}) %all-to-all-start.4) | async-done | bytes 65568 | tf_op jit(solution)/shard_map/all_to_all | solution.py:370
  94.4 0.1 fusion.4
  94.6 0.6 fusion.19
  (35 shorter events, 0.4 us)
Async XLA Ops:
  0.6 17.2 %copy-start = (bf16[2048,256]{1,0:T(8,128)(2,1)S(1)}, bf16[2048,256]{1,0:T(8,128)(2,1)}, u32[]{:S(2)}) copy-start(bf16[2048,256]{1,0:T(8,128)(2,1)} %param.29) | copy-start | bytes 3145732
  0.6 32.2 %copy-start.4 = (f32[2048]{0:T(1024)S(1)}, f32[2048]{0:T(1024)}, u32[]{:S(2)}) copy-start(f32[2048]{0:T(1024)} %param.27) | copy-start | bytes 24580
  0.7 25.5 %copy-start.9 = (f32[256]{0:T(256)S(1)}, f32[256]{0:T(256)}, u32[]{:S(2)}) copy-start(f32[256]{0:T(256)} %param.37) | copy-start | bytes 3076
  0.7 32.2 %copy-start.10 = (f32[16]{0:T(128)S(1)}, f32[16]{0:T(128)}, u32[]{:S(2)}) copy-start(f32[16]{0:T(128)} %param.31) | copy-start | bytes 196
  0.7 32.2 %copy-start.5 = (bf16[2048,16]{0,1:T(8,128)(2,1)S(1)}, bf16[2048,16]{0,1:T(8,128)(2,1)}, u32[]{:S(2)}) copy-start(bf16[2048,16]{0,1:T(8,128)(2,1)} %param.30) | copy-start | bytes 196612
  0.7 34.5 %copy-start.7 = (f32[1024]{0:T(1024)S(1)}, f32[1024]{0:T(1024)}, u32[]{:S(2)}) copy-start(f32[1024]{0:T(1024)} %param.35) | copy-start | bytes 12292
  2.2 15.3 %all-to-all-start = ((bf16[8,4,2048]{2,1,0:T(4,128)(2,1)}), bf16[8,4,2048]{2,1,0:T(4,128)(2,1)S(1)}, u32[]{:S(2)}, u32[]{:S(2)}) async-start(bf16[8,4,2048]{2,1,0:T(4,128)(2,1)} %broadcast_in_dim.15), calls=%async_computation | async-start | bytes 262144 | tf_op jit(solution)/shard_map/all_to_all | solution.py:234
  20.4 35.5 %copy-start.8 = (s32[1,4,2]{1,2,0:T(2,128)S(1)}, s32[1,4,2]{1,2,0:T(2,128)}, u32[]{:S(2)}) copy-start(s32[1,4,2]{1,2,0:T(2,128)} %param.26) | copy-start | bytes 100
  26.1 30.4 %copy-start.3 = (bf16[32,1024]{1,0:T(8,128)(2,1)S(1)}, bf16[32,1024]{1,0:T(8,128)(2,1)}, u32[]{:S(2)}) copy-start(bf16[32,1024]{1,0:T(8,128)(2,1)} %get-tuple-element.13) | copy-start | bytes 196612
  26.1 37.8 %copy-start.2 = (bf16[1,4,2048]{2,1,0:T(4,128)(2,1)S(1)}, bf16[1,4,2048]{2,1,0:T(4,128)(2,1)}, u32[]{:S(2)}) copy-start(bf16[1,4,2048]{2,1,0:T(4,128)(2,1)} %param.22) | copy-start | bytes 49156
  26.1 38.0 %copy-start.6 = (f32[2048]{0:T(1024)S(1)}, f32[2048]{0:T(1024)}, u32[]{:S(2)}) copy-start(f32[2048]{0:T(1024)} %param.40) | copy-start | bytes 24580
  26.2 38.0 %copy-start.11 = (bf16[2048,8]{0,1:T(8,128)(2,1)S(1)}, bf16[2048,8]{0,1:T(8,128)(2,1)}, u32[]{:S(2)}) copy-start(bf16[2048,8]{0,1:T(8,128)(2,1)} %param.41) | copy-start | bytes 98308
  26.9 13.3 %all-to-all-start.1 = ((bf16[8,4,8,256]{3,2,1,0:T(8,128)(2,1)}), bf16[8,4,8,256]{3,2,1,0:T(8,128)(2,1)S(1)}, u32[]{:S(2)}, u32[]{:S(2)}) async-start(bf16[8,4,8,256]{3,2,1,0:T(8,128)(2,1)} %broadcast_in_dim.17), calls=%async_computation.1 | async-start | bytes 262144 | tf_op jit(solution)/shard_map/all_to_all | solution.py:234
  40.2 0.7 copy-start.1
  52.3 11.6 %all-to-all-start.2 = ((f32[8,4,2048]{2,1,0:T(4,128)}), f32[8,4,2048]{2,1,0:T(4,128)S(1)}, u32[]{:S(2)}, u32[]{:S(2)}) async-start(f32[8,4,2048]{2,1,0:T(4,128)} %fusion), calls=%async_computation.2 | async-start | bytes 524288 | tf_op jit(solution)/shard_map/all_to_all | solution.py:349
  65.2 10.2 %all-to-all-start.3 = ((bf16[8,2,2048]{2,1,0:T(2,128)(2,1)}), bf16[8,2,2048]{2,1,0:T(2,128)(2,1)S(1)}, u32[]{:S(2)}, u32[]{:S(2)}) async-start(bf16[8,2,2048]{2,1,0:T(2,128)(2,1)} %reshape_broadcast_in_dim_reshape.3), calls=%async_computation.3 | async-start | bytes 131072 | tf_op jit(solution)/shard_map/all_to_all | solution.py:364
  84.2 10.2 %all-to-all-start.4 = ((bf16[8,2,2048]{2,1,0:T(2,128)(2,1)}), bf16[8,2,2048]{2,1,0:T(2,128)(2,1)S(1)}, u32[]{:S(2)}, u32[]{:S(2)}) async-start(bf16[8,2,2048]{2,1,0:T(2,128)(2,1)} %convert_element_type.100), calls=%async_computation.4 | async-start | bytes 131072 | tf_op jit(solution)/shard_map/all_to_all | solution.py:370

commit v16 on v15

--- a/solution.py
+++ b/solution.py
@@ -73,8 +73,16 @@
     )(rows, weight)
 
 
-def xz_matmul_kernel(head_dim, a_ref, w_ref, x_ref, z_ref):
-    product = jnp.dot(a_ref[...], w_ref[...], preferred_element_type=jnp.float32)
+def xz_matmul_kernel(head_dim, a_ref, g_ref, w_ref, n_ref, x_ref, z_ref, normed_ref):
+    @pl.when(pl.program_id(0) == 0)
+    def _():
+        values = a_ref[...].astype(jnp.float32)
+        mean_square = jnp.mean(values * values, axis=-1, keepdims=True)
+        normed = (values * lax.rsqrt(mean_square + eps) * g_ref[...]).astype(jnp.bfloat16)
+        normed_ref[...] = normed
+        n_ref[...] = normed
+
+    product = jnp.dot(normed_ref[...], w_ref[...], preferred_element_type=jnp.float32)
     width = z_ref.shape[1]
     for h in range(width // head_dim):
         x_ref[:, h * head_dim : (h + 1) * head_dim] = product[
@@ -85,7 +93,7 @@
         ]
 
 
-def xz_matmul(rows, weight, head_dim):
+def xz_matmul(rows, gain, weight, head_dim):
     m, k = rows.shape
     cols = weight.shape[1]
     block = min(512, cols)
@@ -94,22 +102,26 @@
         grid=(cols // block,),
         in_specs=[
             pl.BlockSpec((m, k), lambda j: (0, 0)),
+            pl.BlockSpec((1, k), lambda j: (0, 0)),
             pl.BlockSpec((k, block), lambda j: (0, j)),
         ],
         out_specs=[
+            pl.BlockSpec((m, k), lambda j: (0, 0)),
             pl.BlockSpec((m, block // 2), lambda j: (0, j)),
             pl.BlockSpec((m, block // 2), lambda j: (0, j)),
         ],
         out_shape=[
+            jax.ShapeDtypeStruct((m, k), jnp.bfloat16),
             jax.ShapeDtypeStruct((m, cols // 2), jnp.bfloat16),
             jax.ShapeDtypeStruct((m, cols // 2), jnp.float32),
         ],
+        scratch_shapes=[pltpu.VMEM((m, k), jnp.bfloat16)],
         cost_estimate=pl.CostEstimate(
             flops=2 * m * k * cols,
-            transcendentals=0,
-            bytes_accessed=2 * (m * k + k * cols) + 3 * m * cols,
+            transcendentals=m,
+            bytes_accessed=2 * (2 * m * k + k * cols) + 3 * m * cols,
         ),
-    )(rows, weight)
+    )(rows, gain.reshape(1, k), weight)
 
 
 def ssm_scan_kernel(s_ref, dec_ref, dx_ref, b_ref, c_ref, s_out_ref, read_ref, bb_ref, cb_ref):
@@ -268,14 +280,13 @@
     state_dim = ssm_state.shape[4]
     gathered = broadcast_gather(tokens[0], head_count)
     inputs = gathered.reshape(requests * STEPS, width)
-    normed = norm_rows(inputs.astype(jnp.float32), mixer_gain).astype(jnp.bfloat16)
+    normed, x_rows, z_rows = xz_matmul(inputs, mixer_gain, weight_xz, head_dim)
     bc_fresh = (
         jnp.dot(normed, weight_bc, preferred_element_type=jnp.float32)
         .reshape(requests, STEPS, -1)
         .astype(jnp.bfloat16)
     )
     bc_conv, conv_bc_new = causal_conv(conv_bc_state[0], bc_fresh, conv_bc_kernel, conv_bc_bias)
-    x_rows, z_rows = xz_matmul(normed, weight_xz, head_dim)
     bc_conv, x_rows, z_rows = lax.optimization_barrier((bc_conv.astype(jnp.bfloat16), x_rows, z_rows))
     bc_blocks = broadcast_gather(bc_conv, head_count)
     x_fresh = x_rows.reshape(requests, STEPS, heads_local * head_dim)

time: 96.3 us -> 95.4 us (level)
  other arithmetic: 5.88 us -> 4.28 us
  matrix products: 13.6 us -> 14.7 us
    convert_element_type x1 -> x0, other arithmetic: 1.43 us -> none  [shards(): norm_rows(inputs.astype(jnp.float32), mixer_gain).astype(jnp.bfloat16)]
    unnamed x29 -> x26, local copies, waits for them, and re-layouts: 4.16 us -> 3.44 us
  transfers between devices with their start and end apart: 5 -> 5, of which waited for: 4 -> 4; matrix products, arithmetic and copies ran while one was open for 17% -> 18% of each run, Pallas kernels for 0% -> 0%
where the time goes in v16:
time: 95.4 us; the launch traced here: 94.3 us
  starting transfers between devices  23.4 us (25%)
  waiting for transfers between devices  20.5 us (21%)
  local copies, waits for them, and re-layouts  17.8 us (19%)
  matrix products  14.7 us (15%)
  Pallas kernels  12.7 us (13%)
  other arithmetic  4.28 us (4%)
    all_to_all x2, starting transfers between devices, broadcast_gather(): return lax.all_to_all(copies, 'head', 0, 0, tiled=True)  13.2 us
    dot_general x1, matrix products, shards(): jnp.dot(hidden, weight_down, preferred_element_type=jnp.float32)  8.05 us
    pallas_call x1, Pallas kernels, ssm_scan_direct(): pl.pallas_call(functools.partial(ssm_scan_direct_kernel, head_dim), grid_...  6.88 us
    all_to_all x1, waiting for transfers between devices, shards(): lax.all_to_all(computed.astype(jnp.bfloat16), 'head', split_axis=0, conca...  6.81 us
    all_to_all x1, waiting for transfers between devices, shards(): lax.all_to_all(outgoing, 'head', split_axis=0, concat_axis=0, tiled=True)  6.55 us
    pallas_call x1, Pallas kernels, xz_matmul(): pl.pallas_call(functools.partial(xz_matmul_kernel, head_dim), grid=(cols...  5.85 us
    all_to_all x1, waiting for transfers between devices, shards(): lax.all_to_all(mixer_part.reshape(head_count, tok_local, width), 'head',...  4.44 us
    dot_general x1, matrix products, shards(): jnp.dot(group_normed, weight_out, preferred_element_type=jnp.float32)  3.72 us
  transfers between devices with their start and end apart: 5, of which 4 were waited for; matrix products, arithmetic and copies ran while one was open for 18% of the time, Pallas kernels for 0%

profile of v16, /device:TPU:0, one launch (start us, length us, event | category | flops | bytes accessed | tf_op | source)
XLA Modules:
  0.0 94.3 jit_solution(12801520826827994629)
XLA Ops:
  0.6 0.0 copy-start
  0.6 0.0 copy-start.8
  0.7 1.5 %broadcast_in_dim.15 = bf16[8,4,2048]{2,1,0:T(4,128)(2,1)} broadcast(bf16[4,2048]{1,0:T(4,128)(2,1)} %bitcast.83), dimensions={1,2} | broadcast | bytes 147456 | tf_op jit(solution)/shard_map/broadcast_in_dim | solution.py:245
  2.2 7.3 %all-to-all-start = ((bf16[8,4,2048]{2,1,0:T(4,128)(2,1)}), bf16[8,4,2048]{2,1,0:T(4,128)(2,1)S(1)}, u32[]{:S(2)}, u32[]{:S(2)}) async-start(bf16[8,4,2048]{2,1,0:T(4,128)(2,1)} %broadcast_in_dim.15), calls=%async_computation | async-start | bytes 262144 | tf_op jit(solution)/shard_map/all_to_all | solution.py:246
  9.4 0.7 exponential_negate_fusion
  10.1 0.8 copy.68
  10.9 0.1 reshape_squeeze.7
  10.9 0.1 fusion.24
  11.0 0.8 fusion.30
  11.9 0.2 select_reduce_fusion
  12.1 0.7 copy.63
  12.8 0.7 mul.196
  13.5 0.1 mul.197
  13.6 0.8 copy.83
  14.3 2.3 %copy.64.s_ref = bf16[4,8,128,128]{3,2,1,0:T(8,128)(2,1)} copy(bf16[4,8,128,128]{2,3,1,0:T(8,128)(2,1)} %bitcast.81) | data formatting | bytes 2097152 | tf_op jit(solution)/shard_map/reshape | solution.py:319
  16.6 0.9 fusion.29
  17.5 0.0 all-to-all-done
  17.5 0.7 reshape.143.a_ref
  18.2 5.8 %shard_map.237 = (bf16[32,2048]{1,0:T(8,128)(2,1)}, bf16[32,1024]{1,0:T(8,128)(2,1)}, f32[32,1024]{1,0:T(8,128)}) custom-call(bf16[32,2048]{1,0:T(8,128)(2,1)} %reshape.143.a_ref, f32[1,2048]{1,0:T(1,128)} %bitcast.92, bf16[2048,2048]{1,0:T(8,128)(2,1)} %w_ref.1), custom_call_target="tpu_custom_call" | custom-call | flops 268435456 | bytes 8847360 | tf_op jit(solution)/shard_map/pallas_call | solution.py:100
  24.0 0.0 copy-start.2
  24.0 0.0 copy-start.5
  24.0 0.0 copy-start.10
  24.1 0.0 copy-done
  24.1 1.2 %fusion.5 = bf16[4,8,256]{2,1,0:T(8,128)(2,1)S(1)} fusion(bf16[32,2048]{1,0:T(8,128)(2,1)} %get-tuple-element.12, bf16[2048,256]{1,0:T(8,128)(2,1)S(1)} %copy-done), kind=kOutput, calls=%fused_computation.10 | convolution fusion | flops 33562624 | bytes 1196032 | tf_op jit(solution)/shard_map/dot_general | solution.py:285
  25.3 0.0 copy-done.8
  25.4 0.7 broadcast_in_dim.17
  26.0 6.0 %all-to-all-start.1 = ((bf16[8,4,8,256]{3,2,1,0:T(8,128)(2,1)}), bf16[8,4,8,256]{3,2,1,0:T(8,128)(2,1)S(1)}, u32[]{:S(2)}, u32[]{:S(2)}) async-start(bf16[8,4,8,256]{3,2,1,0:T(8,128)(2,1)} %broadcast_in_dim.17), calls=%async_computation.1 | async-start | bytes 262144 | tf_op jit(solution)/shard_map/all_to_all | solution.py:246
  32.0 1.1 %multiply_exponential_fusion = (f32[4,8,16]{2,1,0:T(8,128)S(1)}, f32[4,8,16]{2,1,0:T(8,128)S(1)}) fusion(f32[16]{0:T(128)S(1)} %exponential_negate_fusion, f32[16]{0:T(128)S(1)} %copy-done.9, bf16[32,2048]{1,0:T(8,128)(2,1)} %get-tuple-element.12, bf16[2048,16]{0,1:T(8,128)(2,1)S(1)} %copy-done.4), kind=kOutput, calls=%fused_computation.48 | convolution fusion | flops 2101248 | bytes 200832 | tf_op jit(solution)/shard_map/dot_general | solution.py:295
  33.1 0.1 broadcast_in_dim.16
  33.3 0.8 reshape.146.dec_ref
  34.1 0.1 mul.167
  34.2 0.1 mul.168
  34.3 0.9 maximum_convert_fusion
  35.2 0.7 broadcast_multiply_fusion
  36.0 0.7 mul.195.dx_ref
  36.6 2.8 %all-to-all-done.1.b_ref.c_ref = bf16[8,4,8,256]{3,2,1,0:T(8,128)(2,1)S(1)} async-done(((bf16[8,4,8,256]{3,2,1,0:T(8,128)(2,1)}), bf16[8,4,8,256]{3,2,1,0:T(8,128)(2,1)S(1)}, u32[]{:S(2)}, u32[]{:S(2)}) %all-to-all-start.1) | async-done | bytes 131104 | tf_op jit(solution)/shard_map/all_to_all | solution.py:246
  39.4 0.6 copy-done.1
  40.0 6.9 %shard_map.238 = (bf16[4,8,128,128]{3,2,1,0:T(8,128)(2,1)}, f32[4,8,1024]{2,1,0:T(8,128)}, bf16[4,8,1024]{2,1,0:T(8,128)(2,1)}) custom-call(s32[1]{0:T(128)S(6)} %select_n.16.group_ref, bf16[4,8,128,128]{3,2,1,0:T(8,128)(2,1)} %copy.64.s_ref, f32[4,8,1024]{2,1,0:T(8,128)} %reshape.146.dec_ref, f32[4,8,1024]{2,1,0:T(8,128)} %mul.195.dx_ref, ...), custom_call_target="tpu_custom_call" | custom-call | tf_op jit(solution)/shard_map/pallas_call | solution.py:215
  46.9 0.9 dot_general.31
  47.8 3.7 %fusion = f32[8,4,2048]{2,1,0:T(4,128)} fusion(bf16[8,4,1024]{2,1,0:T(4,128)(2,1)S(1)} %dot_general.31, bf16[1024,2048]{1,0:T(8,128)(2,1)} %param.39), kind=kOutput, calls=%fused_computation | convolution fusion | flops 134217728 | bytes 4521984 | tf_op jit(solution)/shard_map/dot_general | solution.py:359
  51.5 3.4 %all-to-all-start.2 = ((f32[8,4,2048]{2,1,0:T(4,128)}), f32[8,4,2048]{2,1,0:T(4,128)S(1)}, u32[]{:S(2)}, u32[]{:S(2)}) async-start(f32[8,4,2048]{2,1,0:T(4,128)} %fusion), calls=%async_computation.2 | async-start | bytes 524288 | tf_op jit(solution)/shard_map/all_to_all | solution.py:360
  54.9 0.1 copy.67
  55.0 0.1 iota_compare_fusion.3
  55.1 0.6 copy.84
  55.7 0.0 copy-done.3
  55.7 0.6 copy.72
  56.4 2.3 %copy.70 = bf16[4,8,128,128]{2,3,1,0:T(8,128)(2,1)} copy(bf16[4,8,128,128]{3,2,1,0:T(8,128)(2,1)} %get-tuple-element.19) | data formatting | bytes 2097152 | tf_op jit(solution)/shard_map/pallas_call | solution.py:215
  58.6 4.4 %all-to-all-done.2 = f32[8,4,2048]{2,1,0:T(4,128)S(1)} async-done(((f32[8,4,2048]{2,1,0:T(4,128)}), f32[8,4,2048]{2,1,0:T(4,128)S(1)}, u32[]{:S(2)}, u32[]{:S(2)}) %all-to-all-start.2) | async-done | bytes 262176 | tf_op jit(solution)/shard_map/all_to_all | solution.py:360
  63.1 0.1 fusion.12
  63.3 0.0 copy-done.5
  63.3 0.1 fusion.14
  63.4 0.1 fusion.31
  63.5 0.1 convolution_convert_fusion
  63.7 0.7 reshape_broadcast_in_dim_reshape.3
  64.4 3.3 %all-to-all-start.3 = ((bf16[8,2,2048]{2,1,0:T(2,128)(2,1)}), bf16[8,2,2048]{2,1,0:T(2,128)(2,1)S(1)}, u32[]{:S(2)}, u32[]{:S(2)}) async-start(bf16[8,2,2048]{2,1,0:T(2,128)(2,1)} %reshape_broadcast_in_dim_reshape.3), calls=%async_computation.3 | async-start | bytes 131072 | tf_op jit(solution)/shard_map/all_to_all | solution.py:375
  67.7 0.2 fusion.21
  67.9 0.1 copy.77
  68.0 6.5 %all-to-all-done.3 = bf16[8,2,2048]{2,1,0:T(2,128)(2,1)S(1)} async-done(((bf16[8,2,2048]{2,1,0:T(2,128)(2,1)}), bf16[8,2,2048]{2,1,0:T(2,128)(2,1)S(1)}, u32[]{:S(2)}, u32[]{:S(2)}) %all-to-all-start.3) | async-done | bytes 65568 | tf_op jit(solution)/shard_map/all_to_all | solution.py:375
  74.6 8.0 %convolution_convert_fusion.1 = bf16[16,2048]{1,0:T(8,128)(2,1)S(1)} fusion(bf16[2048,2048]{1,0:T(8,128)(2,1)} %param.43, bf16[16,2048]{1,0:T(8,128)(2,1)S(1)} %reshape.150, bf16[2048,2048]{1,0:T(8,128)(2,1)} %param.42), kind=kOutput, calls=%fused_computation.6 | convolution fusion | flops 268566528 | bytes 16908288 | tf_op jit(solution)/shard_map/dot_general | solution.py:378
  82.7 0.7 convert_element_type.76
  83.3 3.3 %all-to-all-start.4 = ((bf16[8,2,2048]{2,1,0:T(2,128)(2,1)}), bf16[8,2,2048]{2,1,0:T(2,128)(2,1)S(1)}, u32[]{:S(2)}, u32[]{:S(2)}) async-start(bf16[8,2,2048]{2,1,0:T(2,128)(2,1)} %convert_element_type.76), calls=%async_computation.4 | async-start | bytes 131072 | tf_op jit(solution)/shard_map/all_to_all | solution.py:381
  86.7 6.8 %all-to-all-done.4 = bf16[8,2,2048]{2,1,0:T(2,128)(2,1)S(1)} async-done(((bf16[8,2,2048]{2,1,0:T(2,128)(2,1)}), bf16[8,2,2048]{2,1,0:T(2,128)(2,1)S(1)}, u32[]{:S(2)}, u32[]{:S(2)}) %all-to-all-start.4) | async-done | bytes 65568 | tf_op jit(solution)/shard_map/all_to_all | solution.py:381
  93.6 0.1 fusion.4
  93.7 0.6 fusion.19
  (27 shorter events, 0.3 us)
Async XLA Ops:
  0.6 23.4 %copy-start = (bf16[2048,256]{1,0:T(8,128)(2,1)S(1)}, bf16[2048,256]{1,0:T(8,128)(2,1)}, u32[]{:S(2)}) copy-start(bf16[2048,256]{1,0:T(8,128)(2,1)} %param.29) | copy-start | bytes 3145732
  0.6 24.7 %copy-start.8 = (f32[256]{0:T(256)S(1)}, f32[256]{0:T(256)}, u32[]{:S(2)}) copy-start(f32[256]{0:T(256)} %param.37) | copy-start | bytes 3076
  0.7 31.4 %copy-start.9 = (f32[16]{0:T(128)S(1)}, f32[16]{0:T(128)}, u32[]{:S(2)}) copy-start(f32[16]{0:T(128)} %param.31) | copy-start | bytes 196
  0.7 31.4 %copy-start.4 = (bf16[2048,16]{0,1:T(8,128)(2,1)S(1)}, bf16[2048,16]{0,1:T(8,128)(2,1)}, u32[]{:S(2)}) copy-start(bf16[2048,16]{0,1:T(8,128)(2,1)} %param.30) | copy-start | bytes 196612
  0.7 34.5 %copy-start.6 = (f32[1024]{0:T(1024)S(1)}, f32[1024]{0:T(1024)}, u32[]{:S(2)}) copy-start(f32[1024]{0:T(1024)} %param.35) | copy-start | bytes 12292
  2.2 15.3 %all-to-all-start = ((bf16[8,4,2048]{2,1,0:T(4,128)(2,1)}), bf16[8,4,2048]{2,1,0:T(4,128)(2,1)S(1)}, u32[]{:S(2)}, u32[]{:S(2)}) async-start(bf16[8,4,2048]{2,1,0:T(4,128)(2,1)} %broadcast_in_dim.15), calls=%async_computation | async-start | bytes 262144 | tf_op jit(solution)/shard_map/all_to_all | solution.py:246
  24.0 30.9 %copy-start.7 = (s32[1,4,2]{1,2,0:T(2,128)S(1)}, s32[1,4,2]{1,2,0:T(2,128)}, u32[]{:S(2)}) copy-start(s32[1,4,2]{1,2,0:T(2,128)} %param.26) | copy-start | bytes 100
  24.0 31.7 %copy-start.3 = (bf16[32,1024]{1,0:T(8,128)(2,1)S(1)}, bf16[32,1024]{1,0:T(8,128)(2,1)}, u32[]{:S(2)}) copy-start(bf16[32,1024]{1,0:T(8,128)(2,1)} %get-tuple-element.15) | copy-start | bytes 196612
  24.0 39.1 %copy-start.2 = (bf16[1,4,2048]{2,1,0:T(4,128)(2,1)S(1)}, bf16[1,4,2048]{2,1,0:T(4,128)(2,1)}, u32[]{:S(2)}) copy-start(bf16[1,4,2048]{2,1,0:T(4,128)(2,1)} %param.22) | copy-start | bytes 49156
  24.0 39.2 %copy-start.5 = (f32[2048]{0:T(1024)S(1)}, f32[2048]{0:T(1024)}, u32[]{:S(2)}) copy-start(f32[2048]{0:T(1024)} %param.40) | copy-start | bytes 24580
  24.0 39.3 %copy-start.10 = (bf16[2048,8]{0,1:T(8,128)(2,1)S(1)}, bf16[2048,8]{0,1:T(8,128)(2,1)}, u32[]{:S(2)}) copy-start(bf16[2048,8]{0,1:T(8,128)(2,1)} %param.41) | copy-start | bytes 98308
  26.0 13.3 %all-to-all-start.1 = ((bf16[8,4,8,256]{3,2,1,0:T(8,128)(2,1)}), bf16[8,4,8,256]{3,2,1,0:T(8,128)(2,1)S(1)}, u32[]{:S(2)}, u32[]{:S(2)}) async-start(bf16[8,4,8,256]{3,2,1,0:T(8,128)(2,1)} %broadcast_in_dim.17), calls=%async_computation.1 | async-start | bytes 262144 | tf_op jit(solution)/shard_map/all_to_all | solution.py:246
  39.4 0.6 copy-start.1
  51.5 11.6 %all-to-all-start.2 = ((f32[8,4,2048]{2,1,0:T(4,128)}), f32[8,4,2048]{2,1,0:T(4,128)S(1)}, u32[]{:S(2)}, u32[]{:S(2)}) async-start(f32[8,4,2048]{2,1,0:T(4,128)} %fusion), calls=%async_computation.2 | async-start | bytes 524288 | tf_op jit(solution)/shard_map/all_to_all | solution.py:360
  64.4 10.2 %all-to-all-start.3 = ((bf16[8,2,2048]{2,1,0:T(2,128)(2,1)}), bf16[8,2,2048]{2,1,0:T(2,128)(2,1)S(1)}, u32[]{:S(2)}, u32[]{:S(2)}) async-start(bf16[8,2,2048]{2,1,0:T(2,128)(2,1)} %reshape_broadcast_in_dim_reshape.3), calls=%async_computation.3 | async-start | bytes 131072 | tf_op jit(solution)/shard_map/all_to_all | solution.py:375
  83.3 10.2 %all-to-all-start.4 = ((bf16[8,2,2048]{2,1,0:T(2,128)(2,1)}), bf16[8,2,2048]{2,1,0:T(2,128)(2,1)S(1)}, u32[]{:S(2)}, u32[]{:S(2)}) async-start(bf16[8,2,2048]{2,1,0:T(2,128)(2,1)} %convert_element_type.76), calls=%async_computation.4 | async-start | bytes 131072 | tf_op jit(solution)/shard_map/all_to_all | solution.py:381

commit v17 on v16

--- a/solution.py
+++ b/solution.py
@@ -378,9 +378,7 @@
     computed = jnp.dot(hidden, weight_down, preferred_element_type=jnp.float32).reshape(
         received.shape[0], received.shape[1], width
     )
-    returned = lax.all_to_all(
-        computed.astype(jnp.bfloat16), "head", split_axis=0, concat_axis=0, tiled=True
-    ).astype(computed.dtype)
+    returned = lax.all_to_all(computed, "head", split_axis=0, concat_axis=0, tiled=True)
     summed = (
         returned.reshape(EXPERTS, per_expert, CAP, width).sum(axis=1).reshape(EXPERTS * CAP, width)
     )

time: 95.4 us -> 96.1 us (level)
  transfers between devices with their start and end apart: 5 -> 5, of which waited for: 4 -> 4; matrix products, arithmetic and copies ran while one was open for 18% -> 17% of each run, Pallas kernels for 0% -> 0%
where the time goes in v17:
time: 96.1 us; the launch traced here: 95 us
  starting transfers between devices  23.4 us (24%)
  waiting for transfers between devices  21 us (22%)
  local copies, waits for them, and re-layouts  17.9 us (19%)
  matrix products  14.7 us (15%)
  Pallas kernels  12.7 us (13%)
  other arithmetic  4.28 us (4%)
    all_to_all x2, starting transfers between devices, broadcast_gather(): return lax.all_to_all(copies, 'head', 0, 0, tiled=True)  13.2 us
    dot_general x1, matrix products, shards(): jnp.dot(hidden, weight_down, preferred_element_type=jnp.float32)  8.05 us
    all_to_all x1, waiting for transfers between devices, shards(): lax.all_to_all(computed, 'head', split_axis=0, concat_axis=0, tiled=True)  7.25 us
    pallas_call x1, Pallas kernels, ssm_scan_direct(): pl.pallas_call(functools.partial(ssm_scan_direct_kernel, head_dim), grid_...  6.88 us
    all_to_all x1, waiting for transfers between devices, shards(): lax.all_to_all(outgoing, 'head', split_axis=0, concat_axis=0, tiled=True)  6.55 us
    pallas_call x1, Pallas kernels, xz_matmul(): pl.pallas_call(functools.partial(xz_matmul_kernel, head_dim), grid=(cols...  5.85 us
    all_to_all x1, waiting for transfers between devices, shards(): lax.all_to_all(mixer_part.reshape(head_count, tok_local, width), 'head',...  4.44 us
    dot_general x1, matrix products, shards(): jnp.dot(group_normed, weight_out, preferred_element_type=jnp.float32)  3.72 us
  transfers between devices with their start and end apart: 5, of which 4 were waited for; matrix products, arithmetic and copies ran while one was open for 17% of the time, Pallas kernels for 0%

profile of v17, /device:TPU:0, one launch (start us, length us, event | category | flops | bytes accessed | tf_op | source)
XLA Modules:
  0.0 95.0 jit_solution(1754931705180004110)
XLA Ops:
  0.6 0.0 copy-start
  0.7 1.5 %broadcast_in_dim.15 = bf16[8,4,2048]{2,1,0:T(4,128)(2,1)} broadcast(bf16[4,2048]{1,0:T(4,128)(2,1)} %bitcast.83), dimensions={1,2} | broadcast | bytes 147456 | tf_op jit(solution)/shard_map/broadcast_in_dim | solution.py:245
  2.2 7.3 %all-to-all-start = ((bf16[8,4,2048]{2,1,0:T(4,128)(2,1)}), bf16[8,4,2048]{2,1,0:T(4,128)(2,1)S(1)}, u32[]{:S(2)}, u32[]{:S(2)}) async-start(bf16[8,4,2048]{2,1,0:T(4,128)(2,1)} %broadcast_in_dim.15), calls=%async_computation | async-start | bytes 262144 | tf_op jit(solution)/shard_map/all_to_all | solution.py:246
  9.4 0.7 exponential_negate_fusion
  10.1 0.8 copy.68
  10.9 0.1 reshape_squeeze.7
  10.9 0.1 fusion.25
  11.0 0.8 fusion.31
  11.9 0.2 select_reduce_fusion
  12.1 0.7 copy.63
  12.8 0.7 mul.196
  13.5 0.1 mul.197
  13.6 0.8 copy.83
  14.3 2.3 %copy.64.s_ref = bf16[4,8,128,128]{3,2,1,0:T(8,128)(2,1)} copy(bf16[4,8,128,128]{2,3,1,0:T(8,128)(2,1)} %bitcast.81) | data formatting | bytes 2097152 | tf_op jit(solution)/shard_map/reshape | solution.py:319
  16.6 0.9 fusion.30
  17.5 0.0 all-to-all-done
  17.5 0.7 reshape.144.a_ref
  18.2 5.8 %shard_map.237 = (bf16[32,2048]{1,0:T(8,128)(2,1)}, bf16[32,1024]{1,0:T(8,128)(2,1)}, f32[32,1024]{1,0:T(8,128)}) custom-call(bf16[32,2048]{1,0:T(8,128)(2,1)} %reshape.144.a_ref, f32[1,2048]{1,0:T(1,128)} %bitcast.92, bf16[2048,2048]{1,0:T(8,128)(2,1)} %w_ref.1), custom_call_target="tpu_custom_call" | custom-call | flops 268435456 | bytes 8847360 | tf_op jit(solution)/shard_map/pallas_call | solution.py:100
  24.0 0.0 copy-start.2
  24.0 0.0 copy-start.5
  24.0 0.0 copy-start.10
  24.1 0.0 copy-done
  24.1 1.2 %fusion.5 = bf16[4,8,256]{2,1,0:T(8,128)(2,1)S(1)} fusion(bf16[32,2048]{1,0:T(8,128)(2,1)} %get-tuple-element.12, bf16[2048,256]{1,0:T(8,128)(2,1)S(1)} %copy-done), kind=kOutput, calls=%fused_computation.9 | convolution fusion | flops 33562624 | bytes 1196032 | tf_op jit(solution)/shard_map/dot_general | solution.py:285
  25.3 0.0 copy-done.8
  25.4 0.7 broadcast_in_dim.17
  26.0 6.0 %all-to-all-start.1 = ((bf16[8,4,8,256]{3,2,1,0:T(8,128)(2,1)}), bf16[8,4,8,256]{3,2,1,0:T(8,128)(2,1)S(1)}, u32[]{:S(2)}, u32[]{:S(2)}) async-start(bf16[8,4,8,256]{3,2,1,0:T(8,128)(2,1)} %broadcast_in_dim.17), calls=%async_computation.1 | async-start | bytes 262144 | tf_op jit(solution)/shard_map/all_to_all | solution.py:246
  32.0 1.1 %multiply_exponential_fusion = (f32[4,8,16]{2,1,0:T(8,128)S(1)}, f32[4,8,16]{2,1,0:T(8,128)S(1)}) fusion(f32[16]{0:T(128)S(1)} %exponential_negate_fusion, f32[16]{0:T(128)S(1)} %copy-done.9, bf16[32,2048]{1,0:T(8,128)(2,1)} %get-tuple-element.12, bf16[2048,16]{0,1:T(8,128)(2,1)S(1)} %copy-done.4), kind=kOutput, calls=%fused_computation.48 | convolution fusion | flops 2101248 | bytes 200832 | tf_op jit(solution)/shard_map/dot_general | solution.py:295
  33.1 0.1 broadcast_in_dim.16
  33.3 0.8 reshape.147.dec_ref
  34.1 0.1 mul.167
  34.2 0.1 mul.168
  34.3 0.9 maximum_convert_fusion
  35.2 0.7 broadcast_multiply_fusion
  36.0 0.7 mul.195.dx_ref
  36.6 2.8 %all-to-all-done.1.b_ref.c_ref = bf16[8,4,8,256]{3,2,1,0:T(8,128)(2,1)S(1)} async-done(((bf16[8,4,8,256]{3,2,1,0:T(8,128)(2,1)}), bf16[8,4,8,256]{3,2,1,0:T(8,128)(2,1)S(1)}, u32[]{:S(2)}, u32[]{:S(2)}) %all-to-all-start.1) | async-done | bytes 131104 | tf_op jit(solution)/shard_map/all_to_all | solution.py:246
  39.4 0.6 copy-done.1
  40.0 6.9 %shard_map.238 = (bf16[4,8,128,128]{3,2,1,0:T(8,128)(2,1)}, f32[4,8,1024]{2,1,0:T(8,128)}, bf16[4,8,1024]{2,1,0:T(8,128)(2,1)}) custom-call(s32[1]{0:T(128)S(6)} %select_n.16.group_ref, bf16[4,8,128,128]{3,2,1,0:T(8,128)(2,1)} %copy.64.s_ref, f32[4,8,1024]{2,1,0:T(8,128)} %reshape.147.dec_ref, f32[4,8,1024]{2,1,0:T(8,128)} %mul.195.dx_ref, ...), custom_call_target="tpu_custom_call" | custom-call | tf_op jit(solution)/shard_map/pallas_call | solution.py:215
  46.9 0.9 dot_general.31
  47.8 3.7 %fusion = f32[8,4,2048]{2,1,0:T(4,128)} fusion(bf16[8,4,1024]{2,1,0:T(4,128)(2,1)S(1)} %dot_general.31, bf16[1024,2048]{1,0:T(8,128)(2,1)} %param.39), kind=kOutput, calls=%fused_computation | convolution fusion | flops 134217728 | bytes 4521984 | tf_op jit(solution)/shard_map/dot_general | solution.py:359
  51.5 3.4 %all-to-all-start.2 = ((f32[8,4,2048]{2,1,0:T(4,128)}), f32[8,4,2048]{2,1,0:T(4,128)S(1)}, u32[]{:S(2)}, u32[]{:S(2)}) async-start(f32[8,4,2048]{2,1,0:T(4,128)} %fusion), calls=%async_computation.2 | async-start | bytes 524288 | tf_op jit(solution)/shard_map/all_to_all | solution.py:360
  54.9 0.1 copy.67
  55.0 0.1 iota_compare_fusion.3
  55.1 0.6 copy.84
  55.7 0.0 copy-done.3
  55.7 0.6 copy.72
  56.4 2.3 %copy.70 = bf16[4,8,128,128]{2,3,1,0:T(8,128)(2,1)} copy(bf16[4,8,128,128]{3,2,1,0:T(8,128)(2,1)} %get-tuple-element.19) | data formatting | bytes 2097152 | tf_op jit(solution)/shard_map/pallas_call | solution.py:215
  58.6 4.4 %all-to-all-done.2 = f32[8,4,2048]{2,1,0:T(4,128)S(1)} async-done(((f32[8,4,2048]{2,1,0:T(4,128)}), f32[8,4,2048]{2,1,0:T(4,128)S(1)}, u32[]{:S(2)}, u32[]{:S(2)}) %all-to-all-start.2) | async-done | bytes 262176 | tf_op jit(solution)/shard_map/all_to_all | solution.py:360
  63.1 0.1 fusion.13
  63.3 0.0 copy-done.5
  63.3 0.1 fusion.15
  63.4 0.1 fusion.32
  63.5 0.1 convolution_convert_fusion
  63.7 0.7 reshape_broadcast_in_dim_reshape.3
  64.4 3.3 %all-to-all-start.3 = ((bf16[8,2,2048]{2,1,0:T(2,128)(2,1)}), bf16[8,2,2048]{2,1,0:T(2,128)(2,1)S(1)}, u32[]{:S(2)}, u32[]{:S(2)}) async-start(bf16[8,2,2048]{2,1,0:T(2,128)(2,1)} %reshape_broadcast_in_dim_reshape.3), calls=%async_computation.3 | async-start | bytes 131072 | tf_op jit(solution)/shard_map/all_to_all | solution.py:375
  67.7 0.2 fusion.22
  67.9 0.1 copy.77
  68.0 6.5 %all-to-all-done.3 = bf16[8,2,2048]{2,1,0:T(2,128)(2,1)S(1)} async-done(((bf16[8,2,2048]{2,1,0:T(2,128)(2,1)}), bf16[8,2,2048]{2,1,0:T(2,128)(2,1)S(1)}, u32[]{:S(2)}, u32[]{:S(2)}) %all-to-all-start.3) | async-done | bytes 65568 | tf_op jit(solution)/shard_map/all_to_all | solution.py:375
  74.6 8.0 %fusion.7 = f32[16,2048]{1,0:T(8,128)S(1)} fusion(bf16[2048,2048]{1,0:T(8,128)(2,1)} %param.43, bf16[16,2048]{1,0:T(8,128)(2,1)S(1)} %reshape.151, bf16[2048,2048]{1,0:T(8,128)(2,1)} %param.42), kind=kOutput, calls=%fused_computation.12 | convolution fusion | flops 268533760 | bytes 16973824 | tf_op jit(solution)/shard_map/dot_general | solution.py:378
  82.7 0.7 reshape.152
  83.4 3.4 %all-to-all-start.4 = ((f32[8,2,2048]{2,1,0:T(2,128)}), f32[8,2,2048]{2,1,0:T(2,128)S(1)}, u32[]{:S(2)}, u32[]{:S(2)}) async-start(f32[8,2,2048]{2,1,0:T(2,128)} %reshape.152), calls=%async_computation.4 | async-start | bytes 262144 | tf_op jit(solution)/shard_map/all_to_all | solution.py:381
  86.8 7.2 %all-to-all-done.4 = f32[8,2,2048]{2,1,0:T(2,128)S(1)} async-done(((f32[8,2,2048]{2,1,0:T(2,128)}), f32[8,2,2048]{2,1,0:T(2,128)S(1)}, u32[]{:S(2)}, u32[]{:S(2)}) %all-to-all-start.4) | async-done | bytes 131104 | tf_op jit(solution)/shard_map/all_to_all | solution.py:381
  94.0 0.1 reshape.158
  94.1 0.2 fusion.4
  94.3 0.6 fusion.20
  (27 shorter events, 0.3 us)
Async XLA Ops:
  0.6 23.4 %copy-start = (bf16[2048,256]{1,0:T(8,128)(2,1)S(1)}, bf16[2048,256]{1,0:T(8,128)(2,1)}, u32[]{:S(2)}) copy-start(bf16[2048,256]{1,0:T(8,128)(2,1)} %param.29) | copy-start | bytes 3145732
  0.6 24.7 %copy-start.8 = (f32[256]{0:T(256)S(1)}, f32[256]{0:T(256)}, u32[]{:S(2)}) copy-start(f32[256]{0:T(256)} %param.37) | copy-start | bytes 3076
  0.7 31.4 %copy-start.9 = (f32[16]{0:T(128)S(1)}, f32[16]{0:T(128)}, u32[]{:S(2)}) copy-start(f32[16]{0:T(128)} %param.31) | copy-start | bytes 196
  0.7 31.4 %copy-start.4 = (bf16[2048,16]{0,1:T(8,128)(2,1)S(1)}, bf16[2048,16]{0,1:T(8,128)(2,1)}, u32[]{:S(2)}) copy-start(bf16[2048,16]{0,1:T(8,128)(2,1)} %param.30) | copy-start | bytes 196612
  0.7 34.5 %copy-start.6 = (f32[1024]{0:T(1024)S(1)}, f32[1024]{0:T(1024)}, u32[]{:S(2)}) copy-start(f32[1024]{0:T(1024)} %param.35) | copy-start | bytes 12292
  2.2 15.3 %all-to-all-start = ((bf16[8,4,2048]{2,1,0:T(4,128)(2,1)}), bf16[8,4,2048]{2,1,0:T(4,128)(2,1)S(1)}, u32[]{:S(2)}, u32[]{:S(2)}) async-start(bf16[8,4,2048]{2,1,0:T(4,128)(2,1)} %broadcast_in_dim.15), calls=%async_computation | async-start | bytes 262144 | tf_op jit(solution)/shard_map/all_to_all | solution.py:246
  24.0 30.9 %copy-start.7 = (s32[1,4,2]{1,2,0:T(2,128)S(1)}, s32[1,4,2]{1,2,0:T(2,128)}, u32[]{:S(2)}) copy-start(s32[1,4,2]{1,2,0:T(2,128)} %param.26) | copy-start | bytes 100
  24.0 31.7 %copy-start.3 = (bf16[32,1024]{1,0:T(8,128)(2,1)S(1)}, bf16[32,1024]{1,0:T(8,128)(2,1)}, u32[]{:S(2)}) copy-start(bf16[32,1024]{1,0:T(8,128)(2,1)} %get-tuple-element.15) | copy-start | bytes 196612
  24.0 39.1 %copy-start.2 = (bf16[1,4,2048]{2,1,0:T(4,128)(2,1)S(1)}, bf16[1,4,2048]{2,1,0:T(4,128)(2,1)}, u32[]{:S(2)}) copy-start(bf16[1,4,2048]{2,1,0:T(4,128)(2,1)} %param.22) | copy-start | bytes 49156
  24.0 39.2 %copy-start.5 = (f32[2048]{0:T(1024)S(1)}, f32[2048]{0:T(1024)}, u32[]{:S(2)}) copy-start(f32[2048]{0:T(1024)} %param.40) | copy-start | bytes 24580
  24.0 39.3 %copy-start.10 = (bf16[2048,8]{0,1:T(8,128)(2,1)S(1)}, bf16[2048,8]{0,1:T(8,128)(2,1)}, u32[]{:S(2)}) copy-start(bf16[2048,8]{0,1:T(8,128)(2,1)} %param.41) | copy-start | bytes 98308
  26.0 13.3 %all-to-all-start.1 = ((bf16[8,4,8,256]{3,2,1,0:T(8,128)(2,1)}), bf16[8,4,8,256]{3,2,1,0:T(8,128)(2,1)S(1)}, u32[]{:S(2)}, u32[]{:S(2)}) async-start(bf16[8,4,8,256]{3,2,1,0:T(8,128)(2,1)} %broadcast_in_dim.17), calls=%async_computation.1 | async-start | bytes 262144 | tf_op jit(solution)/shard_map/all_to_all | solution.py:246
  39.4 0.6 copy-start.1
  51.5 11.6 %all-to-all-start.2 = ((f32[8,4,2048]{2,1,0:T(4,128)}), f32[8,4,2048]{2,1,0:T(4,128)S(1)}, u32[]{:S(2)}, u32[]{:S(2)}) async-start(f32[8,4,2048]{2,1,0:T(4,128)} %fusion), calls=%async_computation.2 | async-start | bytes 524288 | tf_op jit(solution)/shard_map/all_to_all | solution.py:360
  64.4 10.2 %all-to-all-start.3 = ((bf16[8,2,2048]{2,1,0:T(2,128)(2,1)}), bf16[8,2,2048]{2,1,0:T(2,128)(2,1)S(1)}, u32[]{:S(2)}, u32[]{:S(2)}) async-start(bf16[8,2,2048]{2,1,0:T(2,128)(2,1)} %reshape_broadcast_in_dim_reshape.3), calls=%async_computation.3 | async-start | bytes 131072 | tf_op jit(solution)/shard_map/all_to_all | solution.py:375
  83.4 10.7 %all-to-all-start.4 = ((f32[8,2,2048]{2,1,0:T(2,128)}), f32[8,2,2048]{2,1,0:T(2,128)S(1)}, u32[]{:S(2)}, u32[]{:S(2)}) async-start(f32[8,2,2048]{2,1,0:T(2,128)} %reshape.152), calls=%async_computation.4 | async-start | bytes 262144 | tf_op jit(solution)/shard_map/all_to_all | solution.py:381

commit v18 on v16

--- a/solution.py
+++ b/solution.py
@@ -96,7 +96,7 @@
 def xz_matmul(rows, gain, weight, head_dim):
     m, k = rows.shape
     cols = weight.shape[1]
-    block = min(512, cols)
+    block = min(1024, cols)
     return pl.pallas_call(
         functools.partial(xz_matmul_kernel, head_dim),
         grid=(cols // block,),

time: 95.4 us -> 94.6 us (level)
  no operation moved by 1% of the time
where the time goes in v18:
time: 94.6 us; the launch traced here: 93.6 us
  starting transfers between devices  23.4 us (25%)
  waiting for transfers between devices  20.5 us (22%)
  local copies, waits for them, and re-layouts  17.8 us (19%)
  matrix products  14.7 us (16%)
  Pallas kernels  12 us (13%)
  other arithmetic  4.28 us (5%)
    all_to_all x2, starting transfers between devices, broadcast_gather(): return lax.all_to_all(copies, 'head', 0, 0, tiled=True)  13.2 us
    dot_general x1, matrix products, shards(): jnp.dot(hidden, weight_down, preferred_element_type=jnp.float32)  8.05 us
    pallas_call x1, Pallas kernels, ssm_scan_direct(): pl.pallas_call(functools.partial(ssm_scan_direct_kernel, head_dim), grid_...  6.88 us
    all_to_all x1, waiting for transfers between devices, shards(): lax.all_to_all(computed.astype(jnp.bfloat16), 'head', split_axis=0, conca...  6.81 us
    all_to_all x1, waiting for transfers between devices, shards(): lax.all_to_all(outgoing, 'head', split_axis=0, concat_axis=0, tiled=True)  6.55 us
    pallas_call x1, Pallas kernels, xz_matmul(): pl.pallas_call(functools.partial(xz_matmul_kernel, head_dim), grid=(cols...  5.09 us
    all_to_all x1, waiting for transfers between devices, shards(): lax.all_to_all(mixer_part.reshape(head_count, tok_local, width), 'head',...  4.44 us
    dot_general x1, matrix products, shards(): jnp.dot(group_normed, weight_out, preferred_element_type=jnp.float32)  3.72 us
  transfers between devices with their start and end apart: 5, of which 4 were waited for; matrix products, arithmetic and copies ran while one was open for 18% of the time, Pallas kernels for 0%

profile of v18, /device:TPU:0, one launch (start us, length us, event | category | flops | bytes accessed | tf_op | source)
XLA Modules:
  0.0 93.6 jit_solution(7765640185196258518)
XLA Ops:
  0.6 0.0 copy-start
  0.6 0.0 copy-start.8
  0.7 1.5 %broadcast_in_dim.15 = bf16[8,4,2048]{2,1,0:T(4,128)(2,1)} broadcast(bf16[4,2048]{1,0:T(4,128)(2,1)} %bitcast.83), dimensions={1,2} | broadcast | bytes 147456 | tf_op jit(solution)/shard_map/broadcast_in_dim | solution.py:245
  2.2 7.3 %all-to-all-start = ((bf16[8,4,2048]{2,1,0:T(4,128)(2,1)}), bf16[8,4,2048]{2,1,0:T(4,128)(2,1)S(1)}, u32[]{:S(2)}, u32[]{:S(2)}) async-start(bf16[8,4,2048]{2,1,0:T(4,128)(2,1)} %broadcast_in_dim.15), calls=%async_computation | async-start | bytes 262144 | tf_op jit(solution)/shard_map/all_to_all | solution.py:246
  9.4 0.7 exponential_negate_fusion
  10.1 0.8 copy.68
  10.9 0.1 reshape_squeeze.7
  10.9 0.1 fusion.24
  11.0 0.8 fusion.30
  11.9 0.2 select_reduce_fusion
  12.1 0.7 copy.63
  12.8 0.7 mul.196
  13.5 0.1 mul.197
  13.6 0.8 copy.83
  14.3 2.3 %copy.64.s_ref = bf16[4,8,128,128]{3,2,1,0:T(8,128)(2,1)} copy(bf16[4,8,128,128]{2,3,1,0:T(8,128)(2,1)} %bitcast.81) | data formatting | bytes 2097152 | tf_op jit(solution)/shard_map/reshape | solution.py:319
  16.6 0.9 fusion.29
  17.5 0.0 all-to-all-done
  17.5 0.7 reshape.143.a_ref
  18.2 5.1 %shard_map.237 = (bf16[32,2048]{1,0:T(8,128)(2,1)}, bf16[32,1024]{1,0:T(8,128)(2,1)}, f32[32,1024]{1,0:T(8,128)}) custom-call(bf16[32,2048]{1,0:T(8,128)(2,1)} %reshape.143.a_ref, f32[1,2048]{1,0:T(1,128)} %bitcast.92, bf16[2048,2048]{1,0:T(8,128)(2,1)} %w_ref.1), custom_call_target="tpu_custom_call" | custom-call | flops 268435456 | bytes 8847360 | tf_op jit(solution)/shard_map/pallas_call | solution.py:100
  23.3 0.0 copy-start.2
  23.3 0.0 copy-start.5
  23.3 0.0 copy-start.10
  23.3 1.2 %fusion.5 = bf16[4,8,256]{2,1,0:T(8,128)(2,1)S(1)} fusion(bf16[32,2048]{1,0:T(8,128)(2,1)} %get-tuple-element.12, bf16[2048,256]{1,0:T(8,128)(2,1)S(1)} %copy-done), kind=kOutput, calls=%fused_computation.10 | convolution fusion | flops 33562624 | bytes 1196032 | tf_op jit(solution)/shard_map/dot_general | solution.py:285
  24.6 0.7 broadcast_in_dim.17
  25.3 6.0 %all-to-all-start.1 = ((bf16[8,4,8,256]{3,2,1,0:T(8,128)(2,1)}), bf16[8,4,8,256]{3,2,1,0:T(8,128)(2,1)S(1)}, u32[]{:S(2)}, u32[]{:S(2)}) async-start(bf16[8,4,8,256]{3,2,1,0:T(8,128)(2,1)} %broadcast_in_dim.17), calls=%async_computation.1 | async-start | bytes 262144 | tf_op jit(solution)/shard_map/all_to_all | solution.py:246
  31.3 0.0 copy-done.4
  31.3 1.1 %multiply_exponential_fusion = (f32[4,8,16]{2,1,0:T(8,128)S(1)}, f32[4,8,16]{2,1,0:T(8,128)S(1)}) fusion(f32[16]{0:T(128)S(1)} %exponential_negate_fusion, f32[16]{0:T(128)S(1)} %copy-done.9, bf16[32,2048]{1,0:T(8,128)(2,1)} %get-tuple-element.12, bf16[2048,16]{0,1:T(8,128)(2,1)S(1)} %copy-done.4), kind=kOutput, calls=%fused_computation.48 | convolution fusion | flops 2101248 | bytes 200832 | tf_op jit(solution)/shard_map/dot_general | solution.py:295
  32.4 0.1 broadcast_in_dim.16
  32.5 0.8 reshape.146.dec_ref
  33.3 0.1 mul.167
  33.4 0.1 mul.168
  33.6 0.9 maximum_convert_fusion
  34.4 0.7 broadcast_multiply_fusion
  35.2 0.7 mul.195.dx_ref
  35.9 2.8 %all-to-all-done.1.b_ref.c_ref = bf16[8,4,8,256]{3,2,1,0:T(8,128)(2,1)S(1)} async-done(((bf16[8,4,8,256]{3,2,1,0:T(8,128)(2,1)}), bf16[8,4,8,256]{3,2,1,0:T(8,128)(2,1)S(1)}, u32[]{:S(2)}, u32[]{:S(2)}) %all-to-all-start.1) | async-done | bytes 131104 | tf_op jit(solution)/shard_map/all_to_all | solution.py:246
  38.6 0.6 copy-done.1
  39.3 6.9 %shard_map.238 = (bf16[4,8,128,128]{3,2,1,0:T(8,128)(2,1)}, f32[4,8,1024]{2,1,0:T(8,128)}, bf16[4,8,1024]{2,1,0:T(8,128)(2,1)}) custom-call(s32[1]{0:T(128)S(6)} %select_n.16.group_ref, bf16[4,8,128,128]{3,2,1,0:T(8,128)(2,1)} %copy.64.s_ref, f32[4,8,1024]{2,1,0:T(8,128)} %reshape.146.dec_ref, f32[4,8,1024]{2,1,0:T(8,128)} %mul.195.dx_ref, ...), custom_call_target="tpu_custom_call" | custom-call | tf_op jit(solution)/shard_map/pallas_call | solution.py:215
  46.1 0.9 dot_general.31
  47.0 3.7 %fusion = f32[8,4,2048]{2,1,0:T(4,128)} fusion(bf16[8,4,1024]{2,1,0:T(4,128)(2,1)S(1)} %dot_general.31, bf16[1024,2048]{1,0:T(8,128)(2,1)} %param.39), kind=kOutput, calls=%fused_computation | convolution fusion | flops 134217728 | bytes 4521984 | tf_op jit(solution)/shard_map/dot_general | solution.py:359
  50.7 3.4 %all-to-all-start.2 = ((f32[8,4,2048]{2,1,0:T(4,128)}), f32[8,4,2048]{2,1,0:T(4,128)S(1)}, u32[]{:S(2)}, u32[]{:S(2)}) async-start(f32[8,4,2048]{2,1,0:T(4,128)} %fusion), calls=%async_computation.2 | async-start | bytes 524288 | tf_op jit(solution)/shard_map/all_to_all | solution.py:360
  54.2 0.0 copy-done.7
  54.2 0.1 copy.67
  54.3 0.1 iota_compare_fusion.3
  54.4 0.6 copy.84
  55.0 0.0 copy-done.3
  55.0 0.6 copy.72
  55.6 2.3 %copy.70 = bf16[4,8,128,128]{2,3,1,0:T(8,128)(2,1)} copy(bf16[4,8,128,128]{3,2,1,0:T(8,128)(2,1)} %get-tuple-element.19) | data formatting | bytes 2097152 | tf_op jit(solution)/shard_map/pallas_call | solution.py:215
  57.9 4.4 %all-to-all-done.2 = f32[8,4,2048]{2,1,0:T(4,128)S(1)} async-done(((f32[8,4,2048]{2,1,0:T(4,128)}), f32[8,4,2048]{2,1,0:T(4,128)S(1)}, u32[]{:S(2)}, u32[]{:S(2)}) %all-to-all-start.2) | async-done | bytes 262176 | tf_op jit(solution)/shard_map/all_to_all | solution.py:360
  62.4 0.1 fusion.12
  62.5 0.0 copy-done.5
  62.5 0.1 fusion.14
  62.6 0.1 fusion.31
  62.8 0.1 convolution_convert_fusion
  62.9 0.7 reshape_broadcast_in_dim_reshape.3
  63.6 3.3 %all-to-all-start.3 = ((bf16[8,2,2048]{2,1,0:T(2,128)(2,1)}), bf16[8,2,2048]{2,1,0:T(2,128)(2,1)S(1)}, u32[]{:S(2)}, u32[]{:S(2)}) async-start(bf16[8,2,2048]{2,1,0:T(2,128)(2,1)} %reshape_broadcast_in_dim_reshape.3), calls=%async_computation.3 | async-start | bytes 131072 | tf_op jit(solution)/shard_map/all_to_all | solution.py:375
  67.0 0.2 fusion.21
  67.2 0.1 copy.77
  67.3 6.5 %all-to-all-done.3 = bf16[8,2,2048]{2,1,0:T(2,128)(2,1)S(1)} async-done(((bf16[8,2,2048]{2,1,0:T(2,128)(2,1)}), bf16[8,2,2048]{2,1,0:T(2,128)(2,1)S(1)}, u32[]{:S(2)}, u32[]{:S(2)}) %all-to-all-start.3) | async-done | bytes 65568 | tf_op jit(solution)/shard_map/all_to_all | solution.py:375
  73.8 8.0 %convolution_convert_fusion.1 = bf16[16,2048]{1,0:T(8,128)(2,1)S(1)} fusion(bf16[2048,2048]{1,0:T(8,128)(2,1)} %param.43, bf16[16,2048]{1,0:T(8,128)(2,1)S(1)} %reshape.150, bf16[2048,2048]{1,0:T(8,128)(2,1)} %param.42), kind=kOutput, calls=%fused_computation.6 | convolution fusion | flops 268566528 | bytes 16908288 | tf_op jit(solution)/shard_map/dot_general | solution.py:378
  81.9 0.7 convert_element_type.76
  82.6 3.3 %all-to-all-start.4 = ((bf16[8,2,2048]{2,1,0:T(2,128)(2,1)}), bf16[8,2,2048]{2,1,0:T(2,128)(2,1)S(1)}, u32[]{:S(2)}, u32[]{:S(2)}) async-start(bf16[8,2,2048]{2,1,0:T(2,128)(2,1)} %convert_element_type.76), calls=%async_computation.4 | async-start | bytes 131072 | tf_op jit(solution)/shard_map/all_to_all | solution.py:381
  86.0 6.8 %all-to-all-done.4 = bf16[8,2,2048]{2,1,0:T(2,128)(2,1)S(1)} async-done(((bf16[8,2,2048]{2,1,0:T(2,128)(2,1)}), bf16[8,2,2048]{2,1,0:T(2,128)(2,1)S(1)}, u32[]{:S(2)}, u32[]{:S(2)}) %all-to-all-start.4) | async-done | bytes 65568 | tf_op jit(solution)/shard_map/all_to_all | solution.py:381
  92.8 0.1 fusion.4
  93.0 0.6 fusion.19
  (27 shorter events, 0.3 us)
Async XLA Ops:
  0.6 22.7 %copy-start = (bf16[2048,256]{1,0:T(8,128)(2,1)S(1)}, bf16[2048,256]{1,0:T(8,128)(2,1)}, u32[]{:S(2)}) copy-start(bf16[2048,256]{1,0:T(8,128)(2,1)} %param.29) | copy-start | bytes 3145732
  0.6 23.9 %copy-start.8 = (f32[256]{0:T(256)S(1)}, f32[256]{0:T(256)}, u32[]{:S(2)}) copy-start(f32[256]{0:T(256)} %param.37) | copy-start | bytes 3076
  0.7 30.6 %copy-start.9 = (f32[16]{0:T(128)S(1)}, f32[16]{0:T(128)}, u32[]{:S(2)}) copy-start(f32[16]{0:T(128)} %param.31) | copy-start | bytes 196
  0.7 30.6 %copy-start.4 = (bf16[2048,16]{0,1:T(8,128)(2,1)S(1)}, bf16[2048,16]{0,1:T(8,128)(2,1)}, u32[]{:S(2)}) copy-start(bf16[2048,16]{0,1:T(8,128)(2,1)} %param.30) | copy-start | bytes 196612
  0.7 33.8 %copy-start.6 = (f32[1024]{0:T(1024)S(1)}, f32[1024]{0:T(1024)}, u32[]{:S(2)}) copy-start(f32[1024]{0:T(1024)} %param.35) | copy-start | bytes 12292
  2.2 15.3 %all-to-all-start = ((bf16[8,4,2048]{2,1,0:T(4,128)(2,1)}), bf16[8,4,2048]{2,1,0:T(4,128)(2,1)S(1)}, u32[]{:S(2)}, u32[]{:S(2)}) async-start(bf16[8,4,2048]{2,1,0:T(4,128)(2,1)} %broadcast_in_dim.15), calls=%async_computation | async-start | bytes 262144 | tf_op jit(solution)/shard_map/all_to_all | solution.py:246
  23.3 30.9 %copy-start.7 = (s32[1,4,2]{1,2,0:T(2,128)S(1)}, s32[1,4,2]{1,2,0:T(2,128)}, u32[]{:S(2)}) copy-start(s32[1,4,2]{1,2,0:T(2,128)} %param.26) | copy-start | bytes 100
  23.3 31.7 %copy-start.3 = (bf16[32,1024]{1,0:T(8,128)(2,1)S(1)}, bf16[32,1024]{1,0:T(8,128)(2,1)}, u32[]{:S(2)}) copy-start(bf16[32,1024]{1,0:T(8,128)(2,1)} %get-tuple-element.15) | copy-start | bytes 196612
  23.3 39.1 %copy-start.2 = (bf16[1,4,2048]{2,1,0:T(4,128)(2,1)S(1)}, bf16[1,4,2048]{2,1,0:T(4,128)(2,1)}, u32[]{:S(2)}) copy-start(bf16[1,4,2048]{2,1,0:T(4,128)(2,1)} %param.22) | copy-start | bytes 49156
  23.3 39.2 %copy-start.5 = (f32[2048]{0:T(1024)S(1)}, f32[2048]{0:T(1024)}, u32[]{:S(2)}) copy-start(f32[2048]{0:T(1024)} %param.40) | copy-start | bytes 24580
  23.3 39.3 %copy-start.10 = (bf16[2048,8]{0,1:T(8,128)(2,1)S(1)}, bf16[2048,8]{0,1:T(8,128)(2,1)}, u32[]{:S(2)}) copy-start(bf16[2048,8]{0,1:T(8,128)(2,1)} %param.41) | copy-start | bytes 98308
  25.3 13.3 %all-to-all-start.1 = ((bf16[8,4,8,256]{3,2,1,0:T(8,128)(2,1)}), bf16[8,4,8,256]{3,2,1,0:T(8,128)(2,1)S(1)}, u32[]{:S(2)}, u32[]{:S(2)}) async-start(bf16[8,4,8,256]{3,2,1,0:T(8,128)(2,1)} %broadcast_in_dim.17), calls=%async_computation.1 | async-start | bytes 262144 | tf_op jit(solution)/shard_map/all_to_all | solution.py:246
  38.6 0.6 copy-start.1
  50.7 11.6 %all-to-all-start.2 = ((f32[8,4,2048]{2,1,0:T(4,128)}), f32[8,4,2048]{2,1,0:T(4,128)S(1)}, u32[]{:S(2)}, u32[]{:S(2)}) async-start(f32[8,4,2048]{2,1,0:T(4,128)} %fusion), calls=%async_computation.2 | async-start | bytes 524288 | tf_op jit(solution)/shard_map/all_to_all | solution.py:360
  63.6 10.2 %all-to-all-start.3 = ((bf16[8,2,2048]{2,1,0:T(2,128)(2,1)}), bf16[8,2,2048]{2,1,0:T(2,128)(2,1)S(1)}, u32[]{:S(2)}, u32[]{:S(2)}) async-start(bf16[8,2,2048]{2,1,0:T(2,128)(2,1)} %reshape_broadcast_in_dim_reshape.3), calls=%async_computation.3 | async-start | bytes 131072 | tf_op jit(solution)/shard_map/all_to_all | solution.py:375
  82.6 10.2 %all-to-all-start.4 = ((bf16[8,2,2048]{2,1,0:T(2,128)(2,1)}), bf16[8,2,2048]{2,1,0:T(2,128)(2,1)S(1)}, u32[]{:S(2)}, u32[]{:S(2)}) async-start(bf16[8,2,2048]{2,1,0:T(2,128)(2,1)} %convert_element_type.76), calls=%async_computation.4 | async-start | bytes 131072 | tf_op jit(solution)/shard_map/all_to_all | solution.py:381
